TPU v7x, 32 devices: a whole 2x2x4 slice. The times are simulated.
32 devices in a mesh: pipe: 2 (over y), ctx: 4 (over z), dp: 4 (over x, core).
Axes of the slice: x: 2, y: 2, z: 4, core: 2. Of those that a mesh axis runs over, the one named last changes fastest.
Arguments:
- query: bfloat16 [8, 512, 2048], P(('dp', 'pipe'), 'ctx'), parts along dimension 0, may hold values from -6 to 6
- keys: bfloat16 [8, 512, 512], P(('dp', 'pipe'), 'ctx'), parts along dimension 0, may hold values from -6 to 6
- values: bfloat16 [8, 512, 512], P(('dp', 'pipe'), 'ctx'), parts along dimension 0, may hold values from -6 to 6
- grad_out: bfloat16 [8, 512, 2048], P(('dp', 'pipe'), 'ctx'), parts along dimension 0, may hold values from -6 to 6
- random_blocks: int32 [2, 8, 16, 8], P('pipe', 'ctx'), may hold values from 0 to 1, as said below
- global_ids: int32 [2, 2], P('pipe'), may hold values from 0 to 7, as said below
Outputs:
- next_input: bfloat16 [8, 512, 2048], P(('dp', 'pipe'), 'ctx'), parts along dimension 0
- grad_query: bfloat16 [8, 512, 2048], P(('dp', 'pipe'), 'ctx'), parts along dimension 0
- grad_key: bfloat16 [8, 512, 512], P(('dp', 'pipe'), 'ctx'), parts along dimension 0
- grad_value: bfloat16 [8, 512, 512], P(('dp', 'pipe'), 'ctx'), parts along dimension 0
There are 4 independent parts, one for each index of `dp`. A program takes and returns all parts, laid end to end along the dimension named above; an argument that names none is the same for every part. Nothing has to cross between parts.
Inputs may be any that keep to these rules, and one draw needn't show every extreme that they name: `random_blocks`: for each section, query block and head exactly 3 entries are 1 and the others 0. `global_ids`: for each section, 2 different block numbers; those of section 0 include block 0 and block 7.
All inputs are finite; a program needn't handle non-finite values.
Results may differ from a plain program's by a relative error of at most 0.014.
Values may be sent and summed in bfloat16 or wider, within the bound.
No kernel may reach another device: no remote copies, remote signals or barrier semaphores. Data moves between devices by JAX's collectives and lax.ppermute only.
A program may use at most 64 MiB of HBM per device.

v0:
```python
import jax
import jax.numpy as jnp
from jax import lax
from jax.sharding import PartitionSpec as P

H = 16
KVH = 4
HD = 128
BLOCK = 64


NEG_FILL = -1e30


def passed_along(value, axis, steps):
    count = lax.axis_size(axis)
    pairs = [(source, (source + steps) % count) for source in range(count)]
    return lax.ppermute(value, axis, pairs)


def block_table(random_rows, global_row, first_block):
    query_blocks, head_count, key_blocks = random_rows.shape
    query_ids = first_block + jnp.arange(query_blocks, dtype=jnp.int32)
    key_ids = jnp.arange(key_blocks, dtype=jnp.int32)
    query_global = jnp.any(query_ids[:, None] == global_row[None, :], axis=1)
    key_global = jnp.any(key_ids[:, None] == global_row[None, :], axis=1)
    nearby = jnp.abs(query_ids[:, None] - key_ids[None, :]) <= 1
    fixed_part = nearby | query_global[:, None] | key_global[None, :]
    return (random_rows > 0) | fixed_part[:, None, :]


def token_mask(table_part, first_query, first_key):
    query_blocks, head_count, key_blocks = table_part.shape
    expanded = jnp.broadcast_to(
        table_part[:, None, :, :, None], (query_blocks, BLOCK, head_count, key_blocks, BLOCK)
    )
    expanded = expanded.reshape(query_blocks * BLOCK, head_count, key_blocks * BLOCK)
    query_pos = first_query + jnp.arange(query_blocks * BLOCK, dtype=jnp.int32)
    key_pos = first_key + jnp.arange(key_blocks * BLOCK, dtype=jnp.int32)
    return expanded & (key_pos[None, None, :] <= query_pos[:, None, None])


def local(query, keys, values, grad_out, random_blocks, global_ids):
    tok_rows = query.shape[1]
    query_width = query.shape[2]
    key_width = keys.shape[2]
    ctx_count = lax.axis_size("ctx")
    seq_len = tok_rows * ctx_count
    group_size = H // KVH
    score_scale = HD ** (-0.5)
    ctx_index = lax.axis_index("ctx")
    first_query = ctx_index * tok_rows
    query_blocks = tok_rows // BLOCK
    table = block_table(random_blocks[0], global_ids[0], ctx_index * query_blocks)
    block_count = table.shape[2]
    query_ids = ctx_index * query_blocks + jnp.arange(query_blocks, dtype=jnp.int32)
    key_ids = jnp.arange(block_count, dtype=jnp.int32)
    usable = table & (key_ids[None, None, :] <= query_ids[:, None, None])
    query_heads = query[0].reshape(tok_rows, KVH, group_size, HD)
    grad_heads = grad_out[0].reshape(tok_rows, KVH, group_size, HD)
    shards_per_step = max(1, min(ctx_count, 512 // tok_rows))
    while ctx_count % shards_per_step != 0:
        shards_per_step = shards_per_step - 1
    step_rows = shards_per_step * tok_rows
    step_count = seq_len // step_rows

    def piece_hit(first_row, piece_rows):
        return jnp.any(lax.dynamic_slice_in_dim(usable, first_row // BLOCK, piece_rows // BLOCK, 2))

    def scores_for(key_piece, first_row):
        piece_rows = key_piece.shape[0]
        raw_scores = (
            jnp.einsum("tkgd,ukd->tkgu", query_heads, key_piece, preferred_element_type=jnp.float32)
            * score_scale
        )
        table_part = lax.dynamic_slice_in_dim(table, first_row // BLOCK, piece_rows // BLOCK, 2)
        allowed = token_mask(table_part, first_query, first_row).reshape(
            tok_rows, KVH, group_size, piece_rows
        )
        return (raw_scores, allowed)

    start_state = (
        jnp.full((tok_rows, KVH, group_size), NEG_FILL, jnp.float32),
        jnp.zeros((tok_rows, KVH, group_size), jnp.float32),
        jnp.zeros((tok_rows, KVH, group_size, HD), jnp.float32),
    )
    first_row = jnp.int32(0)
    key_piece = lax.all_gather(keys, "ctx", axis=1, tiled=True)[0].reshape(-1, KVH, HD)
    value_piece = lax.all_gather(values, "ctx", axis=1, tiled=True)[0].reshape(-1, KVH, HD)
    piece_rows = key_piece.shape[0]

    def update(state_old):
        run_high, row_total, accumulated = state_old
        raw_scores, allowed = scores_for(key_piece, first_row)
        new_high = jnp.maximum(run_high, jnp.max(jnp.where(allowed, raw_scores, NEG_FILL), axis=-1))
        weights = jnp.where(allowed, jnp.exp(raw_scores - new_high[..., None]), 0.0)
        row_total = jnp.sum(weights, axis=-1)
        accumulated = jnp.einsum(
            "tkgu,ukd->tkgd",
            weights.astype(jnp.bfloat16),
            value_piece,
            preferred_element_type=jnp.float32,
        )
        return (new_high, row_total, accumulated)

    final_state = lax.cond(
        piece_hit(first_row, piece_rows), update, lambda state_same: state_same, start_state
    )
    whole_keys, whole_values = (
        lax.all_gather(keys, "ctx", axis=1, tiled=True),
        lax.all_gather(values, "ctx", axis=1, tiled=True),
    )
    run_high, row_total, accumulated = final_state
    attended = (accumulated / row_total[..., None]).astype(jnp.bfloat16)
    log_total = run_high + jnp.log(row_total)
    next_input = passed_along(attended.reshape(tok_rows, query_width)[None], "pipe", 1)
    delta = jnp.sum(grad_heads.astype(jnp.float32) * attended.astype(jnp.float32), axis=-1)

    def backward_step(query_accum, step_index):
        first_row = step_index * step_rows
        key_piece = lax.dynamic_slice_in_dim(whole_keys[0], first_row, step_rows, 0).reshape(
            step_rows, KVH, HD
        )
        value_piece = lax.dynamic_slice_in_dim(whole_values[0], first_row, step_rows, 0).reshape(
            step_rows, KVH, HD
        )

        def compute(accum_old):
            raw_scores, allowed = scores_for(key_piece, first_row)
            row_probs = jnp.where(allowed, jnp.exp(raw_scores - log_total[..., None]), 0.0)
            value_term = jnp.einsum(
                "tkgu,tkgd->ukd",
                row_probs.astype(jnp.bfloat16),
                grad_heads,
                preferred_element_type=jnp.float32,
            )
            prob_grads = jnp.einsum(
                "tkgd,ukd->tkgu", grad_heads, value_piece, preferred_element_type=jnp.float32
            )
            score_grads = (row_probs * (prob_grads - delta[..., None])).astype(jnp.bfloat16)
            accum_new = accum_old + jnp.einsum(
                "tkgu,ukd->tkgd", score_grads, key_piece, preferred_element_type=jnp.float32
            )
            key_term = (
                jnp.einsum(
                    "tkgu,tkgd->ukd", score_grads, query_heads, preferred_element_type=jnp.float32
                )
                * score_scale
            )
            return (
                accum_new,
                key_term.reshape(step_rows, key_width),
                value_term.reshape(step_rows, key_width),
            )

        def skip_piece(accum_old):
            zero_term = jnp.zeros((step_rows, key_width), jnp.float32)
            return (accum_old, zero_term, zero_term)

        accum_new, key_term, value_term = lax.cond(
            piece_hit(first_row, step_rows), compute, skip_piece, query_accum
        )
        return (accum_new, (key_term, value_term))

    query_accum, step_terms = lax.scan(
        backward_step,
        jnp.zeros((tok_rows, KVH, group_size, HD), jnp.float32),
        jnp.arange(step_count, dtype=jnp.int32),
    )
    key_terms = step_terms[0].reshape(seq_len, key_width)
    value_terms = step_terms[1].reshape(seq_len, key_width)
    key_own, value_own = (
        lax.psum_scatter(
            key_terms.astype(jnp.bfloat16), "ctx", scatter_dimension=0, tiled=True
        ).astype(jnp.float32),
        lax.psum_scatter(
            value_terms.astype(jnp.bfloat16), "ctx", scatter_dimension=0, tiled=True
        ).astype(jnp.float32),
    )
    query_grad = (query_accum * score_scale).astype(jnp.bfloat16).reshape(tok_rows, query_width)
    packed = jnp.concatenate(
        [query_grad, key_own.astype(jnp.bfloat16), value_own.astype(jnp.bfloat16)], axis=1
    )
    returned = passed_along(packed[None], "pipe", -1)
    grad_query = returned[:, :, :query_width]
    grad_key = returned[:, :, query_width : query_width + key_width]
    grad_value = returned[:, :, query_width + key_width :]
    return (next_input, grad_query, grad_key, grad_value)


def solution(mesh):
    placed = (
        P(("dp", "pipe"), "ctx", None),
        P(("dp", "pipe"), "ctx", None),
        P(("dp", "pipe"), "ctx", None),
        P(("dp", "pipe"), "ctx", None),
        P("pipe", "ctx", None, None),
        P("pipe", None),
    )
    return jax.shard_map(
        local,
        mesh=mesh,
        in_specs=placed,
        out_specs=(
            P(("dp", "pipe"), "ctx", None),
            P(("dp", "pipe"), "ctx", None),
            P(("dp", "pipe"), "ctx", None),
            P(("dp", "pipe"), "ctx", None),
        ),
        check_vma=False,
    )
```

profile of v0, /device:TPU:0, one launch (start us, length us, event | category | flops | bytes accessed | tf_op | source)
XLA Modules:
  0.0 169.6 jit_solution(14056376339397560336)
XLA Ops:
  7.2 0.0 reduce-scatter.3.cloned.1.call-start
  7.2 0.7 compare_reduce_fusion
  8.0 0.8 compare_reduce_fusion.1
  8.8 0.7 broadcast_compare_fusion
  9.5 0.1 copy.123
  9.6 0.1 or_or_fusion
  9.7 0.7 and_reduce_fusion
  11.0 1.0 copy.85
  12.0 1.0 copy.87
  13.1 17.1 %all_gather.9 = bf16[1,512,512]{1,2,0:T(8,128)(2,1)} all-gather(bf16[1,128,512]{1,2,0:T(8,128)(2,1)S(1)} %copy.87), channel_id=1, replica_groups=mesh['pipe'=2,'ctx'=4,'dp'=4] {'ctx'}, dimensions={1}, use_global_device_ids=true | all-gather | bytes 655360 | tf_op jit(solution)/shard_map/all_gather | solution.py:89
  30.1 14.8 %all_gather.8 = bf16[1,512,512]{1,2,0:T(8,128)(2,1)S(1)} all-gather(bf16[1,128,512]{1,2,0:T(8,128)(2,1)S(1)} %copy.85), channel_id=1, replica_groups=mesh['pipe'=2,'ctx'=4,'dp'=4] {'ctx'}, dimensions={1}, use_global_device_ids=true | all-gather | bytes 655360 | tf_op jit(solution)/shard_map/all_gather | solution.py:88
  44.9 1.3 copy.86
  46.2 16.4 %conditional.2 = (f32[128,4,4]{0,2,1:T(4,128)}, f32[128,4,4]{0,2,1:T(4,128)}, f32[128,4,4]{0,2,1:T(4,128)S(1)}, f32[128,4,4,128]{0,3,2,1:T(8,128)S(1)}) conditional(s32[]{:T(128)} %convert_element_type.40, () %tuple.32, (pred[2,16,8]{2,0,1:T(4,128)(4,1)S(1)}, s32[]{:T(128)}, bf16[512,4,128]{0,2,1:T(8,128)(2,1)S(1)}, ...), branch_computations={%region_3.4_spmd, %region_4.7_spmd} | conditional | flops 551614592 | bytes 28116288 | solution.py:106
  46.3 2.0 %broadcast_in_dim.33 = pred[2,64,16,8,64]{4,3,1,0,2:T(8,128)(4,1)} broadcast(pred[2,16,8]{2,0,1:T(4,128)(4,1)S(1)} %get-tuple-element.103), dimensions={0,2,3} | broadcast | bytes 1048832 | tf_op jit(solution)/shard_map/cond/branch_1_fun/broadcast_in_dim | solution.py:34
  48.3 5.5 %reshape.182 = pred[128,4,4,512]{3,0,2,1:T(32,128)(4,1)S(1)} reshape(pred[2,64,16,8,64]{4,3,1,0,2:T(8,128)(4,1)} %broadcast_in_dim.33) | data formatting | bytes 2097152 | tf_op jit(solution)/shard_map/cond/branch_1_fun/reshape | solution.py:37
  53.8 1.2 copy.76
  55.0 1.2 fusion
  56.2 0.0 copy-start.3
  56.2 0.6 broadcast_maximum_fusion
  56.8 2.5 %fusion.4 = f32[128,4,4]{0,2,1:T(4,128)} fusion(f32[4,512,128,4]{2,1,3,0:T(8,128)S(1)} %get-tuple-element.204, pred[128,4,4,512]{0,3,2,1:T(32,128)(4,1)S(1)} %copy.76, f32[128,4,4]{0,2,1:T(4,128)} %broadcast_maximum_fusion, pred[128,512]{0,1:T(8,128)(4,1)S(1)} %iota_compare_fusion), kind=kLoop, calls=%fused_computation.6 | loop fusion | flops 5240832 | bytes 5324800 | tf_op jit(solution)/shard_map/cond/branch_1_fun/reduce_sum | solution.py:97
  59.3 0.0 copy-done.3
  59.3 2.3 %fusion.8 = f32[128,4,4,128]{3,0,2,1:T(8,128)S(1)} fusion(f32[4,512,128,4]{2,1,3,0:T(8,128)S(1)} %get-tuple-element.204, pred[128,4,4,512]{0,3,2,1:T(32,128)(4,1)S(1)} %copy.76, f32[128,4,4]{0,2,1:T(4,128)} %broadcast_maximum_fusion, pred[128,512]{0,1:T(8,128)(4,1)S(1)} %iota_compare_fusion, bf16[512,4,128]{0,2,1:T(8,128)(2,1)S(1)} %copy-done.3), kind=kOutput, calls=%fused_computation.9 | convolution fusion | flops 273678336 | bytes 6889472 | tf_op jit(solution)/shard_map/cond/branch_1_fun/tkgu,ukd->tkgd/dot_general | solution.py:98
  61.6 0.3 copy.122
  61.9 0.7 log.5
  62.6 1.7 fusion.32
  64.3 0.1 broadcast.148
  64.4 19.4 %conditional.3 = (f32[128,4,4,128]{3,0,2,1:T(8,128)S(1)}, bf16[512,512]{0,1:T(8,128)(2,1)S(1)}, bf16[512,512]{0,1:T(8,128)(2,1)}) conditional(s32[]{:T(128)} %convert_element_type.40, f32[128,4,4,128]{3,0,2,1:T(8,128)S(1)} %broadcast.148, (pred[2,16,8]{2,0,1:T(4,128)(4,1)S(1)}, s32[]{:T(128)}, bf16[512,4,128]{0,2,1:T(8,128)(2,1)S(1)}, ...), branch_computations={%region_7.8_spmd, %region_8.10_spmd} | conditional | flops 1356398720 | bytes 40101204 | solution.py:160
  64.6 0.7 add.71
  65.4 2.0 %copy.94 = bf16[1,128,2048]{1,2,0:T(8,128)(2,1)} copy(bf16[1,128,2048]{2,1,0:T(8,128)(2,1)} %get-tuple-element.194) | data formatting | bytes 1048576 | tf_op jit(solution)/shard_map
  67.4 1.2 multiply_reduce_fusion
  68.6 2.0 %broadcast_in_dim.37 = pred[2,64,16,8,64]{4,3,1,0,2:T(8,128)(4,1)} broadcast(pred[2,16,8]{2,0,1:T(4,128)(4,1)S(1)} %get-tuple-element.109), dimensions={0,2,3} | broadcast | bytes 1048832 | tf_op jit(solution)/shard_map/while/body/eval_jaxpr/cond/branch_1_fun/broadcast_in_dim | solution.py:34
  70.6 5.5 %reshape.183 = pred[128,4,4,512]{3,0,2,1:T(32,128)(4,1)S(1)} reshape(pred[2,64,16,8,64]{4,3,1,0,2:T(8,128)(4,1)} %broadcast_in_dim.37) | data formatting | bytes 2097152 | tf_op jit(solution)/shard_map/while/body/eval_jaxpr/cond/branch_1_fun/reshape | solution.py:37
  76.1 0.0 copy-start.1
  76.1 1.2 copy.78
  77.3 0.7 fusion.28
  78.0 0.0 copy-done.1
  78.0 0.0 copy-start.4
  78.0 2.1 %fusion.21 = bf16[4,512,128,1]{1,2,3,0:T(8,128)(2,1)} fusion(bf16[128,4,4,128]{0,3,2,1:T(8,128)(2,1)S(1)} %bitcast.109, f32[4,512,128,4]{2,1,3,0:T(8,128)S(1)} %fusion.28, pred[128,4,4,512]{0,3,2,1:T(32,128)(4,1)S(1)} %copy.78, f32[128,4,4]{0,2,1:T(4,128)S(1)} %add.71, pred[128,512]{0,1:T(8,128)(4,1)S(1)} %iota_compare_fusion.1), kind=kOutput, calls=%fused_computation.25 | convolution fusion | flops 273678336 | bytes 6365184 | tf_op jit(solution)/shard_map/while/body/eval_jaxpr/cond/branch_1_fun/tkgu,tkgd->ukd/dot_general | solution.py:131
  80.1 0.0 copy-done.4
  80.1 1.7 fusion.17
  81.8 1.2 fusion.24
  83.0 0.8 fusion.25
  83.9 0.0 copy-start.2
  83.9 0.8 copy-done.2
  84.7 2.1 %copy.97 = bf16[512,512]{1,0:T(8,128)(2,1)} copy(bf16[512,512]{0,1:T(8,128)(2,1)} %copy-done.2) | data formatting | bytes 1048576 | tf_op jit(solution)/shard_map/while/body/eval_jaxpr/cond | solution.py:160
  86.8 0.0 reduce-scatter.3.cloned.1.call-update
  86.8 0.0 reduce-scatter.5.cloned.1.call-start
  86.9 2.1 %copy.98 = bf16[512,512]{1,0:T(8,128)(2,1)} copy(bf16[512,512]{0,1:T(8,128)(2,1)} %get-tuple-element.135) | data formatting | bytes 1048576 | tf_op jit(solution)/shard_map/while/body/eval_jaxpr/cond | solution.py:160
  88.9 0.0 reduce-scatter.5.cloned.1.call-update
  88.9 0.1 multiply_convert_fusion
  89.1 0.4 copy.96
  89.5 0.4 reshape.187
  89.9 18.4 %reduce-scatter.3.cloned.1.call-done = bf16[128,512]{1,0:T(8,128)(2,1)} async-done(((bf16[512,512]{1,0:T(8,128)(2,1)}), bf16[128,512]{1,0:T(8,128)(2,1)}) %reduce-scatter.3.cloned.1.call-update) | async-done | bytes 131088 | tf_op jit(solution)/shard_map/reduce_scatter | solution.py:173
  108.3 22.2 %reduce-scatter.5.cloned.1.call-done = bf16[128,512]{1,0:T(8,128)(2,1)} async-done(((bf16[512,512]{1,0:T(8,128)(2,1)}), bf16[128,512]{1,0:T(8,128)(2,1)}) %reduce-scatter.5.cloned.1.call-update) | async-done | bytes 131088 | tf_op jit(solution)/shard_map/reduce_scatter | solution.py:176
  130.5 1.0 maximum_bitcast_fusion
  131.5 1.6 collective-permute-start.1
  133.1 0.0 copy-done
  133.1 0.2 copy.120
  133.3 0.6 collective-permute-start
  133.9 26.5 %collective-permute-done = bf16[1,128,2048]{2,1,0:T(8,128)(2,1)S(1)} collective-permute-done((bf16[1,128,2048]{2,1,0:T(8,128)(2,1)S(1)}, bf16[1,128,2048]{2,1,0:T(8,128)(2,1)S(1)}, u32[]{:S(2)}, u32[]{:S(2)}) %collective-permute-start) | collective-permute-done | bytes 524320 | tf_op jit(solution)/shard_map/ppermute | solution.py:18
  160.4 0.0 collective-permute-done.1
  160.4 0.7 fusion.33
  161.1 0.8 slice.12
  162.0 0.8 copy.144
  (6 shorter events, 0.1 us)
Async XLA Ops:
  7.2 101.1 %reduce-scatter.3.cloned.1.call-start = ((), (), s32[]{:S(2)}) async-start(), calls=%async_computation.2 | async-start | bytes 655360 | tf_op jit(solution)/shard_map/reduce_scatter | solution.py:173
  56.2 3.2 %copy-start.3 = (bf16[512,4,128]{0,2,1:T(8,128)(2,1)S(1)}, bf16[512,4,128]{0,2,1:T(8,128)(2,1)}, u32[]{:S(2)}) copy-start(bf16[512,4,128]{0,2,1:T(8,128)(2,1)} %get-tuple-element.187) | copy-start | bytes 1572868 | tf_op jit(solution)/shard_map/cond
  76.1 1.9 %copy-start.1 = (bf16[1,128,2048]{1,2,0:T(8,128)(2,1)S(1)}, bf16[1,128,2048]{1,2,0:T(8,128)(2,1)}, u32[]{:S(2)}) copy-start(bf16[1,128,2048]{1,2,0:T(8,128)(2,1)} %copy.94) | copy-start | bytes 1572868 | tf_op jit(solution)/shard_map/while/body/eval_jaxpr/cond
  78.0 2.1 %copy-start.4 = (bf16[512,4,128]{0,2,1:T(8,128)(2,1)S(1)}, bf16[512,4,128]{0,2,1:T(8,128)(2,1)}, u32[]{:S(2)}) copy-start(bf16[512,4,128]{0,2,1:T(8,128)(2,1)} %get-tuple-element.195) | copy-start | bytes 1572868 | tf_op jit(solution)/shard_map/while/body/eval_jaxpr/cond
  83.9 0.8 copy-start.2
  84.7 48.4 %copy-start = (bf16[128,4,4,128]{0,3,2,1:T(8,128)(2,1)S(1)}, bf16[128,4,4,128]{0,3,2,1:T(8,128)(2,1)}, u32[]{:S(2)}) copy-start(bf16[128,4,4,128]{0,3,2,1:T(8,128)(2,1)} %get-tuple-element.200) | copy-start | bytes 1572868
  86.8 43.7 %reduce-scatter.5.cloned.1.call-start = ((), (), s32[]{:S(2)}) async-start(), calls=%async_computation.3 | async-start | bytes 655360 | tf_op jit(solution)/shard_map/reduce_scatter | solution.py:176
  131.5 28.9 %collective-permute-start.1 = (bf16[1,128,3072]{2,1,0:T(8,128)(2,1)S(1)}, bf16[1,128,3072]{2,1,0:T(8,128)(2,1)S(1)}, u32[]{:S(2)}, u32[]{:S(2)}) collective-permute-start(bf16[1,128,3072]{2,1,0:T(8,128)(2,1)S(1)} %maximum_bitcast_fusion), channel_id=1, source_target_pairs={{0,16},{16,0},{1,17},{17,1},{2,18},{18,2},{3,19},{19,3},{4,20},{20... | collective-permute-start | bytes 2359304 | tf_op jit(solution)/shard_map/ppermute | solution.py:18
  133.3 27.1 %collective-permute-start = (bf16[1,128,2048]{2,1,0:T(8,128)(2,1)S(1)}, bf16[1,128,2048]{2,1,0:T(8,128)(2,1)S(1)}, u32[]{:S(2)}, u32[]{:S(2)}) collective-permute-start(bf16[1,128,2048]{2,1,0:T(8,128)(2,1)S(1)} %copy.120), channel_id=1, source_target_pairs={{0,16},{16,0},{1,17},{17,1},{2,18},{18,2},{3,19},{19,3},{4,20},{20... | collective-permute-start | bytes 1572872 | tf_op jit(solution)/shard_map/ppermute | solution.py:18
Sparse Core Ops, SparseCore 0:
  86.9 21.3 reduce-scatter.2
  110.6 19.8 reduce-scatter.4
where the time goes:
time: 170 us
  waiting for transfers between devices  67.1 us (39%)
  local copies, waits for them, and re-layouts  32.3 us (19%)
  blocking collectives  31.8 us (19%)
  between operations  14.8 us (9%)
  other arithmetic  11 us (6%)
  matrix products  10 us (6%)
  starting transfers between devices  2.24 us (1%)
    ppermute x2, waiting for transfers between devices, passed_along(): return lax.ppermute(value, axis, pairs)  26.5 us
    reduce_scatter x1, waiting for transfers between devices, local(): lax.psum_scatter(value_terms.astype(jnp.bfloat16), 'ctx', scatter_dimensi...  22.2 us
    reduce_scatter x1, waiting for transfers between devices, local(): lax.psum_scatter(key_terms.astype(jnp.bfloat16), 'ctx', scatter_dimension...  18.4 us
    all_gather x1, blocking collectives, local(): lax.all_gather(values, 'ctx', axis=1, tiled=True)[0].reshape(-1, KVH, HD)  17.1 us
    all_gather x1, blocking collectives, local(): lax.all_gather(keys, 'ctx', axis=1, tiled=True)[0].reshape(-1, KVH, HD)  14.8 us
    reshape x4, local copies, waits for them, and re-layouts, token_mask(): expanded.reshape(query_blocks * BLOCK, head_count, key_blocks * BLOCK)  13.4 us
    unnamed x9, local copies, waits for them, and re-layouts  5.05 us
    cond x2, local copies, waits for them, and re-layouts, backward_step(): lax.cond(piece_hit(first_row, step_rows), compute, skip_piece, query_accum)  4.17 us
  transfers between devices with their start and end apart: 4, of which 3 were waited for; matrix products, arithmetic and copies ran while one was open for 2% of the time, Pallas kernels for 0%

commit v1 on v0

v1 whole, which is shorter than its diff:
```python
import jax
import jax.numpy as jnp
from jax import lax
from jax.sharding import PartitionSpec as P

H = 16
KVH = 4
HD = 128
BLOCK = 64


NEG_FILL = -1e30


def passed_along(value, axis, steps):
    count = lax.axis_size(axis)
    pairs = [(source, (source + steps) % count) for source in range(count)]
    return lax.ppermute(value, axis, pairs)


def shifted_open(value, axis, steps):
    count = lax.axis_size(axis)
    pairs = [(source, source + steps) for source in range(count) if 0 <= source + steps < count]
    return lax.ppermute(value, axis, pairs)


def piece_mask(random_rows, global_row, ctx_index, shift, tok_rows, group_size):
    query_blocks, head_count, block_count = random_rows.shape
    key_shard = ctx_index - shift
    query_ids = ctx_index * query_blocks + jnp.arange(query_blocks, dtype=jnp.int32)
    key_ids = key_shard * query_blocks + jnp.arange(query_blocks, dtype=jnp.int32)
    start = jnp.clip(key_shard * query_blocks, 0, block_count - query_blocks)
    random_part = lax.dynamic_slice_in_dim(random_rows, start, query_blocks, 2) > 0
    query_global = jnp.any(query_ids[:, None] == global_row[None, :], axis=1)
    key_global = jnp.any(key_ids[:, None] == global_row[None, :], axis=1)
    nearby = jnp.abs(query_ids[:, None] - key_ids[None, :]) <= 1
    fixed_part = nearby | query_global[:, None] | key_global[None, :]
    table = (random_part | fixed_part[:, None, :]) & (key_shard >= 0)
    table = table.reshape(query_blocks, KVH, group_size, query_blocks)
    row_pos = lax.broadcasted_iota(jnp.int32, (tok_rows, 1, 1, tok_rows), 0)
    col_pos = lax.broadcasted_iota(jnp.int32, (tok_rows, 1, 1, tok_rows), 3)
    row_block = row_pos // BLOCK
    col_block = col_pos // BLOCK
    allowed = jnp.zeros((tok_rows, KVH, group_size, tok_rows), jnp.bool_)
    for qi in range(query_blocks):
        for kj in range(query_blocks):
            hit = (row_block == qi) & (col_block == kj)
            allowed = allowed | (hit & table[qi, :, :, kj][None, :, :, None])
    causal = key_shard * tok_rows + col_pos <= ctx_index * tok_rows + row_pos
    return allowed & causal


def local(query, keys, values, grad_out, random_blocks, global_ids):
    tok_rows = query.shape[1]
    query_width = query.shape[2]
    key_width = keys.shape[2]
    ctx_count = lax.axis_size("ctx")
    group_size = H // KVH
    score_scale = HD ** (-0.5)
    ctx_index = lax.axis_index("ctx")
    random_rows = random_blocks[0]
    global_row = global_ids[0]
    query_heads = query[0].reshape(tok_rows, KVH, group_size, HD)
    grad_heads = grad_out[0].reshape(tok_rows, KVH, group_size, HD)

    own = (keys[0], values[0])
    pieces = [own] + [shifted_open(own, "ctx", shift) for shift in range(1, ctx_count)]

    masks = []
    scores = []
    highs = []
    for shift in range(ctx_count):
        key_piece = pieces[shift][0].reshape(tok_rows, KVH, HD)
        allowed = piece_mask(random_rows, global_row, ctx_index, shift, tok_rows, group_size)
        raw = (
            jnp.einsum("tkgd,ukd->tkgu", query_heads, key_piece, preferred_element_type=jnp.float32)
            * score_scale
        )
        masks.append(allowed)
        scores.append(raw)
        highs.append(jnp.max(jnp.where(allowed, raw, NEG_FILL), axis=-1))
    row_high = highs[0]
    for more in highs[1:]:
        row_high = jnp.maximum(row_high, more)

    row_total = None
    accumulated = None
    for shift in range(ctx_count):
        value_piece = pieces[shift][1].reshape(tok_rows, KVH, HD)
        weights = jnp.where(masks[shift], jnp.exp(scores[shift] - row_high[..., None]), 0.0)
        part_total = jnp.sum(weights, axis=-1)
        part_acc = jnp.einsum(
            "tkgu,ukd->tkgd",
            weights.astype(jnp.bfloat16),
            value_piece,
            preferred_element_type=jnp.float32,
        )
        row_total = part_total if row_total is None else row_total + part_total
        accumulated = part_acc if accumulated is None else accumulated + part_acc
    attended = (accumulated / row_total[..., None]).astype(jnp.bfloat16)
    log_total = row_high + jnp.log(row_total)
    next_input = passed_along(attended.reshape(tok_rows, query_width)[None], "pipe", 1)
    delta = jnp.sum(grad_heads.astype(jnp.float32) * attended.astype(jnp.float32), axis=-1)

    query_accum = None
    key_own = None
    value_own = None
    received = []
    recompute = ctx_count * tok_rows > 512
    for shift in reversed(range(ctx_count)):
        key_piece = pieces[shift][0].reshape(tok_rows, KVH, HD)
        value_piece = pieces[shift][1].reshape(tok_rows, KVH, HD)
        raw = scores[shift]
        allowed = masks[shift]
        if recompute:
            key_piece, value_piece, log_total = lax.optimization_barrier(
                (key_piece, value_piece, log_total)
            )
            allowed = piece_mask(random_rows, global_row, ctx_index, shift, tok_rows, group_size)
            raw = (
                jnp.einsum("tkgd,ukd->tkgu", query_heads, key_piece, preferred_element_type=jnp.float32)
                * score_scale
            )
        row_probs = jnp.where(allowed, jnp.exp(raw - log_total[..., None]), 0.0)
        value_term = jnp.einsum(
            "tkgu,tkgd->ukd",
            row_probs.astype(jnp.bfloat16),
            grad_heads,
            preferred_element_type=jnp.float32,
        ).astype(jnp.bfloat16)
        prob_grads = jnp.einsum(
            "tkgd,ukd->tkgu", grad_heads, value_piece, preferred_element_type=jnp.float32
        )
        score_grads = (row_probs * (prob_grads - delta[..., None])).astype(jnp.bfloat16)
        part_q = jnp.einsum(
            "tkgu,ukd->tkgd", score_grads, key_piece, preferred_element_type=jnp.float32
        )
        query_accum = part_q if query_accum is None else query_accum + part_q
        key_term = (
            jnp.einsum("tkgu,tkgd->ukd", score_grads, query_heads, preferred_element_type=jnp.float32)
            * score_scale
        ).astype(jnp.bfloat16)
        key_term = key_term.reshape(tok_rows, key_width)
        value_term = value_term.reshape(tok_rows, key_width)
        if shift == 0:
            key_own = key_term
            value_own = value_term
        else:
            received.append(shifted_open((key_term, value_term), "ctx", -shift))

    query_grad = (query_accum * score_scale).astype(jnp.bfloat16).reshape(tok_rows, query_width)
    grad_query = passed_along(query_grad[None], "pipe", -1)
    key_sum = key_own.astype(jnp.float32)
    value_sum = value_own.astype(jnp.float32)
    for key_in, value_in in received:
        key_sum = key_sum + key_in.astype(jnp.float32)
        value_sum = value_sum + value_in.astype(jnp.float32)
    returned = passed_along(
        (key_sum.astype(jnp.bfloat16)[None], value_sum.astype(jnp.bfloat16)[None]), "pipe", -1
    )
    grad_key, grad_value = returned
    return (next_input, grad_query, grad_key, grad_value)


def solution(mesh):
    placed = (
        P(("dp", "pipe"), "ctx", None),
        P(("dp", "pipe"), "ctx", None),
        P(("dp", "pipe"), "ctx", None),
        P(("dp", "pipe"), "ctx", None),
        P("pipe", "ctx", None, None),
        P("pipe", None),
    )
    return jax.shard_map(
        local,
        mesh=mesh,
        in_specs=placed,
        out_specs=(
            P(("dp", "pipe"), "ctx", None),
            P(("dp", "pipe"), "ctx", None),
            P(("dp", "pipe"), "ctx", None),
            P(("dp", "pipe"), "ctx", None),
        ),
        check_vma=False,
    )
```

time: 170 us -> 126 us (0.74)
  the two profiles are of different devices: /device:TPU:0 before, /device:TPU:24 now
where the time goes in v1:
time: 126 us; the launch traced here: 125 us
  starting transfers between devices  31 us (25%)
  local copies, waits for them, and re-layouts  30.9 us (25%)
  matrix products  30.6 us (24%)
  waiting for transfers between devices  24.5 us (19%)
  other arithmetic  6.05 us (5%)
  between operations  1.48 us (1%)
    ppermute x12, starting transfers between devices, shifted_open(): return lax.ppermute(value, axis, pairs)  26.8 us
    ppermute x4, waiting for transfers between devices, passed_along(): return lax.ppermute(value, axis, pairs)  23.7 us
    unnamed x148, local copies, waits for them, and re-layouts  12 us
    dot_general x4, matrix products, local(): jnp.einsum('tkgu,ukd->tkgd', weights.astype(jnp.bfloat16), value_piece, p...  11 us
    dot_general x4, matrix products, local(): jnp.einsum('tkgu,tkgd->ukd', row_probs.astype(jnp.bfloat16), grad_heads,...  5.47 us
    ppermute x3, local copies, waits for them, and re-layouts, shifted_open(): return lax.ppermute(value, axis, pairs)  4.98 us
    dot_general x4, matrix products, local(): jnp.einsum('tkgu,ukd->tkgd', score_grads, key_piece, preferred_element_ty...  4.44 us
    ppermute x4, starting transfers between devices, passed_along(): return lax.ppermute(value, axis, pairs)  4.25 us
  transfers between devices with their start and end apart: 16, of which 3 were waited for; matrix products, arithmetic and copies ran while one was open for 31% of the time, Pallas kernels for 0%

profile of v1, /device:TPU:24, one launch (start us, length us, event | category | flops | bytes accessed | tf_op | source)
XLA Modules:
  0.0 124.6 jit_solution(6363655549738400038)
XLA Ops:
  0.6 1.7 %copy.64 = bf16[1,128,512]{1,2,0:T(8,128)(2,1)} copy(bf16[1,128,512]{2,1,0:T(8,128)(2,1)} %param.7) | data formatting | bytes 262144 | tf_op args[1]
  2.4 1.4 %collective-permute-start.2 = (bf16[128,512]{0,1:T(8,128)(2,1)}, bf16[128,512]{0,1:T(8,128)(2,1)S(1)}, u32[]{:S(2)}, u32[]{:S(2)}) collective-permute-start(bf16[128,512]{0,1:T(8,128)(2,1)} %bitcast.11), channel_id=1, source_target_pairs={{0,12},{1,13},{2,14},{3,15},{16,28},{17,29},{18,30},{19,31}} | collective-permute-start | bytes 393224 | tf_op jit(solution)/shard_map/ppermute | solution.py:24
  3.8 1.3 %collective-permute-start.1 = (bf16[128,512]{0,1:T(8,128)(2,1)}, bf16[128,512]{0,1:T(8,128)(2,1)S(1)}, u32[]{:S(2)}, u32[]{:S(2)}) collective-permute-start(bf16[128,512]{0,1:T(8,128)(2,1)} %bitcast.11), channel_id=1, source_target_pairs={{0,8},{4,12},{1,9},{5,13},{2,10},{6,14},{3,11},{7,15},{16,24},{20,... | collective-permute-start | bytes 393224 | tf_op jit(solution)/shard_map/ppermute | solution.py:24
  5.1 1.3 %collective-permute-start = (bf16[128,512]{0,1:T(8,128)(2,1)}, bf16[128,512]{0,1:T(8,128)(2,1)}, u32[]{:S(2)}, u32[]{:S(2)}) collective-permute-start(bf16[128,512]{0,1:T(8,128)(2,1)} %bitcast.11), channel_id=1, source_target_pairs={{0,4},{4,8},{8,12},{1,5},{5,9},{9,13},{2,6},{6,10},{10,14},{3,7},{... | collective-permute-start | bytes 393224 | tf_op jit(solution)/shard_map/ppermute | solution.py:24
  6.4 1.3 %collective-permute-start.5 = (bf16[128,512]{1,0:T(8,128)(2,1)}, bf16[128,512]{1,0:T(8,128)(2,1)}, u32[]{:S(2)}, u32[]{:S(2)}) collective-permute-start(bf16[128,512]{1,0:T(8,128)(2,1)} %bitcast.30), channel_id=1, source_target_pairs={{0,12},{1,13},{2,14},{3,15},{16,28},{17,29},{18,30},{19,31}} | collective-permute-start | bytes 393224 | tf_op jit(solution)/shard_map/ppermute | solution.py:24
  7.7 1.3 %collective-permute-start.4 = (bf16[128,512]{1,0:T(8,128)(2,1)}, bf16[128,512]{1,0:T(8,128)(2,1)}, u32[]{:S(2)}, u32[]{:S(2)}) collective-permute-start(bf16[128,512]{1,0:T(8,128)(2,1)} %bitcast.30), channel_id=1, source_target_pairs={{0,8},{4,12},{1,9},{5,13},{2,10},{6,14},{3,11},{7,15},{16,24},{20,... | collective-permute-start | bytes 393224 | tf_op jit(solution)/shard_map/ppermute | solution.py:24
  9.1 1.6 %reshape_squeeze.16 = bf16[128,4,128]{2,1,0:T(4,128)(2,1)} reshape(bf16[1,128,512]{2,1,0:T(8,128)(2,1)} %param.8) | data formatting | bytes 262144 | tf_op jit(solution)/shard_map/reshape;squeeze | solution.py:89
  10.8 0.7 copy-done.70
  12.6 0.6 slice_bitcast_fusion.11
  13.4 0.6 slice_bitcast_fusion.15
  14.5 0.8 copy-done.9
  16.0 1.3 %collective-permute-start.3 = (bf16[128,512]{1,0:T(8,128)(2,1)}, bf16[128,512]{1,0:T(8,128)(2,1)}, u32[]{:S(2)}, u32[]{:S(2)}) collective-permute-start(bf16[128,512]{1,0:T(8,128)(2,1)} %bitcast.30), channel_id=1, source_target_pairs={{0,4},{4,8},{8,12},{1,5},{5,9},{9,13},{2,6},{6,10},{10,14},{3,7},{... | collective-permute-start | bytes 393224 | tf_op jit(solution)/shard_map/ppermute | solution.py:24
  17.7 0.8 collective-permute-done.1
  19.6 1.9 %select_reduce_fusion.2 = (f32[128,4,4]{0,2,1:T(4,128)S(1)}, f32[128,4,4]{0,2,1:T(4,128)S(1)}, f32[128,4,4,128]{0,3,2,1:T(8,128)S(1)}) fusion(pred[128,128]{0,1:T(8,128)(4,1)S(1)} %get-tuple-element.49, pred[4,4]{1,0:T(4,128)(4,1)S(1)} %copy-done.38, pred[128,128]{0,1:T(8,128)(4,1)S(1)} %get-tuple-element.39, pred[4,4]{1,0:T(4,128)(4,1)S(1)} %copy-done.41, ...), kind=kOutput, calls=%fused_computation.68 | convolution fusion | flops 72609792 | bytes 2867328 | tf_op jit(solution)/shard_map/tkgd,ukd->tkgu/dot_general | solution.py:76
  22.2 1.1 select_reduce_fusion.3
  23.3 1.2 fusion.42
  24.5 1.2 fusion.40
  25.8 0.6 log_add_fusion
  26.4 1.4 %fusion.34 = f32[4,128,128]{1,2,0:T(8,128)} fusion(bf16[128,4,4,128]{0,3,2,1:T(8,128)(2,1)S(1)} %bitcast.290, f32[128,4,4,128]{0,3,2,1:T(8,128)S(1)} %get-tuple-element.50, f32[128,4,4]{0,2,1:T(4,128)S(1)} %bitcast.327, pred[128,128]{0,1:T(8,128)(4,1)S(1)} %get-tuple-element.48, pred[4,4]{1,0:T(4,128)(4,1)S(1)} %copy-done.50, ...), kind=kOutput, calls=%fused_computation.53 | convolution fusion | flops 70123520 | bytes 1925184 | tf_op jit(solution)/shard_map/tkgu,tkgd->ukd/dot_general | solution.py:125
  27.8 1.4 %fusion.35 = bf16[4,128,128]{1,2,0:T(8,128)(2,1)} fusion(bf16[128,4,4,128]{0,3,2,1:T(8,128)(2,1)S(1)} %bitcast.291, f32[128,4,4,128]{0,3,2,1:T(8,128)S(1)} %fusion.14, f32[128,4,4]{0,2,1:T(4,128)S(1)} %bitcast.328, pred[128,128]{0,1:T(8,128)(4,1)S(1)} %get-tuple-element.47, pred[4,4]{1,0:T(4,128)(4,1)S(1)} %get-tuple-element.31, ...), kind=kOutput, calls=%fused_computation.54 | convolution fusion | flops 70057984 | bytes 1794112 | tf_op jit(solution)/shard_map/tkgu,tkgd->ukd/dot_general | solution.py:125
  29.2 1.7 %copy.77 = bf16[128,512]{0,1:T(8,128)(2,1)} copy(bf16[128,512]{1,0:T(8,128)(2,1)} %collective-permute-done.5) | data formatting | bytes 262144 | tf_op jit(solution)/shard_map/ppermute | solution.py:24
  30.8 0.7 copy-done.60
  31.5 2.7 %fusion.54 = f32[4,128,4,128]{1,3,2,0:T(8,128)} fusion(bf16[128,4,128,1]{0,2,3,1:T(8,128)(2,1)} %bitcast.317, f32[128,4,4,128]{0,3,2,1:T(8,128)S(1)} %fusion.14, f32[128,4,4]{0,2,1:T(4,128)S(1)} %bitcast.308, pred[128,128]{0,1:T(8,128)(4,1)S(1)} %get-tuple-element.47, pred[4,4]{1,0:T(4,128)(4,1)S(1)} %copy-done.63, pred[4,4]{1,0:T(4,128)(4,1)S(1)} %copy-done.66, ...), kind=kOutput, calls=%fused_computation.86 | convolution fusion | flops 69992448 | bytes 2318400 | tf_op jit(solution)/shard_map/tkgu,ukd->tkgd/dot_general | solution.py:92
  34.9 1.7 %fusion.58 = f32[4,128,4,128]{1,3,2,0:T(8,128)} fusion(f32[128,4,4,128]{0,3,2,1:T(8,128)S(1)} %copy-done.3, f32[128,4,4]{0,2,1:T(4,128)S(1)} %bitcast.309, bf16[128,4,128,1]{2,1,0,3:T(4,128)(2,1)S(1)} %bitcast.312, pred[128,128]{0,1:T(8,128)(4,1)S(1)} %get-tuple-element.48, pred[4,4]{1,0:T(4,128)(4,1)S(1)} %copy-done.51, ...), kind=kOutput, calls=%fused_computation.87 | convolution fusion | flops 69992448 | bytes 2318400 | tf_op jit(solution)/shard_map/tkgu,ukd->tkgd/dot_general | solution.py:92
  36.6 1.3 %fusion.36 = bf16[4,128,128]{1,2,0:T(8,128)(2,1)} fusion(bf16[128,4,4,128]{0,3,2,1:T(8,128)(2,1)S(1)} %bitcast.292, f32[128,4,4,128]{0,3,2,1:T(8,128)S(1)} %fusion.15, f32[128,4,4]{0,2,1:T(4,128)S(1)} %bitcast.329, pred[128,128]{0,1:T(8,128)(4,1)S(1)} %get-tuple-element.46, pred[4,4]{1,0:T(4,128)(4,1)S(1)} %copy-done.27, pred[4,4]{1,0:T(4,128)(4,1)S(1)} %copy-done.30, ...), kind=kOutput, calls=%fused_computation.55 | convolution fusion | flops 70057984 | bytes 1794112 | tf_op jit(solution)/shard_map/tkgu,tkgd->ukd/dot_general | solution.py:125
  37.9 1.7 %copy.73 = bf16[128,512]{0,1:T(8,128)(2,1)} copy(bf16[128,512]{1,0:T(8,128)(2,1)} %collective-permute-done.3) | data formatting | bytes 262144 | tf_op jit(solution)/shard_map/ppermute | solution.py:24
  39.6 0.6 copy-done.36
  40.3 3.4 %convolution_add_fusion.2 = f32[4,128,4,128]{1,3,2,0:T(8,128)} fusion(f32[4,128,4,128]{1,3,2,0:T(8,128)} %fusion.58, bf16[128,4,128,1]{0,2,3,1:T(8,128)(2,1)} %bitcast.319, f32[128,4,4,128]{0,3,2,1:T(8,128)} %copy-done.5, f32[128,4,4]{0,2,1:T(4,128)S(1)} %bitcast.310, pred[128,128]{0,1:T(8,128)(4,1)S(1)} %get-tuple-element.49, ...), kind=kOutput, calls=%fused_computation.8 | convolution fusion | flops 70254592 | bytes 3366976 | tf_op jit(solution)/shard_map/tkgu,ukd->tkgd/dot_general | solution.py:92
  43.7 1.4 %fusion.37 = bf16[4,128,128]{1,2,0:T(8,128)(2,1)} fusion(bf16[128,4,4,128]{0,3,2,1:T(8,128)(2,1)S(1)} %bitcast.293, f32[128,4,4,128]{0,3,2,1:T(8,128)S(1)} %copy-done.6, f32[128,4,4]{0,2,1:T(4,128)S(1)} %bitcast.330, pred[128,128]{0,1:T(8,128)(4,1)S(1)} %get-tuple-element.49, pred[4,4]{1,0:T(4,128)(4,1)S(1)} %copy-done.39, pred[4,4]{1,0:T(4,128)(4,1)S(1)} %copy-done.42, ...), kind=kOutput, calls=%fused_computation.56 | convolution fusion | flops 70057984 | bytes 1794112 | tf_op jit(solution)/shard_map/tkgu,tkgd->ukd/dot_general | solution.py:125
  45.0 1.7 %copy.75 = bf16[128,512]{0,1:T(8,128)(2,1)} copy(bf16[128,512]{1,0:T(8,128)(2,1)} %collective-permute-done.4) | data formatting | bytes 262144 | tf_op jit(solution)/shard_map/ppermute | solution.py:24
  46.7 0.7 copy-done.34
  47.4 3.3 %multiply_reduce_fusion = (f32[128,4,4]{0,2,1:T(4,128)S(1)}, bf16[128,4,4,128]{0,3,2,1:T(8,128)(2,1)}) fusion(bf16[128,4,4,128]{0,3,2,1:T(8,128)(2,1)S(1)} %bitcast.294, f32[128,4,4]{0,2,1:T(4,128)} %bitcast.335, f32[4,128,4,128]{1,3,2,0:T(8,128)} %fusion.54, f32[4,128,4,128]{1,3,2,0:T(8,128)} %convolution_add_fusion.2, ...), kind=kOutput, calls=%fused_computation.60 | convolution fusion | flops 72087552 | bytes 4431936 | tf_op jit(solution)/shard_map/tkgu,ukd->tkgd/dot_general | solution.py:92
  50.7 0.7 fusion.19
  52.0 0.9 fusion.20
  53.2 0.7 fusion.21
  54.1 1.8 %fusion.18 = bf16[128,4,4,128]{0,3,2,1:T(8,128)(2,1)S(1)} fusion(bf16[128,4,128,1]{0,2,3,1:T(8,128)(2,1)S(1)} %bitcast.318, bf16[128,4,4,128]{0,3,2,1:T(8,128)(2,1)} %bitcast.298, f32[128,4,4,128]{0,3,2,1:T(8,128)S(1)} %fusion.14, f32[128,4,4]{0,2,1:T(4,128)S(1)} %get-tuple-element.52, f32[128,4,4]{0,2,1:T(4,128)S(1)} %bitcast.334, ...), kind=kOutput, calls=%fused_computation.29 | convolution fusion | flops 70516736 | bytes 2326592 | tf_op jit(solution)/shard_map/tkgd,ukd->tkgu/dot_general | solution.py:131
  55.9 1.0 fusion.32
  58.1 2.2 %fusion.93 = f32[4,128,4,128]{1,3,2,0:T(8,128)} fusion(bf16[128,4,128,1]{0,2,3,1:T(8,128)(2,1)} %bitcast.95, bf16[128,4,4,128]{0,3,2,1:T(8,128)(2,1)S(1)} %fusion.20), kind=kOutput, calls=%fused_computation.179 | convolution fusion | flops 67108864 | bytes 1703936 | tf_op jit(solution)/shard_map/tkgu,ukd->tkgd/dot_general | solution.py:135
  60.3 0.8 copy.109
  61.1 1.7 %copy.112 = bf16[128,512]{1,0:T(8,128)(2,1)} copy(bf16[128,512]{0,1:T(8,128)(2,1)} %bitcast.315) | data formatting | bytes 262144 | tf_op jit(solution)/shard_map/reshape | solution.py:144
  62.8 0.8 copy.114
  63.6 10.1 %collective-permute-start.14 = (bf16[128,512]{1,0:T(8,128)(2,1)}, bf16[128,512]{1,0:T(8,128)(2,1)}, u32[]{:S(2)}, u32[]{:S(2)}) collective-permute-start(bf16[128,512]{1,0:T(8,128)(2,1)} %copy.114), channel_id=1, source_target_pairs={{4,0},{8,4},{12,8},{5,1},{9,5},{13,9},{6,2},{10,6},{14,10},{7,3},{... | collective-permute-start | bytes 393224 | tf_op jit(solution)/shard_map/ppermute | solution.py:24
  73.7 2.3 %collective-permute-start.13 = (bf16[128,512]{1,0:T(8,128)(2,1)}, bf16[128,512]{1,0:T(8,128)(2,1)}, u32[]{:S(2)}, u32[]{:S(2)}) collective-permute-start(bf16[128,512]{1,0:T(8,128)(2,1)} %copy.112), channel_id=1, source_target_pairs={{8,0},{12,4},{9,1},{13,5},{10,2},{14,6},{11,3},{15,7},{24,16},{28,... | collective-permute-start | bytes 393224 | tf_op jit(solution)/shard_map/ppermute | solution.py:24
  76.0 1.9 %collective-permute-start.12 = (bf16[128,512]{1,0:T(8,128)(2,1)}, bf16[128,512]{1,0:T(8,128)(2,1)}, u32[]{:S(2)}, u32[]{:S(2)}) collective-permute-start(bf16[128,512]{1,0:T(8,128)(2,1)} %copy.109), channel_id=1, source_target_pairs={{12,0},{13,1},{14,2},{15,3},{28,16},{29,17},{30,18},{31,19}} | collective-permute-start | bytes 393224 | tf_op jit(solution)/shard_map/ppermute | solution.py:24
  78.0 1.8 %copy.110 = f32[128,512]{1,0:T(8,128)} copy(f32[128,512]{0,1:T(8,128)} %bitcast.305) | data formatting | bytes 524288 | tf_op jit(solution)/shard_map/convert_element_type | solution.py:154
  79.7 2.0 %copy.79 = bf16[1,128,2048]{2,1,0:T(8,128)(2,1)} copy(bf16[1,128,2048]{1,2,0:T(8,128)(2,1)} %bitcast.299) | data formatting | bytes 1048576 | tf_op jit(solution)/shard_map/broadcast_in_dim;reshape | solution.py:102
  82.1 0.8 copy.99
  82.9 0.8 copy.106
  83.8 0.8 copy.103
  84.5 1.3 %collective-permute-start.9 = (bf16[128,512]{1,0:T(8,128)(2,1)}, bf16[128,512]{1,0:T(8,128)(2,1)S(1)}, u32[]{:S(2)}, u32[]{:S(2)}) collective-permute-start(bf16[128,512]{1,0:T(8,128)(2,1)} %copy.103), channel_id=1, source_target_pairs={{8,0},{12,4},{9,1},{13,5},{10,2},{14,6},{11,3},{15,7},{24,16},{28,... | collective-permute-start | bytes 393224 | tf_op jit(solution)/shard_map/ppermute | solution.py:24
  85.8 2.0 %collective-permute-start.10 = (bf16[128,512]{1,0:T(8,128)(2,1)}, bf16[128,512]{1,0:T(8,128)(2,1)}, u32[]{:S(2)}, u32[]{:S(2)}) collective-permute-start(bf16[128,512]{1,0:T(8,128)(2,1)} %copy.106), channel_id=1, source_target_pairs={{4,0},{8,4},{12,8},{5,1},{9,5},{13,9},{6,2},{10,6},{14,10},{7,3},{... | collective-permute-start | bytes 393224 | tf_op jit(solution)/shard_map/ppermute | solution.py:24
  87.8 1.6 %fusion.22 = bf16[4,128,4,128]{1,3,2,0:T(8,128)(2,1)S(1)} fusion(f32[4,128,4,128]{1,3,2,0:T(8,128)S(1)} %fusion.94, f32[4,128,4,128]{1,3,2,0:T(8,128)} %fusion.93, f32[4,128,4,128]{1,3,2,0:T(8,128)S(1)} %fusion.92, bf16[128,4,128,1]{0,2,3,1:T(8,128)(2,1)} %bitcast.302, bf16[128,4,4,128]{0,3,2,1:T(8,128)(2,1)S(1)} %fusion.18), kind=kOutput, calls=%fused_computation.33 | convolution fusion | flops 68419584 | bytes 4325376 | tf_op jit(solution)/shard_map/tkgu,ukd->tkgd/dot_general | solution.py:135
  89.7 0.6 copy-done.18
  90.3 1.3 %collective-permute-start.8 = (bf16[128,512]{1,0:T(8,128)(2,1)S(1)}, bf16[128,512]{1,0:T(8,128)(2,1)S(1)}, u32[]{:S(2)}, u32[]{:S(2)}) collective-permute-start(bf16[128,512]{1,0:T(8,128)(2,1)S(1)} %copy-done.18), channel_id=1, source_target_pairs={{12,0},{13,1},{14,2},{15,3},{28,16},{29,17},{30,18},{31,19}} | collective-permute-start | bytes 393224 | tf_op jit(solution)/shard_map/ppermute | solution.py:24
  91.6 1.6 %collective-permute-start.7 = (bf16[1,128,2048]{2,1,0:T(8,128)(2,1)S(1)}, bf16[1,128,2048]{2,1,0:T(8,128)(2,1)S(1)}, u32[]{:S(2)}, u32[]{:S(2)}) collective-permute-start(bf16[1,128,2048]{2,1,0:T(8,128)(2,1)S(1)} %copy.94), channel_id=1, source_target_pairs={{0,16},{16,0},{1,17},{17,1},{2,18},{18,2},{3,19},{19,3},{4,20},{20... | collective-permute-start | bytes 1572872 | tf_op jit(solution)/shard_map/ppermute | solution.py:18
  93.7 1.1 fusion.77
  94.8 1.6 %collective-permute-start.15 = (bf16[1,128,512]{2,1,0:T(8,128)(2,1)S(1)}, bf16[1,128,512]{2,1,0:T(8,128)(2,1)S(1)}, u32[]{:S(2)}, u32[]{:S(2)}) collective-permute-start(bf16[1,128,512]{2,1,0:T(8,128)(2,1)S(1)} %fusion.77), channel_id=1, source_target_pairs={{0,16},{16,0},{1,17},{17,1},{2,18},{18,2},{3,19},{19,3},{4,20},{20... | collective-permute-start | bytes 393224 | tf_op jit(solution)/shard_map/ppermute | solution.py:18
  96.5 1.0 fusion.76
  98.0 22.3 %collective-permute-done.15 = bf16[1,128,512]{2,1,0:T(8,128)(2,1)S(1)} collective-permute-done((bf16[1,128,512]{2,1,0:T(8,128)(2,1)S(1)}, bf16[1,128,512]{2,1,0:T(8,128)(2,1)S(1)}, u32[]{:S(2)}, u32[]{:S(2)}) %collective-permute-start.15) | collective-permute-done | bytes 131104 | tf_op jit(solution)/shard_map/ppermute | solution.py:18
  120.3 1.4 %collective-permute-done.11 = bf16[1,128,512]{2,1,0:T(8,128)(2,1)S(1)} collective-permute-done((bf16[1,128,512]{2,1,0:T(8,128)(2,1)S(1)}, bf16[1,128,512]{2,1,0:T(8,128)(2,1)S(1)}, u32[]{:S(2)}, u32[]{:S(2)}) %collective-permute-start.11) | collective-permute-done | bytes 131104 | tf_op jit(solution)/shard_map/ppermute | solution.py:18
  121.7 0.8 copy.188
  122.5 0.8 copy.189
  123.3 0.7 copy.190
  123.9 0.7 copy.191
  (186 shorter events, 9.3 us)
Async XLA Ops:
  0.6 8.4 %copy-start.12 = (bf16[1,128,512]{2,1,0:T(8,128)(2,1)S(1)}, bf16[1,128,512]{2,1,0:T(8,128)(2,1)}, u32[]{:S(2)}) copy-start(bf16[1,128,512]{2,1,0:T(8,128)(2,1)} %param.7) | copy-start | bytes 393220
  2.4 11.9 %copy-start.8 = (bf16[1,128,2048]{2,1,0:T(8,128)(2,1)S(1)}, bf16[1,128,2048]{2,1,0:T(8,128)(2,1)}, u32[]{:S(2)}) copy-start(bf16[1,128,2048]{2,1,0:T(8,128)(2,1)} %param.6) | copy-start | bytes 1572868
  2.4 13.7 %collective-permute-start.2 = (bf16[128,512]{0,1:T(8,128)(2,1)}, bf16[128,512]{0,1:T(8,128)(2,1)S(1)}, u32[]{:S(2)}, u32[]{:S(2)}) collective-permute-start(bf16[128,512]{0,1:T(8,128)(2,1)} %bitcast.11), channel_id=1, source_target_pairs={{0,12},{1,13},{2,14},{3,15},{16,28},{17,29},{18,30},{19,31}} | collective-permute-start | bytes 393224 | tf_op jit(solution)/shard_map/ppermute | solution.py:24
  3.8 14.7 %collective-permute-start.1 = (bf16[128,512]{0,1:T(8,128)(2,1)}, bf16[128,512]{0,1:T(8,128)(2,1)S(1)}, u32[]{:S(2)}, u32[]{:S(2)}) collective-permute-start(bf16[128,512]{0,1:T(8,128)(2,1)} %bitcast.11), channel_id=1, source_target_pairs={{0,8},{4,12},{1,9},{5,13},{2,10},{6,14},{3,11},{7,15},{16,24},{20,... | collective-permute-start | bytes 393224 | tf_op jit(solution)/shard_map/ppermute | solution.py:24
  5.1 13.8 %collective-permute-start = (bf16[128,512]{0,1:T(8,128)(2,1)}, bf16[128,512]{0,1:T(8,128)(2,1)}, u32[]{:S(2)}, u32[]{:S(2)}) collective-permute-start(bf16[128,512]{0,1:T(8,128)(2,1)} %bitcast.11), channel_id=1, source_target_pairs={{0,4},{4,8},{8,12},{1,5},{5,9},{9,13},{2,6},{6,10},{10,14},{3,7},{... | collective-permute-start | bytes 393224 | tf_op jit(solution)/shard_map/ppermute | solution.py:24
  6.4 22.8 %collective-permute-start.5 = (bf16[128,512]{1,0:T(8,128)(2,1)}, bf16[128,512]{1,0:T(8,128)(2,1)}, u32[]{:S(2)}, u32[]{:S(2)}) collective-permute-start(bf16[128,512]{1,0:T(8,128)(2,1)} %bitcast.30), channel_id=1, source_target_pairs={{0,12},{1,13},{2,14},{3,15},{16,28},{17,29},{18,30},{19,31}} | collective-permute-start | bytes 393224 | tf_op jit(solution)/shard_map/ppermute | solution.py:24
  7.7 37.4 %collective-permute-start.4 = (bf16[128,512]{1,0:T(8,128)(2,1)}, bf16[128,512]{1,0:T(8,128)(2,1)}, u32[]{:S(2)}, u32[]{:S(2)}) collective-permute-start(bf16[128,512]{1,0:T(8,128)(2,1)} %bitcast.30), channel_id=1, source_target_pairs={{0,8},{4,12},{1,9},{5,13},{2,10},{6,14},{3,11},{7,15},{16,24},{20,... | collective-permute-start | bytes 393224 | tf_op jit(solution)/shard_map/ppermute | solution.py:24
  9.1 1.6 %copy-start.22 = (s32[1,2,16,8]{2,3,1,0:T(8,128)S(1)}, s32[1,2,16,8]{2,3,1,0:T(8,128)}, u32[]{:S(2)}) copy-start(s32[1,2,16,8]{2,3,1,0:T(8,128)} %param.10) | copy-start | bytes 3076
  12.5 10.8 %copy-start.23 = (pred[4,4]{1,0:T(4,128)(4,1)}, pred[4,4]{1,0:T(4,128)(4,1)S(1)}, u32[]{:S(2)}) copy-start(pred[4,4]{1,0:T(4,128)(4,1)S(1)} %get-tuple-element.22) | copy-start | bytes 52
  12.5 10.8 %copy-start.26 = (pred[4,4]{1,0:T(4,128)(4,1)}, pred[4,4]{1,0:T(4,128)(4,1)S(1)}, u32[]{:S(2)}) copy-start(pred[4,4]{1,0:T(4,128)(4,1)S(1)} %get-tuple-element.23) | copy-start | bytes 52
  14.3 1.0 copy-start.9
  15.6 37.3 %copy-start.10 = (bf16[1,128,2048]{1,2,0:T(8,128)(2,1)}, bf16[1,128,2048]{1,2,0:T(8,128)(2,1)S(1)}, u32[]{:S(2)}) copy-start(bf16[1,128,2048]{1,2,0:T(8,128)(2,1)S(1)} %copy.80) | copy-start | bytes 1572868
  16.0 11.8 %copy-start.59 = (pred[4,4]{1,0:T(4,128)(4,1)}, pred[4,4]{1,0:T(4,128)(4,1)S(1)}, u32[]{:S(2)}) copy-start(pred[4,4]{1,0:T(4,128)(4,1)S(1)} %get-tuple-element.30) | copy-start | bytes 52
  16.0 11.8 %copy-start.62 = (pred[4,4]{1,0:T(4,128)(4,1)}, pred[4,4]{1,0:T(4,128)(4,1)S(1)}, u32[]{:S(2)}) copy-start(pred[4,4]{1,0:T(4,128)(4,1)S(1)} %get-tuple-element.31) | copy-start | bytes 52
  16.0 11.8 %copy-start.65 = (pred[4,4]{1,0:T(4,128)(4,1)}, pred[4,4]{1,0:T(4,128)(4,1)S(1)}, u32[]{:S(2)}) copy-start(pred[4,4]{1,0:T(4,128)(4,1)S(1)} %get-tuple-element.32) | copy-start | bytes 52
  16.0 11.8 %copy-start.68 = (pred[4,4]{1,0:T(4,128)(4,1)}, pred[4,4]{1,0:T(4,128)(4,1)S(1)}, u32[]{:S(2)}) copy-start(pred[4,4]{1,0:T(4,128)(4,1)S(1)} %get-tuple-element.33) | copy-start | bytes 52
  16.0 1.7 %copy-start.13 = (bf16[128,512]{0,1:T(8,128)(2,1)}, bf16[128,512]{0,1:T(8,128)(2,1)S(1)}, u32[]{:S(2)}) copy-start(bf16[128,512]{0,1:T(8,128)(2,1)S(1)} %collective-permute-done.2) | copy-start | bytes 393220
  16.0 21.9 %collective-permute-start.3 = (bf16[128,512]{1,0:T(8,128)(2,1)}, bf16[128,512]{1,0:T(8,128)(2,1)}, u32[]{:S(2)}, u32[]{:S(2)}) collective-permute-start(bf16[128,512]{1,0:T(8,128)(2,1)} %bitcast.30), channel_id=1, source_target_pairs={{0,4},{4,8},{8,12},{1,5},{5,9},{9,13},{2,6},{6,10},{10,14},{3,7},{... | collective-permute-start | bytes 393224 | tf_op jit(solution)/shard_map/ppermute | solution.py:24
  19.6 2.0 %copy-start.56 = (pred[4,4]{1,0:T(4,128)(4,1)S(1)}, pred[4,4]{1,0:T(4,128)(4,1)}, u32[]{:S(2)}) copy-start(pred[4,4]{1,0:T(4,128)(4,1)} %get-tuple-element.37) | copy-start | bytes 52
  21.5 3.0 %copy-start.5 = (f32[128,4,4,128]{0,3,2,1:T(8,128)}, f32[128,4,4,128]{0,3,2,1:T(8,128)S(1)}, u32[]{:S(2)}) copy-start(f32[128,4,4,128]{0,3,2,1:T(8,128)S(1)} %get-tuple-element.51) | copy-start | bytes 3145732
  23.3 3.1 %copy-start.2 = (f32[128,4,4,128]{0,3,2,1:T(8,128)}, f32[128,4,4,128]{0,3,2,1:T(8,128)S(1)}, u32[]{:S(2)}) copy-start(f32[128,4,4,128]{0,3,2,1:T(8,128)S(1)} %get-tuple-element.50) | copy-start | bytes 3145732
  31.5 2.7 %copy-start.3 = (f32[128,4,4,128]{0,3,2,1:T(8,128)S(1)}, f32[128,4,4,128]{0,3,2,1:T(8,128)}, u32[]{:S(2)}) copy-start(f32[128,4,4,128]{0,3,2,1:T(8,128)} %copy-done.2) | copy-start | bytes 3145732
  31.5 2.7 %copy-start.14 = (bf16[128,4,128]{2,1,0:T(4,128)(2,1)S(1)}, bf16[128,4,128]{2,1,0:T(4,128)(2,1)}, u32[]{:S(2)}) copy-start(bf16[128,4,128]{2,1,0:T(4,128)(2,1)} %reshape_squeeze.16) | copy-start | bytes 393220
  31.5 2.7 %copy-start.57 = (pred[4,4]{1,0:T(4,128)(4,1)S(1)}, pred[4,4]{1,0:T(4,128)(4,1)}, u32[]{:S(2)}) copy-start(pred[4,4]{1,0:T(4,128)(4,1)} %get-tuple-element.37) | copy-start | bytes 52
  34.9 1.7 %copy-start.24 = (pred[4,4]{1,0:T(4,128)(4,1)S(1)}, pred[4,4]{1,0:T(4,128)(4,1)}, u32[]{:S(2)}) copy-start(pred[4,4]{1,0:T(4,128)(4,1)} %copy-done.23) | copy-start | bytes 52
  34.9 1.7 %copy-start.27 = (pred[4,4]{1,0:T(4,128)(4,1)S(1)}, pred[4,4]{1,0:T(4,128)(4,1)}, u32[]{:S(2)}) copy-start(pred[4,4]{1,0:T(4,128)(4,1)} %copy-done.26) | copy-start | bytes 52
  34.9 1.7 %copy-start.30 = (pred[4,4]{1,0:T(4,128)(4,1)S(1)}, pred[4,4]{1,0:T(4,128)(4,1)}, u32[]{:S(2)}) copy-start(pred[4,4]{1,0:T(4,128)(4,1)} %get-tuple-element.24) | copy-start | bytes 52
  34.9 1.7 %copy-start.33 = (pred[4,4]{1,0:T(4,128)(4,1)S(1)}, pred[4,4]{1,0:T(4,128)(4,1)}, u32[]{:S(2)}) copy-start(pred[4,4]{1,0:T(4,128)(4,1)} %get-tuple-element.25) | copy-start | bytes 52
  40.3 3.4 %copy-start.6 = (f32[128,4,4,128]{0,3,2,1:T(8,128)S(1)}, f32[128,4,4,128]{0,3,2,1:T(8,128)}, u32[]{:S(2)}) copy-start(f32[128,4,4,128]{0,3,2,1:T(8,128)} %copy-done.5) | copy-start | bytes 3145732
  40.3 3.4 %copy-start.45 = (pred[4,4]{1,0:T(4,128)(4,1)S(1)}, pred[4,4]{1,0:T(4,128)(4,1)}, u32[]{:S(2)}) copy-start(pred[4,4]{1,0:T(4,128)(4,1)} %get-tuple-element.29) | copy-start | bytes 52
  47.4 3.3 %copy-start.21 = (bf16[128,512]{0,1:T(8,128)(2,1)S(1)}, bf16[128,512]{0,1:T(8,128)(2,1)}, u32[]{:S(2)}) copy-start(bf16[128,512]{0,1:T(8,128)(2,1)} %copy.75) | copy-start | bytes 393220
  50.7 1.2 copy-start.7
  50.7 1.2 copy-start.20
  50.7 1.2 copy-start.37
  50.7 1.2 copy-start.40
  50.7 1.2 copy-start.43
  50.7 1.2 copy-start.46
  51.9 1.2 copy-start.4
  51.9 1.2 copy-start.15
  51.9 1.2 copy-start.49
  51.9 1.2 copy-start.52
  52.0 1.2 copy-start.55
  52.0 1.2 copy-start.58
  53.2 0.9 copy-start.19
  53.2 0.9 copy-start.61
  53.2 0.9 copy-start.64
  53.2 0.9 copy-start.67
  53.2 0.9 copy-start.69
  58.1 2.2 %copy-start.16 = (bf16[4,128,128]{1,2,0:T(8,128)(2,1)S(1)}, bf16[4,128,128]{1,2,0:T(8,128)(2,1)}, u32[]{:S(2)}) copy-start(bf16[4,128,128]{1,2,0:T(8,128)(2,1)} %fusion.35) | copy-start | bytes 393220
  61.1 1.7 %copy-start.17 = (bf16[4,128,128]{1,2,0:T(8,128)(2,1)S(1)}, bf16[4,128,128]{1,2,0:T(8,128)(2,1)}, u32[]{:S(2)}) copy-start(bf16[4,128,128]{1,2,0:T(8,128)(2,1)} %fusion.37) | copy-start | bytes 393220
  63.6 26.1 %collective-permute-start.14 = (bf16[128,512]{1,0:T(8,128)(2,1)}, bf16[128,512]{1,0:T(8,128)(2,1)}, u32[]{:S(2)}, u32[]{:S(2)}) collective-permute-start(bf16[128,512]{1,0:T(8,128)(2,1)} %copy.114), channel_id=1, source_target_pairs={{4,0},{8,4},{12,8},{5,1},{9,5},{13,9},{6,2},{10,6},{14,10},{7,3},{... | collective-permute-start | bytes 393224 | tf_op jit(solution)/shard_map/ppermute | solution.py:24
  73.7 17.9 %collective-permute-start.13 = (bf16[128,512]{1,0:T(8,128)(2,1)}, bf16[128,512]{1,0:T(8,128)(2,1)}, u32[]{:S(2)}, u32[]{:S(2)}) collective-permute-start(bf16[128,512]{1,0:T(8,128)(2,1)} %copy.112), channel_id=1, source_target_pairs={{8,0},{12,4},{9,1},{13,5},{10,2},{14,6},{11,3},{15,7},{24,16},{28,... | collective-permute-start | bytes 393224 | tf_op jit(solution)/shard_map/ppermute | solution.py:24
  76.0 17.2 %collective-permute-start.12 = (bf16[128,512]{1,0:T(8,128)(2,1)}, bf16[128,512]{1,0:T(8,128)(2,1)}, u32[]{:S(2)}, u32[]{:S(2)}) collective-permute-start(bf16[128,512]{1,0:T(8,128)(2,1)} %copy.109), channel_id=1, source_target_pairs={{12,0},{13,1},{14,2},{15,3},{28,16},{29,17},{30,18},{31,19}} | collective-permute-start | bytes 393224 | tf_op jit(solution)/shard_map/ppermute | solution.py:24
  82.1 1.6 %copy-start.1 = (f32[4,128,128]{1,2,0:T(8,128)S(1)}, f32[4,128,128]{1,2,0:T(8,128)}, u32[]{:S(2)}) copy-start(f32[4,128,128]{1,2,0:T(8,128)} %fusion.32) | copy-start | bytes 786436
  84.5 10.3 %collective-permute-start.9 = (bf16[128,512]{1,0:T(8,128)(2,1)}, bf16[128,512]{1,0:T(8,128)(2,1)S(1)}, u32[]{:S(2)}, u32[]{:S(2)}) collective-permute-start(bf16[128,512]{1,0:T(8,128)(2,1)} %copy.103), channel_id=1, source_target_pairs={{8,0},{12,4},{9,1},{13,5},{10,2},{14,6},{11,3},{15,7},{24,16},{28,... | collective-permute-start | bytes 393224 | tf_op jit(solution)/shard_map/ppermute | solution.py:24
  85.8 10.6 %collective-permute-start.10 = (bf16[128,512]{1,0:T(8,128)(2,1)}, bf16[128,512]{1,0:T(8,128)(2,1)}, u32[]{:S(2)}, u32[]{:S(2)}) collective-permute-start(bf16[128,512]{1,0:T(8,128)(2,1)} %copy.106), channel_id=1, source_target_pairs={{4,0},{8,4},{12,8},{5,1},{9,5},{13,9},{6,2},{10,6},{14,10},{7,3},{... | collective-permute-start | bytes 393224 | tf_op jit(solution)/shard_map/ppermute | solution.py:24
  89.4 0.9 copy-start.18
  89.4 3.8 %copy-start.11 = (bf16[1,128,2048]{2,1,0:T(8,128)(2,1)S(1)}, bf16[1,128,2048]{2,1,0:T(8,128)(2,1)}, u32[]{:S(2)}) copy-start(bf16[1,128,2048]{2,1,0:T(8,128)(2,1)} %copy.79) | copy-start | bytes 1572868
  89.5 4.3 %copy-start = (f32[128,512]{1,0:T(8,128)S(1)}, f32[128,512]{1,0:T(8,128)}, u32[]{:S(2)}) copy-start(f32[128,512]{1,0:T(8,128)} %copy.110) | copy-start | bytes 786436
  90.3 6.1 %collective-permute-start.8 = (bf16[128,512]{1,0:T(8,128)(2,1)S(1)}, bf16[128,512]{1,0:T(8,128)(2,1)S(1)}, u32[]{:S(2)}, u32[]{:S(2)}) collective-permute-start(bf16[128,512]{1,0:T(8,128)(2,1)S(1)} %copy-done.18), channel_id=1, source_target_pairs={{12,0},{13,1},{14,2},{15,3},{28,16},{29,17},{30,18},{31,19}} | collective-permute-start | bytes 393224 | tf_op jit(solution)/shard_map/ppermute | solution.py:24
  91.6 30.0 %collective-permute-start.7 = (bf16[1,128,2048]{2,1,0:T(8,128)(2,1)S(1)}, bf16[1,128,2048]{2,1,0:T(8,128)(2,1)S(1)}, u32[]{:S(2)}, u32[]{:S(2)}) collective-permute-start(bf16[1,128,2048]{2,1,0:T(8,128)(2,1)S(1)} %copy.94), channel_id=1, source_target_pairs={{0,16},{16,0},{1,17},{17,1},{2,18},{18,2},{3,19},{19,3},{4,20},{20... | collective-permute-start | bytes 1572872 | tf_op jit(solution)/shard_map/ppermute | solution.py:18
  93.2 28.4 %collective-permute-start.6 = (bf16[1,128,2048]{2,1,0:T(8,128)(2,1)S(1)}, bf16[1,128,2048]{2,1,0:T(8,128)(2,1)S(1)}, u32[]{:S(2)}, u32[]{:S(2)}) collective-permute-start(bf16[1,128,2048]{2,1,0:T(8,128)(2,1)S(1)} %copy-done.11), channel_id=1, source_target_pairs={{0,16},{16,0},{1,17},{17,1},{2,18},{18,2},{3,19},{19,3},{4,20},{20... | collective-permute-start | bytes 1572872 | tf_op jit(solution)/shard_map/ppermute | solution.py:18
  94.8 25.4 %collective-permute-start.15 = (bf16[1,128,512]{2,1,0:T(8,128)(2,1)S(1)}, bf16[1,128,512]{2,1,0:T(8,128)(2,1)S(1)}, u32[]{:S(2)}, u32[]{:S(2)}) collective-permute-start(bf16[1,128,512]{2,1,0:T(8,128)(2,1)S(1)} %fusion.77), channel_id=1, source_target_pairs={{0,16},{16,0},{1,17},{17,1},{2,18},{18,2},{3,19},{19,3},{4,20},{20... | collective-permute-start | bytes 393224 | tf_op jit(solution)/shard_map/ppermute | solution.py:18
  97.4 24.2 %collective-permute-start.11 = (bf16[1,128,512]{2,1,0:T(8,128)(2,1)S(1)}, bf16[1,128,512]{2,1,0:T(8,128)(2,1)S(1)}, u32[]{:S(2)}, u32[]{:S(2)}) collective-permute-start(bf16[1,128,512]{2,1,0:T(8,128)(2,1)S(1)} %fusion.76), channel_id=1, source_target_pairs={{0,16},{16,0},{1,17},{17,1},{2,18},{18,2},{3,19},{19,3},{4,20},{20... | collective-permute-start | bytes 393224 | tf_op jit(solution)/shard_map/ppermute | solution.py:18
  (23 other events, 15.2 us)

commit v2 on v1

v2 whole, which is shorter than its diff:
```python
import functools

import jax
import jax.numpy as jnp
from jax import lax
from jax.experimental import pallas as pl
from jax.experimental.pallas import tpu as pltpu
from jax.sharding import PartitionSpec as P

H = 16
KVH = 4
HD = 128
BLOCK = 64


NEG_FILL = -1e30


def passed_along(value, axis, steps):
    count = lax.axis_size(axis)
    pairs = [(source, (source + steps) % count) for source in range(count)]
    return lax.ppermute(value, axis, pairs)


def shifted_open(value, axis, steps):
    count = lax.axis_size(axis)
    pairs = [(source, source + steps) for source in range(count) if 0 <= source + steps < count]
    return lax.ppermute(value, axis, pairs)


def block_masks(random_rows, global_row, ctx_index, piece_count, tok_rows):
    query_blocks, head_count, block_count = random_rows.shape
    shifts = jnp.arange(piece_count, dtype=jnp.int32)
    key_shard = ctx_index - shifts
    query_ids = ctx_index * query_blocks + jnp.arange(query_blocks, dtype=jnp.int32)
    key_ids = key_shard[:, None] * query_blocks + jnp.arange(query_blocks, dtype=jnp.int32)[None, :]
    safe_ids = jnp.clip(key_ids, 0, block_count - 1).reshape(-1)
    random_part = jnp.take(random_rows, safe_ids, axis=2).reshape(
        query_blocks, head_count, piece_count, query_blocks
    )
    random_part = jnp.transpose(random_part, (2, 1, 0, 3)) > 0
    query_global = jnp.any(query_ids[:, None] == global_row[None, :], axis=1)
    key_global = jnp.any(key_ids[:, :, None] == global_row[None, None, :], axis=2)
    nearby = jnp.abs(query_ids[None, :, None] - key_ids[:, None, :]) <= 1
    fixed_part = nearby | query_global[None, :, None] | key_global[:, None, :]
    table = (random_part | fixed_part[:, None, :, :]) & (key_shard >= 0)[:, None, None, None]
    expanded = jnp.repeat(table, tok_rows // query_blocks, axis=3)
    return expanded.astype(jnp.float32)


def piece_allowed(mask_rows, shift, tok_rows):
    query_blocks = mask_rows.shape[0]
    row = lax.broadcasted_iota(jnp.int32, (tok_rows, tok_rows), 0)
    picked = jnp.broadcast_to(mask_rows[0:1, :], (tok_rows, tok_rows))
    for block in range(1, query_blocks):
        picked = jnp.where(row // BLOCK == block, mask_rows[block : block + 1, :], picked)
    allowed = picked > 0.5
    if shift == 0:
        col = lax.broadcasted_iota(jnp.int32, (tok_rows, tok_rows), 1)
        allowed = allowed & (col <= row)
    return allowed


def dot_nt(a, b):
    return lax.dot_general(a, b, (((1,), (1,)), ((), ())), preferred_element_type=jnp.float32)


def dot_tn(a, b):
    return lax.dot_general(a, b, (((0,), (0,)), ((), ())), preferred_element_type=jnp.float32)


def forward_kernel(piece_count, group_size, query_ref, kv_ref, mask_ref, out_ref, lse_ref, score_ref):
    tok_rows = query_ref.shape[0]
    score_scale = HD ** (-0.5)
    for head in range(group_size):
        cols = slice(head * HD, (head + 1) * HD)
        query_head = query_ref[:, cols]
        row_high = jnp.full((tok_rows, 1), NEG_FILL, jnp.float32)
        for shift in range(piece_count):
            raw = dot_nt(query_head, kv_ref[shift, 0]) * score_scale
            score_ref[shift] = raw
            allowed = piece_allowed(mask_ref[shift, head], shift, tok_rows)
            row_high = jnp.maximum(
                row_high, jnp.max(jnp.where(allowed, raw, NEG_FILL), axis=1, keepdims=True)
            )
        row_total = jnp.zeros((tok_rows, 1), jnp.float32)
        accumulated = jnp.zeros((tok_rows, HD), jnp.float32)
        for shift in range(piece_count):
            allowed = piece_allowed(mask_ref[shift, head], shift, tok_rows)
            weights = jnp.where(allowed, jnp.exp(score_ref[shift] - row_high), 0.0)
            row_total = row_total + jnp.sum(weights, axis=1, keepdims=True)
            accumulated = accumulated + jnp.dot(
                weights.astype(jnp.bfloat16), kv_ref[shift, 1], preferred_element_type=jnp.float32
            )
        out_ref[:, cols] = (accumulated / row_total).astype(out_ref.dtype)
        lse_ref[0, :, head : head + 1] = row_high + jnp.log(row_total)


def backward_kernel(
    piece_count, group_size, query_ref, grad_ref, out_ref, kv_ref, mask_ref, lse_ref,
    dq_ref, dkv_ref, dk_acc, dv_acc,
):
    tok_rows = query_ref.shape[0]
    score_scale = HD ** (-0.5)
    for head in range(group_size):
        cols = slice(head * HD, (head + 1) * HD)
        query_head = query_ref[:, cols]
        grad_head = grad_ref[:, cols]
        delta = jnp.sum(
            grad_head.astype(jnp.float32) * out_ref[:, cols].astype(jnp.float32), axis=1, keepdims=True
        )
        log_total = lse_ref[0, :, head : head + 1]
        query_accum = jnp.zeros((tok_rows, HD), jnp.float32)
        for shift in range(piece_count):
            key_piece = kv_ref[shift, 0]
            value_piece = kv_ref[shift, 1]
            raw = dot_nt(query_head, key_piece) * score_scale
            allowed = piece_allowed(mask_ref[shift, head], shift, tok_rows)
            row_probs = jnp.where(allowed, jnp.exp(raw - log_total), 0.0)
            value_term = dot_tn(row_probs.astype(jnp.bfloat16), grad_head)
            prob_grads = dot_nt(grad_head, value_piece)
            score_grads = (row_probs * (prob_grads - delta)).astype(jnp.bfloat16)
            query_accum = query_accum + jnp.dot(
                score_grads, key_piece, preferred_element_type=jnp.float32
            )
            key_term = dot_tn(score_grads, query_head)
            if head == 0:
                dk_acc[shift] = key_term
                dv_acc[shift] = value_term
            else:
                dk_acc[shift] = dk_acc[shift] + key_term
                dv_acc[shift] = dv_acc[shift] + value_term
        dq_ref[:, cols] = (query_accum * score_scale).astype(dq_ref.dtype)
    for shift in range(piece_count):
        dkv_ref[shift, 0] = (dk_acc[shift] * score_scale).astype(dkv_ref.dtype)
        dkv_ref[shift, 1] = dv_acc[shift].astype(dkv_ref.dtype)


def attention_forward(query_rows, kv_pieces, masks):
    tok_rows, query_width = query_rows.shape
    piece_count = kv_pieces.shape[0]
    group_size = H // KVH
    group_width = group_size * HD
    flops = 4 * tok_rows * tok_rows * HD * H * piece_count
    return pl.pallas_call(
        functools.partial(forward_kernel, piece_count, group_size),
        grid=(KVH,),
        in_specs=[
            pl.BlockSpec((tok_rows, group_width), lambda g: (0, g)),
            pl.BlockSpec((piece_count, 2, tok_rows, HD), lambda g: (0, 0, 0, g)),
            pl.BlockSpec((piece_count, group_size) + masks.shape[2:], lambda g: (0, g, 0, 0)),
        ],
        out_specs=[
            pl.BlockSpec((tok_rows, group_width), lambda g: (0, g)),
            pl.BlockSpec((1, tok_rows, group_size), lambda g: (g, 0, 0)),
        ],
        out_shape=[
            jax.ShapeDtypeStruct((tok_rows, query_width), jnp.bfloat16),
            jax.ShapeDtypeStruct((KVH, tok_rows, group_size), jnp.float32),
        ],
        scratch_shapes=[pltpu.VMEM((piece_count, tok_rows, tok_rows), jnp.float32)],
        cost_estimate=pl.CostEstimate(
            flops=flops,
            transcendentals=tok_rows * tok_rows * H * piece_count,
            bytes_accessed=2 * query_rows.size * 2 + kv_pieces.size * 2,
        ),
    )(query_rows, kv_pieces, masks)


def attention_backward(query_rows, grad_rows, attended, kv_pieces, masks, log_total):
    tok_rows, query_width = query_rows.shape
    piece_count = kv_pieces.shape[0]
    group_size = H // KVH
    group_width = group_size * HD
    flops = 10 * tok_rows * tok_rows * HD * H * piece_count
    return pl.pallas_call(
        functools.partial(backward_kernel, piece_count, group_size),
        grid=(KVH,),
        in_specs=[
            pl.BlockSpec((tok_rows, group_width), lambda g: (0, g)),
            pl.BlockSpec((tok_rows, group_width), lambda g: (0, g)),
            pl.BlockSpec((tok_rows, group_width), lambda g: (0, g)),
            pl.BlockSpec((piece_count, 2, tok_rows, HD), lambda g: (0, 0, 0, g)),
            pl.BlockSpec((piece_count, group_size) + masks.shape[2:], lambda g: (0, g, 0, 0)),
            pl.BlockSpec((1, tok_rows, group_size), lambda g: (g, 0, 0)),
        ],
        out_specs=[
            pl.BlockSpec((tok_rows, group_width), lambda g: (0, g)),
            pl.BlockSpec((piece_count, 2, tok_rows, HD), lambda g: (0, 0, 0, g)),
        ],
        out_shape=[
            jax.ShapeDtypeStruct((tok_rows, query_width), jnp.bfloat16),
            jax.ShapeDtypeStruct(kv_pieces.shape, jnp.bfloat16),
        ],
        scratch_shapes=[
            pltpu.VMEM((piece_count, tok_rows, HD), jnp.float32),
            pltpu.VMEM((piece_count, tok_rows, HD), jnp.float32),
        ],
        cost_estimate=pl.CostEstimate(
            flops=flops,
            transcendentals=tok_rows * tok_rows * H * piece_count,
            bytes_accessed=4 * query_rows.size * 2 + 2 * kv_pieces.size * 2,
        ),
    )(query_rows, grad_rows, attended, kv_pieces, masks, log_total)


def local(query, keys, values, grad_out, random_blocks, global_ids):
    tok_rows = query.shape[1]
    ctx_count = lax.axis_size("ctx")
    ctx_index = lax.axis_index("ctx")
    masks = block_masks(random_blocks[0], global_ids[0], ctx_index, ctx_count, tok_rows)

    own = jnp.stack([keys[0], values[0]])
    pieces = [own] + [shifted_open(own, "ctx", shift) for shift in range(1, ctx_count)]
    kv_pieces = jnp.stack(pieces)

    attended, log_total = attention_forward(query[0], kv_pieces, masks)
    next_input = passed_along(attended[None], "pipe", 1)

    query_grad, kv_terms = attention_backward(
        query[0], grad_out[0], attended, kv_pieces, masks, log_total
    )
    grad_query = passed_along(query_grad[None], "pipe", -1)

    kv_sum = kv_terms[0].astype(jnp.float32)
    for shift in range(1, ctx_count):
        kv_sum = kv_sum + shifted_open(kv_terms[shift], "ctx", -shift).astype(jnp.float32)
    returned = passed_along(kv_sum.astype(jnp.bfloat16), "pipe", -1)
    grad_key = returned[0:1]
    grad_value = returned[1:2]
    return (next_input, grad_query, grad_key, grad_value)


def solution(mesh):
    placed = (
        P(("dp", "pipe"), "ctx", None),
        P(("dp", "pipe"), "ctx", None),
        P(("dp", "pipe"), "ctx", None),
        P(("dp", "pipe"), "ctx", None),
        P("pipe", "ctx", None, None),
        P("pipe", None),
    )
    return jax.shard_map(
        local,
        mesh=mesh,
        in_specs=placed,
        out_specs=(
            P(("dp", "pipe"), "ctx", None),
            P(("dp", "pipe"), "ctx", None),
            P(("dp", "pipe"), "ctx", None),
            P(("dp", "pipe"), "ctx", None),
        ),
        check_vma=False,
    )
```

time: 126 us -> 103 us (0.82)
  the two profiles are of different devices: /device:TPU:24 before, /device:TPU:0 now
where the time goes in v2:
time: 103 us; the launch traced here: 102 us
  waiting for transfers between devices  43.8 us (43%)
  Pallas kernels  29.3 us (28%)
  starting transfers between devices  18.3 us (18%)
  local copies, waits for them, and re-layouts  7.42 us (7%)
  other arithmetic  2.93 us (3%)
    ppermute x6, waiting for transfers between devices, shifted_open(): return lax.ppermute(value, axis, pairs)  37.6 us
    pallas_call x1, Pallas kernels, attention_backward(): pl.pallas_call(functools.partial(backward_kernel, piece_count, group_size...  21.6 us
    ppermute x6, starting transfers between devices, shifted_open(): return lax.ppermute(value, axis, pairs)  14.6 us
    pallas_call x1, Pallas kernels, attention_forward(): pl.pallas_call(functools.partial(forward_kernel, piece_count, group_size)...  7.65 us
    ppermute x3, waiting for transfers between devices, passed_along(): return lax.ppermute(value, axis, pairs)  6.19 us
    ppermute x3, starting transfers between devices, passed_along(): return lax.ppermute(value, axis, pairs)  3.67 us
    unnamed x14, local copies, waits for them, and re-layouts  3.47 us
  transfers between devices with their start and end apart: 9, of which 6 were waited for; matrix products, arithmetic and copies ran while one was open for 4% of the time, Pallas kernels for 0%

profile of v2, /device:TPU:0, one launch (start us, length us, event | category | flops | bytes accessed | tf_op | source)
XLA Modules:
  0.0 102.5 jit_solution(13177700699555726516)
XLA Ops:
  0.6 0.0 copy-start
  0.6 0.9 constant_dynamic-update-slice_fusion.1
  1.6 0.0 copy-done
  1.6 7.0 %collective-permute-start.2 = (bf16[2,128,512]{2,1,0:T(8,128)(2,1)S(1)}, bf16[2,128,512]{2,1,0:T(8,128)(2,1)S(1)}, u32[]{:S(2)}, u32[]{:S(2)}) collective-permute-start(bf16[2,128,512]{2,1,0:T(8,128)(2,1)S(1)} %constant_dynamic-update-slice_fusion), channel_id=1, source_target_pairs={{0,12},{1,13},{2,14},{3,15},{16,28},{17,29},{18,30},{19,31}} | collective-permute-start | bytes 786440 | tf_op jit(solution)/shard_map/ppermute | solution.py:28
  8.6 1.3 %collective-permute-start.1 = (bf16[2,128,512]{2,1,0:T(8,128)(2,1)S(1)}, bf16[2,128,512]{2,1,0:T(8,128)(2,1)S(1)}, u32[]{:S(2)}, u32[]{:S(2)}) collective-permute-start(bf16[2,128,512]{2,1,0:T(8,128)(2,1)S(1)} %constant_dynamic-update-slice_fusion), channel_id=1, source_target_pairs={{0,8},{4,12},{1,9},{5,13},{2,10},{6,14},{3,11},{7,15},{16,24},{20,... | collective-permute-start | bytes 786440 | tf_op jit(solution)/shard_map/ppermute | solution.py:28
  9.9 2.5 %collective-permute-start = (bf16[2,128,512]{2,1,0:T(8,128)(2,1)S(1)}, bf16[2,128,512]{2,1,0:T(8,128)(2,1)S(1)}, u32[]{:S(2)}, u32[]{:S(2)}) collective-permute-start(bf16[2,128,512]{2,1,0:T(8,128)(2,1)S(1)} %constant_dynamic-update-slice_fusion), channel_id=1, source_target_pairs={{0,4},{4,8},{8,12},{1,5},{5,9},{9,13},{2,6},{6,10},{10,14},{3,7},{... | collective-permute-start | bytes 786440 | tf_op jit(solution)/shard_map/ppermute | solution.py:28
  12.4 0.1 compare_and_fusion
  12.5 0.1 iota_add_fusion
  12.6 0.1 min.12
  12.7 0.1 copy.14
  12.7 0.0 copy-start.2
  12.7 0.7 copy-done.2
  13.4 0.2 compare_reduce_fusion.1
  13.6 0.0 copy-start.1
  13.6 0.2 compare_reduce_fusion
  13.8 0.1 copy.15
  13.9 0.1 or_or_fusion
  14.0 0.3 copy-done.1
  14.3 0.6 gather_fusion
  14.9 0.1 fusion.4
  15.0 0.1 copy.16
  15.1 0.2 broadcast_in_dim.18
  15.3 0.8 convert_element_type.24.mask_ref
  16.1 0.0 collective-permute-done.2
  16.1 4.9 %collective-permute-done.1 = bf16[2,128,512]{2,1,0:T(8,128)(2,1)S(1)} collective-permute-done((bf16[2,128,512]{2,1,0:T(8,128)(2,1)S(1)}, bf16[2,128,512]{2,1,0:T(8,128)(2,1)S(1)}, u32[]{:S(2)}, u32[]{:S(2)}) %collective-permute-start.1) | collective-permute-done | bytes 262176 | tf_op jit(solution)/shard_map/ppermute | solution.py:28
  21.0 4.5 %collective-permute-done = bf16[2,128,512]{2,1,0:T(8,128)(2,1)S(1)} collective-permute-done((bf16[2,128,512]{2,1,0:T(8,128)(2,1)S(1)}, bf16[2,128,512]{2,1,0:T(8,128)(2,1)S(1)}, u32[]{:S(2)}, u32[]{:S(2)}) %collective-permute-start) | collective-permute-done | bytes 262176 | tf_op jit(solution)/shard_map/ppermute | solution.py:28
  25.5 1.1 %pad_maximum_fusion.kv_ref = bf16[4,2,128,512]{3,2,1,0:T(8,128)(2,1)} fusion(bf16[1,2,128,512]{3,2,1,0:T(8,128)(2,1)S(1)} %bitcast.33, bf16[1,2,128,512]{3,2,1,0:T(8,128)(2,1)S(1)} %bitcast.34, bf16[1,2,128,512]{3,2,1,0:T(8,128)(2,1)S(1)} %bitcast.35, bf16[1,2,128,512]{3,2,1,0:T(8,128)(2,1)S(1)} %bitcast.32), kind=kLoop, calls=%fused_computation.1 | loop fusion | flops 1572864 | bytes 2097152 | tf_op jit(solution)/shard_map/stack | solution.py:215
  26.6 7.7 %shard_map.93 = (bf16[128,2048]{1,0:T(8,128)(2,1)}, f32[4,128,4]{2,1,0:T(8,128)}) custom-call(bf16[128,2048]{1,0:T(8,128)(2,1)} %bitcast.40, bf16[4,2,128,512]{3,2,1,0:T(8,128)(2,1)} %pad_maximum_fusion.kv_ref, f32[4,16,2,128]{3,2,1,0:T(2,128)} %convert_element_type.24.mask_ref), custom_call_target="tpu_custom_call" | custom-call | flops 536870912 | bytes 2097152 | tf_op jit(solution)/shard_map/pallas_call | solution.py:145
  34.2 21.6 %shard_map.94 = (bf16[128,2048]{1,0:T(8,128)(2,1)}, bf16[4,2,128,512]{3,2,1,0:T(8,128)(2,1)}) custom-call(bf16[128,2048]{1,0:T(8,128)(2,1)} %bitcast.41, bf16[128,2048]{1,0:T(8,128)(2,1)} %bitcast.42, bf16[128,2048]{1,0:T(8,128)(2,1)} %get-tuple-element.8.out_ref, bf16[4,2,128,512]{3,2,1,0:T(8,128)(2,1)} %pad_maximum_fusion.kv_ref, ...), custom_call_target="tpu_custom_call" | custom-call | flops 1342177280 | bytes 4194304 | tf_op jit(solution)/shard_map/pallas_call | solution.py:176
  55.8 0.0 copy-start.4
  55.8 0.0 copy-start.3
  55.8 1.2 %slice_bitcast_fusion.2 = (bf16[2,128,512]{2,1,0:T(8,128)(2,1)S(1)}, bf16[2,128,512]{2,1,0:T(8,128)(2,1)S(1)}, bf16[2,128,512]{2,1,0:T(8,128)(2,1)S(1)}) fusion(bf16[4,2,128,512]{3,2,1,0:T(8,128)(2,1)} %get-tuple-element.11), kind=kLoop, calls=%fused_computation.8 | loop fusion | bytes 1572864 | tf_op jit(solution)/shard_map/squeeze | solution.py:227
  57.1 1.3 %collective-permute-start.5 = (bf16[2,128,512]{2,1,0:T(8,128)(2,1)S(1)}, bf16[2,128,512]{2,1,0:T(8,128)(2,1)S(1)}, u32[]{:S(2)}, u32[]{:S(2)}) collective-permute-start(bf16[2,128,512]{2,1,0:T(8,128)(2,1)S(1)} %get-tuple-element.12), channel_id=1, source_target_pairs={{4,0},{8,4},{12,8},{5,1},{9,5},{13,9},{6,2},{10,6},{14,10},{7,3},{... | collective-permute-start | bytes 786440 | tf_op jit(solution)/shard_map/ppermute | solution.py:28
  58.4 1.3 %collective-permute-start.7 = (bf16[2,128,512]{2,1,0:T(8,128)(2,1)S(1)}, bf16[2,128,512]{2,1,0:T(8,128)(2,1)S(1)}, u32[]{:S(2)}, u32[]{:S(2)}) collective-permute-start(bf16[2,128,512]{2,1,0:T(8,128)(2,1)S(1)} %get-tuple-element.13), channel_id=1, source_target_pairs={{12,0},{13,1},{14,2},{15,3},{28,16},{29,17},{30,18},{31,19}} | collective-permute-start | bytes 786440 | tf_op jit(solution)/shard_map/ppermute | solution.py:28
  59.7 1.3 %collective-permute-start.6 = (bf16[2,128,512]{2,1,0:T(8,128)(2,1)S(1)}, bf16[2,128,512]{2,1,0:T(8,128)(2,1)S(1)}, u32[]{:S(2)}, u32[]{:S(2)}) collective-permute-start(bf16[2,128,512]{2,1,0:T(8,128)(2,1)S(1)} %get-tuple-element.14), channel_id=1, source_target_pairs={{8,0},{12,4},{9,1},{13,5},{10,2},{14,6},{11,3},{15,7},{24,16},{28,... | collective-permute-start | bytes 786440 | tf_op jit(solution)/shard_map/ppermute | solution.py:28
  61.0 0.0 copy-done.4
  61.0 1.6 %collective-permute-start.4 = (bf16[1,128,2048]{2,1,0:T(8,128)(2,1)S(1)}, bf16[1,128,2048]{2,1,0:T(8,128)(2,1)S(1)}, u32[]{:S(2)}, u32[]{:S(2)}) collective-permute-start(bf16[1,128,2048]{2,1,0:T(8,128)(2,1)S(1)} %bitcast.44), channel_id=1, source_target_pairs={{0,16},{16,0},{1,17},{17,1},{2,18},{18,2},{3,19},{19,3},{4,20},{20... | collective-permute-start | bytes 1572872 | tf_op jit(solution)/shard_map/ppermute | solution.py:22
  62.6 0.0 copy-done.3
  62.6 0.5 collective-permute-start.3
  63.1 9.4 %collective-permute-done.5 = bf16[2,128,512]{2,1,0:T(8,128)(2,1)S(1)} collective-permute-done((bf16[2,128,512]{2,1,0:T(8,128)(2,1)S(1)}, bf16[2,128,512]{2,1,0:T(8,128)(2,1)S(1)}, u32[]{:S(2)}, u32[]{:S(2)}) %collective-permute-start.5) | collective-permute-done | bytes 262176 | tf_op jit(solution)/shard_map/ppermute | solution.py:28
  72.5 9.7 %collective-permute-done.7 = bf16[2,128,512]{2,1,0:T(8,128)(2,1)S(1)} collective-permute-done((bf16[2,128,512]{2,1,0:T(8,128)(2,1)S(1)}, bf16[2,128,512]{2,1,0:T(8,128)(2,1)S(1)}, u32[]{:S(2)}, u32[]{:S(2)}) %collective-permute-start.7) | collective-permute-done | bytes 262176 | tf_op jit(solution)/shard_map/ppermute | solution.py:28
  82.3 9.0 %collective-permute-done.6 = bf16[2,128,512]{2,1,0:T(8,128)(2,1)S(1)} collective-permute-done((bf16[2,128,512]{2,1,0:T(8,128)(2,1)S(1)}, bf16[2,128,512]{2,1,0:T(8,128)(2,1)S(1)}, u32[]{:S(2)}, u32[]{:S(2)}) %collective-permute-start.6) | collective-permute-done | bytes 262176 | tf_op jit(solution)/shard_map/ppermute | solution.py:28
  91.3 1.1 %fusion.2 = bf16[2,128,512]{2,1,0:T(8,128)(2,1)S(1)} fusion(bf16[2,128,512]{2,1,0:T(8,128)(2,1)S(1)} %collective-permute-done.7, bf16[2,128,512]{2,1,0:T(8,128)(2,1)S(1)} %collective-permute-done.6, bf16[2,128,512]{2,1,0:T(8,128)(2,1)S(1)} %collective-permute-done.5, bf16[4,2,128,512]{3,2,1,0:T(8,128)(2,1)} %get-tuple-element.11), kind=kLoop, calls=%fused_computation.5 | loop fusion | flops 1048576 | bytes 1310720 | tf_op jit(solution)/shard_map/convert_element_type | solution.py:228
  92.4 1.6 %collective-permute-start.8 = (bf16[2,128,512]{2,1,0:T(8,128)(2,1)S(1)}, bf16[2,128,512]{2,1,0:T(8,128)(2,1)S(1)}, u32[]{:S(2)}, u32[]{:S(2)}) collective-permute-start(bf16[2,128,512]{2,1,0:T(8,128)(2,1)S(1)} %fusion.2), channel_id=1, source_target_pairs={{0,16},{16,0},{1,17},{17,1},{2,18},{18,2},{3,19},{19,3},{4,20},{20... | collective-permute-start | bytes 786440 | tf_op jit(solution)/shard_map/ppermute | solution.py:22
  94.0 0.0 collective-permute-done.4
  94.0 0.0 collective-permute-done.3
  94.0 6.2 %collective-permute-done.8 = bf16[2,128,512]{2,1,0:T(8,128)(2,1)S(1)} collective-permute-done((bf16[2,128,512]{2,1,0:T(8,128)(2,1)S(1)}, bf16[2,128,512]{2,1,0:T(8,128)(2,1)S(1)}, u32[]{:S(2)}, u32[]{:S(2)}) %collective-permute-start.8) | collective-permute-done | bytes 262176 | tf_op jit(solution)/shard_map/ppermute | solution.py:22
  100.2 0.7 fusion.8
  100.9 0.8 copy.22
  101.7 0.8 copy.23
  (7 shorter events, 0.0 us)
Async XLA Ops:
  0.6 1.0 copy-start
  1.6 14.5 %collective-permute-start.2 = (bf16[2,128,512]{2,1,0:T(8,128)(2,1)S(1)}, bf16[2,128,512]{2,1,0:T(8,128)(2,1)S(1)}, u32[]{:S(2)}, u32[]{:S(2)}) collective-permute-start(bf16[2,128,512]{2,1,0:T(8,128)(2,1)S(1)} %constant_dynamic-update-slice_fusion), channel_id=1, source_target_pairs={{0,12},{1,13},{2,14},{3,15},{16,28},{17,29},{18,30},{19,31}} | collective-permute-start | bytes 786440 | tf_op jit(solution)/shard_map/ppermute | solution.py:28
  8.6 12.4 %collective-permute-start.1 = (bf16[2,128,512]{2,1,0:T(8,128)(2,1)S(1)}, bf16[2,128,512]{2,1,0:T(8,128)(2,1)S(1)}, u32[]{:S(2)}, u32[]{:S(2)}) collective-permute-start(bf16[2,128,512]{2,1,0:T(8,128)(2,1)S(1)} %constant_dynamic-update-slice_fusion), channel_id=1, source_target_pairs={{0,8},{4,12},{1,9},{5,13},{2,10},{6,14},{3,11},{7,15},{16,24},{20,... | collective-permute-start | bytes 786440 | tf_op jit(solution)/shard_map/ppermute | solution.py:28
  9.9 15.5 %collective-permute-start = (bf16[2,128,512]{2,1,0:T(8,128)(2,1)S(1)}, bf16[2,128,512]{2,1,0:T(8,128)(2,1)S(1)}, u32[]{:S(2)}, u32[]{:S(2)}) collective-permute-start(bf16[2,128,512]{2,1,0:T(8,128)(2,1)S(1)} %constant_dynamic-update-slice_fusion), channel_id=1, source_target_pairs={{0,4},{4,8},{8,12},{1,5},{5,9},{9,13},{2,6},{6,10},{10,14},{3,7},{... | collective-permute-start | bytes 786440 | tf_op jit(solution)/shard_map/ppermute | solution.py:28
  12.7 0.7 copy-start.2
  13.6 0.7 copy-start.1
  55.8 5.2 %copy-start.4 = (bf16[128,2048]{1,0:T(8,128)(2,1)S(1)}, bf16[128,2048]{1,0:T(8,128)(2,1)}, u32[]{:S(2)}) copy-start(bf16[128,2048]{1,0:T(8,128)(2,1)} %get-tuple-element.10) | copy-start | bytes 1572868
  55.8 6.8 %copy-start.3 = (bf16[128,2048]{1,0:T(8,128)(2,1)S(1)}, bf16[128,2048]{1,0:T(8,128)(2,1)}, u32[]{:S(2)}) copy-start(bf16[128,2048]{1,0:T(8,128)(2,1)} %get-tuple-element.8.out_ref) | copy-start | bytes 1572868
  57.1 15.4 %collective-permute-start.5 = (bf16[2,128,512]{2,1,0:T(8,128)(2,1)S(1)}, bf16[2,128,512]{2,1,0:T(8,128)(2,1)S(1)}, u32[]{:S(2)}, u32[]{:S(2)}) collective-permute-start(bf16[2,128,512]{2,1,0:T(8,128)(2,1)S(1)} %get-tuple-element.12), channel_id=1, source_target_pairs={{4,0},{8,4},{12,8},{5,1},{9,5},{13,9},{6,2},{10,6},{14,10},{7,3},{... | collective-permute-start | bytes 786440 | tf_op jit(solution)/shard_map/ppermute | solution.py:28
  58.4 23.9 %collective-permute-start.7 = (bf16[2,128,512]{2,1,0:T(8,128)(2,1)S(1)}, bf16[2,128,512]{2,1,0:T(8,128)(2,1)S(1)}, u32[]{:S(2)}, u32[]{:S(2)}) collective-permute-start(bf16[2,128,512]{2,1,0:T(8,128)(2,1)S(1)} %get-tuple-element.13), channel_id=1, source_target_pairs={{12,0},{13,1},{14,2},{15,3},{28,16},{29,17},{30,18},{31,19}} | collective-permute-start | bytes 786440 | tf_op jit(solution)/shard_map/ppermute | solution.py:28
  59.7 31.6 %collective-permute-start.6 = (bf16[2,128,512]{2,1,0:T(8,128)(2,1)S(1)}, bf16[2,128,512]{2,1,0:T(8,128)(2,1)S(1)}, u32[]{:S(2)}, u32[]{:S(2)}) collective-permute-start(bf16[2,128,512]{2,1,0:T(8,128)(2,1)S(1)} %get-tuple-element.14), channel_id=1, source_target_pairs={{8,0},{12,4},{9,1},{13,5},{10,2},{14,6},{11,3},{15,7},{24,16},{28,... | collective-permute-start | bytes 786440 | tf_op jit(solution)/shard_map/ppermute | solution.py:28
  61.0 33.0 %collective-permute-start.4 = (bf16[1,128,2048]{2,1,0:T(8,128)(2,1)S(1)}, bf16[1,128,2048]{2,1,0:T(8,128)(2,1)S(1)}, u32[]{:S(2)}, u32[]{:S(2)}) collective-permute-start(bf16[1,128,2048]{2,1,0:T(8,128)(2,1)S(1)} %bitcast.44), channel_id=1, source_target_pairs={{0,16},{16,0},{1,17},{17,1},{2,18},{18,2},{3,19},{19,3},{4,20},{20... | collective-permute-start | bytes 1572872 | tf_op jit(solution)/shard_map/ppermute | solution.py:22
  62.6 31.4 %collective-permute-start.3 = (bf16[1,128,2048]{2,1,0:T(8,128)(2,1)S(1)}, bf16[1,128,2048]{2,1,0:T(8,128)(2,1)S(1)}, u32[]{:S(2)}, u32[]{:S(2)}) collective-permute-start(bf16[1,128,2048]{2,1,0:T(8,128)(2,1)S(1)} %bitcast.43), channel_id=1, source_target_pairs={{0,16},{16,0},{1,17},{17,1},{2,18},{18,2},{3,19},{19,3},{4,20},{20... | collective-permute-start | bytes 1572872 | tf_op jit(solution)/shard_map/ppermute | solution.py:22
  92.4 7.8 %collective-permute-start.8 = (bf16[2,128,512]{2,1,0:T(8,128)(2,1)S(1)}, bf16[2,128,512]{2,1,0:T(8,128)(2,1)S(1)}, u32[]{:S(2)}, u32[]{:S(2)}) collective-permute-start(bf16[2,128,512]{2,1,0:T(8,128)(2,1)S(1)} %fusion.2), channel_id=1, source_target_pairs={{0,16},{16,0},{1,17},{17,1},{2,18},{18,2},{3,19},{19,3},{4,20},{20... | collective-permute-start | bytes 786440 | tf_op jit(solution)/shard_map/ppermute | solution.py:22

commit v3 on v2

v3 whole, which is shorter than its diff:
```python
import functools

import jax
import jax.numpy as jnp
from jax import lax
from jax.experimental import pallas as pl
from jax.experimental.pallas import tpu as pltpu
from jax.sharding import PartitionSpec as P

H = 16
KVH = 4
HD = 128
BLOCK = 64


NEG_FILL = -1e30


def passed_along(value, axis, steps):
    count = lax.axis_size(axis)
    pairs = [(source, (source + steps) % count) for source in range(count)]
    return lax.ppermute(value, axis, pairs)


def shifted_open(value, axis, steps):
    count = lax.axis_size(axis)
    pairs = [(source, source + steps) for source in range(count) if 0 <= source + steps < count]
    return lax.ppermute(value, axis, pairs)


def block_masks(random_rows, global_row, ctx_index, piece_count, tok_rows):
    query_blocks, head_count, block_count = random_rows.shape
    shifts = jnp.arange(piece_count, dtype=jnp.int32)
    key_shard = ctx_index - shifts
    query_ids = ctx_index * query_blocks + jnp.arange(query_blocks, dtype=jnp.int32)
    key_ids = key_shard[:, None] * query_blocks + jnp.arange(query_blocks, dtype=jnp.int32)[None, :]
    safe_ids = jnp.clip(key_ids, 0, block_count - 1).reshape(-1)
    random_part = jnp.take(random_rows, safe_ids, axis=2).reshape(
        query_blocks, head_count, piece_count, query_blocks
    )
    random_part = jnp.transpose(random_part, (2, 1, 0, 3)) > 0
    query_global = jnp.any(query_ids[:, None] == global_row[None, :], axis=1)
    key_global = jnp.any(key_ids[:, :, None] == global_row[None, None, :], axis=2)
    nearby = jnp.abs(query_ids[None, :, None] - key_ids[:, None, :]) <= 1
    fixed_part = nearby | query_global[None, :, None] | key_global[:, None, :]
    table = (random_part | fixed_part[:, None, :, :]) & (key_shard >= 0)[:, None, None, None]
    expanded = jnp.repeat(table, tok_rows // query_blocks, axis=3)
    return expanded.astype(jnp.float32)


def piece_allowed(mask_ref, shift, group_size, tok_rows):
    query_blocks = mask_ref.shape[2]
    rows = group_size * tok_rows
    row = lax.broadcasted_iota(jnp.int32, (rows, tok_rows), 0)
    row_block = row // BLOCK
    picked = jnp.broadcast_to(mask_ref[shift, 0, 0:1, :], (rows, tok_rows))
    for head in range(group_size):
        for block in range(query_blocks):
            if head == 0 and block == 0:
                continue
            picked = jnp.where(
                row_block == head * query_blocks + block,
                mask_ref[shift, head, block : block + 1, :],
                picked,
            )
    allowed = picked > 0.5
    if shift == 0:
        col = lax.broadcasted_iota(jnp.int32, (rows, tok_rows), 1)
        allowed = allowed & (col <= row % tok_rows)
    return allowed


def dot_nt(a, b):
    return lax.dot_general(a, b, (((1,), (1,)), ((), ())), preferred_element_type=jnp.float32)


def dot_tn(a, b):
    return lax.dot_general(a, b, (((0,), (0,)), ((), ())), preferred_element_type=jnp.float32)


def stacked(ref, group_size):
    return jnp.concatenate([ref[:, head * HD : (head + 1) * HD] for head in range(group_size)], axis=0)


def forward_kernel(
    piece_count, group_size, query_ref, grad_ref, kv_ref, mask_ref, out_ref, lse_ref, delta_ref, score_ref
):
    tok_rows = query_ref.shape[0]
    rows = group_size * tok_rows
    score_scale = HD ** (-0.5)
    query_rows = stacked(query_ref, group_size)
    row_high = jnp.full((rows, 1), NEG_FILL, jnp.float32)
    for shift in range(piece_count):
        raw = dot_nt(query_rows, kv_ref[shift, 0]) * score_scale
        score_ref[shift] = raw
        allowed = piece_allowed(mask_ref, shift, group_size, tok_rows)
        row_high = jnp.maximum(
            row_high, jnp.max(jnp.where(allowed, raw, NEG_FILL), axis=1, keepdims=True)
        )
    row_total = jnp.zeros((rows, 1), jnp.float32)
    accumulated = jnp.zeros((rows, HD), jnp.float32)
    for shift in range(piece_count):
        allowed = piece_allowed(mask_ref, shift, group_size, tok_rows)
        weights = jnp.where(allowed, jnp.exp(score_ref[shift] - row_high), 0.0)
        row_total = row_total + jnp.sum(weights, axis=1, keepdims=True)
        accumulated = accumulated + jnp.dot(
            weights.astype(jnp.bfloat16), kv_ref[shift, 1], preferred_element_type=jnp.float32
        )
    attended = (accumulated / row_total).astype(out_ref.dtype)
    for head in range(group_size):
        out_ref[:, head * HD : (head + 1) * HD] = attended[head * tok_rows : (head + 1) * tok_rows]
    lse_ref[0] = row_high + jnp.log(row_total)
    grad_rows = stacked(grad_ref, group_size)
    delta_ref[0] = jnp.sum(
        grad_rows.astype(jnp.float32) * attended.astype(jnp.float32), axis=1, keepdims=True
    )


def backward_kernel(
    piece_count, group_size, query_ref, grad_ref, kv_ref, mask_ref, lse_ref, delta_ref, *rest
):
    dq_ref, dkv_ref = rest[-2:]
    tok_rows = query_ref.shape[0]
    score_scale = HD ** (-0.5)
    query_rows = stacked(query_ref, group_size)
    grad_rows = stacked(grad_ref, group_size)
    log_total = lse_ref[0]
    delta = delta_ref[0]
    query_accum = None
    for shift in range(piece_count):
        key_piece = kv_ref[shift, 0]
        value_piece = kv_ref[shift, 1]
        raw = dot_nt(query_rows, key_piece) * score_scale
        allowed = piece_allowed(mask_ref, shift, group_size, tok_rows)
        row_probs = jnp.where(allowed, jnp.exp(raw - log_total), 0.0)
        dkv_ref[shift, 1] = dot_tn(row_probs.astype(jnp.bfloat16), grad_rows).astype(dkv_ref.dtype)
        prob_grads = dot_nt(grad_rows, value_piece)
        score_grads = (row_probs * (prob_grads - delta)).astype(jnp.bfloat16)
        part_q = jnp.dot(score_grads, key_piece, preferred_element_type=jnp.float32)
        query_accum = part_q if query_accum is None else query_accum + part_q
        dkv_ref[shift, 0] = (dot_tn(score_grads, query_rows) * score_scale).astype(dkv_ref.dtype)
    query_grad = (query_accum * score_scale).astype(dq_ref.dtype)
    for head in range(group_size):
        dq_ref[:, head * HD : (head + 1) * HD] = query_grad[head * tok_rows : (head + 1) * tok_rows]


def attention_forward(query_rows, grad_rows, kv_pieces, masks):
    tok_rows, query_width = query_rows.shape
    piece_count = kv_pieces.shape[0]
    group_size = H // KVH
    group_width = group_size * HD
    rows = group_size * tok_rows
    flops = 4 * tok_rows * tok_rows * HD * H * piece_count
    return pl.pallas_call(
        functools.partial(forward_kernel, piece_count, group_size),
        grid=(KVH,),
        in_specs=[
            pl.BlockSpec((tok_rows, group_width), lambda g: (0, g)),
            pl.BlockSpec((tok_rows, group_width), lambda g: (0, g)),
            pl.BlockSpec((piece_count, 2, tok_rows, HD), lambda g: (0, 0, 0, g)),
            pl.BlockSpec((piece_count, group_size) + masks.shape[2:], lambda g: (0, g, 0, 0)),
        ],
        out_specs=[
            pl.BlockSpec((tok_rows, group_width), lambda g: (0, g)),
            pl.BlockSpec((1, rows, 1), lambda g: (g, 0, 0)),
            pl.BlockSpec((1, rows, 1), lambda g: (g, 0, 0)),
        ],
        out_shape=[
            jax.ShapeDtypeStruct((tok_rows, query_width), jnp.bfloat16),
            jax.ShapeDtypeStruct((KVH, rows, 1), jnp.float32),
            jax.ShapeDtypeStruct((KVH, rows, 1), jnp.float32),
        ],
        scratch_shapes=[pltpu.VMEM((piece_count, rows, tok_rows), jnp.float32)],
        cost_estimate=pl.CostEstimate(
            flops=flops,
            transcendentals=tok_rows * tok_rows * H * piece_count,
            bytes_accessed=3 * query_rows.size * 2 + kv_pieces.size * 2,
        ),
    )(query_rows, grad_rows, kv_pieces, masks)


def attention_backward(query_rows, grad_rows, kv_pieces, masks, log_total, delta, first_group, group_count, extra):
    tok_rows, query_width = query_rows.shape
    piece_count = kv_pieces.shape[0]
    group_size = H // KVH
    group_width = group_size * HD
    rows = group_size * tok_rows
    flops = 10 * tok_rows * tok_rows * HD * group_size * group_count * piece_count
    aliases = {}
    if extra and extra[0] is not None:
        aliases = {6: 0, 7: 1}
    else:
        extra = extra[1:] if extra else extra
    shift_g = lambda g: g + first_group
    return pl.pallas_call(
        functools.partial(backward_kernel, piece_count, group_size),
        grid=(group_count,),
        in_specs=[
            pl.BlockSpec((tok_rows, group_width), lambda g: (0, shift_g(g))),
            pl.BlockSpec((tok_rows, group_width), lambda g: (0, shift_g(g))),
            pl.BlockSpec((piece_count, 2, tok_rows, HD), lambda g: (0, 0, 0, shift_g(g))),
            pl.BlockSpec((piece_count, group_size) + masks.shape[2:], lambda g: (0, shift_g(g), 0, 0)),
            pl.BlockSpec((1, rows, 1), lambda g: (shift_g(g), 0, 0)),
            pl.BlockSpec((1, rows, 1), lambda g: (shift_g(g), 0, 0)),
        ]
        + [pl.BlockSpec(memory_space=pl.ANY) for _ in extra],
        out_specs=[
            pl.BlockSpec((tok_rows, group_width), lambda g: (0, shift_g(g))),
            pl.BlockSpec((piece_count, 2, tok_rows, HD), lambda g: (0, 0, 0, shift_g(g))),
        ],
        out_shape=[
            jax.ShapeDtypeStruct((tok_rows, query_width), jnp.bfloat16),
            jax.ShapeDtypeStruct(kv_pieces.shape, jnp.bfloat16),
        ],
        input_output_aliases=aliases,
        cost_estimate=pl.CostEstimate(
            flops=flops,
            transcendentals=tok_rows * tok_rows * group_size * group_count * piece_count,
            bytes_accessed=(2 * query_rows.size * 2 + 2 * kv_pieces.size * 2) * group_count // KVH,
        ),
    )(query_rows, grad_rows, kv_pieces, masks, log_total, delta, *extra)


def local(query, keys, values, grad_out, random_blocks, global_ids):
    tok_rows = query.shape[1]
    ctx_count = lax.axis_size("ctx")
    ctx_index = lax.axis_index("ctx")
    masks = block_masks(random_blocks[0], global_ids[0], ctx_index, ctx_count, tok_rows)

    own = jnp.stack([keys[0], values[0]])
    pieces = [own] + [shifted_open(own, "ctx", shift) for shift in range(1, ctx_count)]
    kv_pieces = jnp.stack(pieces)

    attended, log_total, delta = attention_forward(query[0], grad_out[0], kv_pieces, masks)
    next_input = passed_along(attended[None], "pipe", 1)

    half = KVH // 2
    first_dq, first_dkv = attention_backward(
        query[0], grad_out[0], kv_pieces, masks, log_total, delta, 0, half, [None]
    )
    query_grad, kv_terms = attention_backward(
        query[0], grad_out[0], kv_pieces, masks, log_total, delta, half, KVH - half,
        [first_dq, first_dkv, next_input],
    )
    grad_query = passed_along(query_grad[None], "pipe", -1)

    kv_sum = kv_terms[0].astype(jnp.float32)
    for shift in range(1, ctx_count):
        kv_sum = kv_sum + shifted_open(kv_terms[shift], "ctx", -shift).astype(jnp.float32)
    returned = passed_along(kv_sum.astype(jnp.bfloat16), "pipe", -1)
    grad_key = returned[0:1]
    grad_value = returned[1:2]
    return (next_input, grad_query, grad_key, grad_value)


def solution(mesh):
    placed = (
        P(("dp", "pipe"), "ctx", None),
        P(("dp", "pipe"), "ctx", None),
        P(("dp", "pipe"), "ctx", None),
        P(("dp", "pipe"), "ctx", None),
        P("pipe", "ctx", None, None),
        P("pipe", None),
    )
    return jax.shard_map(
        local,
        mesh=mesh,
        in_specs=placed,
        out_specs=(
            P(("dp", "pipe"), "ctx", None),
            P(("dp", "pipe"), "ctx", None),
            P(("dp", "pipe"), "ctx", None),
            P(("dp", "pipe"), "ctx", None),
        ),
        check_vma=False,
    )
```

time: 103 us -> 92.5 us (0.90)
  Pallas kernels: 29.3 us -> 16 us
    pallas_call x1 -> x2, Pallas kernels: 21.6 us -> 10.1 us  [attention_backward(): pl.pallas_call(functools.partial(backward_kernel, piece_count, group_size...]
    ppermute x3, waiting for transfers between devices: 6.19 us -> 11.3 us  [passed_along(): return lax.ppermute(value, axis, pairs)]
    ppermute x6, waiting for transfers between devices: 37.6 us -> 33.2 us  [shifted_open(): return lax.ppermute(value, axis, pairs)]
    pallas_call x1, Pallas kernels: 7.65 us -> 5.97 us  [attention_forward(): pl.pallas_call(functools.partial(forward_kernel, piece_count, group_size)...]
    unnamed x14 -> x16, local copies, waits for them, and re-layouts: 3.47 us -> 4.51 us
  transfers between devices with their start and end apart: 9 -> 9, of which waited for: 6 -> 6; matrix products, arithmetic and copies ran while one was open for 4% -> 5% of each run, Pallas kernels for 0% -> 5%
where the time goes in v3:
time: 92.5 us; the launch traced here: 92 us
  waiting for transfers between devices  44.4 us (48%)
  starting transfers between devices  19.3 us (21%)
  Pallas kernels  16 us (17%)
  local copies, waits for them, and re-layouts  8.44 us (9%)
  other arithmetic  2.94 us (3%)
    ppermute x6, waiting for transfers between devices, shifted_open(): return lax.ppermute(value, axis, pairs)  33.2 us
    ppermute x6, starting transfers between devices, shifted_open(): return lax.ppermute(value, axis, pairs)  14.6 us
    ppermute x3, waiting for transfers between devices, passed_along(): return lax.ppermute(value, axis, pairs)  11.3 us
    pallas_call x2, Pallas kernels, attention_backward(): pl.pallas_call(functools.partial(backward_kernel, piece_count, group_size...  10.1 us
    pallas_call x1, Pallas kernels, attention_forward(): pl.pallas_call(functools.partial(forward_kernel, piece_count, group_size)...  5.97 us
    ppermute x3, starting transfers between devices, passed_along(): return lax.ppermute(value, axis, pairs)  4.69 us
    unnamed x16, local copies, waits for them, and re-layouts  4.51 us
  transfers between devices with their start and end apart: 9, of which 6 were waited for; matrix products, arithmetic and copies ran while one was open for 5% of the time, Pallas kernels for 5%

profile of v3, /device:TPU:0, one launch (start us, length us, event | category | flops | bytes accessed | tf_op | source)
XLA Modules:
  0.0 92.0 jit_solution(3773330068290499589)
XLA Ops:
  0.6 0.0 copy-start.3
  0.6 0.9 %constant_dynamic-update-slice_fusion.1 = bf16[2,128,512]{2,1,0:T(8,128)(2,1)S(1)} fusion(bf16[1,128,512]{2,1,0:T(8,128)(2,1)} %param.7), kind=kLoop, calls=%fused_computation.17 | loop fusion | bytes 262144
  1.6 0.0 copy-done.3
  1.6 4.9 %collective-permute-start = (bf16[2,128,512]{2,1,0:T(8,128)(2,1)S(1)}, bf16[2,128,512]{2,1,0:T(8,128)(2,1)S(1)}, u32[]{:S(2)}, u32[]{:S(2)}) collective-permute-start(bf16[2,128,512]{2,1,0:T(8,128)(2,1)S(1)} %constant_dynamic-update-slice_fusion), channel_id=1, source_target_pairs={{0,4},{4,8},{8,12},{1,5},{5,9},{9,13},{2,6},{6,10},{10,14},{3,7},{... | collective-permute-start | bytes 786440 | tf_op jit(solution)/shard_map/ppermute | solution.py:28
  6.6 4.5 %collective-permute-start.1 = (bf16[2,128,512]{2,1,0:T(8,128)(2,1)S(1)}, bf16[2,128,512]{2,1,0:T(8,128)(2,1)S(1)}, u32[]{:S(2)}, u32[]{:S(2)}) collective-permute-start(bf16[2,128,512]{2,1,0:T(8,128)(2,1)S(1)} %constant_dynamic-update-slice_fusion), channel_id=1, source_target_pairs={{0,8},{4,12},{1,9},{5,13},{2,10},{6,14},{3,11},{7,15},{16,24},{20,... | collective-permute-start | bytes 786440 | tf_op jit(solution)/shard_map/ppermute | solution.py:28
  11.1 1.3 %collective-permute-start.2 = (bf16[2,128,512]{2,1,0:T(8,128)(2,1)S(1)}, bf16[2,128,512]{2,1,0:T(8,128)(2,1)S(1)}, u32[]{:S(2)}, u32[]{:S(2)}) collective-permute-start(bf16[2,128,512]{2,1,0:T(8,128)(2,1)S(1)} %constant_dynamic-update-slice_fusion), channel_id=1, source_target_pairs={{0,12},{1,13},{2,14},{3,15},{16,28},{17,29},{18,30},{19,31}} | collective-permute-start | bytes 786440 | tf_op jit(solution)/shard_map/ppermute | solution.py:28
  12.4 0.1 iota_add_fusion
  12.5 0.1 compare_and_fusion
  12.6 0.1 copy.16
  12.7 0.0 copy-start.5
  12.7 0.7 copy-done.5
  13.3 0.2 compare_reduce_fusion
  13.5 0.1 copy.17
  13.6 0.2 compare_reduce_fusion.1
  13.8 0.0 copy-start.4
  13.8 0.1 min.12
  13.9 0.1 or_or_fusion
  14.0 0.5 copy-done.4
  14.5 0.6 gather_fusion
  15.1 0.1 fusion.4
  15.2 0.1 copy.18
  15.3 0.2 broadcast_in_dim.18
  15.5 0.8 convert_element_type.24.mask_ref
  16.3 0.0 collective-permute-done
  16.3 2.6 %collective-permute-done.1 = bf16[2,128,512]{2,1,0:T(8,128)(2,1)S(1)} collective-permute-done((bf16[2,128,512]{2,1,0:T(8,128)(2,1)S(1)}, bf16[2,128,512]{2,1,0:T(8,128)(2,1)S(1)}, u32[]{:S(2)}, u32[]{:S(2)}) %collective-permute-start.1) | collective-permute-done | bytes 262176 | tf_op jit(solution)/shard_map/ppermute | solution.py:28
  18.9 4.5 %collective-permute-done.2 = bf16[2,128,512]{2,1,0:T(8,128)(2,1)S(1)} collective-permute-done((bf16[2,128,512]{2,1,0:T(8,128)(2,1)S(1)}, bf16[2,128,512]{2,1,0:T(8,128)(2,1)S(1)}, u32[]{:S(2)}, u32[]{:S(2)}) %collective-permute-start.2) | collective-permute-done | bytes 262176 | tf_op jit(solution)/shard_map/ppermute | solution.py:28
  23.4 1.1 %pad_maximum_fusion.kv_ref = bf16[4,2,128,512]{3,2,1,0:T(8,128)(2,1)} fusion(bf16[1,2,128,512]{3,2,1,0:T(8,128)(2,1)S(1)} %bitcast.42, bf16[1,2,128,512]{3,2,1,0:T(8,128)(2,1)S(1)} %bitcast.41, bf16[1,2,128,512]{3,2,1,0:T(8,128)(2,1)S(1)} %bitcast.40, bf16[1,2,128,512]{3,2,1,0:T(8,128)(2,1)S(1)} %bitcast.38), kind=kLoop, calls=%fused_computation.1 | loop fusion | flops 1572864 | bytes 2097152 | tf_op jit(solution)/shard_map/stack | solution.py:232
  24.5 6.0 %shard_map.93 = (bf16[128,2048]{1,0:T(8,128)(2,1)}, f32[4,512,1]{2,1,0:T(8,128)}, f32[4,512,1]{2,1,0:T(8,128)}) custom-call(bf16[128,2048]{1,0:T(8,128)(2,1)} %bitcast.32, bf16[128,2048]{1,0:T(8,128)(2,1)} %bitcast.35, bf16[4,2,128,512]{3,2,1,0:T(8,128)(2,1)} %pad_maximum_fusion.kv_ref, f32[4,16,2,128]{3,2,1,0:T(2,128)} %convert_element_type.24.mask_ref), custom_call_target="tpu_custom_call" | custom-call | flops 536870912 | bytes 2621440 | tf_op jit(solution)/shard_map/pallas_call | solution.py:154
  30.5 1.5 %collective-permute-start.3 = (bf16[1,128,2048]{2,1,0:T(8,128)(2,1)}, bf16[1,128,2048]{2,1,0:T(8,128)(2,1)S(1)}, u32[]{:S(2)}, u32[]{:S(2)}) collective-permute-start(bf16[1,128,2048]{2,1,0:T(8,128)(2,1)} %bitcast.47), channel_id=1, source_target_pairs={{0,16},{16,0},{1,17},{17,1},{2,18},{18,2},{3,19},{19,3},{4,20},{20... | collective-permute-start | bytes 1572872 | tf_op jit(solution)/shard_map/ppermute | solution.py:22
  32.0 5.0 %shard_map.94 = (bf16[128,2048]{1,0:T(8,128)(2,1)}, bf16[4,2,128,512]{3,2,1,0:T(8,128)(2,1)}) custom-call(bf16[128,2048]{1,0:T(8,128)(2,1)} %bitcast.33, bf16[128,2048]{1,0:T(8,128)(2,1)} %bitcast.36, bf16[4,2,128,512]{3,2,1,0:T(8,128)(2,1)} %pad_maximum_fusion.kv_ref, f32[4,16,2,128]{3,2,1,0:T(2,128)} %convert_element_type.24.mask_ref, ...), custom_call_target="tpu_custom_call" | custom-call | flops 671088640 | bytes 1572864 | tf_op jit(solution)/shard_map/pallas_call | solution.py:195
  37.0 6.4 %collective-permute-done.3.rest_2_ = bf16[1,128,2048]{2,1,0:T(8,128)(2,1)S(1)} collective-permute-done((bf16[1,128,2048]{2,1,0:T(8,128)(2,1)}, bf16[1,128,2048]{2,1,0:T(8,128)(2,1)S(1)}, u32[]{:S(2)}, u32[]{:S(2)}) %collective-permute-start.3) | collective-permute-done | bytes 524320 | tf_op jit(solution)/shard_map/ppermute | solution.py:22
  43.5 0.0 copy-start
  43.5 0.8 copy-done
  44.3 5.0 %shard_map.95 = (bf16[128,2048]{1,0:T(8,128)(2,1)}, bf16[4,2,128,512]{3,2,1,0:T(8,128)(2,1)}) custom-call(bf16[128,2048]{1,0:T(8,128)(2,1)} %bitcast.34, bf16[128,2048]{1,0:T(8,128)(2,1)} %bitcast.37, bf16[4,2,128,512]{3,2,1,0:T(8,128)(2,1)} %pad_maximum_fusion.kv_ref, ...), custom_call_target="tpu_custom_call", output_to_operand_aliasing={{0}: (6, {}), {1}: (7, {})} | custom-call | flops 671088640 | bytes 1572864 | tf_op jit(solution)/shard_map/pallas_call | solution.py:195
  49.3 0.0 copy-start.2
  49.3 1.2 %slice_bitcast_fusion.2 = (bf16[2,128,512]{2,1,0:T(8,128)(2,1)S(1)}, bf16[2,128,512]{2,1,0:T(8,128)(2,1)S(1)}, bf16[2,128,512]{2,1,0:T(8,128)(2,1)S(1)}) fusion(bf16[4,2,128,512]{3,2,1,0:T(8,128)(2,1)} %get-tuple-element.17), kind=kLoop, calls=%fused_computation.8 | loop fusion | bytes 1572864 | tf_op jit(solution)/shard_map/squeeze | solution.py:249
  50.5 1.3 %collective-permute-start.5 = (bf16[2,128,512]{2,1,0:T(8,128)(2,1)S(1)}, bf16[2,128,512]{2,1,0:T(8,128)(2,1)S(1)}, u32[]{:S(2)}, u32[]{:S(2)}) collective-permute-start(bf16[2,128,512]{2,1,0:T(8,128)(2,1)S(1)} %get-tuple-element.18), channel_id=1, source_target_pairs={{4,0},{8,4},{12,8},{5,1},{9,5},{13,9},{6,2},{10,6},{14,10},{7,3},{... | collective-permute-start | bytes 786440 | tf_op jit(solution)/shard_map/ppermute | solution.py:28
  51.8 1.3 %collective-permute-start.6 = (bf16[2,128,512]{2,1,0:T(8,128)(2,1)S(1)}, bf16[2,128,512]{2,1,0:T(8,128)(2,1)S(1)}, u32[]{:S(2)}, u32[]{:S(2)}) collective-permute-start(bf16[2,128,512]{2,1,0:T(8,128)(2,1)S(1)} %get-tuple-element.20), channel_id=1, source_target_pairs={{8,0},{12,4},{9,1},{13,5},{10,2},{14,6},{11,3},{15,7},{24,16},{28,... | collective-permute-start | bytes 786440 | tf_op jit(solution)/shard_map/ppermute | solution.py:28
  53.1 1.3 %collective-permute-start.7 = (bf16[2,128,512]{2,1,0:T(8,128)(2,1)S(1)}, bf16[2,128,512]{2,1,0:T(8,128)(2,1)S(1)}, u32[]{:S(2)}, u32[]{:S(2)}) collective-permute-start(bf16[2,128,512]{2,1,0:T(8,128)(2,1)S(1)} %get-tuple-element.19), channel_id=1, source_target_pairs={{12,0},{13,1},{14,2},{15,3},{28,16},{29,17},{30,18},{31,19}} | collective-permute-start | bytes 786440 | tf_op jit(solution)/shard_map/ppermute | solution.py:28
  54.4 0.0 copy-done.2
  54.5 1.6 %collective-permute-start.4 = (bf16[1,128,2048]{2,1,0:T(8,128)(2,1)S(1)}, bf16[1,128,2048]{2,1,0:T(8,128)(2,1)S(1)}, u32[]{:S(2)}, u32[]{:S(2)}) collective-permute-start(bf16[1,128,2048]{2,1,0:T(8,128)(2,1)S(1)} %bitcast.39), channel_id=1, source_target_pairs={{0,16},{16,0},{1,17},{17,1},{2,18},{18,2},{3,19},{19,3},{4,20},{20... | collective-permute-start | bytes 1572872 | tf_op jit(solution)/shard_map/ppermute | solution.py:22
  56.0 9.1 %collective-permute-done.5 = bf16[2,128,512]{2,1,0:T(8,128)(2,1)S(1)} collective-permute-done((bf16[2,128,512]{2,1,0:T(8,128)(2,1)S(1)}, bf16[2,128,512]{2,1,0:T(8,128)(2,1)S(1)}, u32[]{:S(2)}, u32[]{:S(2)}) %collective-permute-start.5) | collective-permute-done | bytes 262176 | tf_op jit(solution)/shard_map/ppermute | solution.py:28
  65.2 17.0 %collective-permute-done.6 = bf16[2,128,512]{2,1,0:T(8,128)(2,1)S(1)} collective-permute-done((bf16[2,128,512]{2,1,0:T(8,128)(2,1)S(1)}, bf16[2,128,512]{2,1,0:T(8,128)(2,1)S(1)}, u32[]{:S(2)}, u32[]{:S(2)}) %collective-permute-start.6) | collective-permute-done | bytes 262176 | tf_op jit(solution)/shard_map/ppermute | solution.py:28
  82.1 0.0 collective-permute-done.7
  82.1 1.1 %fusion.2 = bf16[2,128,512]{2,1,0:T(8,128)(2,1)S(1)} fusion(bf16[2,128,512]{2,1,0:T(8,128)(2,1)S(1)} %collective-permute-done.7, bf16[2,128,512]{2,1,0:T(8,128)(2,1)S(1)} %collective-permute-done.6, bf16[2,128,512]{2,1,0:T(8,128)(2,1)S(1)} %collective-permute-done.5, bf16[4,2,128,512]{3,2,1,0:T(8,128)(2,1)} %get-tuple-element.17), kind=kLoop, calls=%fused_computation.5 | loop fusion | flops 1048576 | bytes 1310720 | tf_op jit(solution)/shard_map/convert_element_type | solution.py:250
  83.2 0.0 copy-start.1
  83.2 1.6 %collective-permute-start.8 = (bf16[2,128,512]{2,1,0:T(8,128)(2,1)S(1)}, bf16[2,128,512]{2,1,0:T(8,128)(2,1)S(1)}, u32[]{:S(2)}, u32[]{:S(2)}) collective-permute-start(bf16[2,128,512]{2,1,0:T(8,128)(2,1)S(1)} %fusion.2), channel_id=1, source_target_pairs={{0,16},{16,0},{1,17},{17,1},{2,18},{18,2},{3,19},{19,3},{4,20},{20... | collective-permute-start | bytes 786440 | tf_op jit(solution)/shard_map/ppermute | solution.py:22
  84.8 4.9 %collective-permute-done.8 = bf16[2,128,512]{2,1,0:T(8,128)(2,1)S(1)} collective-permute-done((bf16[2,128,512]{2,1,0:T(8,128)(2,1)S(1)}, bf16[2,128,512]{2,1,0:T(8,128)(2,1)S(1)}, u32[]{:S(2)}, u32[]{:S(2)}) %collective-permute-start.8) | collective-permute-done | bytes 262176 | tf_op jit(solution)/shard_map/ppermute | solution.py:22
  89.7 0.7 fusion.8
  90.4 0.0 collective-permute-done.4
  90.4 0.0 copy-done.1
  90.4 0.8 copy.26
  91.2 0.8 copy.27
  (7 shorter events, 0.0 us)
Async XLA Ops:
  0.6 1.0 %copy-start.3 = (bf16[1,128,512]{2,1,0:T(8,128)(2,1)S(1)}, bf16[1,128,512]{2,1,0:T(8,128)(2,1)}, u32[]{:S(2)}) copy-start(bf16[1,128,512]{2,1,0:T(8,128)(2,1)} %param.8) | copy-start | bytes 393220
  1.6 14.7 %collective-permute-start = (bf16[2,128,512]{2,1,0:T(8,128)(2,1)S(1)}, bf16[2,128,512]{2,1,0:T(8,128)(2,1)S(1)}, u32[]{:S(2)}, u32[]{:S(2)}) collective-permute-start(bf16[2,128,512]{2,1,0:T(8,128)(2,1)S(1)} %constant_dynamic-update-slice_fusion), channel_id=1, source_target_pairs={{0,4},{4,8},{8,12},{1,5},{5,9},{9,13},{2,6},{6,10},{10,14},{3,7},{... | collective-permute-start | bytes 786440 | tf_op jit(solution)/shard_map/ppermute | solution.py:28
  6.6 12.3 %collective-permute-start.1 = (bf16[2,128,512]{2,1,0:T(8,128)(2,1)S(1)}, bf16[2,128,512]{2,1,0:T(8,128)(2,1)S(1)}, u32[]{:S(2)}, u32[]{:S(2)}) collective-permute-start(bf16[2,128,512]{2,1,0:T(8,128)(2,1)S(1)} %constant_dynamic-update-slice_fusion), channel_id=1, source_target_pairs={{0,8},{4,12},{1,9},{5,13},{2,10},{6,14},{3,11},{7,15},{16,24},{20,... | collective-permute-start | bytes 786440 | tf_op jit(solution)/shard_map/ppermute | solution.py:28
  11.1 12.3 %collective-permute-start.2 = (bf16[2,128,512]{2,1,0:T(8,128)(2,1)S(1)}, bf16[2,128,512]{2,1,0:T(8,128)(2,1)S(1)}, u32[]{:S(2)}, u32[]{:S(2)}) collective-permute-start(bf16[2,128,512]{2,1,0:T(8,128)(2,1)S(1)} %constant_dynamic-update-slice_fusion), channel_id=1, source_target_pairs={{0,12},{1,13},{2,14},{3,15},{16,28},{17,29},{18,30},{19,31}} | collective-permute-start | bytes 786440 | tf_op jit(solution)/shard_map/ppermute | solution.py:28
  12.7 0.7 copy-start.5
  13.8 0.7 copy-start.4
  30.5 13.0 %collective-permute-start.3 = (bf16[1,128,2048]{2,1,0:T(8,128)(2,1)}, bf16[1,128,2048]{2,1,0:T(8,128)(2,1)S(1)}, u32[]{:S(2)}, u32[]{:S(2)}) collective-permute-start(bf16[1,128,2048]{2,1,0:T(8,128)(2,1)} %bitcast.47), channel_id=1, source_target_pairs={{0,16},{16,0},{1,17},{17,1},{2,18},{18,2},{3,19},{19,3},{4,20},{20... | collective-permute-start | bytes 1572872 | tf_op jit(solution)/shard_map/ppermute | solution.py:22
  43.5 0.8 copy-start
  49.3 5.2 %copy-start.2 = (bf16[128,2048]{1,0:T(8,128)(2,1)S(1)}, bf16[128,2048]{1,0:T(8,128)(2,1)}, u32[]{:S(2)}) copy-start(bf16[128,2048]{1,0:T(8,128)(2,1)} %get-tuple-element.16) | copy-start | bytes 1572868
  50.5 14.6 %collective-permute-start.5 = (bf16[2,128,512]{2,1,0:T(8,128)(2,1)S(1)}, bf16[2,128,512]{2,1,0:T(8,128)(2,1)S(1)}, u32[]{:S(2)}, u32[]{:S(2)}) collective-permute-start(bf16[2,128,512]{2,1,0:T(8,128)(2,1)S(1)} %get-tuple-element.18), channel_id=1, source_target_pairs={{4,0},{8,4},{12,8},{5,1},{9,5},{13,9},{6,2},{10,6},{14,10},{7,3},{... | collective-permute-start | bytes 786440 | tf_op jit(solution)/shard_map/ppermute | solution.py:28
  51.8 30.3 %collective-permute-start.6 = (bf16[2,128,512]{2,1,0:T(8,128)(2,1)S(1)}, bf16[2,128,512]{2,1,0:T(8,128)(2,1)S(1)}, u32[]{:S(2)}, u32[]{:S(2)}) collective-permute-start(bf16[2,128,512]{2,1,0:T(8,128)(2,1)S(1)} %get-tuple-element.20), channel_id=1, source_target_pairs={{8,0},{12,4},{9,1},{13,5},{10,2},{14,6},{11,3},{15,7},{24,16},{28,... | collective-permute-start | bytes 786440 | tf_op jit(solution)/shard_map/ppermute | solution.py:28
  53.1 29.0 %collective-permute-start.7 = (bf16[2,128,512]{2,1,0:T(8,128)(2,1)S(1)}, bf16[2,128,512]{2,1,0:T(8,128)(2,1)S(1)}, u32[]{:S(2)}, u32[]{:S(2)}) collective-permute-start(bf16[2,128,512]{2,1,0:T(8,128)(2,1)S(1)} %get-tuple-element.19), channel_id=1, source_target_pairs={{12,0},{13,1},{14,2},{15,3},{28,16},{29,17},{30,18},{31,19}} | collective-permute-start | bytes 786440 | tf_op jit(solution)/shard_map/ppermute | solution.py:28
  54.5 35.9 %collective-permute-start.4 = (bf16[1,128,2048]{2,1,0:T(8,128)(2,1)S(1)}, bf16[1,128,2048]{2,1,0:T(8,128)(2,1)S(1)}, u32[]{:S(2)}, u32[]{:S(2)}) collective-permute-start(bf16[1,128,2048]{2,1,0:T(8,128)(2,1)S(1)} %bitcast.39), channel_id=1, source_target_pairs={{0,16},{16,0},{1,17},{17,1},{2,18},{18,2},{3,19},{19,3},{4,20},{20... | collective-permute-start | bytes 1572872 | tf_op jit(solution)/shard_map/ppermute | solution.py:22
  83.2 7.2 %copy-start.1 = (bf16[1,128,2048]{2,1,0:T(8,128)(2,1)S(1)}, bf16[1,128,2048]{2,1,0:T(8,128)(2,1)}, u32[]{:S(2)}) copy-start(bf16[1,128,2048]{2,1,0:T(8,128)(2,1)} %copy-done) | copy-start | bytes 1572868
  83.2 6.4 %collective-permute-start.8 = (bf16[2,128,512]{2,1,0:T(8,128)(2,1)S(1)}, bf16[2,128,512]{2,1,0:T(8,128)(2,1)S(1)}, u32[]{:S(2)}, u32[]{:S(2)}) collective-permute-start(bf16[2,128,512]{2,1,0:T(8,128)(2,1)S(1)} %fusion.2), channel_id=1, source_target_pairs={{0,16},{16,0},{1,17},{17,1},{2,18},{18,2},{3,19},{19,3},{4,20},{20... | collective-permute-start | bytes 786440 | tf_op jit(solution)/shard_map/ppermute | solution.py:22

commit v4 on v3

--- a/solution.py
+++ b/solution.py
@@ -228,25 +228,30 @@
     masks = block_masks(random_blocks[0], global_ids[0], ctx_index, ctx_count, tok_rows)
 
     own = jnp.stack([keys[0], values[0]])
-    pieces = [own] + [shifted_open(own, "ctx", shift) for shift in range(1, ctx_count)]
+    pieces = [own]
+    for shift in range(1, ctx_count):
+        pieces.append(shifted_open(pieces[-1], "ctx", 1))
     kv_pieces = jnp.stack(pieces)
 
     attended, log_total, delta = attention_forward(query[0], grad_out[0], kv_pieces, masks)
     next_input = passed_along(attended[None], "pipe", 1)
 
-    half = KVH // 2
-    first_dq, first_dkv = attention_backward(
-        query[0], grad_out[0], kv_pieces, masks, log_total, delta, 0, half, [None]
-    )
     query_grad, kv_terms = attention_backward(
-        query[0], grad_out[0], kv_pieces, masks, log_total, delta, half, KVH - half,
-        [first_dq, first_dkv, next_input],
-    )
+        query[0], grad_out[0], kv_pieces, masks, log_total, delta, 0, KVH, [None]
+    )
+    next_input, kv_terms = lax.optimization_barrier((next_input, kv_terms))
     grad_query = passed_along(query_grad[None], "pipe", -1)
 
+    carried = None
+    for step in range(1, ctx_count):
+        part = kv_terms[ctx_count - step].astype(jnp.float32)
+        if carried is not None:
+            part = part + carried.astype(jnp.float32)
+        carried = shifted_open(part.astype(jnp.bfloat16), "ctx", -1)
     kv_sum = kv_terms[0].astype(jnp.float32)
-    for shift in range(1, ctx_count):
-        kv_sum = kv_sum + shifted_open(kv_terms[shift], "ctx", -shift).astype(jnp.float32)
+    if carried is not None:
+        grad_query, carried = lax.optimization_barrier((grad_query, carried))
+        kv_sum = kv_sum + carried.astype(jnp.float32)
     returned = passed_along(kv_sum.astype(jnp.bfloat16), "pipe", -1)
     grad_key = returned[0:1]
     grad_value = returned[1:2]

time: 92.5 us -> 85.7 us (0.926)
  waiting for transfers between devices: 44.4 us -> 38.3 us
  starting transfers between devices: 19.3 us -> 22.3 us
  Pallas kernels: 16 us -> 14.1 us
  local copies, waits for them, and re-layouts: 8.44 us -> 6.87 us
    ppermute x3, waiting for transfers between devices: 11.3 us -> 6.44 us  [passed_along(): return lax.ppermute(value, axis, pairs)]
    ppermute x6, starting transfers between devices: 14.6 us -> 17.6 us  [shifted_open(): return lax.ppermute(value, axis, pairs)]
    pallas_call x2 -> x1, Pallas kernels: 10.1 us -> 8.12 us  [attention_backward(): pl.pallas_call(functools.partial(backward_kernel, piece_count, group_size...]
    ppermute x6, waiting for transfers between devices: 33.2 us -> 31.8 us  [shifted_open(): return lax.ppermute(value, axis, pairs)]
    unnamed x16 -> x12, local copies, waits for them, and re-layouts: 4.51 us -> 3.21 us
    convert_element_type x0 -> x2, other arithmetic: none -> 1.08 us  [local(): carried = shifted_open(part.astype(jnp.bfloat16), 'ctx', -1)]
    convert_element_type x1, other arithmetic: 1.09 us -> 0.07 us  [local(): returned = passed_along(kv_sum.astype(jnp.bfloat16), 'pipe', -1)]
  transfers between devices with their start and end apart: 9 -> 9, of which waited for: 6 -> 8; matrix products, arithmetic and copies ran while one was open for 5% -> 3% of each run, Pallas kernels for 5% -> 10%
where the time goes in v4:
time: 85.7 us; the launch traced here: 85.3 us
  waiting for transfers between devices  38.3 us (45%)
  starting transfers between devices  22.3 us (26%)
  Pallas kernels  14.1 us (16%)
  local copies, waits for them, and re-layouts  6.87 us (8%)
  other arithmetic  2.99 us (3%)
    ppermute x6, waiting for transfers between devices, shifted_open(): return lax.ppermute(value, axis, pairs)  31.8 us
    ppermute x6, starting transfers between devices, shifted_open(): return lax.ppermute(value, axis, pairs)  17.6 us
    pallas_call x1, Pallas kernels, attention_backward(): pl.pallas_call(functools.partial(backward_kernel, piece_count, group_size...  8.12 us
    ppermute x3, waiting for transfers between devices, passed_along(): return lax.ppermute(value, axis, pairs)  6.44 us
    pallas_call x1, Pallas kernels, attention_forward(): pl.pallas_call(functools.partial(forward_kernel, piece_count, group_size)...  5.97 us
    ppermute x3, starting transfers between devices, passed_along(): return lax.ppermute(value, axis, pairs)  4.68 us
    unnamed x12, local copies, waits for them, and re-layouts  3.21 us
  transfers between devices with their start and end apart: 9, of which 8 were waited for; matrix products, arithmetic and copies ran while one was open for 3% of the time, Pallas kernels for 10%

profile of v4, /device:TPU:0, one launch (start us, length us, event | category | flops | bytes accessed | tf_op | source)
XLA Modules:
  0.0 85.3 jit_solution(12853327881755325150)
XLA Ops:
  0.6 0.0 copy-start.1
  0.6 0.9 %constant_dynamic-update-slice_fusion.1 = bf16[2,128,512]{2,1,0:T(8,128)(2,1)S(1)} fusion(bf16[1,128,512]{2,1,0:T(8,128)(2,1)} %param.7), kind=kLoop, calls=%fused_computation.17 | loop fusion | bytes 262144
  1.6 0.0 copy-done.1
  1.6 4.9 %collective-permute-start = (bf16[2,128,512]{2,1,0:T(8,128)(2,1)S(1)}, bf16[2,128,512]{2,1,0:T(8,128)(2,1)S(1)}, u32[]{:S(2)}, u32[]{:S(2)}) collective-permute-start(bf16[2,128,512]{2,1,0:T(8,128)(2,1)S(1)} %constant_dynamic-update-slice_fusion), channel_id=1, source_target_pairs={{0,4},{4,8},{8,12},{1,5},{5,9},{9,13},{2,6},{6,10},{10,14},{3,7},{... | collective-permute-start | bytes 786440 | tf_op jit(solution)/shard_map/ppermute | solution.py:28
  6.6 0.1 compare_and_fusion
  6.7 0.1 iota_add_fusion
  6.7 0.1 copy.14
  6.8 0.0 copy-start.3
  6.8 0.7 copy-done.3
  7.5 0.2 compare_reduce_fusion
  7.7 0.2 compare_reduce_fusion.1
  7.9 0.1 min.12
  8.0 0.0 copy-start.2
  8.0 4.1 %collective-permute-done = bf16[2,128,512]{2,1,0:T(8,128)(2,1)S(1)} collective-permute-done((bf16[2,128,512]{2,1,0:T(8,128)(2,1)S(1)}, bf16[2,128,512]{2,1,0:T(8,128)(2,1)S(1)}, u32[]{:S(2)}, u32[]{:S(2)}) %collective-permute-start) | collective-permute-done | bytes 262176 | tf_op jit(solution)/shard_map/ppermute | solution.py:28
  12.1 4.4 %collective-permute-start.1 = (bf16[2,128,512]{2,1,0:T(8,128)(2,1)S(1)}, bf16[2,128,512]{2,1,0:T(8,128)(2,1)S(1)}, u32[]{:S(2)}, u32[]{:S(2)}) collective-permute-start(bf16[2,128,512]{2,1,0:T(8,128)(2,1)S(1)} %collective-permute-done), channel_id=1, source_target_pairs={{0,4},{4,8},{8,12},{1,5},{5,9},{9,13},{2,6},{6,10},{10,14},{3,7},{... | collective-permute-start | bytes 786440 | tf_op jit(solution)/shard_map/ppermute | solution.py:28
  16.5 0.1 copy.15
  16.6 0.1 or_or_fusion
  16.7 4.5 %collective-permute-done.1 = bf16[2,128,512]{2,1,0:T(8,128)(2,1)S(1)} collective-permute-done((bf16[2,128,512]{2,1,0:T(8,128)(2,1)S(1)}, bf16[2,128,512]{2,1,0:T(8,128)(2,1)S(1)}, u32[]{:S(2)}, u32[]{:S(2)}) %collective-permute-start.1) | collective-permute-done | bytes 262176 | tf_op jit(solution)/shard_map/ppermute | solution.py:28
  21.2 4.4 %collective-permute-start.2 = (bf16[2,128,512]{2,1,0:T(8,128)(2,1)S(1)}, bf16[2,128,512]{2,1,0:T(8,128)(2,1)S(1)}, u32[]{:S(2)}, u32[]{:S(2)}) collective-permute-start(bf16[2,128,512]{2,1,0:T(8,128)(2,1)S(1)} %collective-permute-done.1), channel_id=1, source_target_pairs={{0,4},{4,8},{8,12},{1,5},{5,9},{9,13},{2,6},{6,10},{10,14},{3,7},{... | collective-permute-start | bytes 786440 | tf_op jit(solution)/shard_map/ppermute | solution.py:28
  25.6 0.0 copy-done.2
  25.6 0.6 gather_fusion
  26.2 0.1 fusion.4
  26.3 0.1 copy.16
  26.4 0.2 broadcast_in_dim.18
  26.6 0.8 convert_element_type.44.mask_ref
  27.4 2.0 %collective-permute-done.2 = bf16[2,128,512]{2,1,0:T(8,128)(2,1)S(1)} collective-permute-done((bf16[2,128,512]{2,1,0:T(8,128)(2,1)S(1)}, bf16[2,128,512]{2,1,0:T(8,128)(2,1)S(1)}, u32[]{:S(2)}, u32[]{:S(2)}) %collective-permute-start.2) | collective-permute-done | bytes 262176 | tf_op jit(solution)/shard_map/ppermute | solution.py:28
  29.4 1.1 %pad_maximum_fusion.kv_ref = bf16[4,2,128,512]{3,2,1,0:T(8,128)(2,1)} fusion(bf16[1,2,128,512]{3,2,1,0:T(8,128)(2,1)S(1)} %bitcast.41, bf16[1,2,128,512]{3,2,1,0:T(8,128)(2,1)S(1)} %bitcast.40, bf16[1,2,128,512]{3,2,1,0:T(8,128)(2,1)S(1)} %bitcast.39, bf16[1,2,128,512]{3,2,1,0:T(8,128)(2,1)S(1)} %bitcast.34), kind=kLoop, calls=%fused_computation.1 | loop fusion | flops 1572864 | bytes 2097152 | tf_op jit(solution)/shard_map/stack | solution.py:234
  30.5 6.0 %shard_map.93 = (bf16[128,2048]{1,0:T(8,128)(2,1)}, f32[4,512,1]{2,1,0:T(8,128)}, f32[4,512,1]{2,1,0:T(8,128)}) custom-call(bf16[128,2048]{1,0:T(8,128)(2,1)} %bitcast.35, bf16[128,2048]{1,0:T(8,128)(2,1)} %bitcast.37, bf16[4,2,128,512]{3,2,1,0:T(8,128)(2,1)} %pad_maximum_fusion.kv_ref, f32[4,16,2,128]{3,2,1,0:T(2,128)} %convert_element_type.44.mask_ref), custom_call_target="tpu_custom_call" | custom-call | flops 536870912 | bytes 2621440 | tf_op jit(solution)/shard_map/pallas_call | solution.py:154
  36.5 1.5 %collective-permute-start.3 = (bf16[1,128,2048]{2,1,0:T(8,128)(2,1)}, bf16[1,128,2048]{2,1,0:T(8,128)(2,1)S(1)}, u32[]{:S(2)}, u32[]{:S(2)}) collective-permute-start(bf16[1,128,2048]{2,1,0:T(8,128)(2,1)} %bitcast.47), channel_id=1, source_target_pairs={{0,16},{16,0},{1,17},{17,1},{2,18},{18,2},{3,19},{19,3},{4,20},{20... | collective-permute-start | bytes 1572872 | tf_op jit(solution)/shard_map/ppermute | solution.py:22
  38.0 8.1 %shard_map.94 = (bf16[128,2048]{1,0:T(8,128)(2,1)}, bf16[4,2,128,512]{3,2,1,0:T(8,128)(2,1)}) custom-call(bf16[128,2048]{1,0:T(8,128)(2,1)} %bitcast.36, bf16[128,2048]{1,0:T(8,128)(2,1)} %bitcast.38, bf16[4,2,128,512]{3,2,1,0:T(8,128)(2,1)} %pad_maximum_fusion.kv_ref, f32[4,16,2,128]{3,2,1,0:T(2,128)} %convert_element_type.44.mask_ref, ...), custom_call_target="tpu_custom_call" | custom-call | flops 1342177280 | bytes 3145728 | tf_op jit(solution)/shard_map/pallas_call | solution.py:195
  46.1 0.0 copy-start
  46.1 1.6 %collective-permute-done.3 = bf16[1,128,2048]{2,1,0:T(8,128)(2,1)S(1)} collective-permute-done((bf16[1,128,2048]{2,1,0:T(8,128)(2,1)}, bf16[1,128,2048]{2,1,0:T(8,128)(2,1)S(1)}, u32[]{:S(2)}, u32[]{:S(2)}) %collective-permute-start.3) | collective-permute-done | bytes 524320 | tf_op jit(solution)/shard_map/ppermute | solution.py:22
  47.7 1.0 %slice_bitcast_fusion = bf16[2,128,512]{2,1,0:T(8,128)(2,1)S(1)} fusion(bf16[4,2,128,512]{3,2,1,0:T(8,128)(2,1)} %get-tuple-element.19), kind=kLoop, calls=%fused_computation.8 | loop fusion | bytes 524288 | tf_op jit(solution)/shard_map/squeeze | solution.py:247
  48.7 1.3 %collective-permute-start.5 = (bf16[2,128,512]{2,1,0:T(8,128)(2,1)S(1)}, bf16[2,128,512]{2,1,0:T(8,128)(2,1)S(1)}, u32[]{:S(2)}, u32[]{:S(2)}) collective-permute-start(bf16[2,128,512]{2,1,0:T(8,128)(2,1)S(1)} %slice_bitcast_fusion), channel_id=1, source_target_pairs={{4,0},{8,4},{12,8},{5,1},{9,5},{13,9},{6,2},{10,6},{14,10},{7,3},{... | collective-permute-start | bytes 786440 | tf_op jit(solution)/shard_map/ppermute | solution.py:28
  50.0 7.1 %collective-permute-done.5 = bf16[2,128,512]{2,1,0:T(8,128)(2,1)S(1)} collective-permute-done((bf16[2,128,512]{2,1,0:T(8,128)(2,1)S(1)}, bf16[2,128,512]{2,1,0:T(8,128)(2,1)S(1)}, u32[]{:S(2)}, u32[]{:S(2)}) %collective-permute-start.5) | collective-permute-done | bytes 262176 | tf_op jit(solution)/shard_map/ppermute | solution.py:28
  57.1 1.0 %fusion.1 = bf16[2,128,512]{2,1,0:T(8,128)(2,1)S(1)} fusion(bf16[2,128,512]{2,1,0:T(8,128)(2,1)S(1)} %collective-permute-done.5, bf16[4,2,128,512]{3,2,1,0:T(8,128)(2,1)} %get-tuple-element.19), kind=kLoop, calls=%fused_computation.5 | loop fusion | flops 524288 | bytes 786432 | tf_op jit(solution)/shard_map/convert_element_type | solution.py:250
  58.1 1.3 %collective-permute-start.6 = (bf16[2,128,512]{2,1,0:T(8,128)(2,1)S(1)}, bf16[2,128,512]{2,1,0:T(8,128)(2,1)S(1)}, u32[]{:S(2)}, u32[]{:S(2)}) collective-permute-start(bf16[2,128,512]{2,1,0:T(8,128)(2,1)S(1)} %fusion.1), channel_id=1, source_target_pairs={{4,0},{8,4},{12,8},{5,1},{9,5},{13,9},{6,2},{10,6},{14,10},{7,3},{... | collective-permute-start | bytes 786440 | tf_op jit(solution)/shard_map/ppermute | solution.py:28
  59.4 1.6 %collective-permute-start.4 = (bf16[1,128,2048]{2,1,0:T(8,128)(2,1)}, bf16[1,128,2048]{2,1,0:T(8,128)(2,1)S(1)}, u32[]{:S(2)}, u32[]{:S(2)}) collective-permute-start(bf16[1,128,2048]{2,1,0:T(8,128)(2,1)} %bitcast.46), channel_id=1, source_target_pairs={{0,16},{16,0},{1,17},{17,1},{2,18},{18,2},{3,19},{19,3},{4,20},{20... | collective-permute-start | bytes 1572872 | tf_op jit(solution)/shard_map/ppermute | solution.py:22
  61.0 6.8 %collective-permute-done.6 = bf16[2,128,512]{2,1,0:T(8,128)(2,1)S(1)} collective-permute-done((bf16[2,128,512]{2,1,0:T(8,128)(2,1)S(1)}, bf16[2,128,512]{2,1,0:T(8,128)(2,1)S(1)}, u32[]{:S(2)}, u32[]{:S(2)}) %collective-permute-start.6) | collective-permute-done | bytes 262176 | tf_op jit(solution)/shard_map/ppermute | solution.py:28
  67.8 0.0 copy-done
  67.9 0.1 fusion.2
  67.9 1.3 %collective-permute-start.7 = (bf16[2,128,512]{2,1,0:T(8,128)(2,1)S(1)}, bf16[2,128,512]{2,1,0:T(8,128)(2,1)S(1)}, u32[]{:S(2)}, u32[]{:S(2)}) collective-permute-start(bf16[2,128,512]{2,1,0:T(8,128)(2,1)S(1)} %fusion.2), channel_id=1, source_target_pairs={{4,0},{8,4},{12,8},{5,1},{9,5},{13,9},{6,2},{10,6},{14,10},{7,3},{... | collective-permute-start | bytes 786440 | tf_op jit(solution)/shard_map/ppermute | solution.py:28
  69.2 0.0 collective-permute-done.4
  69.2 7.3 %collective-permute-done.7 = bf16[2,128,512]{2,1,0:T(8,128)(2,1)S(1)} collective-permute-done((bf16[2,128,512]{2,1,0:T(8,128)(2,1)S(1)}, bf16[2,128,512]{2,1,0:T(8,128)(2,1)S(1)}, u32[]{:S(2)}, u32[]{:S(2)}) %collective-permute-start.7) | collective-permute-done | bytes 262176 | tf_op jit(solution)/shard_map/ppermute | solution.py:28
  76.5 0.1 fusion
  76.6 1.6 %collective-permute-start.8 = (bf16[2,128,512]{2,1,0:T(8,128)(2,1)S(1)}, bf16[2,128,512]{2,1,0:T(8,128)(2,1)S(1)}, u32[]{:S(2)}, u32[]{:S(2)}) collective-permute-start(bf16[2,128,512]{2,1,0:T(8,128)(2,1)S(1)} %fusion), channel_id=1, source_target_pairs={{0,16},{16,0},{1,17},{17,1},{2,18},{18,2},{3,19},{19,3},{4,20},{20... | collective-permute-start | bytes 786440 | tf_op jit(solution)/shard_map/ppermute | solution.py:22
  78.2 4.9 %collective-permute-done.8 = bf16[2,128,512]{2,1,0:T(8,128)(2,1)S(1)} collective-permute-done((bf16[2,128,512]{2,1,0:T(8,128)(2,1)S(1)}, bf16[2,128,512]{2,1,0:T(8,128)(2,1)S(1)}, u32[]{:S(2)}, u32[]{:S(2)}) %collective-permute-start.8) | collective-permute-done | bytes 262176 | tf_op jit(solution)/shard_map/ppermute | solution.py:22
  83.0 0.7 fusion.8
  83.7 0.8 copy.22
  84.5 0.8 copy.23
  (7 shorter events, 0.0 us)
Async XLA Ops:
  0.6 1.0 %copy-start.1 = (bf16[1,128,512]{2,1,0:T(8,128)(2,1)S(1)}, bf16[1,128,512]{2,1,0:T(8,128)(2,1)}, u32[]{:S(2)}) copy-start(bf16[1,128,512]{2,1,0:T(8,128)(2,1)} %param.8) | copy-start | bytes 393220
  1.6 10.5 %collective-permute-start = (bf16[2,128,512]{2,1,0:T(8,128)(2,1)S(1)}, bf16[2,128,512]{2,1,0:T(8,128)(2,1)S(1)}, u32[]{:S(2)}, u32[]{:S(2)}) collective-permute-start(bf16[2,128,512]{2,1,0:T(8,128)(2,1)S(1)} %constant_dynamic-update-slice_fusion), channel_id=1, source_target_pairs={{0,4},{4,8},{8,12},{1,5},{5,9},{9,13},{2,6},{6,10},{10,14},{3,7},{... | collective-permute-start | bytes 786440 | tf_op jit(solution)/shard_map/ppermute | solution.py:28
  6.8 0.7 copy-start.3
  8.0 17.6 %copy-start.2 = (s32[1,2,16,8]{2,3,1,0:T(8,128)S(1)}, s32[1,2,16,8]{2,3,1,0:T(8,128)}, u32[]{:S(2)}) copy-start(s32[1,2,16,8]{2,3,1,0:T(8,128)} %param.10) | copy-start | bytes 3076
  12.1 9.1 %collective-permute-start.1 = (bf16[2,128,512]{2,1,0:T(8,128)(2,1)S(1)}, bf16[2,128,512]{2,1,0:T(8,128)(2,1)S(1)}, u32[]{:S(2)}, u32[]{:S(2)}) collective-permute-start(bf16[2,128,512]{2,1,0:T(8,128)(2,1)S(1)} %collective-permute-done), channel_id=1, source_target_pairs={{0,4},{4,8},{8,12},{1,5},{5,9},{9,13},{2,6},{6,10},{10,14},{3,7},{... | collective-permute-start | bytes 786440 | tf_op jit(solution)/shard_map/ppermute | solution.py:28
  21.2 8.3 %collective-permute-start.2 = (bf16[2,128,512]{2,1,0:T(8,128)(2,1)S(1)}, bf16[2,128,512]{2,1,0:T(8,128)(2,1)S(1)}, u32[]{:S(2)}, u32[]{:S(2)}) collective-permute-start(bf16[2,128,512]{2,1,0:T(8,128)(2,1)S(1)} %collective-permute-done.1), channel_id=1, source_target_pairs={{0,4},{4,8},{8,12},{1,5},{5,9},{9,13},{2,6},{6,10},{10,14},{3,7},{... | collective-permute-start | bytes 786440 | tf_op jit(solution)/shard_map/ppermute | solution.py:28
  36.5 11.2 %collective-permute-start.3 = (bf16[1,128,2048]{2,1,0:T(8,128)(2,1)}, bf16[1,128,2048]{2,1,0:T(8,128)(2,1)S(1)}, u32[]{:S(2)}, u32[]{:S(2)}) collective-permute-start(bf16[1,128,2048]{2,1,0:T(8,128)(2,1)} %bitcast.47), channel_id=1, source_target_pairs={{0,16},{16,0},{1,17},{17,1},{2,18},{18,2},{3,19},{19,3},{4,20},{20... | collective-permute-start | bytes 1572872 | tf_op jit(solution)/shard_map/ppermute | solution.py:22
  46.1 21.7 %copy-start = (bf16[4,2,128,512]{3,2,1,0:T(8,128)(2,1)S(1)}, bf16[4,2,128,512]{3,2,1,0:T(8,128)(2,1)}, u32[]{:S(2)}) copy-start(bf16[4,2,128,512]{3,2,1,0:T(8,128)(2,1)} %get-tuple-element.19) | copy-start | bytes 3145732
  48.7 8.4 %collective-permute-start.5 = (bf16[2,128,512]{2,1,0:T(8,128)(2,1)S(1)}, bf16[2,128,512]{2,1,0:T(8,128)(2,1)S(1)}, u32[]{:S(2)}, u32[]{:S(2)}) collective-permute-start(bf16[2,128,512]{2,1,0:T(8,128)(2,1)S(1)} %slice_bitcast_fusion), channel_id=1, source_target_pairs={{4,0},{8,4},{12,8},{5,1},{9,5},{13,9},{6,2},{10,6},{14,10},{7,3},{... | collective-permute-start | bytes 786440 | tf_op jit(solution)/shard_map/ppermute | solution.py:28
  58.1 9.7 %collective-permute-start.6 = (bf16[2,128,512]{2,1,0:T(8,128)(2,1)S(1)}, bf16[2,128,512]{2,1,0:T(8,128)(2,1)S(1)}, u32[]{:S(2)}, u32[]{:S(2)}) collective-permute-start(bf16[2,128,512]{2,1,0:T(8,128)(2,1)S(1)} %fusion.1), channel_id=1, source_target_pairs={{4,0},{8,4},{12,8},{5,1},{9,5},{13,9},{6,2},{10,6},{14,10},{7,3},{... | collective-permute-start | bytes 786440 | tf_op jit(solution)/shard_map/ppermute | solution.py:28
  59.4 9.8 %collective-permute-start.4 = (bf16[1,128,2048]{2,1,0:T(8,128)(2,1)}, bf16[1,128,2048]{2,1,0:T(8,128)(2,1)S(1)}, u32[]{:S(2)}, u32[]{:S(2)}) collective-permute-start(bf16[1,128,2048]{2,1,0:T(8,128)(2,1)} %bitcast.46), channel_id=1, source_target_pairs={{0,16},{16,0},{1,17},{17,1},{2,18},{18,2},{3,19},{19,3},{4,20},{20... | collective-permute-start | bytes 1572872 | tf_op jit(solution)/shard_map/ppermute | solution.py:22
  67.9 8.6 %collective-permute-start.7 = (bf16[2,128,512]{2,1,0:T(8,128)(2,1)S(1)}, bf16[2,128,512]{2,1,0:T(8,128)(2,1)S(1)}, u32[]{:S(2)}, u32[]{:S(2)}) collective-permute-start(bf16[2,128,512]{2,1,0:T(8,128)(2,1)S(1)} %fusion.2), channel_id=1, source_target_pairs={{4,0},{8,4},{12,8},{5,1},{9,5},{13,9},{6,2},{10,6},{14,10},{7,3},{... | collective-permute-start | bytes 786440 | tf_op jit(solution)/shard_map/ppermute | solution.py:28
  76.6 6.4 %collective-permute-start.8 = (bf16[2,128,512]{2,1,0:T(8,128)(2,1)S(1)}, bf16[2,128,512]{2,1,0:T(8,128)(2,1)S(1)}, u32[]{:S(2)}, u32[]{:S(2)}) collective-permute-start(bf16[2,128,512]{2,1,0:T(8,128)(2,1)S(1)} %fusion), channel_id=1, source_target_pairs={{0,16},{16,0},{1,17},{17,1},{2,18},{18,2},{3,19},{19,3},{4,20},{20... | collective-permute-start | bytes 786440 | tf_op jit(solution)/shard_map/ppermute | solution.py:22

commit v5 on v4

--- a/solution.py
+++ b/solution.py
@@ -117,31 +117,36 @@
 
 
 def backward_kernel(
-    piece_count, group_size, query_ref, grad_ref, kv_ref, mask_ref, lse_ref, delta_ref, *rest
+    piece_ids, group_size, last, query_ref, grad_ref, kv_ref, mask_ref, lse_ref, delta_ref, *rest
 ):
-    dq_ref, dkv_ref = rest[-2:]
+    if len(rest) == 3:
+        acc_in_ref, dq_ref, dkv_ref = rest[0], rest[-2], rest[-1]
+    else:
+        acc_in_ref, dq_ref, dkv_ref = None, rest[-2], rest[-1]
     tok_rows = query_ref.shape[0]
     score_scale = HD ** (-0.5)
     query_rows = stacked(query_ref, group_size)
     grad_rows = stacked(grad_ref, group_size)
     log_total = lse_ref[0]
     delta = delta_ref[0]
-    query_accum = None
-    for shift in range(piece_count):
+    query_accum = None if acc_in_ref is None else stacked(acc_in_ref, group_size)
+    for place, shift in enumerate(piece_ids):
         key_piece = kv_ref[shift, 0]
         value_piece = kv_ref[shift, 1]
         raw = dot_nt(query_rows, key_piece) * score_scale
         allowed = piece_allowed(mask_ref, shift, group_size, tok_rows)
         row_probs = jnp.where(allowed, jnp.exp(raw - log_total), 0.0)
-        dkv_ref[shift, 1] = dot_tn(row_probs.astype(jnp.bfloat16), grad_rows).astype(dkv_ref.dtype)
+        dkv_ref[place, 1] = dot_tn(row_probs.astype(jnp.bfloat16), grad_rows).astype(dkv_ref.dtype)
         prob_grads = dot_nt(grad_rows, value_piece)
         score_grads = (row_probs * (prob_grads - delta)).astype(jnp.bfloat16)
         part_q = jnp.dot(score_grads, key_piece, preferred_element_type=jnp.float32)
         query_accum = part_q if query_accum is None else query_accum + part_q
-        dkv_ref[shift, 0] = (dot_tn(score_grads, query_rows) * score_scale).astype(dkv_ref.dtype)
-    query_grad = (query_accum * score_scale).astype(dq_ref.dtype)
+        dkv_ref[place, 0] = (dot_tn(score_grads, query_rows) * score_scale).astype(dkv_ref.dtype)
+    if last:
+        query_accum = query_accum * score_scale
+    query_accum = query_accum.astype(dq_ref.dtype)
     for head in range(group_size):
-        dq_ref[:, head * HD : (head + 1) * HD] = query_grad[head * tok_rows : (head + 1) * tok_rows]
+        dq_ref[:, head * HD : (head + 1) * HD] = query_accum[head * tok_rows : (head + 1) * tok_rows]
 
 
 def attention_forward(query_rows, grad_rows, kv_pieces, masks):
@@ -179,44 +184,39 @@
     )(query_rows, grad_rows, kv_pieces, masks)
 
 
-def attention_backward(query_rows, grad_rows, kv_pieces, masks, log_total, delta, first_group, group_count, extra):
+def attention_backward(query_rows, grad_rows, kv_pieces, masks, log_total, delta, piece_ids, acc_in, last):
     tok_rows, query_width = query_rows.shape
     piece_count = kv_pieces.shape[0]
     group_size = H // KVH
     group_width = group_size * HD
     rows = group_size * tok_rows
-    flops = 10 * tok_rows * tok_rows * HD * group_size * group_count * piece_count
-    aliases = {}
-    if extra and extra[0] is not None:
-        aliases = {6: 0, 7: 1}
-    else:
-        extra = extra[1:] if extra else extra
-    shift_g = lambda g: g + first_group
+    flops = 10 * tok_rows * tok_rows * HD * H * len(piece_ids)
+    group_block = pl.BlockSpec((tok_rows, group_width), lambda g: (0, g))
+    extra = [] if acc_in is None else [acc_in]
     return pl.pallas_call(
-        functools.partial(backward_kernel, piece_count, group_size),
-        grid=(group_count,),
+        functools.partial(backward_kernel, tuple(piece_ids), group_size, last),
+        grid=(KVH,),
         in_specs=[
-            pl.BlockSpec((tok_rows, group_width), lambda g: (0, shift_g(g))),
-            pl.BlockSpec((tok_rows, group_width), lambda g: (0, shift_g(g))),
-            pl.BlockSpec((piece_count, 2, tok_rows, HD), lambda g: (0, 0, 0, shift_g(g))),
-            pl.BlockSpec((piece_count, group_size) + masks.shape[2:], lambda g: (0, shift_g(g), 0, 0)),
-            pl.BlockSpec((1, rows, 1), lambda g: (shift_g(g), 0, 0)),
-            pl.BlockSpec((1, rows, 1), lambda g: (shift_g(g), 0, 0)),
+            group_block,
+            group_block,
+            pl.BlockSpec((piece_count, 2, tok_rows, HD), lambda g: (0, 0, 0, g)),
+            pl.BlockSpec((piece_count, group_size) + masks.shape[2:], lambda g: (0, g, 0, 0)),
+            pl.BlockSpec((1, rows, 1), lambda g: (g, 0, 0)),
+            pl.BlockSpec((1, rows, 1), lambda g: (g, 0, 0)),
         ]
-        + [pl.BlockSpec(memory_space=pl.ANY) for _ in extra],
+        + [group_block for _ in extra],
         out_specs=[
-            pl.BlockSpec((tok_rows, group_width), lambda g: (0, shift_g(g))),
-            pl.BlockSpec((piece_count, 2, tok_rows, HD), lambda g: (0, 0, 0, shift_g(g))),
+            group_block,
+            pl.BlockSpec((len(piece_ids), 2, tok_rows, HD), lambda g: (0, 0, 0, g)),
         ],
         out_shape=[
-            jax.ShapeDtypeStruct((tok_rows, query_width), jnp.bfloat16),
-            jax.ShapeDtypeStruct(kv_pieces.shape, jnp.bfloat16),
-        ],
-        input_output_aliases=aliases,
+            jax.ShapeDtypeStruct((tok_rows, query_width), jnp.bfloat16 if last else jnp.float32),
+            jax.ShapeDtypeStruct((len(piece_ids),) + kv_pieces.shape[1:], jnp.bfloat16),
+        ],
         cost_estimate=pl.CostEstimate(
             flops=flops,
-            transcendentals=tok_rows * tok_rows * group_size * group_count * piece_count,
-            bytes_accessed=(2 * query_rows.size * 2 + 2 * kv_pieces.size * 2) * group_count // KVH,
+            transcendentals=tok_rows * tok_rows * H * len(piece_ids),
+            bytes_accessed=2 * query_rows.size * 2 + 2 * kv_pieces.size * 2 * len(piece_ids) // piece_count,
         ),
     )(query_rows, grad_rows, kv_pieces, masks, log_total, delta, *extra)
 
@@ -236,18 +236,25 @@
     attended, log_total, delta = attention_forward(query[0], grad_out[0], kv_pieces, masks)
     next_input = passed_along(attended[None], "pipe", 1)
 
-    query_grad, kv_terms = attention_backward(
-        query[0], grad_out[0], kv_pieces, masks, log_total, delta, 0, KVH, [None]
-    )
-    next_input, kv_terms = lax.optimization_barrier((next_input, kv_terms))
-    grad_query = passed_along(query_grad[None], "pipe", -1)
-
+    acc = None
     carried = None
     for step in range(1, ctx_count):
-        part = kv_terms[ctx_count - step].astype(jnp.float32)
+        shift = ctx_count - step
+        acc, term = attention_backward(
+            query[0], grad_out[0], kv_pieces, masks, log_total, delta, [shift], acc, False
+        )
+        if step == min(2, ctx_count - 1):
+            next_input, term = lax.optimization_barrier((next_input, term))
+        part = term[0].astype(jnp.float32)
         if carried is not None:
             part = part + carried.astype(jnp.float32)
         carried = shifted_open(part.astype(jnp.bfloat16), "ctx", -1)
+    query_grad, kv_own = attention_backward(
+        query[0], grad_out[0], kv_pieces, masks, log_total, delta, [0], acc, True
+    )
+    grad_query = passed_along(query_grad[None], "pipe", -1)
+    kv_terms = kv_own
+
     kv_sum = kv_terms[0].astype(jnp.float32)
     if carried is not None:
         grad_query, carried = lax.optimization_barrier((grad_query, carried))

time: 85.7 us -> 87.6 us (1.022)
  Pallas kernels: 14.1 us -> 28.1 us
  waiting for transfers between devices: 38.3 us -> 28.9 us
  starting transfers between devices: 22.3 us -> 20.1 us
  local copies, waits for them, and re-layouts: 6.87 us -> 5.91 us
    ppermute x6, waiting for transfers between devices: 31.8 us -> 12.7 us  [shifted_open(): return lax.ppermute(value, axis, pairs)]
    pallas_call x1 -> x4, Pallas kernels: 8.12 us -> 22.1 us  [attention_backward(): pl.pallas_call(functools.partial(backward_kernel, tuple(piece_ids), group...]
    ppermute x3, waiting for transfers between devices: 6.44 us -> 16.3 us  [passed_along(): return lax.ppermute(value, axis, pairs)]
    ppermute x3, starting transfers between devices: 4.68 us -> 2.47 us  [passed_along(): return lax.ppermute(value, axis, pairs)]
    squeeze x1 -> x0, local copies, waits for them, and re-layouts: 0.97 us -> none  [local(): part = kv_terms[ctx_count - step].astype(jnp.float32)]
    unnamed x12 -> x14, local copies, waits for them, and re-layouts: 3.21 us -> 3.21 us
  transfers between devices with their start and end apart: 9 -> 9, of which waited for: 8 -> 6; matrix products, arithmetic and copies ran while one was open for 3% -> 3% of each run, Pallas kernels for 10% -> 25%
where the time goes in v5:
time: 87.6 us; the launch traced here: 86.7 us
  waiting for transfers between devices  28.9 us (33%)
  Pallas kernels  28.1 us (32%)
  starting transfers between devices  20.1 us (23%)
  local copies, waits for them, and re-layouts  5.91 us (7%)
  other arithmetic  3 us (3%)
    pallas_call x4, Pallas kernels, attention_backward(): pl.pallas_call(functools.partial(backward_kernel, tuple(piece_ids), group...  22.1 us
    ppermute x6, starting transfers between devices, shifted_open(): return lax.ppermute(value, axis, pairs)  17.6 us
    ppermute x3, waiting for transfers between devices, passed_along(): return lax.ppermute(value, axis, pairs)  16.3 us
    ppermute x6, waiting for transfers between devices, shifted_open(): return lax.ppermute(value, axis, pairs)  12.7 us
    pallas_call x1, Pallas kernels, attention_forward(): pl.pallas_call(functools.partial(forward_kernel, piece_count, group_size)...  5.97 us
    unnamed x14, local copies, waits for them, and re-layouts  3.21 us
    ppermute x3, starting transfers between devices, passed_along(): return lax.ppermute(value, axis, pairs)  2.47 us
  transfers between devices with their start and end apart: 9, of which 6 were waited for; matrix products, arithmetic and copies ran while one was open for 3% of the time, Pallas kernels for 25%

profile of v5, /device:TPU:0, one launch (start us, length us, event | category | flops | bytes accessed | tf_op | source)
XLA Modules:
  0.0 86.7 jit_solution(341338950164031760)
XLA Ops:
  0.6 0.0 copy-start.2
  0.6 0.9 %constant_dynamic-update-slice_fusion.1 = bf16[2,128,512]{2,1,0:T(8,128)(2,1)S(1)} fusion(bf16[1,128,512]{2,1,0:T(8,128)(2,1)} %param.7), kind=kLoop, calls=%fused_computation.16 | loop fusion | bytes 262144
  1.6 0.0 copy-done.2
  1.6 4.9 %collective-permute-start = (bf16[2,128,512]{2,1,0:T(8,128)(2,1)S(1)}, bf16[2,128,512]{2,1,0:T(8,128)(2,1)S(1)}, u32[]{:S(2)}, u32[]{:S(2)}) collective-permute-start(bf16[2,128,512]{2,1,0:T(8,128)(2,1)S(1)} %constant_dynamic-update-slice_fusion), channel_id=1, source_target_pairs={{0,4},{4,8},{8,12},{1,5},{5,9},{9,13},{2,6},{6,10},{10,14},{3,7},{... | collective-permute-start | bytes 786440 | tf_op jit(solution)/shard_map/ppermute | solution.py:28
  6.6 0.1 compare_and_fusion
  6.7 0.1 iota_add_fusion
  6.7 0.1 copy.14
  6.8 0.0 copy-start.4
  6.8 0.7 copy-done.4
  7.5 0.2 compare_reduce_fusion
  7.7 0.2 compare_reduce_fusion.1
  7.9 0.1 min.12
  8.0 0.0 copy-start.3
  8.0 4.1 %collective-permute-done = bf16[2,128,512]{2,1,0:T(8,128)(2,1)S(1)} collective-permute-done((bf16[2,128,512]{2,1,0:T(8,128)(2,1)S(1)}, bf16[2,128,512]{2,1,0:T(8,128)(2,1)S(1)}, u32[]{:S(2)}, u32[]{:S(2)}) %collective-permute-start) | collective-permute-done | bytes 262176 | tf_op jit(solution)/shard_map/ppermute | solution.py:28
  12.1 4.4 %collective-permute-start.1 = (bf16[2,128,512]{2,1,0:T(8,128)(2,1)S(1)}, bf16[2,128,512]{2,1,0:T(8,128)(2,1)S(1)}, u32[]{:S(2)}, u32[]{:S(2)}) collective-permute-start(bf16[2,128,512]{2,1,0:T(8,128)(2,1)S(1)} %collective-permute-done), channel_id=1, source_target_pairs={{0,4},{4,8},{8,12},{1,5},{5,9},{9,13},{2,6},{6,10},{10,14},{3,7},{... | collective-permute-start | bytes 786440 | tf_op jit(solution)/shard_map/ppermute | solution.py:28
  16.5 0.1 copy.15
  16.6 0.1 or_or_fusion
  16.7 4.5 %collective-permute-done.1 = bf16[2,128,512]{2,1,0:T(8,128)(2,1)S(1)} collective-permute-done((bf16[2,128,512]{2,1,0:T(8,128)(2,1)S(1)}, bf16[2,128,512]{2,1,0:T(8,128)(2,1)S(1)}, u32[]{:S(2)}, u32[]{:S(2)}) %collective-permute-start.1) | collective-permute-done | bytes 262176 | tf_op jit(solution)/shard_map/ppermute | solution.py:28
  21.2 4.4 %collective-permute-start.2 = (bf16[2,128,512]{2,1,0:T(8,128)(2,1)S(1)}, bf16[2,128,512]{2,1,0:T(8,128)(2,1)S(1)}, u32[]{:S(2)}, u32[]{:S(2)}) collective-permute-start(bf16[2,128,512]{2,1,0:T(8,128)(2,1)S(1)} %collective-permute-done.1), channel_id=1, source_target_pairs={{0,4},{4,8},{8,12},{1,5},{5,9},{9,13},{2,6},{6,10},{10,14},{3,7},{... | collective-permute-start | bytes 786440 | tf_op jit(solution)/shard_map/ppermute | solution.py:28
  25.6 0.0 copy-done.3
  25.6 0.6 gather_fusion
  26.2 0.1 fusion.4
  26.3 0.1 copy.16
  26.4 0.2 broadcast_in_dim.18
  26.6 0.8 convert_element_type.44.mask_ref
  27.4 2.0 %collective-permute-done.2 = bf16[2,128,512]{2,1,0:T(8,128)(2,1)S(1)} collective-permute-done((bf16[2,128,512]{2,1,0:T(8,128)(2,1)S(1)}, bf16[2,128,512]{2,1,0:T(8,128)(2,1)S(1)}, u32[]{:S(2)}, u32[]{:S(2)}) %collective-permute-start.2) | collective-permute-done | bytes 262176 | tf_op jit(solution)/shard_map/ppermute | solution.py:28
  29.4 1.1 %pad_maximum_fusion.kv_ref = bf16[4,2,128,512]{3,2,1,0:T(8,128)(2,1)} fusion(bf16[1,2,128,512]{3,2,1,0:T(8,128)(2,1)S(1)} %bitcast.46, bf16[1,2,128,512]{3,2,1,0:T(8,128)(2,1)S(1)} %bitcast.45, bf16[1,2,128,512]{3,2,1,0:T(8,128)(2,1)S(1)} %bitcast.44, bf16[1,2,128,512]{3,2,1,0:T(8,128)(2,1)S(1)} %bitcast.43), kind=kLoop, calls=%fused_computation.1 | loop fusion | flops 1572864 | bytes 2097152 | tf_op jit(solution)/shard_map/stack | solution.py:234
  30.5 6.0 %shard_map.93 = (bf16[128,2048]{1,0:T(8,128)(2,1)}, f32[4,512,1]{2,1,0:T(8,128)}, f32[4,512,1]{2,1,0:T(8,128)}) custom-call(bf16[128,2048]{1,0:T(8,128)(2,1)} %bitcast.33, bf16[128,2048]{1,0:T(8,128)(2,1)} %bitcast.38, bf16[4,2,128,512]{3,2,1,0:T(8,128)(2,1)} %pad_maximum_fusion.kv_ref, f32[4,16,2,128]{3,2,1,0:T(2,128)} %convert_element_type.44.mask_ref), custom_call_target="tpu_custom_call" | custom-call | flops 536870912 | bytes 2621440 | tf_op jit(solution)/shard_map/pallas_call | solution.py:159
  36.5 1.5 %collective-permute-start.3 = (bf16[1,128,2048]{2,1,0:T(8,128)(2,1)}, bf16[1,128,2048]{2,1,0:T(8,128)(2,1)S(1)}, u32[]{:S(2)}, u32[]{:S(2)}) collective-permute-start(bf16[1,128,2048]{2,1,0:T(8,128)(2,1)} %bitcast.52), channel_id=1, source_target_pairs={{0,16},{16,0},{1,17},{17,1},{2,18},{18,2},{3,19},{19,3},{4,20},{20... | collective-permute-start | bytes 1572872 | tf_op jit(solution)/shard_map/ppermute | solution.py:22
  38.0 5.4 %shard_map.94 = (f32[128,2048]{1,0:T(8,128)}, bf16[1,2,128,512]{3,2,1,0:T(8,128)(2,1)}) custom-call(bf16[128,2048]{1,0:T(8,128)(2,1)} %bitcast.34, bf16[128,2048]{1,0:T(8,128)(2,1)} %bitcast.39, bf16[4,2,128,512]{3,2,1,0:T(8,128)(2,1)} %pad_maximum_fusion.kv_ref, f32[4,16,2,128]{3,2,1,0:T(2,128)} %convert_element_type.44.mask_ref, ...), custom_call_target="tpu_custom_call" | custom-call | flops 335544320 | bytes 1572864 | tf_op jit(solution)/shard_map/pallas_call | solution.py:196
  43.4 1.3 %collective-permute-start.5 = (bf16[2,128,512]{2,1,0:T(8,128)(2,1)}, bf16[2,128,512]{2,1,0:T(8,128)(2,1)S(1)}, u32[]{:S(2)}, u32[]{:S(2)}) collective-permute-start(bf16[2,128,512]{2,1,0:T(8,128)(2,1)} %bitcast.53), channel_id=1, source_target_pairs={{4,0},{8,4},{12,8},{5,1},{9,5},{13,9},{6,2},{10,6},{14,10},{7,3},{... | collective-permute-start | bytes 786440 | tf_op jit(solution)/shard_map/ppermute | solution.py:28
  44.7 5.6 %shard_map.95 = (f32[128,2048]{1,0:T(8,128)}, bf16[1,2,128,512]{3,2,1,0:T(8,128)(2,1)}) custom-call(bf16[128,2048]{1,0:T(8,128)(2,1)} %bitcast.35, bf16[128,2048]{1,0:T(8,128)(2,1)} %bitcast.40, bf16[4,2,128,512]{3,2,1,0:T(8,128)(2,1)} %pad_maximum_fusion.kv_ref, f32[4,16,2,128]{3,2,1,0:T(2,128)} %convert_element_type.44.mask_ref, ...), custom_call_target="tpu_custom_call" | custom-call | flops 335544320 | bytes 1572864 | tf_op jit(solution)/shard_map/pallas_call | solution.py:196
  50.3 0.0 collective-permute-done.3
  50.3 2.0 %collective-permute-done.5 = bf16[2,128,512]{2,1,0:T(8,128)(2,1)S(1)} collective-permute-done((bf16[2,128,512]{2,1,0:T(8,128)(2,1)}, bf16[2,128,512]{2,1,0:T(8,128)(2,1)S(1)}, u32[]{:S(2)}, u32[]{:S(2)}) %collective-permute-start.5) | collective-permute-done | bytes 262176 | tf_op jit(solution)/shard_map/ppermute | solution.py:28
  52.3 1.0 %fusion.1 = bf16[2,128,512]{2,1,0:T(8,128)(2,1)S(1)} fusion(bf16[2,128,512]{2,1,0:T(8,128)(2,1)S(1)} %collective-permute-done.5, bf16[1,2,128,512]{3,2,1,0:T(8,128)(2,1)} %get-tuple-element.29), kind=kLoop, calls=%fused_computation.5 | loop fusion | flops 524288 | bytes 786432 | tf_op jit(solution)/shard_map/convert_element_type | solution.py:251
  53.3 1.3 %collective-permute-start.6 = (bf16[2,128,512]{2,1,0:T(8,128)(2,1)S(1)}, bf16[2,128,512]{2,1,0:T(8,128)(2,1)S(1)}, u32[]{:S(2)}, u32[]{:S(2)}) collective-permute-start(bf16[2,128,512]{2,1,0:T(8,128)(2,1)S(1)} %fusion.1), channel_id=1, source_target_pairs={{4,0},{8,4},{12,8},{5,1},{9,5},{13,9},{6,2},{10,6},{14,10},{7,3},{... | collective-permute-start | bytes 786440 | tf_op jit(solution)/shard_map/ppermute | solution.py:28
  54.6 5.6 %shard_map.96 = (f32[128,2048]{1,0:T(8,128)}, bf16[1,2,128,512]{3,2,1,0:T(8,128)(2,1)}) custom-call(bf16[128,2048]{1,0:T(8,128)(2,1)} %bitcast.36, bf16[128,2048]{1,0:T(8,128)(2,1)} %bitcast.41, bf16[4,2,128,512]{3,2,1,0:T(8,128)(2,1)} %pad_maximum_fusion.kv_ref, f32[4,16,2,128]{3,2,1,0:T(2,128)} %convert_element_type.44.mask_ref, ...), custom_call_target="tpu_custom_call" | custom-call | flops 335544320 | bytes 1572864 | tf_op jit(solution)/shard_map/pallas_call | solution.py:196
  60.2 0.0 copy-start.1
  60.2 5.6 %shard_map.97 = (bf16[128,2048]{1,0:T(8,128)(2,1)}, bf16[1,2,128,512]{3,2,1,0:T(8,128)(2,1)}) custom-call(bf16[128,2048]{1,0:T(8,128)(2,1)} %bitcast.37, bf16[128,2048]{1,0:T(8,128)(2,1)} %bitcast.42, bf16[4,2,128,512]{3,2,1,0:T(8,128)(2,1)} %pad_maximum_fusion.kv_ref, f32[4,16,2,128]{3,2,1,0:T(2,128)} %convert_element_type.44.mask_ref, ...), custom_call_target="tpu_custom_call" | custom-call | flops 335544320 | bytes 1572864 | tf_op jit(solution)/shard_map/pallas_call | solution.py:196
  65.8 0.5 collective-permute-start.4
  66.3 0.0 collective-permute-done.6
  66.3 0.0 copy-done.1
  66.3 0.0 copy-start
  66.3 0.1 fusion.2
  66.4 1.3 %collective-permute-start.7 = (bf16[2,128,512]{2,1,0:T(8,128)(2,1)S(1)}, bf16[2,128,512]{2,1,0:T(8,128)(2,1)S(1)}, u32[]{:S(2)}, u32[]{:S(2)}) collective-permute-start(bf16[2,128,512]{2,1,0:T(8,128)(2,1)S(1)} %fusion.2), channel_id=1, source_target_pairs={{4,0},{8,4},{12,8},{5,1},{9,5},{13,9},{6,2},{10,6},{14,10},{7,3},{... | collective-permute-start | bytes 786440 | tf_op jit(solution)/shard_map/ppermute | solution.py:28
  67.7 10.3 %collective-permute-done.4 = bf16[1,128,2048]{2,1,0:T(8,128)(2,1)S(1)} collective-permute-done((bf16[1,128,2048]{2,1,0:T(8,128)(2,1)}, bf16[1,128,2048]{2,1,0:T(8,128)(2,1)S(1)}, u32[]{:S(2)}, u32[]{:S(2)}) %collective-permute-start.4) | collective-permute-done | bytes 524320 | tf_op jit(solution)/shard_map/ppermute | solution.py:22
  77.9 0.0 collective-permute-done.7
  77.9 0.0 copy-done
  77.9 0.1 fusion
  78.0 0.4 collective-permute-start.8
  78.5 6.0 %collective-permute-done.8 = bf16[2,128,512]{2,1,0:T(8,128)(2,1)S(1)} collective-permute-done((bf16[2,128,512]{2,1,0:T(8,128)(2,1)S(1)}, bf16[2,128,512]{2,1,0:T(8,128)(2,1)S(1)}, u32[]{:S(2)}, u32[]{:S(2)}) %collective-permute-start.8) | collective-permute-done | bytes 262176 | tf_op jit(solution)/shard_map/ppermute | solution.py:22
  84.4 0.7 fusion.8
  85.2 0.8 copy.22
  86.0 0.8 copy.23
  (7 shorter events, 0.0 us)
Async XLA Ops:
  0.6 1.0 %copy-start.2 = (bf16[1,128,512]{2,1,0:T(8,128)(2,1)S(1)}, bf16[1,128,512]{2,1,0:T(8,128)(2,1)}, u32[]{:S(2)}) copy-start(bf16[1,128,512]{2,1,0:T(8,128)(2,1)} %param.8) | copy-start | bytes 393220
  1.6 10.5 %collective-permute-start = (bf16[2,128,512]{2,1,0:T(8,128)(2,1)S(1)}, bf16[2,128,512]{2,1,0:T(8,128)(2,1)S(1)}, u32[]{:S(2)}, u32[]{:S(2)}) collective-permute-start(bf16[2,128,512]{2,1,0:T(8,128)(2,1)S(1)} %constant_dynamic-update-slice_fusion), channel_id=1, source_target_pairs={{0,4},{4,8},{8,12},{1,5},{5,9},{9,13},{2,6},{6,10},{10,14},{3,7},{... | collective-permute-start | bytes 786440 | tf_op jit(solution)/shard_map/ppermute | solution.py:28
  6.8 0.7 copy-start.4
  8.0 17.6 %copy-start.3 = (s32[1,2,16,8]{2,3,1,0:T(8,128)S(1)}, s32[1,2,16,8]{2,3,1,0:T(8,128)}, u32[]{:S(2)}) copy-start(s32[1,2,16,8]{2,3,1,0:T(8,128)} %param.10) | copy-start | bytes 3076
  12.1 9.1 %collective-permute-start.1 = (bf16[2,128,512]{2,1,0:T(8,128)(2,1)S(1)}, bf16[2,128,512]{2,1,0:T(8,128)(2,1)S(1)}, u32[]{:S(2)}, u32[]{:S(2)}) collective-permute-start(bf16[2,128,512]{2,1,0:T(8,128)(2,1)S(1)} %collective-permute-done), channel_id=1, source_target_pairs={{0,4},{4,8},{8,12},{1,5},{5,9},{9,13},{2,6},{6,10},{10,14},{3,7},{... | collective-permute-start | bytes 786440 | tf_op jit(solution)/shard_map/ppermute | solution.py:28
  21.2 8.3 %collective-permute-start.2 = (bf16[2,128,512]{2,1,0:T(8,128)(2,1)S(1)}, bf16[2,128,512]{2,1,0:T(8,128)(2,1)S(1)}, u32[]{:S(2)}, u32[]{:S(2)}) collective-permute-start(bf16[2,128,512]{2,1,0:T(8,128)(2,1)S(1)} %collective-permute-done.1), channel_id=1, source_target_pairs={{0,4},{4,8},{8,12},{1,5},{5,9},{9,13},{2,6},{6,10},{10,14},{3,7},{... | collective-permute-start | bytes 786440 | tf_op jit(solution)/shard_map/ppermute | solution.py:28
  36.5 13.8 %collective-permute-start.3 = (bf16[1,128,2048]{2,1,0:T(8,128)(2,1)}, bf16[1,128,2048]{2,1,0:T(8,128)(2,1)S(1)}, u32[]{:S(2)}, u32[]{:S(2)}) collective-permute-start(bf16[1,128,2048]{2,1,0:T(8,128)(2,1)} %bitcast.52), channel_id=1, source_target_pairs={{0,16},{16,0},{1,17},{17,1},{2,18},{18,2},{3,19},{19,3},{4,20},{20... | collective-permute-start | bytes 1572872 | tf_op jit(solution)/shard_map/ppermute | solution.py:22
  43.4 8.9 %collective-permute-start.5 = (bf16[2,128,512]{2,1,0:T(8,128)(2,1)}, bf16[2,128,512]{2,1,0:T(8,128)(2,1)S(1)}, u32[]{:S(2)}, u32[]{:S(2)}) collective-permute-start(bf16[2,128,512]{2,1,0:T(8,128)(2,1)} %bitcast.53), channel_id=1, source_target_pairs={{4,0},{8,4},{12,8},{5,1},{9,5},{13,9},{6,2},{10,6},{14,10},{7,3},{... | collective-permute-start | bytes 786440 | tf_op jit(solution)/shard_map/ppermute | solution.py:28
  53.3 13.0 %collective-permute-start.6 = (bf16[2,128,512]{2,1,0:T(8,128)(2,1)S(1)}, bf16[2,128,512]{2,1,0:T(8,128)(2,1)S(1)}, u32[]{:S(2)}, u32[]{:S(2)}) collective-permute-start(bf16[2,128,512]{2,1,0:T(8,128)(2,1)S(1)} %fusion.1), channel_id=1, source_target_pairs={{4,0},{8,4},{12,8},{5,1},{9,5},{13,9},{6,2},{10,6},{14,10},{7,3},{... | collective-permute-start | bytes 786440 | tf_op jit(solution)/shard_map/ppermute | solution.py:28
  60.2 6.1 %copy-start.1 = (bf16[1,2,128,512]{3,2,1,0:T(8,128)(2,1)S(1)}, bf16[1,2,128,512]{3,2,1,0:T(8,128)(2,1)}, u32[]{:S(2)}) copy-start(bf16[1,2,128,512]{3,2,1,0:T(8,128)(2,1)} %get-tuple-element.28) | copy-start | bytes 786436
  65.8 12.2 %collective-permute-start.4 = (bf16[1,128,2048]{2,1,0:T(8,128)(2,1)}, bf16[1,128,2048]{2,1,0:T(8,128)(2,1)S(1)}, u32[]{:S(2)}, u32[]{:S(2)}) collective-permute-start(bf16[1,128,2048]{2,1,0:T(8,128)(2,1)} %bitcast.51), channel_id=1, source_target_pairs={{0,16},{16,0},{1,17},{17,1},{2,18},{18,2},{3,19},{19,3},{4,20},{20... | collective-permute-start | bytes 1572872 | tf_op jit(solution)/shard_map/ppermute | solution.py:22
  66.3 11.6 %copy-start = (bf16[1,2,128,512]{3,2,1,0:T(8,128)(2,1)S(1)}, bf16[1,2,128,512]{3,2,1,0:T(8,128)(2,1)}, u32[]{:S(2)}) copy-start(bf16[1,2,128,512]{3,2,1,0:T(8,128)(2,1)} %get-tuple-element.32) | copy-start | bytes 786436
  66.4 11.6 %collective-permute-start.7 = (bf16[2,128,512]{2,1,0:T(8,128)(2,1)S(1)}, bf16[2,128,512]{2,1,0:T(8,128)(2,1)S(1)}, u32[]{:S(2)}, u32[]{:S(2)}) collective-permute-start(bf16[2,128,512]{2,1,0:T(8,128)(2,1)S(1)} %fusion.2), channel_id=1, source_target_pairs={{4,0},{8,4},{12,8},{5,1},{9,5},{13,9},{6,2},{10,6},{14,10},{7,3},{... | collective-permute-start | bytes 786440 | tf_op jit(solution)/shard_map/ppermute | solution.py:28
  78.0 6.4 %collective-permute-start.8 = (bf16[2,128,512]{2,1,0:T(8,128)(2,1)S(1)}, bf16[2,128,512]{2,1,0:T(8,128)(2,1)S(1)}, u32[]{:S(2)}, u32[]{:S(2)}) collective-permute-start(bf16[2,128,512]{2,1,0:T(8,128)(2,1)S(1)} %fusion), channel_id=1, source_target_pairs={{0,16},{16,0},{1,17},{17,1},{2,18},{18,2},{3,19},{19,3},{4,20},{20... | collective-permute-start | bytes 786440 | tf_op jit(solution)/shard_map/ppermute | solution.py:22

commit v6 on v4

--- a/solution.py
+++ b/solution.py
@@ -51,20 +51,14 @@
 def piece_allowed(mask_ref, shift, group_size, tok_rows):
     query_blocks = mask_ref.shape[2]
     rows = group_size * tok_rows
-    row = lax.broadcasted_iota(jnp.int32, (rows, tok_rows), 0)
-    row_block = row // BLOCK
-    picked = jnp.broadcast_to(mask_ref[shift, 0, 0:1, :], (rows, tok_rows))
-    for head in range(group_size):
-        for block in range(query_blocks):
-            if head == 0 and block == 0:
-                continue
-            picked = jnp.where(
-                row_block == head * query_blocks + block,
-                mask_ref[shift, head, block : block + 1, :],
-                picked,
-            )
-    allowed = picked > 0.5
+    parts = [
+        jnp.broadcast_to(mask_ref[shift, head, block : block + 1, :], (tok_rows // query_blocks, tok_rows))
+        for head in range(group_size)
+        for block in range(query_blocks)
+    ]
+    allowed = jnp.concatenate(parts, axis=0) > 0.5
     if shift == 0:
+        row = lax.broadcasted_iota(jnp.int32, (rows, tok_rows), 0)
         col = lax.broadcasted_iota(jnp.int32, (rows, tok_rows), 1)
         allowed = allowed & (col <= row % tok_rows)
     return allowed
@@ -92,16 +86,14 @@
     row_high = jnp.full((rows, 1), NEG_FILL, jnp.float32)
     for shift in range(piece_count):
         raw = dot_nt(query_rows, kv_ref[shift, 0]) * score_scale
-        score_ref[shift] = raw
         allowed = piece_allowed(mask_ref, shift, group_size, tok_rows)
-        row_high = jnp.maximum(
-            row_high, jnp.max(jnp.where(allowed, raw, NEG_FILL), axis=1, keepdims=True)
-        )
+        masked = jnp.where(allowed, raw, NEG_FILL)
+        score_ref[shift] = masked
+        row_high = jnp.maximum(row_high, jnp.max(masked, axis=1, keepdims=True))
     row_total = jnp.zeros((rows, 1), jnp.float32)
     accumulated = jnp.zeros((rows, HD), jnp.float32)
     for shift in range(piece_count):
-        allowed = piece_allowed(mask_ref, shift, group_size, tok_rows)
-        weights = jnp.where(allowed, jnp.exp(score_ref[shift] - row_high), 0.0)
+        weights = jnp.exp(score_ref[shift] - row_high)
         row_total = row_total + jnp.sum(weights, axis=1, keepdims=True)
         accumulated = accumulated + jnp.dot(
             weights.astype(jnp.bfloat16), kv_ref[shift, 1], preferred_element_type=jnp.float32
@@ -132,7 +124,7 @@
         value_piece = kv_ref[shift, 1]
         raw = dot_nt(query_rows, key_piece) * score_scale
         allowed = piece_allowed(mask_ref, shift, group_size, tok_rows)
-        row_probs = jnp.where(allowed, jnp.exp(raw - log_total), 0.0)
+        row_probs = jnp.exp(jnp.where(allowed, raw, NEG_FILL) - log_total)
         dkv_ref[shift, 1] = dot_tn(row_probs.astype(jnp.bfloat16), grad_rows).astype(dkv_ref.dtype)
         prob_grads = dot_nt(grad_rows, value_piece)
         score_grads = (row_probs * (prob_grads - delta)).astype(jnp.bfloat16)

time: 85.7 us -> 85.6 us (level)
  transfers between devices with their start and end apart: 9 -> 9, of which waited for: 8 -> 8; matrix products, arithmetic and copies ran while one was open for 3% -> 3% of each run, Pallas kernels for 10% -> 9%
where the time goes in v6:
time: 85.6 us; the launch traced here: 85.2 us
  waiting for transfers between devices  38.3 us (45%)
  starting transfers between devices  22.3 us (26%)
  Pallas kernels  14 us (16%)
  local copies, waits for them, and re-layouts  6.87 us (8%)
  other arithmetic  2.99 us (3%)
    ppermute x6, waiting for transfers between devices, shifted_open(): return lax.ppermute(value, axis, pairs)  31.8 us
    ppermute x6, starting transfers between devices, shifted_open(): return lax.ppermute(value, axis, pairs)  17.6 us
    pallas_call x1, Pallas kernels, attention_backward(): pl.pallas_call(functools.partial(backward_kernel, piece_count, group_size...  8.09 us
    ppermute x3, waiting for transfers between devices, passed_along(): return lax.ppermute(value, axis, pairs)  6.47 us
    pallas_call x1, Pallas kernels, attention_forward(): pl.pallas_call(functools.partial(forward_kernel, piece_count, group_size)...  5.86 us
    ppermute x3, starting transfers between devices, passed_along(): return lax.ppermute(value, axis, pairs)  4.69 us
    unnamed x12, local copies, waits for them, and re-layouts  3.21 us
  transfers between devices with their start and end apart: 9, of which 8 were waited for; matrix products, arithmetic and copies ran while one was open for 3% of the time, Pallas kernels for 9%

profile of v6, /device:TPU:0, one launch (start us, length us, event | category | flops | bytes accessed | tf_op | source)
XLA Modules:
  0.0 85.2 jit_solution(13871098643994427421)
XLA Ops:
  0.6 0.0 copy-start.1
  0.6 0.9 %constant_dynamic-update-slice_fusion.1 = bf16[2,128,512]{2,1,0:T(8,128)(2,1)S(1)} fusion(bf16[1,128,512]{2,1,0:T(8,128)(2,1)} %param.7), kind=kLoop, calls=%fused_computation.17 | loop fusion | bytes 262144
  1.6 0.0 copy-done.1
  1.6 4.9 %collective-permute-start = (bf16[2,128,512]{2,1,0:T(8,128)(2,1)S(1)}, bf16[2,128,512]{2,1,0:T(8,128)(2,1)S(1)}, u32[]{:S(2)}, u32[]{:S(2)}) collective-permute-start(bf16[2,128,512]{2,1,0:T(8,128)(2,1)S(1)} %constant_dynamic-update-slice_fusion), channel_id=1, source_target_pairs={{0,4},{4,8},{8,12},{1,5},{5,9},{9,13},{2,6},{6,10},{10,14},{3,7},{... | collective-permute-start | bytes 786440 | tf_op jit(solution)/shard_map/ppermute | solution.py:28
  6.6 0.1 compare_and_fusion
  6.7 0.1 iota_add_fusion
  6.7 0.1 copy.14
  6.8 0.0 copy-start.3
  6.8 0.7 copy-done.3
  7.5 0.2 compare_reduce_fusion
  7.7 0.2 compare_reduce_fusion.1
  7.9 0.1 min.12
  8.0 0.0 copy-start.2
  8.0 4.1 %collective-permute-done = bf16[2,128,512]{2,1,0:T(8,128)(2,1)S(1)} collective-permute-done((bf16[2,128,512]{2,1,0:T(8,128)(2,1)S(1)}, bf16[2,128,512]{2,1,0:T(8,128)(2,1)S(1)}, u32[]{:S(2)}, u32[]{:S(2)}) %collective-permute-start) | collective-permute-done | bytes 262176 | tf_op jit(solution)/shard_map/ppermute | solution.py:28
  12.1 4.4 %collective-permute-start.1 = (bf16[2,128,512]{2,1,0:T(8,128)(2,1)S(1)}, bf16[2,128,512]{2,1,0:T(8,128)(2,1)S(1)}, u32[]{:S(2)}, u32[]{:S(2)}) collective-permute-start(bf16[2,128,512]{2,1,0:T(8,128)(2,1)S(1)} %collective-permute-done), channel_id=1, source_target_pairs={{0,4},{4,8},{8,12},{1,5},{5,9},{9,13},{2,6},{6,10},{10,14},{3,7},{... | collective-permute-start | bytes 786440 | tf_op jit(solution)/shard_map/ppermute | solution.py:28
  16.5 0.1 copy.15
  16.6 0.1 or_or_fusion
  16.7 4.5 %collective-permute-done.1 = bf16[2,128,512]{2,1,0:T(8,128)(2,1)S(1)} collective-permute-done((bf16[2,128,512]{2,1,0:T(8,128)(2,1)S(1)}, bf16[2,128,512]{2,1,0:T(8,128)(2,1)S(1)}, u32[]{:S(2)}, u32[]{:S(2)}) %collective-permute-start.1) | collective-permute-done | bytes 262176 | tf_op jit(solution)/shard_map/ppermute | solution.py:28
  21.2 4.4 %collective-permute-start.2 = (bf16[2,128,512]{2,1,0:T(8,128)(2,1)S(1)}, bf16[2,128,512]{2,1,0:T(8,128)(2,1)S(1)}, u32[]{:S(2)}, u32[]{:S(2)}) collective-permute-start(bf16[2,128,512]{2,1,0:T(8,128)(2,1)S(1)} %collective-permute-done.1), channel_id=1, source_target_pairs={{0,4},{4,8},{8,12},{1,5},{5,9},{9,13},{2,6},{6,10},{10,14},{3,7},{... | collective-permute-start | bytes 786440 | tf_op jit(solution)/shard_map/ppermute | solution.py:28
  25.6 0.0 copy-done.2
  25.6 0.6 gather_fusion
  26.2 0.1 fusion.4
  26.3 0.1 copy.16
  26.4 0.2 broadcast_in_dim.18
  26.6 0.8 convert_element_type.44.mask_ref
  27.4 2.0 %collective-permute-done.2 = bf16[2,128,512]{2,1,0:T(8,128)(2,1)S(1)} collective-permute-done((bf16[2,128,512]{2,1,0:T(8,128)(2,1)S(1)}, bf16[2,128,512]{2,1,0:T(8,128)(2,1)S(1)}, u32[]{:S(2)}, u32[]{:S(2)}) %collective-permute-start.2) | collective-permute-done | bytes 262176 | tf_op jit(solution)/shard_map/ppermute | solution.py:28
  29.4 1.1 %pad_maximum_fusion.kv_ref = bf16[4,2,128,512]{3,2,1,0:T(8,128)(2,1)} fusion(bf16[1,2,128,512]{3,2,1,0:T(8,128)(2,1)S(1)} %bitcast.41, bf16[1,2,128,512]{3,2,1,0:T(8,128)(2,1)S(1)} %bitcast.40, bf16[1,2,128,512]{3,2,1,0:T(8,128)(2,1)S(1)} %bitcast.39, bf16[1,2,128,512]{3,2,1,0:T(8,128)(2,1)S(1)} %bitcast.34), kind=kLoop, calls=%fused_computation.1 | loop fusion | flops 1572864 | bytes 2097152 | tf_op jit(solution)/shard_map/stack | solution.py:226
  30.5 5.9 %shard_map.93 = (bf16[128,2048]{1,0:T(8,128)(2,1)}, f32[4,512,1]{2,1,0:T(8,128)}, f32[4,512,1]{2,1,0:T(8,128)}) custom-call(bf16[128,2048]{1,0:T(8,128)(2,1)} %bitcast.35, bf16[128,2048]{1,0:T(8,128)(2,1)} %bitcast.37, bf16[4,2,128,512]{3,2,1,0:T(8,128)(2,1)} %pad_maximum_fusion.kv_ref, f32[4,16,2,128]{3,2,1,0:T(2,128)} %convert_element_type.44.mask_ref), custom_call_target="tpu_custom_call" | custom-call | flops 536870912 | bytes 2621440 | tf_op jit(solution)/shard_map/pallas_call | solution.py:146
  36.4 1.5 %collective-permute-start.3 = (bf16[1,128,2048]{2,1,0:T(8,128)(2,1)}, bf16[1,128,2048]{2,1,0:T(8,128)(2,1)S(1)}, u32[]{:S(2)}, u32[]{:S(2)}) collective-permute-start(bf16[1,128,2048]{2,1,0:T(8,128)(2,1)} %bitcast.47), channel_id=1, source_target_pairs={{0,16},{16,0},{1,17},{17,1},{2,18},{18,2},{3,19},{19,3},{4,20},{20... | collective-permute-start | bytes 1572872 | tf_op jit(solution)/shard_map/ppermute | solution.py:22
  37.9 8.1 %shard_map.94 = (bf16[128,2048]{1,0:T(8,128)(2,1)}, bf16[4,2,128,512]{3,2,1,0:T(8,128)(2,1)}) custom-call(bf16[128,2048]{1,0:T(8,128)(2,1)} %bitcast.36, bf16[128,2048]{1,0:T(8,128)(2,1)} %bitcast.38, bf16[4,2,128,512]{3,2,1,0:T(8,128)(2,1)} %pad_maximum_fusion.kv_ref, f32[4,16,2,128]{3,2,1,0:T(2,128)} %convert_element_type.44.mask_ref, ...), custom_call_target="tpu_custom_call" | custom-call | flops 1342177280 | bytes 3145728 | tf_op jit(solution)/shard_map/pallas_call | solution.py:187
  46.0 0.0 copy-start
  46.0 1.6 %collective-permute-done.3 = bf16[1,128,2048]{2,1,0:T(8,128)(2,1)S(1)} collective-permute-done((bf16[1,128,2048]{2,1,0:T(8,128)(2,1)}, bf16[1,128,2048]{2,1,0:T(8,128)(2,1)S(1)}, u32[]{:S(2)}, u32[]{:S(2)}) %collective-permute-start.3) | collective-permute-done | bytes 524320 | tf_op jit(solution)/shard_map/ppermute | solution.py:22
  47.6 1.0 %slice_bitcast_fusion = bf16[2,128,512]{2,1,0:T(8,128)(2,1)S(1)} fusion(bf16[4,2,128,512]{3,2,1,0:T(8,128)(2,1)} %get-tuple-element.19), kind=kLoop, calls=%fused_computation.8 | loop fusion | bytes 524288 | tf_op jit(solution)/shard_map/squeeze | solution.py:239
  48.6 1.3 %collective-permute-start.5 = (bf16[2,128,512]{2,1,0:T(8,128)(2,1)S(1)}, bf16[2,128,512]{2,1,0:T(8,128)(2,1)S(1)}, u32[]{:S(2)}, u32[]{:S(2)}) collective-permute-start(bf16[2,128,512]{2,1,0:T(8,128)(2,1)S(1)} %slice_bitcast_fusion), channel_id=1, source_target_pairs={{4,0},{8,4},{12,8},{5,1},{9,5},{13,9},{6,2},{10,6},{14,10},{7,3},{... | collective-permute-start | bytes 786440 | tf_op jit(solution)/shard_map/ppermute | solution.py:28
  49.9 7.1 %collective-permute-done.5 = bf16[2,128,512]{2,1,0:T(8,128)(2,1)S(1)} collective-permute-done((bf16[2,128,512]{2,1,0:T(8,128)(2,1)S(1)}, bf16[2,128,512]{2,1,0:T(8,128)(2,1)S(1)}, u32[]{:S(2)}, u32[]{:S(2)}) %collective-permute-start.5) | collective-permute-done | bytes 262176 | tf_op jit(solution)/shard_map/ppermute | solution.py:28
  57.0 1.0 %fusion.1 = bf16[2,128,512]{2,1,0:T(8,128)(2,1)S(1)} fusion(bf16[2,128,512]{2,1,0:T(8,128)(2,1)S(1)} %collective-permute-done.5, bf16[4,2,128,512]{3,2,1,0:T(8,128)(2,1)} %get-tuple-element.19), kind=kLoop, calls=%fused_computation.5 | loop fusion | flops 524288 | bytes 786432 | tf_op jit(solution)/shard_map/convert_element_type | solution.py:242
  58.0 1.3 %collective-permute-start.6 = (bf16[2,128,512]{2,1,0:T(8,128)(2,1)S(1)}, bf16[2,128,512]{2,1,0:T(8,128)(2,1)S(1)}, u32[]{:S(2)}, u32[]{:S(2)}) collective-permute-start(bf16[2,128,512]{2,1,0:T(8,128)(2,1)S(1)} %fusion.1), channel_id=1, source_target_pairs={{4,0},{8,4},{12,8},{5,1},{9,5},{13,9},{6,2},{10,6},{14,10},{7,3},{... | collective-permute-start | bytes 786440 | tf_op jit(solution)/shard_map/ppermute | solution.py:28
  59.3 1.6 %collective-permute-start.4 = (bf16[1,128,2048]{2,1,0:T(8,128)(2,1)}, bf16[1,128,2048]{2,1,0:T(8,128)(2,1)S(1)}, u32[]{:S(2)}, u32[]{:S(2)}) collective-permute-start(bf16[1,128,2048]{2,1,0:T(8,128)(2,1)} %bitcast.46), channel_id=1, source_target_pairs={{0,16},{16,0},{1,17},{17,1},{2,18},{18,2},{3,19},{19,3},{4,20},{20... | collective-permute-start | bytes 1572872 | tf_op jit(solution)/shard_map/ppermute | solution.py:22
  60.9 6.8 %collective-permute-done.6 = bf16[2,128,512]{2,1,0:T(8,128)(2,1)S(1)} collective-permute-done((bf16[2,128,512]{2,1,0:T(8,128)(2,1)S(1)}, bf16[2,128,512]{2,1,0:T(8,128)(2,1)S(1)}, u32[]{:S(2)}, u32[]{:S(2)}) %collective-permute-start.6) | collective-permute-done | bytes 262176 | tf_op jit(solution)/shard_map/ppermute | solution.py:28
  67.7 0.0 copy-done
  67.7 0.1 fusion.2
  67.8 1.3 %collective-permute-start.7 = (bf16[2,128,512]{2,1,0:T(8,128)(2,1)S(1)}, bf16[2,128,512]{2,1,0:T(8,128)(2,1)S(1)}, u32[]{:S(2)}, u32[]{:S(2)}) collective-permute-start(bf16[2,128,512]{2,1,0:T(8,128)(2,1)S(1)} %fusion.2), channel_id=1, source_target_pairs={{4,0},{8,4},{12,8},{5,1},{9,5},{13,9},{6,2},{10,6},{14,10},{7,3},{... | collective-permute-start | bytes 786440 | tf_op jit(solution)/shard_map/ppermute | solution.py:28
  69.1 0.0 collective-permute-done.4
  69.1 7.3 %collective-permute-done.7 = bf16[2,128,512]{2,1,0:T(8,128)(2,1)S(1)} collective-permute-done((bf16[2,128,512]{2,1,0:T(8,128)(2,1)S(1)}, bf16[2,128,512]{2,1,0:T(8,128)(2,1)S(1)}, u32[]{:S(2)}, u32[]{:S(2)}) %collective-permute-start.7) | collective-permute-done | bytes 262176 | tf_op jit(solution)/shard_map/ppermute | solution.py:28
  76.4 0.1 fusion
  76.5 1.6 %collective-permute-start.8 = (bf16[2,128,512]{2,1,0:T(8,128)(2,1)S(1)}, bf16[2,128,512]{2,1,0:T(8,128)(2,1)S(1)}, u32[]{:S(2)}, u32[]{:S(2)}) collective-permute-start(bf16[2,128,512]{2,1,0:T(8,128)(2,1)S(1)} %fusion), channel_id=1, source_target_pairs={{0,16},{16,0},{1,17},{17,1},{2,18},{18,2},{3,19},{19,3},{4,20},{20... | collective-permute-start | bytes 786440 | tf_op jit(solution)/shard_map/ppermute | solution.py:22
  78.1 4.9 %collective-permute-done.8 = bf16[2,128,512]{2,1,0:T(8,128)(2,1)S(1)} collective-permute-done((bf16[2,128,512]{2,1,0:T(8,128)(2,1)S(1)}, bf16[2,128,512]{2,1,0:T(8,128)(2,1)S(1)}, u32[]{:S(2)}, u32[]{:S(2)}) %collective-permute-start.8) | collective-permute-done | bytes 262176 | tf_op jit(solution)/shard_map/ppermute | solution.py:22
  82.9 0.7 fusion.8
  83.6 0.8 copy.22
  84.4 0.8 copy.23
  (7 shorter events, 0.0 us)
Async XLA Ops:
  0.6 1.0 %copy-start.1 = (bf16[1,128,512]{2,1,0:T(8,128)(2,1)S(1)}, bf16[1,128,512]{2,1,0:T(8,128)(2,1)}, u32[]{:S(2)}) copy-start(bf16[1,128,512]{2,1,0:T(8,128)(2,1)} %param.8) | copy-start | bytes 393220
  1.6 10.5 %collective-permute-start = (bf16[2,128,512]{2,1,0:T(8,128)(2,1)S(1)}, bf16[2,128,512]{2,1,0:T(8,128)(2,1)S(1)}, u32[]{:S(2)}, u32[]{:S(2)}) collective-permute-start(bf16[2,128,512]{2,1,0:T(8,128)(2,1)S(1)} %constant_dynamic-update-slice_fusion), channel_id=1, source_target_pairs={{0,4},{4,8},{8,12},{1,5},{5,9},{9,13},{2,6},{6,10},{10,14},{3,7},{... | collective-permute-start | bytes 786440 | tf_op jit(solution)/shard_map/ppermute | solution.py:28
  6.8 0.7 copy-start.3
  8.0 17.6 %copy-start.2 = (s32[1,2,16,8]{2,3,1,0:T(8,128)S(1)}, s32[1,2,16,8]{2,3,1,0:T(8,128)}, u32[]{:S(2)}) copy-start(s32[1,2,16,8]{2,3,1,0:T(8,128)} %param.10) | copy-start | bytes 3076
  12.1 9.1 %collective-permute-start.1 = (bf16[2,128,512]{2,1,0:T(8,128)(2,1)S(1)}, bf16[2,128,512]{2,1,0:T(8,128)(2,1)S(1)}, u32[]{:S(2)}, u32[]{:S(2)}) collective-permute-start(bf16[2,128,512]{2,1,0:T(8,128)(2,1)S(1)} %collective-permute-done), channel_id=1, source_target_pairs={{0,4},{4,8},{8,12},{1,5},{5,9},{9,13},{2,6},{6,10},{10,14},{3,7},{... | collective-permute-start | bytes 786440 | tf_op jit(solution)/shard_map/ppermute | solution.py:28
  21.2 8.3 %collective-permute-start.2 = (bf16[2,128,512]{2,1,0:T(8,128)(2,1)S(1)}, bf16[2,128,512]{2,1,0:T(8,128)(2,1)S(1)}, u32[]{:S(2)}, u32[]{:S(2)}) collective-permute-start(bf16[2,128,512]{2,1,0:T(8,128)(2,1)S(1)} %collective-permute-done.1), channel_id=1, source_target_pairs={{0,4},{4,8},{8,12},{1,5},{5,9},{9,13},{2,6},{6,10},{10,14},{3,7},{... | collective-permute-start | bytes 786440 | tf_op jit(solution)/shard_map/ppermute | solution.py:28
  36.4 11.2 %collective-permute-start.3 = (bf16[1,128,2048]{2,1,0:T(8,128)(2,1)}, bf16[1,128,2048]{2,1,0:T(8,128)(2,1)S(1)}, u32[]{:S(2)}, u32[]{:S(2)}) collective-permute-start(bf16[1,128,2048]{2,1,0:T(8,128)(2,1)} %bitcast.47), channel_id=1, source_target_pairs={{0,16},{16,0},{1,17},{17,1},{2,18},{18,2},{3,19},{19,3},{4,20},{20... | collective-permute-start | bytes 1572872 | tf_op jit(solution)/shard_map/ppermute | solution.py:22
  46.0 21.8 %copy-start = (bf16[4,2,128,512]{3,2,1,0:T(8,128)(2,1)S(1)}, bf16[4,2,128,512]{3,2,1,0:T(8,128)(2,1)}, u32[]{:S(2)}) copy-start(bf16[4,2,128,512]{3,2,1,0:T(8,128)(2,1)} %get-tuple-element.19) | copy-start | bytes 3145732
  48.6 8.4 %collective-permute-start.5 = (bf16[2,128,512]{2,1,0:T(8,128)(2,1)S(1)}, bf16[2,128,512]{2,1,0:T(8,128)(2,1)S(1)}, u32[]{:S(2)}, u32[]{:S(2)}) collective-permute-start(bf16[2,128,512]{2,1,0:T(8,128)(2,1)S(1)} %slice_bitcast_fusion), channel_id=1, source_target_pairs={{4,0},{8,4},{12,8},{5,1},{9,5},{13,9},{6,2},{10,6},{14,10},{7,3},{... | collective-permute-start | bytes 786440 | tf_op jit(solution)/shard_map/ppermute | solution.py:28
  58.0 9.7 %collective-permute-start.6 = (bf16[2,128,512]{2,1,0:T(8,128)(2,1)S(1)}, bf16[2,128,512]{2,1,0:T(8,128)(2,1)S(1)}, u32[]{:S(2)}, u32[]{:S(2)}) collective-permute-start(bf16[2,128,512]{2,1,0:T(8,128)(2,1)S(1)} %fusion.1), channel_id=1, source_target_pairs={{4,0},{8,4},{12,8},{5,1},{9,5},{13,9},{6,2},{10,6},{14,10},{7,3},{... | collective-permute-start | bytes 786440 | tf_op jit(solution)/shard_map/ppermute | solution.py:28
  59.3 9.8 %collective-permute-start.4 = (bf16[1,128,2048]{2,1,0:T(8,128)(2,1)}, bf16[1,128,2048]{2,1,0:T(8,128)(2,1)S(1)}, u32[]{:S(2)}, u32[]{:S(2)}) collective-permute-start(bf16[1,128,2048]{2,1,0:T(8,128)(2,1)} %bitcast.46), channel_id=1, source_target_pairs={{0,16},{16,0},{1,17},{17,1},{2,18},{18,2},{3,19},{19,3},{4,20},{20... | collective-permute-start | bytes 1572872 | tf_op jit(solution)/shard_map/ppermute | solution.py:22
  67.8 8.6 %collective-permute-start.7 = (bf16[2,128,512]{2,1,0:T(8,128)(2,1)S(1)}, bf16[2,128,512]{2,1,0:T(8,128)(2,1)S(1)}, u32[]{:S(2)}, u32[]{:S(2)}) collective-permute-start(bf16[2,128,512]{2,1,0:T(8,128)(2,1)S(1)} %fusion.2), channel_id=1, source_target_pairs={{4,0},{8,4},{12,8},{5,1},{9,5},{13,9},{6,2},{10,6},{14,10},{7,3},{... | collective-permute-start | bytes 786440 | tf_op jit(solution)/shard_map/ppermute | solution.py:28
  76.5 6.4 %collective-permute-start.8 = (bf16[2,128,512]{2,1,0:T(8,128)(2,1)S(1)}, bf16[2,128,512]{2,1,0:T(8,128)(2,1)S(1)}, u32[]{:S(2)}, u32[]{:S(2)}) collective-permute-start(bf16[2,128,512]{2,1,0:T(8,128)(2,1)S(1)} %fusion), channel_id=1, source_target_pairs={{0,16},{16,0},{1,17},{17,1},{2,18},{18,2},{3,19},{19,3},{4,20},{20... | collective-permute-start | bytes 786440 | tf_op jit(solution)/shard_map/ppermute | solution.py:22

commit v7 on v6

--- a/solution.py
+++ b/solution.py
@@ -220,9 +220,14 @@
     masks = block_masks(random_blocks[0], global_ids[0], ctx_index, ctx_count, tok_rows)
 
     own = jnp.stack([keys[0], values[0]])
-    pieces = [own]
-    for shift in range(1, ctx_count):
-        pieces.append(shifted_open(pieces[-1], "ctx", 1))
+    if ctx_count == 4:
+        step_one = shifted_open(own, "ctx", 1)
+        step_three = shifted_open(own, "ctx", 3)
+        pieces = [own, step_one, shifted_open(step_one, "ctx", 1), step_three]
+    else:
+        pieces = [own]
+        for shift in range(1, ctx_count):
+            pieces.append(shifted_open(pieces[-1], "ctx", 1))
     kv_pieces = jnp.stack(pieces)
 
     attended, log_total, delta = attention_forward(query[0], grad_out[0], kv_pieces, masks)
@@ -238,6 +243,9 @@
     for step in range(1, ctx_count):
         part = kv_terms[ctx_count - step].astype(jnp.float32)
         if carried is not None:
+            if step == 2:
+                next_input = jnp.where(ctx_index < 0, jnp.zeros_like(next_input), next_input)
+                next_input, carried = lax.optimization_barrier((next_input, carried))
             part = part + carried.astype(jnp.float32)
         carried = shifted_open(part.astype(jnp.bfloat16), "ctx", -1)
     kv_sum = kv_terms[0].astype(jnp.float32)

time: 85.6 us -> 83.3 us (0.973)
  starting transfers between devices: 22.3 us -> 21.2 us
    ppermute x6, waiting for transfers between devices: 31.8 us -> 29 us  [shifted_open(): return lax.ppermute(value, axis, pairs)]
    ppermute x3, waiting for transfers between devices: 6.47 us -> 9 us  [passed_along(): return lax.ppermute(value, axis, pairs)]
    ppermute x6, starting transfers between devices: 17.6 us -> 16.5 us  [shifted_open(): return lax.ppermute(value, axis, pairs)]
    convert_element_type x2, other arithmetic: 1.08 us -> 0.13 us  [local(): carried = shifted_open(part.astype(jnp.bfloat16), 'ctx', -1)]
    unnamed x12 -> x13, local copies, waits for them, and re-layouts: 3.21 us -> 2.42 us
  transfers between devices with their start and end apart: 9 -> 9, of which waited for: 8 -> 8; matrix products, arithmetic and copies ran while one was open for 3% -> 4% of each run, Pallas kernels for 9% -> 10%
where the time goes in v7:
time: 83.3 us; the launch traced here: 82.9 us
  waiting for transfers between devices  37.9 us (45%)
  starting transfers between devices  21.2 us (25%)
  Pallas kernels  14 us (17%)
  local copies, waits for them, and re-layouts  6.09 us (7%)
  other arithmetic  2.88 us (3%)
    ppermute x6, waiting for transfers between devices, shifted_open(): return lax.ppermute(value, axis, pairs)  29 us
    ppermute x6, starting transfers between devices, shifted_open(): return lax.ppermute(value, axis, pairs)  16.5 us
    ppermute x3, waiting for transfers between devices, passed_along(): return lax.ppermute(value, axis, pairs)  9 us
    pallas_call x1, Pallas kernels, attention_backward(): pl.pallas_call(functools.partial(backward_kernel, piece_count, group_size...  8.09 us
    pallas_call x1, Pallas kernels, attention_forward(): pl.pallas_call(functools.partial(forward_kernel, piece_count, group_size)...  5.88 us
    ppermute x3, starting transfers between devices, passed_along(): return lax.ppermute(value, axis, pairs)  4.69 us
    unnamed x13, local copies, waits for them, and re-layouts  2.42 us
  transfers between devices with their start and end apart: 9, of which 8 were waited for; matrix products, arithmetic and copies ran while one was open for 4% of the time, Pallas kernels for 10%

profile of v7, /device:TPU:0, one launch (start us, length us, event | category | flops | bytes accessed | tf_op | source)
XLA Modules:
  0.0 82.9 jit_solution(18175792084349255896)
XLA Ops:
  0.6 0.0 copy-start.1
  0.6 0.9 %constant_dynamic-update-slice_fusion.1 = bf16[2,128,512]{2,1,0:T(8,128)(2,1)S(1)} fusion(bf16[1,128,512]{2,1,0:T(8,128)(2,1)} %param.7), kind=kLoop, calls=%fused_computation.18 | loop fusion | bytes 262144
  1.6 0.0 copy-done.1
  1.6 7.0 %collective-permute-start.2 = (bf16[2,128,512]{2,1,0:T(8,128)(2,1)S(1)}, bf16[2,128,512]{2,1,0:T(8,128)(2,1)S(1)}, u32[]{:S(2)}, u32[]{:S(2)}) collective-permute-start(bf16[2,128,512]{2,1,0:T(8,128)(2,1)S(1)} %constant_dynamic-update-slice_fusion), channel_id=1, source_target_pairs={{0,12},{1,13},{2,14},{3,15},{16,28},{17,29},{18,30},{19,31}} | collective-permute-start | bytes 786440 | tf_op jit(solution)/shard_map/ppermute | solution.py:28
  8.6 1.3 %collective-permute-start = (bf16[2,128,512]{2,1,0:T(8,128)(2,1)S(1)}, bf16[2,128,512]{2,1,0:T(8,128)(2,1)S(1)}, u32[]{:S(2)}, u32[]{:S(2)}) collective-permute-start(bf16[2,128,512]{2,1,0:T(8,128)(2,1)S(1)} %constant_dynamic-update-slice_fusion), channel_id=1, source_target_pairs={{0,4},{4,8},{8,12},{1,5},{5,9},{9,13},{2,6},{6,10},{10,14},{3,7},{... | collective-permute-start | bytes 786440 | tf_op jit(solution)/shard_map/ppermute | solution.py:28
  9.9 0.1 compare_and_fusion
  10.0 0.1 iota_add_fusion
  10.1 0.1 min.12
  10.2 0.1 copy.14
  10.3 0.0 copy-start.3
  10.3 0.7 copy-done.3
  10.9 0.2 compare_reduce_fusion.1
  11.1 0.0 copy-start.2
  11.1 0.2 compare_reduce_fusion
  11.3 0.1 copy.15
  11.4 0.1 or_or_fusion
  11.5 8.3 %collective-permute-done = bf16[2,128,512]{2,1,0:T(8,128)(2,1)S(1)} collective-permute-done((bf16[2,128,512]{2,1,0:T(8,128)(2,1)S(1)}, bf16[2,128,512]{2,1,0:T(8,128)(2,1)S(1)}, u32[]{:S(2)}, u32[]{:S(2)}) %collective-permute-start) | collective-permute-done | bytes 262176 | tf_op jit(solution)/shard_map/ppermute | solution.py:28
  19.8 4.4 %collective-permute-start.1 = (bf16[2,128,512]{2,1,0:T(8,128)(2,1)S(1)}, bf16[2,128,512]{2,1,0:T(8,128)(2,1)S(1)}, u32[]{:S(2)}, u32[]{:S(2)}) collective-permute-start(bf16[2,128,512]{2,1,0:T(8,128)(2,1)S(1)} %collective-permute-done), channel_id=1, source_target_pairs={{0,4},{4,8},{8,12},{1,5},{5,9},{9,13},{2,6},{6,10},{10,14},{3,7},{... | collective-permute-start | bytes 786440 | tf_op jit(solution)/shard_map/ppermute | solution.py:28
  24.2 0.0 copy-done.2
  24.2 0.6 gather_fusion
  24.8 0.1 fusion.4
  24.9 0.1 copy.16
  25.0 0.2 broadcast_in_dim.35
  25.2 0.8 convert_element_type.44.mask_ref
  26.0 0.0 collective-permute-done.2
  26.0 2.9 %collective-permute-done.1 = bf16[2,128,512]{2,1,0:T(8,128)(2,1)S(1)} collective-permute-done((bf16[2,128,512]{2,1,0:T(8,128)(2,1)S(1)}, bf16[2,128,512]{2,1,0:T(8,128)(2,1)S(1)}, u32[]{:S(2)}, u32[]{:S(2)}) %collective-permute-start.1) | collective-permute-done | bytes 262176 | tf_op jit(solution)/shard_map/ppermute | solution.py:28
  28.9 1.1 %pad_maximum_fusion.kv_ref = bf16[4,2,128,512]{3,2,1,0:T(8,128)(2,1)} fusion(bf16[1,2,128,512]{3,2,1,0:T(8,128)(2,1)S(1)} %bitcast.39, bf16[1,2,128,512]{3,2,1,0:T(8,128)(2,1)S(1)} %bitcast.41, bf16[1,2,128,512]{3,2,1,0:T(8,128)(2,1)S(1)} %bitcast.40, bf16[1,2,128,512]{3,2,1,0:T(8,128)(2,1)S(1)} %bitcast.34), kind=kLoop, calls=%fused_computation.1 | loop fusion | flops 1572864 | bytes 2097152 | tf_op jit(solution)/shard_map/stack | solution.py:231
  30.0 5.9 %shard_map.93 = (bf16[128,2048]{1,0:T(8,128)(2,1)}, f32[4,512,1]{2,1,0:T(8,128)}, f32[4,512,1]{2,1,0:T(8,128)}) custom-call(bf16[128,2048]{1,0:T(8,128)(2,1)} %bitcast.35, bf16[128,2048]{1,0:T(8,128)(2,1)} %bitcast.37, bf16[4,2,128,512]{3,2,1,0:T(8,128)(2,1)} %pad_maximum_fusion.kv_ref, f32[4,16,2,128]{3,2,1,0:T(2,128)} %convert_element_type.44.mask_ref), custom_call_target="tpu_custom_call" | custom-call | flops 536870912 | bytes 2621440 | tf_op jit(solution)/shard_map/pallas_call | solution.py:146
  35.9 1.5 %collective-permute-start.3 = (bf16[1,128,2048]{2,1,0:T(8,128)(2,1)}, bf16[1,128,2048]{2,1,0:T(8,128)(2,1)S(1)}, u32[]{:S(2)}, u32[]{:S(2)}) collective-permute-start(bf16[1,128,2048]{2,1,0:T(8,128)(2,1)} %bitcast.47), channel_id=1, source_target_pairs={{0,16},{16,0},{1,17},{17,1},{2,18},{18,2},{3,19},{19,3},{4,20},{20... | collective-permute-start | bytes 1572872 | tf_op jit(solution)/shard_map/ppermute | solution.py:22
  37.4 8.1 %shard_map.94 = (bf16[128,2048]{1,0:T(8,128)(2,1)}, bf16[4,2,128,512]{3,2,1,0:T(8,128)(2,1)}) custom-call(bf16[128,2048]{1,0:T(8,128)(2,1)} %bitcast.36, bf16[128,2048]{1,0:T(8,128)(2,1)} %bitcast.38, bf16[4,2,128,512]{3,2,1,0:T(8,128)(2,1)} %pad_maximum_fusion.kv_ref, f32[4,16,2,128]{3,2,1,0:T(2,128)} %convert_element_type.44.mask_ref, ...), custom_call_target="tpu_custom_call" | custom-call | flops 1342177280 | bytes 3145728 | tf_op jit(solution)/shard_map/pallas_call | solution.py:187
  45.5 0.0 copy-start
  45.5 2.5 %collective-permute-done.3 = bf16[1,128,2048]{2,1,0:T(8,128)(2,1)S(1)} collective-permute-done((bf16[1,128,2048]{2,1,0:T(8,128)(2,1)}, bf16[1,128,2048]{2,1,0:T(8,128)(2,1)S(1)}, u32[]{:S(2)}, u32[]{:S(2)}) %collective-permute-start.3) | collective-permute-done | bytes 524320 | tf_op jit(solution)/shard_map/ppermute | solution.py:22
  48.0 1.0 %slice_bitcast_fusion = bf16[2,128,512]{2,1,0:T(8,128)(2,1)S(1)} fusion(bf16[4,2,128,512]{3,2,1,0:T(8,128)(2,1)} %get-tuple-element.20), kind=kLoop, calls=%fused_computation.9 | loop fusion | bytes 524288 | tf_op jit(solution)/shard_map/squeeze | solution.py:244
  49.0 1.3 %collective-permute-start.4 = (bf16[2,128,512]{2,1,0:T(8,128)(2,1)S(1)}, bf16[2,128,512]{2,1,0:T(8,128)(2,1)S(1)}, u32[]{:S(2)}, u32[]{:S(2)}) collective-permute-start(bf16[2,128,512]{2,1,0:T(8,128)(2,1)S(1)} %slice_bitcast_fusion), channel_id=1, source_target_pairs={{4,0},{8,4},{12,8},{5,1},{9,5},{13,9},{6,2},{10,6},{14,10},{7,3},{... | collective-permute-start | bytes 786440 | tf_op jit(solution)/shard_map/ppermute | solution.py:28
  50.3 0.8 %broadcast_select_fusion = bf16[1,128,2048]{2,1,0:T(8,128)(2,1)} fusion(bf16[1,128,2048]{2,1,0:T(8,128)(2,1)S(1)} %collective-permute-done.3, pred[]{:T(512)S(6)} %lt.19), kind=kLoop, calls=%fused_computation.8 | loop fusion | flops 262144 | bytes 1048577 | tf_op jit(solution)/shard_map/jit(_where)/select_n | solution.py:247
  51.1 0.0 copy-start.4
  51.1 6.6 %collective-permute-done.4 = bf16[2,128,512]{2,1,0:T(8,128)(2,1)S(1)} collective-permute-done((bf16[2,128,512]{2,1,0:T(8,128)(2,1)S(1)}, bf16[2,128,512]{2,1,0:T(8,128)(2,1)S(1)}, u32[]{:S(2)}, u32[]{:S(2)}) %collective-permute-start.4) | collective-permute-done | bytes 262176 | tf_op jit(solution)/shard_map/ppermute | solution.py:28
  57.7 0.0 copy-done
  57.7 0.1 fusion.1
  57.8 1.3 %collective-permute-start.6 = (bf16[2,128,512]{2,1,0:T(8,128)(2,1)S(1)}, bf16[2,128,512]{2,1,0:T(8,128)(2,1)S(1)}, u32[]{:S(2)}, u32[]{:S(2)}) collective-permute-start(bf16[2,128,512]{2,1,0:T(8,128)(2,1)S(1)} %fusion.1), channel_id=1, source_target_pairs={{4,0},{8,4},{12,8},{5,1},{9,5},{13,9},{6,2},{10,6},{14,10},{7,3},{... | collective-permute-start | bytes 786440 | tf_op jit(solution)/shard_map/ppermute | solution.py:28
  59.1 0.0 copy-done.4
  59.1 1.6 %collective-permute-start.5 = (bf16[1,128,2048]{2,1,0:T(8,128)(2,1)S(1)}, bf16[1,128,2048]{2,1,0:T(8,128)(2,1)S(1)}, u32[]{:S(2)}, u32[]{:S(2)}) collective-permute-start(bf16[1,128,2048]{2,1,0:T(8,128)(2,1)S(1)} %bitcast.46), channel_id=1, source_target_pairs={{0,16},{16,0},{1,17},{17,1},{2,18},{18,2},{3,19},{19,3},{4,20},{20... | collective-permute-start | bytes 1572872 | tf_op jit(solution)/shard_map/ppermute | solution.py:22
  60.7 5.6 %collective-permute-done.6 = bf16[2,128,512]{2,1,0:T(8,128)(2,1)S(1)} collective-permute-done((bf16[2,128,512]{2,1,0:T(8,128)(2,1)S(1)}, bf16[2,128,512]{2,1,0:T(8,128)(2,1)S(1)}, u32[]{:S(2)}, u32[]{:S(2)}) %collective-permute-start.6) | collective-permute-done | bytes 262176 | tf_op jit(solution)/shard_map/ppermute | solution.py:28
  66.3 0.1 fusion.2
  66.4 1.3 %collective-permute-start.7 = (bf16[2,128,512]{2,1,0:T(8,128)(2,1)S(1)}, bf16[2,128,512]{2,1,0:T(8,128)(2,1)S(1)}, u32[]{:S(2)}, u32[]{:S(2)}) collective-permute-start(bf16[2,128,512]{2,1,0:T(8,128)(2,1)S(1)} %fusion.2), channel_id=1, source_target_pairs={{4,0},{8,4},{12,8},{5,1},{9,5},{13,9},{6,2},{10,6},{14,10},{7,3},{... | collective-permute-start | bytes 786440 | tf_op jit(solution)/shard_map/ppermute | solution.py:28
  67.7 1.6 %collective-permute-done.5 = bf16[1,128,2048]{2,1,0:T(8,128)(2,1)S(1)} collective-permute-done((bf16[1,128,2048]{2,1,0:T(8,128)(2,1)S(1)}, bf16[1,128,2048]{2,1,0:T(8,128)(2,1)S(1)}, u32[]{:S(2)}, u32[]{:S(2)}) %collective-permute-start.5) | collective-permute-done | bytes 524320 | tf_op jit(solution)/shard_map/ppermute | solution.py:22
  69.3 5.6 %collective-permute-done.7 = bf16[2,128,512]{2,1,0:T(8,128)(2,1)S(1)} collective-permute-done((bf16[2,128,512]{2,1,0:T(8,128)(2,1)S(1)}, bf16[2,128,512]{2,1,0:T(8,128)(2,1)S(1)}, u32[]{:S(2)}, u32[]{:S(2)}) %collective-permute-start.7) | collective-permute-done | bytes 262176 | tf_op jit(solution)/shard_map/ppermute | solution.py:28
  74.9 0.1 fusion
  75.0 1.6 %collective-permute-start.8 = (bf16[2,128,512]{2,1,0:T(8,128)(2,1)S(1)}, bf16[2,128,512]{2,1,0:T(8,128)(2,1)S(1)}, u32[]{:S(2)}, u32[]{:S(2)}) collective-permute-start(bf16[2,128,512]{2,1,0:T(8,128)(2,1)S(1)} %fusion), channel_id=1, source_target_pairs={{0,16},{16,0},{1,17},{17,1},{2,18},{18,2},{3,19},{19,3},{4,20},{20... | collective-permute-start | bytes 786440 | tf_op jit(solution)/shard_map/ppermute | solution.py:22
  76.6 4.9 %collective-permute-done.8 = bf16[2,128,512]{2,1,0:T(8,128)(2,1)S(1)} collective-permute-done((bf16[2,128,512]{2,1,0:T(8,128)(2,1)S(1)}, bf16[2,128,512]{2,1,0:T(8,128)(2,1)S(1)}, u32[]{:S(2)}, u32[]{:S(2)}) %collective-permute-start.8) | collective-permute-done | bytes 262176 | tf_op jit(solution)/shard_map/ppermute | solution.py:22
  81.4 0.7 fusion.8
  82.1 0.8 copy.21
  (7 shorter events, 0.0 us)
Async XLA Ops:
  0.6 1.0 %copy-start.1 = (bf16[1,128,512]{2,1,0:T(8,128)(2,1)S(1)}, bf16[1,128,512]{2,1,0:T(8,128)(2,1)}, u32[]{:S(2)}) copy-start(bf16[1,128,512]{2,1,0:T(8,128)(2,1)} %param.8) | copy-start | bytes 393220
  1.6 24.4 %collective-permute-start.2 = (bf16[2,128,512]{2,1,0:T(8,128)(2,1)S(1)}, bf16[2,128,512]{2,1,0:T(8,128)(2,1)S(1)}, u32[]{:S(2)}, u32[]{:S(2)}) collective-permute-start(bf16[2,128,512]{2,1,0:T(8,128)(2,1)S(1)} %constant_dynamic-update-slice_fusion), channel_id=1, source_target_pairs={{0,12},{1,13},{2,14},{3,15},{16,28},{17,29},{18,30},{19,31}} | collective-permute-start | bytes 786440 | tf_op jit(solution)/shard_map/ppermute | solution.py:28
  8.6 11.2 %collective-permute-start = (bf16[2,128,512]{2,1,0:T(8,128)(2,1)S(1)}, bf16[2,128,512]{2,1,0:T(8,128)(2,1)S(1)}, u32[]{:S(2)}, u32[]{:S(2)}) collective-permute-start(bf16[2,128,512]{2,1,0:T(8,128)(2,1)S(1)} %constant_dynamic-update-slice_fusion), channel_id=1, source_target_pairs={{0,4},{4,8},{8,12},{1,5},{5,9},{9,13},{2,6},{6,10},{10,14},{3,7},{... | collective-permute-start | bytes 786440 | tf_op jit(solution)/shard_map/ppermute | solution.py:28
  10.3 0.7 copy-start.3
  11.1 13.1 %copy-start.2 = (s32[1,2,16,8]{2,3,1,0:T(8,128)S(1)}, s32[1,2,16,8]{2,3,1,0:T(8,128)}, u32[]{:S(2)}) copy-start(s32[1,2,16,8]{2,3,1,0:T(8,128)} %param.10) | copy-start | bytes 3076
  19.8 9.1 %collective-permute-start.1 = (bf16[2,128,512]{2,1,0:T(8,128)(2,1)S(1)}, bf16[2,128,512]{2,1,0:T(8,128)(2,1)S(1)}, u32[]{:S(2)}, u32[]{:S(2)}) collective-permute-start(bf16[2,128,512]{2,1,0:T(8,128)(2,1)S(1)} %collective-permute-done), channel_id=1, source_target_pairs={{0,4},{4,8},{8,12},{1,5},{5,9},{9,13},{2,6},{6,10},{10,14},{3,7},{... | collective-permute-start | bytes 786440 | tf_op jit(solution)/shard_map/ppermute | solution.py:28
  35.9 12.1 %collective-permute-start.3 = (bf16[1,128,2048]{2,1,0:T(8,128)(2,1)}, bf16[1,128,2048]{2,1,0:T(8,128)(2,1)S(1)}, u32[]{:S(2)}, u32[]{:S(2)}) collective-permute-start(bf16[1,128,2048]{2,1,0:T(8,128)(2,1)} %bitcast.47), channel_id=1, source_target_pairs={{0,16},{16,0},{1,17},{17,1},{2,18},{18,2},{3,19},{19,3},{4,20},{20... | collective-permute-start | bytes 1572872 | tf_op jit(solution)/shard_map/ppermute | solution.py:22
  45.5 12.2 %copy-start = (bf16[4,2,128,512]{3,2,1,0:T(8,128)(2,1)S(1)}, bf16[4,2,128,512]{3,2,1,0:T(8,128)(2,1)}, u32[]{:S(2)}) copy-start(bf16[4,2,128,512]{3,2,1,0:T(8,128)(2,1)} %get-tuple-element.20) | copy-start | bytes 3145732
  49.0 8.7 %collective-permute-start.4 = (bf16[2,128,512]{2,1,0:T(8,128)(2,1)S(1)}, bf16[2,128,512]{2,1,0:T(8,128)(2,1)S(1)}, u32[]{:S(2)}, u32[]{:S(2)}) collective-permute-start(bf16[2,128,512]{2,1,0:T(8,128)(2,1)S(1)} %slice_bitcast_fusion), channel_id=1, source_target_pairs={{4,0},{8,4},{12,8},{5,1},{9,5},{13,9},{6,2},{10,6},{14,10},{7,3},{... | collective-permute-start | bytes 786440 | tf_op jit(solution)/shard_map/ppermute | solution.py:28
  51.1 8.0 %copy-start.4 = (bf16[128,2048]{1,0:T(8,128)(2,1)S(1)}, bf16[128,2048]{1,0:T(8,128)(2,1)}, u32[]{:S(2)}) copy-start(bf16[128,2048]{1,0:T(8,128)(2,1)} %get-tuple-element.22) | copy-start | bytes 1572868
  57.8 8.5 %collective-permute-start.6 = (bf16[2,128,512]{2,1,0:T(8,128)(2,1)S(1)}, bf16[2,128,512]{2,1,0:T(8,128)(2,1)S(1)}, u32[]{:S(2)}, u32[]{:S(2)}) collective-permute-start(bf16[2,128,512]{2,1,0:T(8,128)(2,1)S(1)} %fusion.1), channel_id=1, source_target_pairs={{4,0},{8,4},{12,8},{5,1},{9,5},{13,9},{6,2},{10,6},{14,10},{7,3},{... | collective-permute-start | bytes 786440 | tf_op jit(solution)/shard_map/ppermute | solution.py:28
  59.1 10.2 %collective-permute-start.5 = (bf16[1,128,2048]{2,1,0:T(8,128)(2,1)S(1)}, bf16[1,128,2048]{2,1,0:T(8,128)(2,1)S(1)}, u32[]{:S(2)}, u32[]{:S(2)}) collective-permute-start(bf16[1,128,2048]{2,1,0:T(8,128)(2,1)S(1)} %bitcast.46), channel_id=1, source_target_pairs={{0,16},{16,0},{1,17},{17,1},{2,18},{18,2},{3,19},{19,3},{4,20},{20... | collective-permute-start | bytes 1572872 | tf_op jit(solution)/shard_map/ppermute | solution.py:22
  66.4 8.5 %collective-permute-start.7 = (bf16[2,128,512]{2,1,0:T(8,128)(2,1)S(1)}, bf16[2,128,512]{2,1,0:T(8,128)(2,1)S(1)}, u32[]{:S(2)}, u32[]{:S(2)}) collective-permute-start(bf16[2,128,512]{2,1,0:T(8,128)(2,1)S(1)} %fusion.2), channel_id=1, source_target_pairs={{4,0},{8,4},{12,8},{5,1},{9,5},{13,9},{6,2},{10,6},{14,10},{7,3},{... | collective-permute-start | bytes 786440 | tf_op jit(solution)/shard_map/ppermute | solution.py:28
  75.0 6.4 %collective-permute-start.8 = (bf16[2,128,512]{2,1,0:T(8,128)(2,1)S(1)}, bf16[2,128,512]{2,1,0:T(8,128)(2,1)S(1)}, u32[]{:S(2)}, u32[]{:S(2)}) collective-permute-start(bf16[2,128,512]{2,1,0:T(8,128)(2,1)S(1)} %fusion), channel_id=1, source_target_pairs={{0,16},{16,0},{1,17},{17,1},{2,18},{18,2},{3,19},{19,3},{4,20},{20... | collective-permute-start | bytes 786440 | tf_op jit(solution)/shard_map/ppermute | solution.py:22

commit v8 on v7

--- a/solution.py
+++ b/solution.py
@@ -76,28 +76,24 @@
     return jnp.concatenate([ref[:, head * HD : (head + 1) * HD] for head in range(group_size)], axis=0)
 
 
-def forward_kernel(
-    piece_count, group_size, query_ref, grad_ref, kv_ref, mask_ref, out_ref, lse_ref, delta_ref, score_ref
-):
+def all_allowed(mask_ref, piece_count, group_size, tok_rows):
+    return jnp.concatenate(
+        [piece_allowed(mask_ref, shift, group_size, tok_rows) for shift in range(piece_count)], axis=1
+    )
+
+
+def forward_kernel(piece_count, group_size, query_ref, grad_ref, kv_ref, mask_ref, out_ref, lse_ref, delta_ref):
     tok_rows = query_ref.shape[0]
-    rows = group_size * tok_rows
     score_scale = HD ** (-0.5)
     query_rows = stacked(query_ref, group_size)
-    row_high = jnp.full((rows, 1), NEG_FILL, jnp.float32)
-    for shift in range(piece_count):
-        raw = dot_nt(query_rows, kv_ref[shift, 0]) * score_scale
-        allowed = piece_allowed(mask_ref, shift, group_size, tok_rows)
-        masked = jnp.where(allowed, raw, NEG_FILL)
-        score_ref[shift] = masked
-        row_high = jnp.maximum(row_high, jnp.max(masked, axis=1, keepdims=True))
-    row_total = jnp.zeros((rows, 1), jnp.float32)
-    accumulated = jnp.zeros((rows, HD), jnp.float32)
-    for shift in range(piece_count):
-        weights = jnp.exp(score_ref[shift] - row_high)
-        row_total = row_total + jnp.sum(weights, axis=1, keepdims=True)
-        accumulated = accumulated + jnp.dot(
-            weights.astype(jnp.bfloat16), kv_ref[shift, 1], preferred_element_type=jnp.float32
-        )
+    all_keys = kv_ref[:, 0].reshape(piece_count * tok_rows, HD)
+    all_values = kv_ref[:, 1].reshape(piece_count * tok_rows, HD)
+    raw = dot_nt(query_rows, all_keys) * score_scale
+    masked = jnp.where(all_allowed(mask_ref, piece_count, group_size, tok_rows), raw, NEG_FILL)
+    row_high = jnp.max(masked, axis=1, keepdims=True)
+    weights = jnp.exp(masked - row_high)
+    row_total = jnp.sum(weights, axis=1, keepdims=True)
+    accumulated = jnp.dot(weights.astype(jnp.bfloat16), all_values, preferred_element_type=jnp.float32)
     attended = (accumulated / row_total).astype(out_ref.dtype)
     for head in range(group_size):
         out_ref[:, head * HD : (head + 1) * HD] = attended[head * tok_rows : (head + 1) * tok_rows]
@@ -116,22 +112,19 @@
     score_scale = HD ** (-0.5)
     query_rows = stacked(query_ref, group_size)
     grad_rows = stacked(grad_ref, group_size)
-    log_total = lse_ref[0]
-    delta = delta_ref[0]
-    query_accum = None
-    for shift in range(piece_count):
-        key_piece = kv_ref[shift, 0]
-        value_piece = kv_ref[shift, 1]
-        raw = dot_nt(query_rows, key_piece) * score_scale
-        allowed = piece_allowed(mask_ref, shift, group_size, tok_rows)
-        row_probs = jnp.exp(jnp.where(allowed, raw, NEG_FILL) - log_total)
-        dkv_ref[shift, 1] = dot_tn(row_probs.astype(jnp.bfloat16), grad_rows).astype(dkv_ref.dtype)
-        prob_grads = dot_nt(grad_rows, value_piece)
-        score_grads = (row_probs * (prob_grads - delta)).astype(jnp.bfloat16)
-        part_q = jnp.dot(score_grads, key_piece, preferred_element_type=jnp.float32)
-        query_accum = part_q if query_accum is None else query_accum + part_q
-        dkv_ref[shift, 0] = (dot_tn(score_grads, query_rows) * score_scale).astype(dkv_ref.dtype)
-    query_grad = (query_accum * score_scale).astype(dq_ref.dtype)
+    all_keys = kv_ref[:, 0].reshape(piece_count * tok_rows, HD)
+    all_values = kv_ref[:, 1].reshape(piece_count * tok_rows, HD)
+    raw = dot_nt(query_rows, all_keys) * score_scale
+    masked = jnp.where(all_allowed(mask_ref, piece_count, group_size, tok_rows), raw, NEG_FILL)
+    row_probs = jnp.exp(masked - lse_ref[0])
+    value_terms = dot_tn(row_probs.astype(jnp.bfloat16), grad_rows)
+    prob_grads = dot_nt(grad_rows, all_values)
+    score_grads = (row_probs * (prob_grads - delta_ref[0])).astype(jnp.bfloat16)
+    query_grad = jnp.dot(score_grads, all_keys, preferred_element_type=jnp.float32)
+    key_terms = dot_tn(score_grads, query_rows) * score_scale
+    dkv_ref[:, 0] = key_terms.reshape(piece_count, tok_rows, HD).astype(dkv_ref.dtype)
+    dkv_ref[:, 1] = value_terms.reshape(piece_count, tok_rows, HD).astype(dkv_ref.dtype)
+    query_grad = (query_grad * score_scale).astype(dq_ref.dtype)
     for head in range(group_size):
         dq_ref[:, head * HD : (head + 1) * HD] = query_grad[head * tok_rows : (head + 1) * tok_rows]
 
@@ -162,7 +155,6 @@
             jax.ShapeDtypeStruct((KVH, rows, 1), jnp.float32),
             jax.ShapeDtypeStruct((KVH, rows, 1), jnp.float32),
         ],
-        scratch_shapes=[pltpu.VMEM((piece_count, rows, tok_rows), jnp.float32)],
         cost_estimate=pl.CostEstimate(
             flops=flops,
             transcendentals=tok_rows * tok_rows * H * piece_count,

time: 83.3 us -> 83.2 us (level)
  Pallas kernels: 14 us -> 12.3 us
  waiting for transfers between devices: 37.9 us -> 39.4 us
    pallas_call x1, Pallas kernels: 8.09 us -> 6.62 us  [attention_backward(): pl.pallas_call(functools.partial(backward_kernel, piece_count, group_size...]
    ppermute x3, waiting for transfers between devices: 9 us -> 10.5 us  [passed_along(): return lax.ppermute(value, axis, pairs)]
  transfers between devices with their start and end apart: 9 -> 9, of which waited for: 8 -> 8; matrix products, arithmetic and copies ran while one was open for 4% -> 4% of each run, Pallas kernels for 10% -> 8%
where the time goes in v8:
time: 83.2 us; the launch traced here: 82.8 us
  waiting for transfers between devices  39.4 us (47%)
  starting transfers between devices  21.2 us (25%)
  Pallas kernels  12.3 us (15%)
  local copies, waits for them, and re-layouts  6.09 us (7%)
  other arithmetic  2.88 us (3%)
    ppermute x6, waiting for transfers between devices, shifted_open(): return lax.ppermute(value, axis, pairs)  28.9 us
    ppermute x6, starting transfers between devices, shifted_open(): return lax.ppermute(value, axis, pairs)  16.5 us
    ppermute x3, waiting for transfers between devices, passed_along(): return lax.ppermute(value, axis, pairs)  10.5 us
    pallas_call x1, Pallas kernels, attention_backward(): pl.pallas_call(functools.partial(backward_kernel, piece_count, group_size...  6.62 us
    pallas_call x1, Pallas kernels, attention_forward(): pl.pallas_call(functools.partial(forward_kernel, piece_count, group_size)...  5.72 us
    ppermute x3, starting transfers between devices, passed_along(): return lax.ppermute(value, axis, pairs)  4.69 us
    unnamed x13, local copies, waits for them, and re-layouts  2.42 us
  transfers between devices with their start and end apart: 9, of which 8 were waited for; matrix products, arithmetic and copies ran while one was open for 4% of the time, Pallas kernels for 8%

profile of v8, /device:TPU:0, one launch (start us, length us, event | category | flops | bytes accessed | tf_op | source)
XLA Modules:
  0.0 82.8 jit_solution(2297515721604769289)
XLA Ops:
  0.6 0.0 copy-start.1
  0.6 0.9 %constant_dynamic-update-slice_fusion.1 = bf16[2,128,512]{2,1,0:T(8,128)(2,1)S(1)} fusion(bf16[1,128,512]{2,1,0:T(8,128)(2,1)} %param.7), kind=kLoop, calls=%fused_computation.18 | loop fusion | bytes 262144
  1.6 0.0 copy-done.1
  1.6 7.0 %collective-permute-start.2 = (bf16[2,128,512]{2,1,0:T(8,128)(2,1)S(1)}, bf16[2,128,512]{2,1,0:T(8,128)(2,1)S(1)}, u32[]{:S(2)}, u32[]{:S(2)}) collective-permute-start(bf16[2,128,512]{2,1,0:T(8,128)(2,1)S(1)} %constant_dynamic-update-slice_fusion), channel_id=1, source_target_pairs={{0,12},{1,13},{2,14},{3,15},{16,28},{17,29},{18,30},{19,31}} | collective-permute-start | bytes 786440 | tf_op jit(solution)/shard_map/ppermute | solution.py:28
  8.6 1.3 %collective-permute-start = (bf16[2,128,512]{2,1,0:T(8,128)(2,1)S(1)}, bf16[2,128,512]{2,1,0:T(8,128)(2,1)S(1)}, u32[]{:S(2)}, u32[]{:S(2)}) collective-permute-start(bf16[2,128,512]{2,1,0:T(8,128)(2,1)S(1)} %constant_dynamic-update-slice_fusion), channel_id=1, source_target_pairs={{0,4},{4,8},{8,12},{1,5},{5,9},{9,13},{2,6},{6,10},{10,14},{3,7},{... | collective-permute-start | bytes 786440 | tf_op jit(solution)/shard_map/ppermute | solution.py:28
  9.9 0.1 compare_and_fusion
  10.0 0.1 iota_add_fusion
  10.1 0.1 min.12
  10.2 0.1 copy.14
  10.3 0.0 copy-start.3
  10.3 0.7 copy-done.3
  10.9 0.2 compare_reduce_fusion.1
  11.1 0.0 copy-start.2
  11.1 0.2 compare_reduce_fusion
  11.3 0.1 copy.15
  11.4 0.1 or_or_fusion
  11.5 8.3 %collective-permute-done = bf16[2,128,512]{2,1,0:T(8,128)(2,1)S(1)} collective-permute-done((bf16[2,128,512]{2,1,0:T(8,128)(2,1)S(1)}, bf16[2,128,512]{2,1,0:T(8,128)(2,1)S(1)}, u32[]{:S(2)}, u32[]{:S(2)}) %collective-permute-start) | collective-permute-done | bytes 262176 | tf_op jit(solution)/shard_map/ppermute | solution.py:28
  19.8 4.4 %collective-permute-start.1 = (bf16[2,128,512]{2,1,0:T(8,128)(2,1)S(1)}, bf16[2,128,512]{2,1,0:T(8,128)(2,1)S(1)}, u32[]{:S(2)}, u32[]{:S(2)}) collective-permute-start(bf16[2,128,512]{2,1,0:T(8,128)(2,1)S(1)} %collective-permute-done), channel_id=1, source_target_pairs={{0,4},{4,8},{8,12},{1,5},{5,9},{9,13},{2,6},{6,10},{10,14},{3,7},{... | collective-permute-start | bytes 786440 | tf_op jit(solution)/shard_map/ppermute | solution.py:28
  24.2 0.0 copy-done.2
  24.2 0.6 gather_fusion
  24.8 0.1 fusion.4
  24.9 0.1 copy.16
  25.0 0.2 broadcast_in_dim.35
  25.2 0.8 convert_element_type.44.mask_ref
  26.0 0.0 collective-permute-done.2
  26.0 2.9 %collective-permute-done.1 = bf16[2,128,512]{2,1,0:T(8,128)(2,1)S(1)} collective-permute-done((bf16[2,128,512]{2,1,0:T(8,128)(2,1)S(1)}, bf16[2,128,512]{2,1,0:T(8,128)(2,1)S(1)}, u32[]{:S(2)}, u32[]{:S(2)}) %collective-permute-start.1) | collective-permute-done | bytes 262176 | tf_op jit(solution)/shard_map/ppermute | solution.py:28
  28.9 1.1 %pad_maximum_fusion.kv_ref = bf16[4,2,128,512]{3,2,1,0:T(8,128)(2,1)} fusion(bf16[1,2,128,512]{3,2,1,0:T(8,128)(2,1)S(1)} %bitcast.39, bf16[1,2,128,512]{3,2,1,0:T(8,128)(2,1)S(1)} %bitcast.41, bf16[1,2,128,512]{3,2,1,0:T(8,128)(2,1)S(1)} %bitcast.40, bf16[1,2,128,512]{3,2,1,0:T(8,128)(2,1)S(1)} %bitcast.34), kind=kLoop, calls=%fused_computation.1 | loop fusion | flops 1572864 | bytes 2097152 | tf_op jit(solution)/shard_map/stack | solution.py:223
  30.0 5.7 %shard_map.93 = (bf16[128,2048]{1,0:T(8,128)(2,1)}, f32[4,512,1]{2,1,0:T(8,128)}, f32[4,512,1]{2,1,0:T(8,128)}) custom-call(bf16[128,2048]{1,0:T(8,128)(2,1)} %bitcast.35, bf16[128,2048]{1,0:T(8,128)(2,1)} %bitcast.37, bf16[4,2,128,512]{3,2,1,0:T(8,128)(2,1)} %pad_maximum_fusion.kv_ref, f32[4,16,2,128]{3,2,1,0:T(2,128)} %convert_element_type.44.mask_ref), custom_call_target="tpu_custom_call" | custom-call | flops 536870912 | bytes 2621440 | tf_op jit(solution)/shard_map/pallas_call | solution.py:139
  35.7 1.5 %collective-permute-start.3 = (bf16[1,128,2048]{2,1,0:T(8,128)(2,1)}, bf16[1,128,2048]{2,1,0:T(8,128)(2,1)S(1)}, u32[]{:S(2)}, u32[]{:S(2)}) collective-permute-start(bf16[1,128,2048]{2,1,0:T(8,128)(2,1)} %bitcast.47), channel_id=1, source_target_pairs={{0,16},{16,0},{1,17},{17,1},{2,18},{18,2},{3,19},{19,3},{4,20},{20... | collective-permute-start | bytes 1572872 | tf_op jit(solution)/shard_map/ppermute | solution.py:22
  37.2 6.6 %shard_map.94 = (bf16[128,2048]{1,0:T(8,128)(2,1)}, bf16[4,2,128,512]{3,2,1,0:T(8,128)(2,1)}) custom-call(bf16[128,2048]{1,0:T(8,128)(2,1)} %bitcast.36, bf16[128,2048]{1,0:T(8,128)(2,1)} %bitcast.38, bf16[4,2,128,512]{3,2,1,0:T(8,128)(2,1)} %pad_maximum_fusion.kv_ref, f32[4,16,2,128]{3,2,1,0:T(2,128)} %convert_element_type.44.mask_ref, ...), custom_call_target="tpu_custom_call" | custom-call | flops 1342177280 | bytes 3145728 | tf_op jit(solution)/shard_map/pallas_call | solution.py:179
  43.9 0.0 copy-start
  43.9 4.0 %collective-permute-done.3 = bf16[1,128,2048]{2,1,0:T(8,128)(2,1)S(1)} collective-permute-done((bf16[1,128,2048]{2,1,0:T(8,128)(2,1)}, bf16[1,128,2048]{2,1,0:T(8,128)(2,1)S(1)}, u32[]{:S(2)}, u32[]{:S(2)}) %collective-permute-start.3) | collective-permute-done | bytes 524320 | tf_op jit(solution)/shard_map/ppermute | solution.py:22
  47.8 1.0 %slice_bitcast_fusion = bf16[2,128,512]{2,1,0:T(8,128)(2,1)S(1)} fusion(bf16[4,2,128,512]{3,2,1,0:T(8,128)(2,1)} %get-tuple-element.20), kind=kLoop, calls=%fused_computation.9 | loop fusion | bytes 524288 | tf_op jit(solution)/shard_map/squeeze | solution.py:236
  48.8 1.3 %collective-permute-start.4 = (bf16[2,128,512]{2,1,0:T(8,128)(2,1)S(1)}, bf16[2,128,512]{2,1,0:T(8,128)(2,1)S(1)}, u32[]{:S(2)}, u32[]{:S(2)}) collective-permute-start(bf16[2,128,512]{2,1,0:T(8,128)(2,1)S(1)} %slice_bitcast_fusion), channel_id=1, source_target_pairs={{4,0},{8,4},{12,8},{5,1},{9,5},{13,9},{6,2},{10,6},{14,10},{7,3},{... | collective-permute-start | bytes 786440 | tf_op jit(solution)/shard_map/ppermute | solution.py:28
  50.1 0.8 %broadcast_select_fusion = bf16[1,128,2048]{2,1,0:T(8,128)(2,1)} fusion(bf16[1,128,2048]{2,1,0:T(8,128)(2,1)S(1)} %collective-permute-done.3, pred[]{:T(512)S(6)} %lt.19), kind=kLoop, calls=%fused_computation.8 | loop fusion | flops 262144 | bytes 1048577 | tf_op jit(solution)/shard_map/jit(_where)/select_n | solution.py:239
  51.0 0.0 copy-start.4
  51.0 6.6 %collective-permute-done.4 = bf16[2,128,512]{2,1,0:T(8,128)(2,1)S(1)} collective-permute-done((bf16[2,128,512]{2,1,0:T(8,128)(2,1)S(1)}, bf16[2,128,512]{2,1,0:T(8,128)(2,1)S(1)}, u32[]{:S(2)}, u32[]{:S(2)}) %collective-permute-start.4) | collective-permute-done | bytes 262176 | tf_op jit(solution)/shard_map/ppermute | solution.py:28
  57.5 0.0 copy-done
  57.6 0.1 fusion.1
  57.6 1.3 %collective-permute-start.6 = (bf16[2,128,512]{2,1,0:T(8,128)(2,1)S(1)}, bf16[2,128,512]{2,1,0:T(8,128)(2,1)S(1)}, u32[]{:S(2)}, u32[]{:S(2)}) collective-permute-start(bf16[2,128,512]{2,1,0:T(8,128)(2,1)S(1)} %fusion.1), channel_id=1, source_target_pairs={{4,0},{8,4},{12,8},{5,1},{9,5},{13,9},{6,2},{10,6},{14,10},{7,3},{... | collective-permute-start | bytes 786440 | tf_op jit(solution)/shard_map/ppermute | solution.py:28
  58.9 0.0 copy-done.4
  58.9 1.6 %collective-permute-start.5 = (bf16[1,128,2048]{2,1,0:T(8,128)(2,1)S(1)}, bf16[1,128,2048]{2,1,0:T(8,128)(2,1)S(1)}, u32[]{:S(2)}, u32[]{:S(2)}) collective-permute-start(bf16[1,128,2048]{2,1,0:T(8,128)(2,1)S(1)} %bitcast.46), channel_id=1, source_target_pairs={{0,16},{16,0},{1,17},{17,1},{2,18},{18,2},{3,19},{19,3},{4,20},{20... | collective-permute-start | bytes 1572872 | tf_op jit(solution)/shard_map/ppermute | solution.py:22
  60.5 5.6 %collective-permute-done.6 = bf16[2,128,512]{2,1,0:T(8,128)(2,1)S(1)} collective-permute-done((bf16[2,128,512]{2,1,0:T(8,128)(2,1)S(1)}, bf16[2,128,512]{2,1,0:T(8,128)(2,1)S(1)}, u32[]{:S(2)}, u32[]{:S(2)}) %collective-permute-start.6) | collective-permute-done | bytes 262176 | tf_op jit(solution)/shard_map/ppermute | solution.py:28
  66.1 0.1 fusion.2
  66.2 1.3 %collective-permute-start.7 = (bf16[2,128,512]{2,1,0:T(8,128)(2,1)S(1)}, bf16[2,128,512]{2,1,0:T(8,128)(2,1)S(1)}, u32[]{:S(2)}, u32[]{:S(2)}) collective-permute-start(bf16[2,128,512]{2,1,0:T(8,128)(2,1)S(1)} %fusion.2), channel_id=1, source_target_pairs={{4,0},{8,4},{12,8},{5,1},{9,5},{13,9},{6,2},{10,6},{14,10},{7,3},{... | collective-permute-start | bytes 786440 | tf_op jit(solution)/shard_map/ppermute | solution.py:28
  67.5 1.6 %collective-permute-done.5 = bf16[1,128,2048]{2,1,0:T(8,128)(2,1)S(1)} collective-permute-done((bf16[1,128,2048]{2,1,0:T(8,128)(2,1)S(1)}, bf16[1,128,2048]{2,1,0:T(8,128)(2,1)S(1)}, u32[]{:S(2)}, u32[]{:S(2)}) %collective-permute-start.5) | collective-permute-done | bytes 524320 | tf_op jit(solution)/shard_map/ppermute | solution.py:22
  69.1 5.6 %collective-permute-done.7 = bf16[2,128,512]{2,1,0:T(8,128)(2,1)S(1)} collective-permute-done((bf16[2,128,512]{2,1,0:T(8,128)(2,1)S(1)}, bf16[2,128,512]{2,1,0:T(8,128)(2,1)S(1)}, u32[]{:S(2)}, u32[]{:S(2)}) %collective-permute-start.7) | collective-permute-done | bytes 262176 | tf_op jit(solution)/shard_map/ppermute | solution.py:28
  74.7 0.1 fusion
  74.8 1.6 %collective-permute-start.8 = (bf16[2,128,512]{2,1,0:T(8,128)(2,1)S(1)}, bf16[2,128,512]{2,1,0:T(8,128)(2,1)S(1)}, u32[]{:S(2)}, u32[]{:S(2)}) collective-permute-start(bf16[2,128,512]{2,1,0:T(8,128)(2,1)S(1)} %fusion), channel_id=1, source_target_pairs={{0,16},{16,0},{1,17},{17,1},{2,18},{18,2},{3,19},{19,3},{4,20},{20... | collective-permute-start | bytes 786440 | tf_op jit(solution)/shard_map/ppermute | solution.py:22
  76.4 4.9 %collective-permute-done.8 = bf16[2,128,512]{2,1,0:T(8,128)(2,1)S(1)} collective-permute-done((bf16[2,128,512]{2,1,0:T(8,128)(2,1)S(1)}, bf16[2,128,512]{2,1,0:T(8,128)(2,1)S(1)}, u32[]{:S(2)}, u32[]{:S(2)}) %collective-permute-start.8) | collective-permute-done | bytes 262176 | tf_op jit(solution)/shard_map/ppermute | solution.py:22
  81.2 0.7 fusion.8
  82.0 0.8 copy.21
  (7 shorter events, 0.0 us)
Async XLA Ops:
  0.6 1.0 %copy-start.1 = (bf16[1,128,512]{2,1,0:T(8,128)(2,1)S(1)}, bf16[1,128,512]{2,1,0:T(8,128)(2,1)}, u32[]{:S(2)}) copy-start(bf16[1,128,512]{2,1,0:T(8,128)(2,1)} %param.8) | copy-start | bytes 393220
  1.6 24.4 %collective-permute-start.2 = (bf16[2,128,512]{2,1,0:T(8,128)(2,1)S(1)}, bf16[2,128,512]{2,1,0:T(8,128)(2,1)S(1)}, u32[]{:S(2)}, u32[]{:S(2)}) collective-permute-start(bf16[2,128,512]{2,1,0:T(8,128)(2,1)S(1)} %constant_dynamic-update-slice_fusion), channel_id=1, source_target_pairs={{0,12},{1,13},{2,14},{3,15},{16,28},{17,29},{18,30},{19,31}} | collective-permute-start | bytes 786440 | tf_op jit(solution)/shard_map/ppermute | solution.py:28
  8.6 11.2 %collective-permute-start = (bf16[2,128,512]{2,1,0:T(8,128)(2,1)S(1)}, bf16[2,128,512]{2,1,0:T(8,128)(2,1)S(1)}, u32[]{:S(2)}, u32[]{:S(2)}) collective-permute-start(bf16[2,128,512]{2,1,0:T(8,128)(2,1)S(1)} %constant_dynamic-update-slice_fusion), channel_id=1, source_target_pairs={{0,4},{4,8},{8,12},{1,5},{5,9},{9,13},{2,6},{6,10},{10,14},{3,7},{... | collective-permute-start | bytes 786440 | tf_op jit(solution)/shard_map/ppermute | solution.py:28
  10.3 0.7 copy-start.3
  11.1 13.1 %copy-start.2 = (s32[1,2,16,8]{2,3,1,0:T(8,128)S(1)}, s32[1,2,16,8]{2,3,1,0:T(8,128)}, u32[]{:S(2)}) copy-start(s32[1,2,16,8]{2,3,1,0:T(8,128)} %param.10) | copy-start | bytes 3076
  19.8 9.1 %collective-permute-start.1 = (bf16[2,128,512]{2,1,0:T(8,128)(2,1)S(1)}, bf16[2,128,512]{2,1,0:T(8,128)(2,1)S(1)}, u32[]{:S(2)}, u32[]{:S(2)}) collective-permute-start(bf16[2,128,512]{2,1,0:T(8,128)(2,1)S(1)} %collective-permute-done), channel_id=1, source_target_pairs={{0,4},{4,8},{8,12},{1,5},{5,9},{9,13},{2,6},{6,10},{10,14},{3,7},{... | collective-permute-start | bytes 786440 | tf_op jit(solution)/shard_map/ppermute | solution.py:28
  35.7 12.1 %collective-permute-start.3 = (bf16[1,128,2048]{2,1,0:T(8,128)(2,1)}, bf16[1,128,2048]{2,1,0:T(8,128)(2,1)S(1)}, u32[]{:S(2)}, u32[]{:S(2)}) collective-permute-start(bf16[1,128,2048]{2,1,0:T(8,128)(2,1)} %bitcast.47), channel_id=1, source_target_pairs={{0,16},{16,0},{1,17},{17,1},{2,18},{18,2},{3,19},{19,3},{4,20},{20... | collective-permute-start | bytes 1572872 | tf_op jit(solution)/shard_map/ppermute | solution.py:22
  43.9 13.7 %copy-start = (bf16[4,2,128,512]{3,2,1,0:T(8,128)(2,1)S(1)}, bf16[4,2,128,512]{3,2,1,0:T(8,128)(2,1)}, u32[]{:S(2)}) copy-start(bf16[4,2,128,512]{3,2,1,0:T(8,128)(2,1)} %get-tuple-element.20) | copy-start | bytes 3145732
  48.8 8.7 %collective-permute-start.4 = (bf16[2,128,512]{2,1,0:T(8,128)(2,1)S(1)}, bf16[2,128,512]{2,1,0:T(8,128)(2,1)S(1)}, u32[]{:S(2)}, u32[]{:S(2)}) collective-permute-start(bf16[2,128,512]{2,1,0:T(8,128)(2,1)S(1)} %slice_bitcast_fusion), channel_id=1, source_target_pairs={{4,0},{8,4},{12,8},{5,1},{9,5},{13,9},{6,2},{10,6},{14,10},{7,3},{... | collective-permute-start | bytes 786440 | tf_op jit(solution)/shard_map/ppermute | solution.py:28
  51.0 8.0 %copy-start.4 = (bf16[128,2048]{1,0:T(8,128)(2,1)S(1)}, bf16[128,2048]{1,0:T(8,128)(2,1)}, u32[]{:S(2)}) copy-start(bf16[128,2048]{1,0:T(8,128)(2,1)} %get-tuple-element.22) | copy-start | bytes 1572868
  57.6 8.5 %collective-permute-start.6 = (bf16[2,128,512]{2,1,0:T(8,128)(2,1)S(1)}, bf16[2,128,512]{2,1,0:T(8,128)(2,1)S(1)}, u32[]{:S(2)}, u32[]{:S(2)}) collective-permute-start(bf16[2,128,512]{2,1,0:T(8,128)(2,1)S(1)} %fusion.1), channel_id=1, source_target_pairs={{4,0},{8,4},{12,8},{5,1},{9,5},{13,9},{6,2},{10,6},{14,10},{7,3},{... | collective-permute-start | bytes 786440 | tf_op jit(solution)/shard_map/ppermute | solution.py:28
  58.9 10.2 %collective-permute-start.5 = (bf16[1,128,2048]{2,1,0:T(8,128)(2,1)S(1)}, bf16[1,128,2048]{2,1,0:T(8,128)(2,1)S(1)}, u32[]{:S(2)}, u32[]{:S(2)}) collective-permute-start(bf16[1,128,2048]{2,1,0:T(8,128)(2,1)S(1)} %bitcast.46), channel_id=1, source_target_pairs={{0,16},{16,0},{1,17},{17,1},{2,18},{18,2},{3,19},{19,3},{4,20},{20... | collective-permute-start | bytes 1572872 | tf_op jit(solution)/shard_map/ppermute | solution.py:22
  66.2 8.5 %collective-permute-start.7 = (bf16[2,128,512]{2,1,0:T(8,128)(2,1)S(1)}, bf16[2,128,512]{2,1,0:T(8,128)(2,1)S(1)}, u32[]{:S(2)}, u32[]{:S(2)}) collective-permute-start(bf16[2,128,512]{2,1,0:T(8,128)(2,1)S(1)} %fusion.2), channel_id=1, source_target_pairs={{4,0},{8,4},{12,8},{5,1},{9,5},{13,9},{6,2},{10,6},{14,10},{7,3},{... | collective-permute-start | bytes 786440 | tf_op jit(solution)/shard_map/ppermute | solution.py:28
  74.8 6.4 %collective-permute-start.8 = (bf16[2,128,512]{2,1,0:T(8,128)(2,1)S(1)}, bf16[2,128,512]{2,1,0:T(8,128)(2,1)S(1)}, u32[]{:S(2)}, u32[]{:S(2)}) collective-permute-start(bf16[2,128,512]{2,1,0:T(8,128)(2,1)S(1)} %fusion), channel_id=1, source_target_pairs={{0,16},{16,0},{1,17},{17,1},{2,18},{18,2},{3,19},{19,3},{4,20},{20... | collective-permute-start | bytes 786440 | tf_op jit(solution)/shard_map/ppermute | solution.py:22

commit v9 on v8

--- a/solution.py
+++ b/solution.py
@@ -228,7 +228,6 @@
     query_grad, kv_terms = attention_backward(
         query[0], grad_out[0], kv_pieces, masks, log_total, delta, 0, KVH, [None]
     )
-    next_input, kv_terms = lax.optimization_barrier((next_input, kv_terms))
     grad_query = passed_along(query_grad[None], "pipe", -1)
 
     carried = None

time: 83.2 us -> 78.8 us (0.947)
  waiting for transfers between devices: 39.4 us -> 36.9 us
  starting transfers between devices: 21.2 us -> 19.2 us
    ppermute x3, starting transfers between devices: 4.69 us -> 2.67 us  [passed_along(): return lax.ppermute(value, axis, pairs)]
    ppermute x6, waiting for transfers between devices: 28.9 us -> 27 us  [shifted_open(): return lax.ppermute(value, axis, pairs)]
  transfers between devices with their start and end apart: 9 -> 9, of which waited for: 8 -> 8; matrix products, arithmetic and copies ran while one was open for 4% -> 6% of each run, Pallas kernels for 8% -> 8%
where the time goes in v9:
time: 78.8 us; the launch traced here: 78.4 us
  waiting for transfers between devices  36.9 us (47%)
  starting transfers between devices  19.2 us (24%)
  Pallas kernels  12.3 us (16%)
  local copies, waits for them, and re-layouts  6.18 us (8%)
  other arithmetic  2.88 us (4%)
  between operations  0.8 us (1%)
    ppermute x6, waiting for transfers between devices, shifted_open(): return lax.ppermute(value, axis, pairs)  27 us
    ppermute x6, starting transfers between devices, shifted_open(): return lax.ppermute(value, axis, pairs)  16.5 us
    ppermute x3, waiting for transfers between devices, passed_along(): return lax.ppermute(value, axis, pairs)  9.98 us
    pallas_call x1, Pallas kernels, attention_backward(): pl.pallas_call(functools.partial(backward_kernel, piece_count, group_size...  6.62 us
    pallas_call x1, Pallas kernels, attention_forward(): pl.pallas_call(functools.partial(forward_kernel, piece_count, group_size)...  5.72 us
    ppermute x3, starting transfers between devices, passed_along(): return lax.ppermute(value, axis, pairs)  2.67 us
    unnamed x13, local copies, waits for them, and re-layouts  2.43 us
  transfers between devices with their start and end apart: 9, of which 8 were waited for; matrix products, arithmetic and copies ran while one was open for 6% of the time, Pallas kernels for 8%

profile of v9, /device:TPU:0, one launch (start us, length us, event | category | flops | bytes accessed | tf_op | source)
XLA Modules:
  0.0 78.4 jit_solution(11513766214226892675)
XLA Ops:
  0.6 0.0 copy-start.1
  0.6 0.9 %constant_dynamic-update-slice_fusion.1 = bf16[2,128,512]{2,1,0:T(8,128)(2,1)S(1)} fusion(bf16[1,128,512]{2,1,0:T(8,128)(2,1)} %param.7), kind=kLoop, calls=%fused_computation.18 | loop fusion | bytes 262144
  1.6 0.0 copy-done.1
  1.6 7.0 %collective-permute-start.2 = (bf16[2,128,512]{2,1,0:T(8,128)(2,1)S(1)}, bf16[2,128,512]{2,1,0:T(8,128)(2,1)S(1)}, u32[]{:S(2)}, u32[]{:S(2)}) collective-permute-start(bf16[2,128,512]{2,1,0:T(8,128)(2,1)S(1)} %constant_dynamic-update-slice_fusion), channel_id=1, source_target_pairs={{0,12},{1,13},{2,14},{3,15},{16,28},{17,29},{18,30},{19,31}} | collective-permute-start | bytes 786440 | tf_op jit(solution)/shard_map/ppermute | solution.py:28
  8.6 1.3 %collective-permute-start = (bf16[2,128,512]{2,1,0:T(8,128)(2,1)S(1)}, bf16[2,128,512]{2,1,0:T(8,128)(2,1)S(1)}, u32[]{:S(2)}, u32[]{:S(2)}) collective-permute-start(bf16[2,128,512]{2,1,0:T(8,128)(2,1)S(1)} %constant_dynamic-update-slice_fusion), channel_id=1, source_target_pairs={{0,4},{4,8},{8,12},{1,5},{5,9},{9,13},{2,6},{6,10},{10,14},{3,7},{... | collective-permute-start | bytes 786440 | tf_op jit(solution)/shard_map/ppermute | solution.py:28
  9.9 0.1 iota_add_fusion
  10.0 0.1 compare_and_fusion
  10.1 0.1 min.12
  10.2 0.1 copy.14
  10.3 0.0 copy-start.3
  10.3 0.7 copy-done.3
  10.9 0.2 compare_reduce_fusion
  11.1 0.0 copy-start.2
  11.1 0.2 compare_reduce_fusion.1
  11.3 0.1 copy.15
  11.4 0.1 or_or_fusion
  11.5 8.3 %collective-permute-done = bf16[2,128,512]{2,1,0:T(8,128)(2,1)S(1)} collective-permute-done((bf16[2,128,512]{2,1,0:T(8,128)(2,1)S(1)}, bf16[2,128,512]{2,1,0:T(8,128)(2,1)S(1)}, u32[]{:S(2)}, u32[]{:S(2)}) %collective-permute-start) | collective-permute-done | bytes 262176 | tf_op jit(solution)/shard_map/ppermute | solution.py:28
  19.8 4.4 %collective-permute-start.1 = (bf16[2,128,512]{2,1,0:T(8,128)(2,1)S(1)}, bf16[2,128,512]{2,1,0:T(8,128)(2,1)S(1)}, u32[]{:S(2)}, u32[]{:S(2)}) collective-permute-start(bf16[2,128,512]{2,1,0:T(8,128)(2,1)S(1)} %collective-permute-done), channel_id=1, source_target_pairs={{0,4},{4,8},{8,12},{1,5},{5,9},{9,13},{2,6},{6,10},{10,14},{3,7},{... | collective-permute-start | bytes 786440 | tf_op jit(solution)/shard_map/ppermute | solution.py:28
  24.2 0.0 copy-done.2
  24.2 0.6 gather_fusion
  24.8 0.1 fusion.4
  24.9 0.1 copy.16
  25.0 0.2 broadcast_in_dim.35
  25.2 0.8 convert_element_type.44.mask_ref
  26.0 0.0 collective-permute-done.2
  26.0 2.9 %collective-permute-done.1 = bf16[2,128,512]{2,1,0:T(8,128)(2,1)S(1)} collective-permute-done((bf16[2,128,512]{2,1,0:T(8,128)(2,1)S(1)}, bf16[2,128,512]{2,1,0:T(8,128)(2,1)S(1)}, u32[]{:S(2)}, u32[]{:S(2)}) %collective-permute-start.1) | collective-permute-done | bytes 262176 | tf_op jit(solution)/shard_map/ppermute | solution.py:28
  28.9 1.1 %pad_maximum_fusion.kv_ref = bf16[4,2,128,512]{3,2,1,0:T(8,128)(2,1)} fusion(bf16[1,2,128,512]{3,2,1,0:T(8,128)(2,1)S(1)} %bitcast.39, bf16[1,2,128,512]{3,2,1,0:T(8,128)(2,1)S(1)} %bitcast.41, bf16[1,2,128,512]{3,2,1,0:T(8,128)(2,1)S(1)} %bitcast.40, bf16[1,2,128,512]{3,2,1,0:T(8,128)(2,1)S(1)} %bitcast.34), kind=kLoop, calls=%fused_computation.1 | loop fusion | flops 1572864 | bytes 2097152 | tf_op jit(solution)/shard_map/stack | solution.py:223
  30.0 5.7 %shard_map.93 = (bf16[128,2048]{1,0:T(8,128)(2,1)}, f32[4,512,1]{2,1,0:T(8,128)}, f32[4,512,1]{2,1,0:T(8,128)}) custom-call(bf16[128,2048]{1,0:T(8,128)(2,1)} %bitcast.35, bf16[128,2048]{1,0:T(8,128)(2,1)} %bitcast.37, bf16[4,2,128,512]{3,2,1,0:T(8,128)(2,1)} %pad_maximum_fusion.kv_ref, f32[4,16,2,128]{3,2,1,0:T(2,128)} %convert_element_type.44.mask_ref), custom_call_target="tpu_custom_call" | custom-call | flops 536870912 | bytes 2621440 | tf_op jit(solution)/shard_map/pallas_call | solution.py:139
  35.7 1.5 %collective-permute-start.3 = (bf16[1,128,2048]{2,1,0:T(8,128)(2,1)}, bf16[1,128,2048]{2,1,0:T(8,128)(2,1)S(1)}, u32[]{:S(2)}, u32[]{:S(2)}) collective-permute-start(bf16[1,128,2048]{2,1,0:T(8,128)(2,1)} %bitcast.47), channel_id=1, source_target_pairs={{0,16},{16,0},{1,17},{17,1},{2,18},{18,2},{3,19},{19,3},{4,20},{20... | collective-permute-start | bytes 1572872 | tf_op jit(solution)/shard_map/ppermute | solution.py:22
  37.2 6.6 %shard_map.94 = (bf16[128,2048]{1,0:T(8,128)(2,1)}, bf16[4,2,128,512]{3,2,1,0:T(8,128)(2,1)}) custom-call(bf16[128,2048]{1,0:T(8,128)(2,1)} %bitcast.36, bf16[128,2048]{1,0:T(8,128)(2,1)} %bitcast.38, bf16[4,2,128,512]{3,2,1,0:T(8,128)(2,1)} %pad_maximum_fusion.kv_ref, f32[4,16,2,128]{3,2,1,0:T(2,128)} %convert_element_type.44.mask_ref, ...), custom_call_target="tpu_custom_call" | custom-call | flops 1342177280 | bytes 3145728 | tf_op jit(solution)/shard_map/pallas_call | solution.py:179
  43.9 0.0 copy-start
  43.9 1.1 %slice_bitcast_fusion = bf16[2,128,512]{2,1,0:T(8,128)(2,1)S(1)} fusion(bf16[4,2,128,512]{3,2,1,0:T(8,128)(2,1)} %get-tuple-element.16), kind=kLoop, calls=%fused_computation.9 | loop fusion | bytes 524288 | tf_op jit(solution)/shard_map/squeeze | solution.py:235
  44.9 1.3 %collective-permute-start.4 = (bf16[2,128,512]{2,1,0:T(8,128)(2,1)S(1)}, bf16[2,128,512]{2,1,0:T(8,128)(2,1)S(1)}, u32[]{:S(2)}, u32[]{:S(2)}) collective-permute-start(bf16[2,128,512]{2,1,0:T(8,128)(2,1)S(1)} %slice_bitcast_fusion), channel_id=1, source_target_pairs={{4,0},{8,4},{12,8},{5,1},{9,5},{13,9},{6,2},{10,6},{14,10},{7,3},{... | collective-permute-start | bytes 786440 | tf_op jit(solution)/shard_map/ppermute | solution.py:28
  46.2 1.6 %collective-permute-done.3 = bf16[1,128,2048]{2,1,0:T(8,128)(2,1)S(1)} collective-permute-done((bf16[1,128,2048]{2,1,0:T(8,128)(2,1)}, bf16[1,128,2048]{2,1,0:T(8,128)(2,1)S(1)}, u32[]{:S(2)}, u32[]{:S(2)}) %collective-permute-start.3) | collective-permute-done | bytes 524320 | tf_op jit(solution)/shard_map/ppermute | solution.py:22
  47.8 0.8 %broadcast_select_fusion = bf16[1,128,2048]{2,1,0:T(8,128)(2,1)} fusion(bf16[1,128,2048]{2,1,0:T(8,128)(2,1)S(1)} %collective-permute-done.3, pred[]{:T(512)S(6)} %lt.19), kind=kLoop, calls=%fused_computation.8 | loop fusion | flops 262144 | bytes 1048577 | tf_op jit(solution)/shard_map/jit(_where)/select_n | solution.py:238
  48.7 0.0 copy-start.4
  48.7 5.0 %collective-permute-done.4 = bf16[2,128,512]{2,1,0:T(8,128)(2,1)S(1)} collective-permute-done((bf16[2,128,512]{2,1,0:T(8,128)(2,1)S(1)}, bf16[2,128,512]{2,1,0:T(8,128)(2,1)S(1)}, u32[]{:S(2)}, u32[]{:S(2)}) %collective-permute-start.4) | collective-permute-done | bytes 262176 | tf_op jit(solution)/shard_map/ppermute | solution.py:28
  53.7 0.0 copy-done
  53.7 0.1 fusion.1
  53.7 1.3 %collective-permute-start.6 = (bf16[2,128,512]{2,1,0:T(8,128)(2,1)S(1)}, bf16[2,128,512]{2,1,0:T(8,128)(2,1)S(1)}, u32[]{:S(2)}, u32[]{:S(2)}) collective-permute-start(bf16[2,128,512]{2,1,0:T(8,128)(2,1)S(1)} %fusion.1), channel_id=1, source_target_pairs={{4,0},{8,4},{12,8},{5,1},{9,5},{13,9},{6,2},{10,6},{14,10},{7,3},{... | collective-permute-start | bytes 786440 | tf_op jit(solution)/shard_map/ppermute | solution.py:28
  55.0 0.0 copy-done.4
  55.0 0.6 collective-permute-start.5
  55.6 6.4 %collective-permute-done.6 = bf16[2,128,512]{2,1,0:T(8,128)(2,1)S(1)} collective-permute-done((bf16[2,128,512]{2,1,0:T(8,128)(2,1)S(1)}, bf16[2,128,512]{2,1,0:T(8,128)(2,1)S(1)}, u32[]{:S(2)}, u32[]{:S(2)}) %collective-permute-start.6) | collective-permute-done | bytes 262176 | tf_op jit(solution)/shard_map/ppermute | solution.py:28
  62.0 0.1 fusion.2
  62.1 1.3 %collective-permute-start.7 = (bf16[2,128,512]{2,1,0:T(8,128)(2,1)S(1)}, bf16[2,128,512]{2,1,0:T(8,128)(2,1)S(1)}, u32[]{:S(2)}, u32[]{:S(2)}) collective-permute-start(bf16[2,128,512]{2,1,0:T(8,128)(2,1)S(1)} %fusion.2), channel_id=1, source_target_pairs={{4,0},{8,4},{12,8},{5,1},{9,5},{13,9},{6,2},{10,6},{14,10},{7,3},{... | collective-permute-start | bytes 786440 | tf_op jit(solution)/shard_map/ppermute | solution.py:28
  63.4 2.5 %collective-permute-done.5 = bf16[1,128,2048]{2,1,0:T(8,128)(2,1)S(1)} collective-permute-done((bf16[1,128,2048]{2,1,0:T(8,128)(2,1)S(1)}, bf16[1,128,2048]{2,1,0:T(8,128)(2,1)S(1)}, u32[]{:S(2)}, u32[]{:S(2)}) %collective-permute-start.5) | collective-permute-done | bytes 524320 | tf_op jit(solution)/shard_map/ppermute | solution.py:22
  65.9 4.5 %collective-permute-done.7 = bf16[2,128,512]{2,1,0:T(8,128)(2,1)S(1)} collective-permute-done((bf16[2,128,512]{2,1,0:T(8,128)(2,1)S(1)}, bf16[2,128,512]{2,1,0:T(8,128)(2,1)S(1)}, u32[]{:S(2)}, u32[]{:S(2)}) %collective-permute-start.7) | collective-permute-done | bytes 262176 | tf_op jit(solution)/shard_map/ppermute | solution.py:28
  70.3 0.1 fusion
  70.4 0.6 collective-permute-start.8
  71.0 5.9 %collective-permute-done.8 = bf16[2,128,512]{2,1,0:T(8,128)(2,1)S(1)} collective-permute-done((bf16[2,128,512]{2,1,0:T(8,128)(2,1)S(1)}, bf16[2,128,512]{2,1,0:T(8,128)(2,1)S(1)}, u32[]{:S(2)}, u32[]{:S(2)}) %collective-permute-start.8) | collective-permute-done | bytes 262176 | tf_op jit(solution)/shard_map/ppermute | solution.py:22
  76.8 0.7 fusion.8
  77.6 0.8 %copy.21 = bf16[1,128,2048]{2,1,0:T(8,128)(2,1)} copy(bf16[1,128,2048]{2,1,0:T(8,128)(2,1)S(1)} %collective-permute-done.5) | data formatting | bytes 1048576
  (7 shorter events, 0.0 us)
Async XLA Ops:
  0.6 1.0 %copy-start.1 = (bf16[1,128,512]{2,1,0:T(8,128)(2,1)S(1)}, bf16[1,128,512]{2,1,0:T(8,128)(2,1)}, u32[]{:S(2)}) copy-start(bf16[1,128,512]{2,1,0:T(8,128)(2,1)} %param.8) | copy-start | bytes 393220
  1.6 24.4 %collective-permute-start.2 = (bf16[2,128,512]{2,1,0:T(8,128)(2,1)S(1)}, bf16[2,128,512]{2,1,0:T(8,128)(2,1)S(1)}, u32[]{:S(2)}, u32[]{:S(2)}) collective-permute-start(bf16[2,128,512]{2,1,0:T(8,128)(2,1)S(1)} %constant_dynamic-update-slice_fusion), channel_id=1, source_target_pairs={{0,12},{1,13},{2,14},{3,15},{16,28},{17,29},{18,30},{19,31}} | collective-permute-start | bytes 786440 | tf_op jit(solution)/shard_map/ppermute | solution.py:28
  8.6 11.2 %collective-permute-start = (bf16[2,128,512]{2,1,0:T(8,128)(2,1)S(1)}, bf16[2,128,512]{2,1,0:T(8,128)(2,1)S(1)}, u32[]{:S(2)}, u32[]{:S(2)}) collective-permute-start(bf16[2,128,512]{2,1,0:T(8,128)(2,1)S(1)} %constant_dynamic-update-slice_fusion), channel_id=1, source_target_pairs={{0,4},{4,8},{8,12},{1,5},{5,9},{9,13},{2,6},{6,10},{10,14},{3,7},{... | collective-permute-start | bytes 786440 | tf_op jit(solution)/shard_map/ppermute | solution.py:28
  10.3 0.7 copy-start.3
  11.1 13.1 %copy-start.2 = (s32[1,2,16,8]{2,3,1,0:T(8,128)S(1)}, s32[1,2,16,8]{2,3,1,0:T(8,128)}, u32[]{:S(2)}) copy-start(s32[1,2,16,8]{2,3,1,0:T(8,128)} %param.10) | copy-start | bytes 3076
  19.8 9.1 %collective-permute-start.1 = (bf16[2,128,512]{2,1,0:T(8,128)(2,1)S(1)}, bf16[2,128,512]{2,1,0:T(8,128)(2,1)S(1)}, u32[]{:S(2)}, u32[]{:S(2)}) collective-permute-start(bf16[2,128,512]{2,1,0:T(8,128)(2,1)S(1)} %collective-permute-done), channel_id=1, source_target_pairs={{0,4},{4,8},{8,12},{1,5},{5,9},{9,13},{2,6},{6,10},{10,14},{3,7},{... | collective-permute-start | bytes 786440 | tf_op jit(solution)/shard_map/ppermute | solution.py:28
  35.7 12.1 %collective-permute-start.3 = (bf16[1,128,2048]{2,1,0:T(8,128)(2,1)}, bf16[1,128,2048]{2,1,0:T(8,128)(2,1)S(1)}, u32[]{:S(2)}, u32[]{:S(2)}) collective-permute-start(bf16[1,128,2048]{2,1,0:T(8,128)(2,1)} %bitcast.47), channel_id=1, source_target_pairs={{0,16},{16,0},{1,17},{17,1},{2,18},{18,2},{3,19},{19,3},{4,20},{20... | collective-permute-start | bytes 1572872 | tf_op jit(solution)/shard_map/ppermute | solution.py:22
  43.9 9.8 %copy-start = (bf16[4,2,128,512]{3,2,1,0:T(8,128)(2,1)S(1)}, bf16[4,2,128,512]{3,2,1,0:T(8,128)(2,1)}, u32[]{:S(2)}) copy-start(bf16[4,2,128,512]{3,2,1,0:T(8,128)(2,1)} %get-tuple-element.16) | copy-start | bytes 3145732
  44.9 8.7 %collective-permute-start.4 = (bf16[2,128,512]{2,1,0:T(8,128)(2,1)S(1)}, bf16[2,128,512]{2,1,0:T(8,128)(2,1)S(1)}, u32[]{:S(2)}, u32[]{:S(2)}) collective-permute-start(bf16[2,128,512]{2,1,0:T(8,128)(2,1)S(1)} %slice_bitcast_fusion), channel_id=1, source_target_pairs={{4,0},{8,4},{12,8},{5,1},{9,5},{13,9},{6,2},{10,6},{14,10},{7,3},{... | collective-permute-start | bytes 786440 | tf_op jit(solution)/shard_map/ppermute | solution.py:28
  48.7 6.4 %copy-start.4 = (bf16[128,2048]{1,0:T(8,128)(2,1)S(1)}, bf16[128,2048]{1,0:T(8,128)(2,1)}, u32[]{:S(2)}) copy-start(bf16[128,2048]{1,0:T(8,128)(2,1)} %get-tuple-element.18) | copy-start | bytes 1572868
  53.7 8.3 %collective-permute-start.6 = (bf16[2,128,512]{2,1,0:T(8,128)(2,1)S(1)}, bf16[2,128,512]{2,1,0:T(8,128)(2,1)S(1)}, u32[]{:S(2)}, u32[]{:S(2)}) collective-permute-start(bf16[2,128,512]{2,1,0:T(8,128)(2,1)S(1)} %fusion.1), channel_id=1, source_target_pairs={{4,0},{8,4},{12,8},{5,1},{9,5},{13,9},{6,2},{10,6},{14,10},{7,3},{... | collective-permute-start | bytes 786440 | tf_op jit(solution)/shard_map/ppermute | solution.py:28
  55.0 10.8 %collective-permute-start.5 = (bf16[1,128,2048]{2,1,0:T(8,128)(2,1)S(1)}, bf16[1,128,2048]{2,1,0:T(8,128)(2,1)S(1)}, u32[]{:S(2)}, u32[]{:S(2)}) collective-permute-start(bf16[1,128,2048]{2,1,0:T(8,128)(2,1)S(1)} %bitcast.46), channel_id=1, source_target_pairs={{0,16},{16,0},{1,17},{17,1},{2,18},{18,2},{3,19},{19,3},{4,20},{20... | collective-permute-start | bytes 1572872 | tf_op jit(solution)/shard_map/ppermute | solution.py:22
  62.1 8.3 %collective-permute-start.7 = (bf16[2,128,512]{2,1,0:T(8,128)(2,1)S(1)}, bf16[2,128,512]{2,1,0:T(8,128)(2,1)S(1)}, u32[]{:S(2)}, u32[]{:S(2)}) collective-permute-start(bf16[2,128,512]{2,1,0:T(8,128)(2,1)S(1)} %fusion.2), channel_id=1, source_target_pairs={{4,0},{8,4},{12,8},{5,1},{9,5},{13,9},{6,2},{10,6},{14,10},{7,3},{... | collective-permute-start | bytes 786440 | tf_op jit(solution)/shard_map/ppermute | solution.py:28
  70.4 6.4 %collective-permute-start.8 = (bf16[2,128,512]{2,1,0:T(8,128)(2,1)S(1)}, bf16[2,128,512]{2,1,0:T(8,128)(2,1)S(1)}, u32[]{:S(2)}, u32[]{:S(2)}) collective-permute-start(bf16[2,128,512]{2,1,0:T(8,128)(2,1)S(1)} %fusion), channel_id=1, source_target_pairs={{0,16},{16,0},{1,17},{17,1},{2,18},{18,2},{3,19},{19,3},{4,20},{20... | collective-permute-start | bytes 786440 | tf_op jit(solution)/shard_map/ppermute | solution.py:22

commit v10 on v9

--- a/solution.py
+++ b/solution.py
@@ -82,12 +82,14 @@
     )
 
 
-def forward_kernel(piece_count, group_size, query_ref, grad_ref, kv_ref, mask_ref, out_ref, lse_ref, delta_ref):
+def forward_kernel(piece_count, group_size, query_ref, grad_ref, mask_ref, *refs):
+    kv_refs = refs[:piece_count]
+    out_ref, lse_ref, delta_ref = refs[piece_count:]
     tok_rows = query_ref.shape[0]
     score_scale = HD ** (-0.5)
     query_rows = stacked(query_ref, group_size)
-    all_keys = kv_ref[:, 0].reshape(piece_count * tok_rows, HD)
-    all_values = kv_ref[:, 1].reshape(piece_count * tok_rows, HD)
+    all_keys = jnp.concatenate([ref[0] for ref in kv_refs], axis=0)
+    all_values = jnp.concatenate([ref[1] for ref in kv_refs], axis=0)
     raw = dot_nt(query_rows, all_keys) * score_scale
     masked = jnp.where(all_allowed(mask_ref, piece_count, group_size, tok_rows), raw, NEG_FILL)
     row_high = jnp.max(masked, axis=1, keepdims=True)
@@ -104,16 +106,16 @@
     )
 
 
-def backward_kernel(
-    piece_count, group_size, query_ref, grad_ref, kv_ref, mask_ref, lse_ref, delta_ref, *rest
-):
-    dq_ref, dkv_ref = rest[-2:]
+def backward_kernel(piece_count, group_size, query_ref, grad_ref, mask_ref, lse_ref, delta_ref, *refs):
+    kv_refs = refs[:piece_count]
+    dq_ref = refs[piece_count]
+    dkv_refs = refs[piece_count + 1 :]
     tok_rows = query_ref.shape[0]
     score_scale = HD ** (-0.5)
     query_rows = stacked(query_ref, group_size)
     grad_rows = stacked(grad_ref, group_size)
-    all_keys = kv_ref[:, 0].reshape(piece_count * tok_rows, HD)
-    all_values = kv_ref[:, 1].reshape(piece_count * tok_rows, HD)
+    all_keys = jnp.concatenate([ref[0] for ref in kv_refs], axis=0)
+    all_values = jnp.concatenate([ref[1] for ref in kv_refs], axis=0)
     raw = dot_nt(query_rows, all_keys) * score_scale
     masked = jnp.where(all_allowed(mask_ref, piece_count, group_size, tok_rows), raw, NEG_FILL)
     row_probs = jnp.exp(masked - lse_ref[0])
@@ -122,29 +124,32 @@
     score_grads = (row_probs * (prob_grads - delta_ref[0])).astype(jnp.bfloat16)
     query_grad = jnp.dot(score_grads, all_keys, preferred_element_type=jnp.float32)
     key_terms = dot_tn(score_grads, query_rows) * score_scale
-    dkv_ref[:, 0] = key_terms.reshape(piece_count, tok_rows, HD).astype(dkv_ref.dtype)
-    dkv_ref[:, 1] = value_terms.reshape(piece_count, tok_rows, HD).astype(dkv_ref.dtype)
+    for shift, ref in enumerate(dkv_refs):
+        piece_rows = slice(shift * tok_rows, (shift + 1) * tok_rows)
+        ref[0] = key_terms[piece_rows].astype(ref.dtype)
+        ref[1] = value_terms[piece_rows].astype(ref.dtype)
     query_grad = (query_grad * score_scale).astype(dq_ref.dtype)
     for head in range(group_size):
         dq_ref[:, head * HD : (head + 1) * HD] = query_grad[head * tok_rows : (head + 1) * tok_rows]
 
 
-def attention_forward(query_rows, grad_rows, kv_pieces, masks):
+def attention_forward(query_rows, grad_rows, pieces, masks):
     tok_rows, query_width = query_rows.shape
-    piece_count = kv_pieces.shape[0]
+    piece_count = len(pieces)
     group_size = H // KVH
     group_width = group_size * HD
     rows = group_size * tok_rows
     flops = 4 * tok_rows * tok_rows * HD * H * piece_count
+    piece_block = pl.BlockSpec((2, tok_rows, HD), lambda g: (0, 0, g))
     return pl.pallas_call(
         functools.partial(forward_kernel, piece_count, group_size),
         grid=(KVH,),
         in_specs=[
             pl.BlockSpec((tok_rows, group_width), lambda g: (0, g)),
             pl.BlockSpec((tok_rows, group_width), lambda g: (0, g)),
-            pl.BlockSpec((piece_count, 2, tok_rows, HD), lambda g: (0, 0, 0, g)),
             pl.BlockSpec((piece_count, group_size) + masks.shape[2:], lambda g: (0, g, 0, 0)),
-        ],
+        ]
+        + [piece_block] * piece_count,
         out_specs=[
             pl.BlockSpec((tok_rows, group_width), lambda g: (0, g)),
             pl.BlockSpec((1, rows, 1), lambda g: (g, 0, 0)),
@@ -158,51 +163,40 @@
         cost_estimate=pl.CostEstimate(
             flops=flops,
             transcendentals=tok_rows * tok_rows * H * piece_count,
-            bytes_accessed=3 * query_rows.size * 2 + kv_pieces.size * 2,
+            bytes_accessed=3 * query_rows.size * 2 + piece_count * pieces[0].size * 2,
         ),
-    )(query_rows, grad_rows, kv_pieces, masks)
-
-
-def attention_backward(query_rows, grad_rows, kv_pieces, masks, log_total, delta, first_group, group_count, extra):
+    )(query_rows, grad_rows, masks, *pieces)
+
+
+def attention_backward(query_rows, grad_rows, pieces, masks, log_total, delta):
     tok_rows, query_width = query_rows.shape
-    piece_count = kv_pieces.shape[0]
+    piece_count = len(pieces)
     group_size = H // KVH
     group_width = group_size * HD
     rows = group_size * tok_rows
-    flops = 10 * tok_rows * tok_rows * HD * group_size * group_count * piece_count
-    aliases = {}
-    if extra and extra[0] is not None:
-        aliases = {6: 0, 7: 1}
-    else:
-        extra = extra[1:] if extra else extra
-    shift_g = lambda g: g + first_group
-    return pl.pallas_call(
+    flops = 10 * tok_rows * tok_rows * HD * H * piece_count
+    piece_block = pl.BlockSpec((2, tok_rows, HD), lambda g: (0, 0, g))
+    outs = pl.pallas_call(
         functools.partial(backward_kernel, piece_count, group_size),
-        grid=(group_count,),
+        grid=(KVH,),
         in_specs=[
-            pl.BlockSpec((tok_rows, group_width), lambda g: (0, shift_g(g))),
-            pl.BlockSpec((tok_rows, group_width), lambda g: (0, shift_g(g))),
-            pl.BlockSpec((piece_count, 2, tok_rows, HD), lambda g: (0, 0, 0, shift_g(g))),
-            pl.BlockSpec((piece_count, group_size) + masks.shape[2:], lambda g: (0, shift_g(g), 0, 0)),
-            pl.BlockSpec((1, rows, 1), lambda g: (shift_g(g), 0, 0)),
-            pl.BlockSpec((1, rows, 1), lambda g: (shift_g(g), 0, 0)),
+            pl.BlockSpec((tok_rows, group_width), lambda g: (0, g)),
+            pl.BlockSpec((tok_rows, group_width), lambda g: (0, g)),
+            pl.BlockSpec((piece_count, group_size) + masks.shape[2:], lambda g: (0, g, 0, 0)),
+            pl.BlockSpec((1, rows, 1), lambda g: (g, 0, 0)),
+            pl.BlockSpec((1, rows, 1), lambda g: (g, 0, 0)),
         ]
-        + [pl.BlockSpec(memory_space=pl.ANY) for _ in extra],
-        out_specs=[
-            pl.BlockSpec((tok_rows, group_width), lambda g: (0, shift_g(g))),
-            pl.BlockSpec((piece_count, 2, tok_rows, HD), lambda g: (0, 0, 0, shift_g(g))),
-        ],
-        out_shape=[
-            jax.ShapeDtypeStruct((tok_rows, query_width), jnp.bfloat16),
-            jax.ShapeDtypeStruct(kv_pieces.shape, jnp.bfloat16),
-        ],
-        input_output_aliases=aliases,
+        + [piece_block] * piece_count,
+        out_specs=[pl.BlockSpec((tok_rows, group_width), lambda g: (0, g))] + [piece_block] * piece_count,
+        out_shape=[jax.ShapeDtypeStruct((tok_rows, query_width), jnp.bfloat16)]
+        + [jax.ShapeDtypeStruct(pieces[0].shape, jnp.bfloat16)] * piece_count,
         cost_estimate=pl.CostEstimate(
             flops=flops,
-            transcendentals=tok_rows * tok_rows * group_size * group_count * piece_count,
-            bytes_accessed=(2 * query_rows.size * 2 + 2 * kv_pieces.size * 2) * group_count // KVH,
+            transcendentals=tok_rows * tok_rows * H * piece_count,
+            bytes_accessed=2 * query_rows.size * 2 + 2 * piece_count * pieces[0].size * 2,
         ),
-    )(query_rows, grad_rows, kv_pieces, masks, log_total, delta, *extra)
+    )(query_rows, grad_rows, masks, log_total, delta, *pieces)
+    return outs[0], outs[1:]
 
 
 def local(query, keys, values, grad_out, random_blocks, global_ids):
@@ -220,14 +214,10 @@
         pieces = [own]
         for shift in range(1, ctx_count):
             pieces.append(shifted_open(pieces[-1], "ctx", 1))
-    kv_pieces = jnp.stack(pieces)
-
-    attended, log_total, delta = attention_forward(query[0], grad_out[0], kv_pieces, masks)
+    attended, log_total, delta = attention_forward(query[0], grad_out[0], pieces, masks)
     next_input = passed_along(attended[None], "pipe", 1)
 
-    query_grad, kv_terms = attention_backward(
-        query[0], grad_out[0], kv_pieces, masks, log_total, delta, 0, KVH, [None]
-    )
+    query_grad, kv_terms = attention_backward(query[0], grad_out[0], pieces, masks, log_total, delta)
     grad_query = passed_along(query_grad[None], "pipe", -1)
 
     carried = None

time: 78.8 us -> 75.7 us (0.961)
  waiting for transfers between devices: 36.9 us -> 34.7 us
  other arithmetic: 2.88 us -> 1.77 us
    ppermute x6, waiting for transfers between devices: 27 us -> 22.4 us  [shifted_open(): return lax.ppermute(value, axis, pairs)]
    ppermute x3, waiting for transfers between devices: 9.98 us -> 12.3 us  [passed_along(): return lax.ppermute(value, axis, pairs)]
    another operation x1 -> x0, other arithmetic: 1.11 us -> none  [local(): kv_pieces = jnp.stack(pieces)]
    squeeze x1 -> x0, local copies, waits for them, and re-layouts: 1.06 us -> none  [local(): part = kv_terms[ctx_count - step].astype(jnp.float32)]
    unnamed x13 -> x25, local copies, waits for them, and re-layouts: 2.43 us -> 3.14 us
  transfers between devices with their start and end apart: 9 -> 9, of which waited for: 8 -> 8; matrix products, arithmetic and copies ran while one was open for 6% -> 5% of each run, Pallas kernels for 8% -> 9%
where the time goes in v10:
time: 75.7 us; the launch traced here: 74.6 us
  waiting for transfers between devices  34.7 us (46%)
  starting transfers between devices  19.3 us (25%)
  Pallas kernels  12.2 us (16%)
  local copies, waits for them, and re-layouts  5.84 us (8%)
  other arithmetic  1.77 us (2%)
  between operations  0.83 us (1%)
    ppermute x6, waiting for transfers between devices, shifted_open(): return lax.ppermute(value, axis, pairs)  22.4 us
    ppermute x6, starting transfers between devices, shifted_open(): return lax.ppermute(value, axis, pairs)  16.7 us
    ppermute x3, waiting for transfers between devices, passed_along(): return lax.ppermute(value, axis, pairs)  12.3 us
    pallas_call x1, Pallas kernels, attention_backward(): pl.pallas_call(functools.partial(backward_kernel, piece_count, group_size...  6.42 us
    pallas_call x1, Pallas kernels, attention_forward(): pl.pallas_call(functools.partial(forward_kernel, piece_count, group_size)...  5.8 us
    unnamed x25, local copies, waits for them, and re-layouts  3.14 us
    ppermute x3, starting transfers between devices, passed_along(): return lax.ppermute(value, axis, pairs)  2.62 us
  transfers between devices with their start and end apart: 9, of which 8 were waited for; matrix products, arithmetic and copies ran while one was open for 5% of the time, Pallas kernels for 9%

profile of v10, /device:TPU:0, one launch (start us, length us, event | category | flops | bytes accessed | tf_op | source)
XLA Modules:
  0.0 74.6 jit_solution(1764211852034938104)
XLA Ops:
  0.6 0.0 copy-start.7
  0.6 0.9 %constant_dynamic-update-slice_fusion.1 = bf16[2,128,512]{2,1,0:T(8,128)(2,1)S(1)} fusion(bf16[1,128,512]{2,1,0:T(8,128)(2,1)} %param.7), kind=kLoop, calls=%fused_computation.13 | loop fusion | bytes 262144
  1.6 0.0 copy-done.7
  1.6 0.0 copy-start
  1.6 4.9 %collective-permute-start = (bf16[2,128,512]{2,1,0:T(8,128)(2,1)S(1)}, bf16[2,128,512]{2,1,0:T(8,128)(2,1)S(1)}, u32[]{:S(2)}, u32[]{:S(2)}) collective-permute-start(bf16[2,128,512]{2,1,0:T(8,128)(2,1)S(1)} %constant_dynamic-update-slice_fusion.refs_0_), channel_id=1, source_target_pairs={{0,4},{4,8},{8,12},{1,5},{5,9},{9,13},{2,6},{6,10},{10,14},{3,7},{... | collective-permute-start | bytes 786440 | tf_op jit(solution)/shard_map/ppermute | solution.py:28
  6.6 3.3 %collective-permute-start.2 = (bf16[2,128,512]{2,1,0:T(8,128)(2,1)S(1)}, bf16[2,128,512]{2,1,0:T(8,128)(2,1)S(1)}, u32[]{:S(2)}, u32[]{:S(2)}) collective-permute-start(bf16[2,128,512]{2,1,0:T(8,128)(2,1)S(1)} %constant_dynamic-update-slice_fusion.refs_0_), channel_id=1, source_target_pairs={{0,12},{1,13},{2,14},{3,15},{16,28},{17,29},{18,30},{19,31}} | collective-permute-start | bytes 786440 | tf_op jit(solution)/shard_map/ppermute | solution.py:28
  9.9 0.1 iota_add_fusion
  10.0 0.1 compare_and_fusion
  10.1 0.1 min.12
  10.2 0.1 copy.14
  10.3 0.0 copy-start.9
  10.3 0.7 copy-done.9
  10.9 0.2 compare_reduce_fusion
  11.1 0.0 copy-start.8
  11.1 0.2 compare_reduce_fusion.1
  11.3 0.1 copy.15
  11.4 0.1 or_or_fusion
  11.5 1.7 %collective-permute-done.refs_1_ = bf16[2,128,512]{2,1,0:T(8,128)(2,1)S(1)} collective-permute-done((bf16[2,128,512]{2,1,0:T(8,128)(2,1)S(1)}, bf16[2,128,512]{2,1,0:T(8,128)(2,1)S(1)}, u32[]{:S(2)}, u32[]{:S(2)}) %collective-permute-start) | collective-permute-done | bytes 262176 | tf_op jit(solution)/shard_map/ppermute | solution.py:28
  13.3 0.0 copy-start.1
  13.3 4.4 %collective-permute-start.1 = (bf16[2,128,512]{2,1,0:T(8,128)(2,1)S(1)}, bf16[2,128,512]{2,1,0:T(8,128)(2,1)S(1)}, u32[]{:S(2)}, u32[]{:S(2)}) collective-permute-start(bf16[2,128,512]{2,1,0:T(8,128)(2,1)S(1)} %collective-permute-done.refs_1_), channel_id=1, source_target_pairs={{0,4},{4,8},{8,12},{1,5},{5,9},{9,13},{2,6},{6,10},{10,14},{3,7},{... | collective-permute-start | bytes 786440 | tf_op jit(solution)/shard_map/ppermute | solution.py:28
  17.7 0.0 copy-done.8
  17.7 0.6 gather_fusion
  18.3 0.1 fusion.1
  18.4 0.1 copy.16
  18.5 0.2 broadcast_in_dim.35
  18.7 0.8 %convert_element_type.35.mask_ref = f32[4,16,2,128]{3,2,1,0:T(2,128)} reshape(f32[4,16,2,2,64]{4,3,2,1,0:T(2,128)S(1)} %broadcast_in_dim.35) | data formatting | bytes 131072 | tf_op jit(solution)/shard_map/convert_element_type | solution.py:48
  19.5 0.0 copy-done
  19.5 0.0 copy-done.1
  19.5 0.0 collective-permute-done.2.refs_3_
  19.5 0.0 copy-start.2
  19.5 3.9 %collective-permute-done.1.refs_2_ = bf16[2,128,512]{2,1,0:T(8,128)(2,1)S(1)} collective-permute-done((bf16[2,128,512]{2,1,0:T(8,128)(2,1)S(1)}, bf16[2,128,512]{2,1,0:T(8,128)(2,1)S(1)}, u32[]{:S(2)}, u32[]{:S(2)}) %collective-permute-start.1) | collective-permute-done | bytes 262176 | tf_op jit(solution)/shard_map/ppermute | solution.py:28
  23.4 0.0 copy-start.4
  23.4 0.0 copy-done.2
  23.4 0.7 copy-done.4
  24.1 5.8 %shard_map.93 = (bf16[128,2048]{1,0:T(8,128)(2,1)}, f32[4,512,1]{2,1,0:T(8,128)}, f32[4,512,1]{2,1,0:T(8,128)}) custom-call(bf16[128,2048]{1,0:T(8,128)(2,1)} %bitcast.19, bf16[128,2048]{1,0:T(8,128)(2,1)} %bitcast.21, f32[4,16,2,128]{3,2,1,0:T(2,128)} %convert_element_type.35.mask_ref, bf16[2,128,512]{2,1,0:T(8,128)(2,1)} %copy-done, ...), custom_call_target="tpu_custom_call" | custom-call | flops 536870912 | bytes 2621440 | tf_op jit(solution)/shard_map/pallas_call | solution.py:144
  29.9 1.5 %collective-permute-start.3 = (bf16[1,128,2048]{2,1,0:T(8,128)(2,1)}, bf16[1,128,2048]{2,1,0:T(8,128)(2,1)S(1)}, u32[]{:S(2)}, u32[]{:S(2)}) collective-permute-start(bf16[1,128,2048]{2,1,0:T(8,128)(2,1)} %bitcast.28), channel_id=1, source_target_pairs={{0,16},{16,0},{1,17},{17,1},{2,18},{18,2},{3,19},{19,3},{4,20},{20... | collective-permute-start | bytes 1572872 | tf_op jit(solution)/shard_map/ppermute | solution.py:22
  31.4 6.4 %shard_map.94 = (bf16[128,2048]{1,0:T(8,128)(2,1)}, bf16[2,128,512]{2,1,0:T(8,128)(2,1)}, bf16[2,128,512]{2,1,0:T(8,128)(2,1)}, bf16[2,128,512]{2,1,0:T(8,128)(2,1)}, bf16[2,128,512]{2,1,0:T(8,128)(2,1)}) custom-call(bf16[128,2048]{1,0:T(8,128)(2,1)} %bitcast.20, bf16[128,2048]{1,0:T(8,128)(2,1)} %bitcast.22, ...), custom_call_target="tpu_custom_call" | custom-call | flops 1342177280 | bytes 3145728 | tf_op jit(solution)/shard_map/pallas_call | solution.py:179
  37.8 0.0 copy-start.6
  37.8 1.4 %collective-permute-start.4 = (bf16[2,128,512]{2,1,0:T(8,128)(2,1)}, bf16[2,128,512]{2,1,0:T(8,128)(2,1)S(1)}, u32[]{:S(2)}, u32[]{:S(2)}) collective-permute-start(bf16[2,128,512]{2,1,0:T(8,128)(2,1)} %get-tuple-element.19), channel_id=1, source_target_pairs={{4,0},{8,4},{12,8},{5,1},{9,5},{13,9},{6,2},{10,6},{14,10},{7,3},{... | collective-permute-start | bytes 786440 | tf_op jit(solution)/shard_map/ppermute | solution.py:28
  39.3 3.6 %collective-permute-done.3 = bf16[1,128,2048]{2,1,0:T(8,128)(2,1)S(1)} collective-permute-done((bf16[1,128,2048]{2,1,0:T(8,128)(2,1)}, bf16[1,128,2048]{2,1,0:T(8,128)(2,1)S(1)}, u32[]{:S(2)}, u32[]{:S(2)}) %collective-permute-start.3) | collective-permute-done | bytes 524320 | tf_op jit(solution)/shard_map/ppermute | solution.py:22
  42.9 0.8 %broadcast_select_fusion = bf16[1,128,2048]{2,1,0:T(8,128)(2,1)} fusion(bf16[1,128,2048]{2,1,0:T(8,128)(2,1)S(1)} %collective-permute-done.3, pred[]{:T(512)S(6)} %lt.19), kind=kLoop, calls=%fused_computation.4 | loop fusion | flops 262144 | bytes 1048577 | tf_op jit(solution)/shard_map/jit(_where)/select_n | solution.py:228
  43.7 0.0 copy-start.10
  43.7 4.0 %collective-permute-done.4 = bf16[2,128,512]{2,1,0:T(8,128)(2,1)S(1)} collective-permute-done((bf16[2,128,512]{2,1,0:T(8,128)(2,1)}, bf16[2,128,512]{2,1,0:T(8,128)(2,1)S(1)}, u32[]{:S(2)}, u32[]{:S(2)}) %collective-permute-start.4) | collective-permute-done | bytes 262176 | tf_op jit(solution)/shard_map/ppermute | solution.py:28
  47.7 0.0 copy-done.6
  47.7 0.0 copy-start.5
  47.7 0.1 add_convert_fusion.2
  47.8 1.3 %collective-permute-start.6 = (bf16[2,128,512]{2,1,0:T(8,128)(2,1)S(1)}, bf16[2,128,512]{2,1,0:T(8,128)(2,1)S(1)}, u32[]{:S(2)}, u32[]{:S(2)}) collective-permute-start(bf16[2,128,512]{2,1,0:T(8,128)(2,1)S(1)} %add_convert_fusion.2), channel_id=1, source_target_pairs={{4,0},{8,4},{12,8},{5,1},{9,5},{13,9},{6,2},{10,6},{14,10},{7,3},{... | collective-permute-start | bytes 786440 | tf_op jit(solution)/shard_map/ppermute | solution.py:28
  49.1 0.0 copy-done.10
  49.1 0.6 collective-permute-start.5
  49.7 6.6 %collective-permute-done.6 = bf16[2,128,512]{2,1,0:T(8,128)(2,1)S(1)} collective-permute-done((bf16[2,128,512]{2,1,0:T(8,128)(2,1)S(1)}, bf16[2,128,512]{2,1,0:T(8,128)(2,1)S(1)}, u32[]{:S(2)}, u32[]{:S(2)}) %collective-permute-start.6) | collective-permute-done | bytes 262176 | tf_op jit(solution)/shard_map/ppermute | solution.py:28
  56.3 0.0 copy-done.5
  56.3 0.0 copy-start.3
  56.3 0.1 add_convert_fusion.1
  56.4 1.3 %collective-permute-start.7 = (bf16[2,128,512]{2,1,0:T(8,128)(2,1)S(1)}, bf16[2,128,512]{2,1,0:T(8,128)(2,1)S(1)}, u32[]{:S(2)}, u32[]{:S(2)}) collective-permute-start(bf16[2,128,512]{2,1,0:T(8,128)(2,1)S(1)} %add_convert_fusion.1), channel_id=1, source_target_pairs={{4,0},{8,4},{12,8},{5,1},{9,5},{13,9},{6,2},{10,6},{14,10},{7,3},{... | collective-permute-start | bytes 786440 | tf_op jit(solution)/shard_map/ppermute | solution.py:28
  57.7 2.8 %collective-permute-done.5 = bf16[1,128,2048]{2,1,0:T(8,128)(2,1)S(1)} collective-permute-done((bf16[1,128,2048]{2,1,0:T(8,128)(2,1)S(1)}, bf16[1,128,2048]{2,1,0:T(8,128)(2,1)S(1)}, u32[]{:S(2)}, u32[]{:S(2)}) %collective-permute-start.5) | collective-permute-done | bytes 524320 | tf_op jit(solution)/shard_map/ppermute | solution.py:22
  60.5 6.2 %collective-permute-done.7 = bf16[2,128,512]{2,1,0:T(8,128)(2,1)S(1)} collective-permute-done((bf16[2,128,512]{2,1,0:T(8,128)(2,1)S(1)}, bf16[2,128,512]{2,1,0:T(8,128)(2,1)S(1)}, u32[]{:S(2)}, u32[]{:S(2)}) %collective-permute-start.7) | collective-permute-done | bytes 262176 | tf_op jit(solution)/shard_map/ppermute | solution.py:28
  66.6 0.0 copy-done.3
  66.6 0.1 add_convert_fusion
  66.7 0.5 collective-permute-start.8
  67.2 5.9 %collective-permute-done.8 = bf16[2,128,512]{2,1,0:T(8,128)(2,1)S(1)} collective-permute-done((bf16[2,128,512]{2,1,0:T(8,128)(2,1)S(1)}, bf16[2,128,512]{2,1,0:T(8,128)(2,1)S(1)}, u32[]{:S(2)}, u32[]{:S(2)}) %collective-permute-start.8) | collective-permute-done | bytes 262176 | tf_op jit(solution)/shard_map/ppermute | solution.py:22
  73.1 0.7 fusion.5
  73.8 0.8 %copy.21 = bf16[1,128,2048]{2,1,0:T(8,128)(2,1)} copy(bf16[1,128,2048]{2,1,0:T(8,128)(2,1)S(1)} %collective-permute-done.5) | data formatting | bytes 1048576
  (7 shorter events, 0.0 us)
Async XLA Ops:
  0.6 1.0 %copy-start.7 = (bf16[1,128,512]{2,1,0:T(8,128)(2,1)S(1)}, bf16[1,128,512]{2,1,0:T(8,128)(2,1)}, u32[]{:S(2)}) copy-start(bf16[1,128,512]{2,1,0:T(8,128)(2,1)} %param.8) | copy-start | bytes 393220
  1.6 17.9 %copy-start = (bf16[2,128,512]{2,1,0:T(8,128)(2,1)}, bf16[2,128,512]{2,1,0:T(8,128)(2,1)S(1)}, u32[]{:S(2)}) copy-start(bf16[2,128,512]{2,1,0:T(8,128)(2,1)S(1)} %constant_dynamic-update-slice_fusion.refs_0_) | copy-start | bytes 786436
  1.6 11.6 %collective-permute-start = (bf16[2,128,512]{2,1,0:T(8,128)(2,1)S(1)}, bf16[2,128,512]{2,1,0:T(8,128)(2,1)S(1)}, u32[]{:S(2)}, u32[]{:S(2)}) collective-permute-start(bf16[2,128,512]{2,1,0:T(8,128)(2,1)S(1)} %constant_dynamic-update-slice_fusion.refs_0_), channel_id=1, source_target_pairs={{0,4},{4,8},{8,12},{1,5},{5,9},{9,13},{2,6},{6,10},{10,14},{3,7},{... | collective-permute-start | bytes 786440 | tf_op jit(solution)/shard_map/ppermute | solution.py:28
  6.6 12.9 %collective-permute-start.2 = (bf16[2,128,512]{2,1,0:T(8,128)(2,1)S(1)}, bf16[2,128,512]{2,1,0:T(8,128)(2,1)S(1)}, u32[]{:S(2)}, u32[]{:S(2)}) collective-permute-start(bf16[2,128,512]{2,1,0:T(8,128)(2,1)S(1)} %constant_dynamic-update-slice_fusion.refs_0_), channel_id=1, source_target_pairs={{0,12},{1,13},{2,14},{3,15},{16,28},{17,29},{18,30},{19,31}} | collective-permute-start | bytes 786440 | tf_op jit(solution)/shard_map/ppermute | solution.py:28
  10.3 0.7 copy-start.9
  11.1 6.5 %copy-start.8 = (s32[1,2,16,8]{2,3,1,0:T(8,128)S(1)}, s32[1,2,16,8]{2,3,1,0:T(8,128)}, u32[]{:S(2)}) copy-start(s32[1,2,16,8]{2,3,1,0:T(8,128)} %param.10) | copy-start | bytes 3076
  13.3 6.2 %copy-start.1 = (bf16[2,128,512]{2,1,0:T(8,128)(2,1)}, bf16[2,128,512]{2,1,0:T(8,128)(2,1)S(1)}, u32[]{:S(2)}) copy-start(bf16[2,128,512]{2,1,0:T(8,128)(2,1)S(1)} %collective-permute-done.refs_1_) | copy-start | bytes 786436
  13.3 10.1 %collective-permute-start.1 = (bf16[2,128,512]{2,1,0:T(8,128)(2,1)S(1)}, bf16[2,128,512]{2,1,0:T(8,128)(2,1)S(1)}, u32[]{:S(2)}, u32[]{:S(2)}) collective-permute-start(bf16[2,128,512]{2,1,0:T(8,128)(2,1)S(1)} %collective-permute-done.refs_1_), channel_id=1, source_target_pairs={{0,4},{4,8},{8,12},{1,5},{5,9},{9,13},{2,6},{6,10},{10,14},{3,7},{... | collective-permute-start | bytes 786440 | tf_op jit(solution)/shard_map/ppermute | solution.py:28
  19.5 3.9 %copy-start.2 = (bf16[2,128,512]{2,1,0:T(8,128)(2,1)}, bf16[2,128,512]{2,1,0:T(8,128)(2,1)S(1)}, u32[]{:S(2)}) copy-start(bf16[2,128,512]{2,1,0:T(8,128)(2,1)S(1)} %collective-permute-done.2.refs_3_) | copy-start | bytes 786436
  23.4 0.7 copy-start.4
  29.9 13.0 %collective-permute-start.3 = (bf16[1,128,2048]{2,1,0:T(8,128)(2,1)}, bf16[1,128,2048]{2,1,0:T(8,128)(2,1)S(1)}, u32[]{:S(2)}, u32[]{:S(2)}) collective-permute-start(bf16[1,128,2048]{2,1,0:T(8,128)(2,1)} %bitcast.28), channel_id=1, source_target_pairs={{0,16},{16,0},{1,17},{17,1},{2,18},{18,2},{3,19},{19,3},{4,20},{20... | collective-permute-start | bytes 1572872 | tf_op jit(solution)/shard_map/ppermute | solution.py:22
  37.8 9.9 %copy-start.6 = (bf16[2,128,512]{2,1,0:T(8,128)(2,1)S(1)}, bf16[2,128,512]{2,1,0:T(8,128)(2,1)}, u32[]{:S(2)}) copy-start(bf16[2,128,512]{2,1,0:T(8,128)(2,1)} %get-tuple-element.23) | copy-start | bytes 786436
  37.8 9.9 %collective-permute-start.4 = (bf16[2,128,512]{2,1,0:T(8,128)(2,1)}, bf16[2,128,512]{2,1,0:T(8,128)(2,1)S(1)}, u32[]{:S(2)}, u32[]{:S(2)}) collective-permute-start(bf16[2,128,512]{2,1,0:T(8,128)(2,1)} %get-tuple-element.19), channel_id=1, source_target_pairs={{4,0},{8,4},{12,8},{5,1},{9,5},{13,9},{6,2},{10,6},{14,10},{7,3},{... | collective-permute-start | bytes 786440 | tf_op jit(solution)/shard_map/ppermute | solution.py:28
  43.7 5.4 %copy-start.10 = (bf16[128,2048]{1,0:T(8,128)(2,1)S(1)}, bf16[128,2048]{1,0:T(8,128)(2,1)}, u32[]{:S(2)}) copy-start(bf16[128,2048]{1,0:T(8,128)(2,1)} %get-tuple-element.21) | copy-start | bytes 1572868
  47.7 8.6 %copy-start.5 = (bf16[2,128,512]{2,1,0:T(8,128)(2,1)S(1)}, bf16[2,128,512]{2,1,0:T(8,128)(2,1)}, u32[]{:S(2)}) copy-start(bf16[2,128,512]{2,1,0:T(8,128)(2,1)} %get-tuple-element.22) | copy-start | bytes 786436
  47.8 8.5 %collective-permute-start.6 = (bf16[2,128,512]{2,1,0:T(8,128)(2,1)S(1)}, bf16[2,128,512]{2,1,0:T(8,128)(2,1)S(1)}, u32[]{:S(2)}, u32[]{:S(2)}) collective-permute-start(bf16[2,128,512]{2,1,0:T(8,128)(2,1)S(1)} %add_convert_fusion.2), channel_id=1, source_target_pairs={{4,0},{8,4},{12,8},{5,1},{9,5},{13,9},{6,2},{10,6},{14,10},{7,3},{... | collective-permute-start | bytes 786440 | tf_op jit(solution)/shard_map/ppermute | solution.py:28
  49.1 11.3 %collective-permute-start.5 = (bf16[1,128,2048]{2,1,0:T(8,128)(2,1)S(1)}, bf16[1,128,2048]{2,1,0:T(8,128)(2,1)S(1)}, u32[]{:S(2)}, u32[]{:S(2)}) collective-permute-start(bf16[1,128,2048]{2,1,0:T(8,128)(2,1)S(1)} %bitcast.27), channel_id=1, source_target_pairs={{0,16},{16,0},{1,17},{17,1},{2,18},{18,2},{3,19},{19,3},{4,20},{20... | collective-permute-start | bytes 1572872 | tf_op jit(solution)/shard_map/ppermute | solution.py:22
  56.3 10.3 %copy-start.3 = (bf16[2,128,512]{2,1,0:T(8,128)(2,1)S(1)}, bf16[2,128,512]{2,1,0:T(8,128)(2,1)}, u32[]{:S(2)}) copy-start(bf16[2,128,512]{2,1,0:T(8,128)(2,1)} %get-tuple-element.26) | copy-start | bytes 786436
  56.4 10.2 %collective-permute-start.7 = (bf16[2,128,512]{2,1,0:T(8,128)(2,1)S(1)}, bf16[2,128,512]{2,1,0:T(8,128)(2,1)S(1)}, u32[]{:S(2)}, u32[]{:S(2)}) collective-permute-start(bf16[2,128,512]{2,1,0:T(8,128)(2,1)S(1)} %add_convert_fusion.1), channel_id=1, source_target_pairs={{4,0},{8,4},{12,8},{5,1},{9,5},{13,9},{6,2},{10,6},{14,10},{7,3},{... | collective-permute-start | bytes 786440 | tf_op jit(solution)/shard_map/ppermute | solution.py:28
  66.7 6.4 %collective-permute-start.8 = (bf16[2,128,512]{2,1,0:T(8,128)(2,1)S(1)}, bf16[2,128,512]{2,1,0:T(8,128)(2,1)S(1)}, u32[]{:S(2)}, u32[]{:S(2)}) collective-permute-start(bf16[2,128,512]{2,1,0:T(8,128)(2,1)S(1)} %add_convert_fusion), channel_id=1, source_target_pairs={{0,16},{16,0},{1,17},{17,1},{2,18},{18,2},{3,19},{19,3},{4,20},{20... | collective-permute-start | bytes 786440 | tf_op jit(solution)/shard_map/ppermute | solution.py:22

commit v11 on v10

--- a/solution.py
+++ b/solution.py
@@ -82,12 +82,14 @@
     )
 
 
-def forward_kernel(piece_count, group_size, query_ref, grad_ref, mask_ref, *refs):
+def attention_kernel(piece_count, group_size, query_ref, grad_ref, mask_ref, *refs):
     kv_refs = refs[:piece_count]
-    out_ref, lse_ref, delta_ref = refs[piece_count:]
+    out_ref, dq_ref = refs[piece_count : piece_count + 2]
+    dkv_refs = refs[piece_count + 2 :]
     tok_rows = query_ref.shape[0]
     score_scale = HD ** (-0.5)
     query_rows = stacked(query_ref, group_size)
+    grad_rows = stacked(grad_ref, group_size)
     all_keys = jnp.concatenate([ref[0] for ref in kv_refs], axis=0)
     all_values = jnp.concatenate([ref[1] for ref in kv_refs], axis=0)
     raw = dot_nt(query_rows, all_keys) * score_scale
@@ -99,29 +101,13 @@
     attended = (accumulated / row_total).astype(out_ref.dtype)
     for head in range(group_size):
         out_ref[:, head * HD : (head + 1) * HD] = attended[head * tok_rows : (head + 1) * tok_rows]
-    lse_ref[0] = row_high + jnp.log(row_total)
-    grad_rows = stacked(grad_ref, group_size)
-    delta_ref[0] = jnp.sum(
-        grad_rows.astype(jnp.float32) * attended.astype(jnp.float32), axis=1, keepdims=True
-    )
-
-
-def backward_kernel(piece_count, group_size, query_ref, grad_ref, mask_ref, lse_ref, delta_ref, *refs):
-    kv_refs = refs[:piece_count]
-    dq_ref = refs[piece_count]
-    dkv_refs = refs[piece_count + 1 :]
-    tok_rows = query_ref.shape[0]
-    score_scale = HD ** (-0.5)
-    query_rows = stacked(query_ref, group_size)
-    grad_rows = stacked(grad_ref, group_size)
-    all_keys = jnp.concatenate([ref[0] for ref in kv_refs], axis=0)
-    all_values = jnp.concatenate([ref[1] for ref in kv_refs], axis=0)
-    raw = dot_nt(query_rows, all_keys) * score_scale
-    masked = jnp.where(all_allowed(mask_ref, piece_count, group_size, tok_rows), raw, NEG_FILL)
-    row_probs = jnp.exp(masked - lse_ref[0])
+    log_total = row_high + jnp.log(row_total)
+    delta = jnp.sum(grad_rows.astype(jnp.float32) * attended.astype(jnp.float32), axis=1, keepdims=True)
+
+    row_probs = jnp.exp(masked - log_total)
     value_terms = dot_tn(row_probs.astype(jnp.bfloat16), grad_rows)
     prob_grads = dot_nt(grad_rows, all_values)
-    score_grads = (row_probs * (prob_grads - delta_ref[0])).astype(jnp.bfloat16)
+    score_grads = (row_probs * (prob_grads - delta)).astype(jnp.bfloat16)
     query_grad = jnp.dot(score_grads, all_keys, preferred_element_type=jnp.float32)
     key_terms = dot_tn(score_grads, query_rows) * score_scale
     for shift, ref in enumerate(dkv_refs):
@@ -133,70 +119,33 @@
         dq_ref[:, head * HD : (head + 1) * HD] = query_grad[head * tok_rows : (head + 1) * tok_rows]
 
 
-def attention_forward(query_rows, grad_rows, pieces, masks):
+def attention(query_rows, grad_rows, pieces, masks):
     tok_rows, query_width = query_rows.shape
     piece_count = len(pieces)
     group_size = H // KVH
     group_width = group_size * HD
-    rows = group_size * tok_rows
-    flops = 4 * tok_rows * tok_rows * HD * H * piece_count
+    flops = 12 * tok_rows * tok_rows * HD * H * piece_count
     piece_block = pl.BlockSpec((2, tok_rows, HD), lambda g: (0, 0, g))
-    return pl.pallas_call(
-        functools.partial(forward_kernel, piece_count, group_size),
+    group_block = pl.BlockSpec((tok_rows, group_width), lambda g: (0, g))
+    outs = pl.pallas_call(
+        functools.partial(attention_kernel, piece_count, group_size),
         grid=(KVH,),
         in_specs=[
-            pl.BlockSpec((tok_rows, group_width), lambda g: (0, g)),
-            pl.BlockSpec((tok_rows, group_width), lambda g: (0, g)),
+            group_block,
+            group_block,
             pl.BlockSpec((piece_count, group_size) + masks.shape[2:], lambda g: (0, g, 0, 0)),
         ]
         + [piece_block] * piece_count,
-        out_specs=[
-            pl.BlockSpec((tok_rows, group_width), lambda g: (0, g)),
-            pl.BlockSpec((1, rows, 1), lambda g: (g, 0, 0)),
-            pl.BlockSpec((1, rows, 1), lambda g: (g, 0, 0)),
-        ],
-        out_shape=[
-            jax.ShapeDtypeStruct((tok_rows, query_width), jnp.bfloat16),
-            jax.ShapeDtypeStruct((KVH, rows, 1), jnp.float32),
-            jax.ShapeDtypeStruct((KVH, rows, 1), jnp.float32),
-        ],
-        cost_estimate=pl.CostEstimate(
-            flops=flops,
-            transcendentals=tok_rows * tok_rows * H * piece_count,
-            bytes_accessed=3 * query_rows.size * 2 + piece_count * pieces[0].size * 2,
-        ),
-    )(query_rows, grad_rows, masks, *pieces)
-
-
-def attention_backward(query_rows, grad_rows, pieces, masks, log_total, delta):
-    tok_rows, query_width = query_rows.shape
-    piece_count = len(pieces)
-    group_size = H // KVH
-    group_width = group_size * HD
-    rows = group_size * tok_rows
-    flops = 10 * tok_rows * tok_rows * HD * H * piece_count
-    piece_block = pl.BlockSpec((2, tok_rows, HD), lambda g: (0, 0, g))
-    outs = pl.pallas_call(
-        functools.partial(backward_kernel, piece_count, group_size),
-        grid=(KVH,),
-        in_specs=[
-            pl.BlockSpec((tok_rows, group_width), lambda g: (0, g)),
-            pl.BlockSpec((tok_rows, group_width), lambda g: (0, g)),
-            pl.BlockSpec((piece_count, group_size) + masks.shape[2:], lambda g: (0, g, 0, 0)),
-            pl.BlockSpec((1, rows, 1), lambda g: (g, 0, 0)),
-            pl.BlockSpec((1, rows, 1), lambda g: (g, 0, 0)),
-        ]
-        + [piece_block] * piece_count,
-        out_specs=[pl.BlockSpec((tok_rows, group_width), lambda g: (0, g))] + [piece_block] * piece_count,
-        out_shape=[jax.ShapeDtypeStruct((tok_rows, query_width), jnp.bfloat16)]
+        out_specs=[group_block, group_block] + [piece_block] * piece_count,
+        out_shape=[jax.ShapeDtypeStruct((tok_rows, query_width), jnp.bfloat16)] * 2
         + [jax.ShapeDtypeStruct(pieces[0].shape, jnp.bfloat16)] * piece_count,
         cost_estimate=pl.CostEstimate(
             flops=flops,
-            transcendentals=tok_rows * tok_rows * H * piece_count,
-            bytes_accessed=2 * query_rows.size * 2 + 2 * piece_count * pieces[0].size * 2,
+            transcendentals=2 * tok_rows * tok_rows * H * piece_count,
+            bytes_accessed=4 * query_rows.size * 2 + 2 * piece_count * pieces[0].size * 2,
         ),
-    )(query_rows, grad_rows, masks, log_total, delta, *pieces)
-    return outs[0], outs[1:]
+    )(query_rows, grad_rows, masks, *pieces)
+    return outs[0], outs[1], outs[2:]
 
 
 def local(query, keys, values, grad_out, random_blocks, global_ids):
@@ -214,17 +163,15 @@
         pieces = [own]
         for shift in range(1, ctx_count):
             pieces.append(shifted_open(pieces[-1], "ctx", 1))
-    attended, log_total, delta = attention_forward(query[0], grad_out[0], pieces, masks)
+    attended, query_grad, kv_terms = attention(query[0], grad_out[0], pieces, masks)
     next_input = passed_along(attended[None], "pipe", 1)
-
-    query_grad, kv_terms = attention_backward(query[0], grad_out[0], pieces, masks, log_total, delta)
     grad_query = passed_along(query_grad[None], "pipe", -1)
 
     carried = None
     for step in range(1, ctx_count):
         part = kv_terms[ctx_count - step].astype(jnp.float32)
         if carried is not None:
-            if step == 2:
+            if step == ctx_count - 1:
                 next_input = jnp.where(ctx_index < 0, jnp.zeros_like(next_input), next_input)
                 next_input, carried = lax.optimization_barrier((next_input, carried))
             part = part + carried.astype(jnp.float32)

time: 75.7 us -> 74 us (0.978); the launches traced: 74.6 us -> 73.7 us
  Pallas kernels: 12.2 us -> 7.78 us
  waiting for transfers between devices: 34.7 us -> 37.2 us
  other arithmetic: 1.77 us -> 2.72 us
    ppermute x6, waiting for transfers between devices: 22.4 us -> 27 us  [shifted_open(): return lax.ppermute(value, axis, pairs)]
    pallas_call x2 -> x1, Pallas kernels: 12.2 us -> 7.78 us  [attention(): pl.pallas_call(functools.partial(attention_kernel, piece_count, group_siz...]
    ppermute x3, waiting for transfers between devices: 12.3 us -> 10.1 us  [passed_along(): return lax.ppermute(value, axis, pairs)]
    convert_element_type x2, other arithmetic: 0.13 us -> 1.08 us  [local(): carried = shifted_open(part.astype(jnp.bfloat16), 'ctx', -1)]
    unnamed x25 -> x21, local copies, waits for them, and re-layouts: 3.14 us -> 3.15 us
  transfers between devices with their start and end apart: 9 -> 9, of which waited for: 8 -> 8; matrix products, arithmetic and copies ran while one was open for 5% -> 6% of each run, Pallas kernels for 9% -> 0%
where the time goes in v11:
time: 74 us; the launch traced here: 73.7 us
  waiting for transfers between devices  37.2 us (50%)
  starting transfers between devices  19.4 us (26%)
  Pallas kernels  7.78 us (11%)
  local copies, waits for them, and re-layouts  5.85 us (8%)
  other arithmetic  2.72 us (4%)
  between operations  0.82 us (1%)
    ppermute x6, waiting for transfers between devices, shifted_open(): return lax.ppermute(value, axis, pairs)  27 us
    ppermute x6, starting transfers between devices, shifted_open(): return lax.ppermute(value, axis, pairs)  16.7 us
    ppermute x3, waiting for transfers between devices, passed_along(): return lax.ppermute(value, axis, pairs)  10.1 us
    pallas_call x1, Pallas kernels, attention(): pl.pallas_call(functools.partial(attention_kernel, piece_count, group_siz...  7.78 us
    unnamed x21, local copies, waits for them, and re-layouts  3.15 us
    ppermute x3, starting transfers between devices, passed_along(): return lax.ppermute(value, axis, pairs)  2.72 us
  transfers between devices with their start and end apart: 9, of which 8 were waited for; matrix products, arithmetic and copies ran while one was open for 6% of the time, Pallas kernels for 0%

profile of v11, /device:TPU:0, one launch (start us, length us, event | category | flops | bytes accessed | tf_op | source)
XLA Modules:
  0.0 73.7 jit_solution(17321986763192374913)
XLA Ops:
  0.6 0.0 copy-start.2
  0.6 0.9 %constant_dynamic-update-slice_fusion.1 = bf16[2,128,512]{2,1,0:T(8,128)(2,1)S(1)} fusion(bf16[1,128,512]{2,1,0:T(8,128)(2,1)} %param.7), kind=kLoop, calls=%fused_computation.13 | loop fusion | bytes 262144
  1.6 0.0 copy-done.2
  1.6 0.0 copy-start.3
  1.6 7.0 %collective-permute-start.2 = (bf16[2,128,512]{2,1,0:T(8,128)(2,1)S(1)}, bf16[2,128,512]{2,1,0:T(8,128)(2,1)S(1)}, u32[]{:S(2)}, u32[]{:S(2)}) collective-permute-start(bf16[2,128,512]{2,1,0:T(8,128)(2,1)S(1)} %constant_dynamic-update-slice_fusion.refs_0_), channel_id=1, source_target_pairs={{0,12},{1,13},{2,14},{3,15},{16,28},{17,29},{18,30},{19,31}} | collective-permute-start | bytes 786440 | tf_op jit(solution)/shard_map/ppermute | solution.py:28
  8.6 1.3 %collective-permute-start = (bf16[2,128,512]{2,1,0:T(8,128)(2,1)S(1)}, bf16[2,128,512]{2,1,0:T(8,128)(2,1)S(1)}, u32[]{:S(2)}, u32[]{:S(2)}) collective-permute-start(bf16[2,128,512]{2,1,0:T(8,128)(2,1)S(1)} %constant_dynamic-update-slice_fusion.refs_0_), channel_id=1, source_target_pairs={{0,4},{4,8},{8,12},{1,5},{5,9},{9,13},{2,6},{6,10},{10,14},{3,7},{... | collective-permute-start | bytes 786440 | tf_op jit(solution)/shard_map/ppermute | solution.py:28
  9.9 0.1 compare_and_fusion
  10.0 0.1 iota_add_fusion
  10.1 0.1 min.12
  10.2 0.1 copy.14
  10.3 0.0 copy-start.5
  10.3 0.7 copy-done.5
  10.9 0.2 compare_reduce_fusion.1
  11.1 0.0 copy-start.4
  11.1 0.2 compare_reduce_fusion
  11.4 0.1 copy.15
  11.5 0.1 or_or_fusion
  11.5 8.3 %collective-permute-done.refs_1_ = bf16[2,128,512]{2,1,0:T(8,128)(2,1)S(1)} collective-permute-done((bf16[2,128,512]{2,1,0:T(8,128)(2,1)S(1)}, bf16[2,128,512]{2,1,0:T(8,128)(2,1)S(1)}, u32[]{:S(2)}, u32[]{:S(2)}) %collective-permute-start) | collective-permute-done | bytes 262176 | tf_op jit(solution)/shard_map/ppermute | solution.py:28
  19.8 0.0 copy-start.7
  19.8 4.4 %collective-permute-start.1 = (bf16[2,128,512]{2,1,0:T(8,128)(2,1)S(1)}, bf16[2,128,512]{2,1,0:T(8,128)(2,1)S(1)}, u32[]{:S(2)}, u32[]{:S(2)}) collective-permute-start(bf16[2,128,512]{2,1,0:T(8,128)(2,1)S(1)} %collective-permute-done.refs_1_), channel_id=1, source_target_pairs={{0,4},{4,8},{8,12},{1,5},{5,9},{9,13},{2,6},{6,10},{10,14},{3,7},{... | collective-permute-start | bytes 786440 | tf_op jit(solution)/shard_map/ppermute | solution.py:28
  24.2 0.0 copy-done.4
  24.2 0.6 gather_fusion
  24.8 0.1 fusion.1
  24.9 0.1 copy.16
  25.0 0.2 broadcast_in_dim.35
  25.2 0.8 %convert_element_type.35.mask_ref = f32[4,16,2,128]{3,2,1,0:T(2,128)} reshape(f32[4,16,2,2,64]{4,3,2,1,0:T(2,128)S(1)} %broadcast_in_dim.35) | data formatting | bytes 131072 | tf_op jit(solution)/shard_map/convert_element_type | solution.py:48
  26.0 0.0 copy-done.3
  26.0 0.0 copy-done.7
  26.0 0.0 collective-permute-done.2.refs_3_
  26.0 0.0 copy-start.6
  26.1 2.9 %collective-permute-done.1.refs_2_ = bf16[2,128,512]{2,1,0:T(8,128)(2,1)S(1)} collective-permute-done((bf16[2,128,512]{2,1,0:T(8,128)(2,1)S(1)}, bf16[2,128,512]{2,1,0:T(8,128)(2,1)S(1)}, u32[]{:S(2)}, u32[]{:S(2)}) %collective-permute-start.1) | collective-permute-done | bytes 262176 | tf_op jit(solution)/shard_map/ppermute | solution.py:28
  28.9 0.0 copy-start.8
  28.9 0.0 copy-done.6
  28.9 0.7 copy-done.8
  29.6 7.8 %shard_map.93 = (bf16[128,2048]{1,0:T(8,128)(2,1)}, bf16[128,2048]{1,0:T(8,128)(2,1)}, bf16[2,128,512]{2,1,0:T(8,128)(2,1)}, bf16[2,128,512]{2,1,0:T(8,128)(2,1)...) custom-call(bf16[128,2048]{1,0:T(8,128)(2,1)} %bitcast.23, bf16[128,2048]{1,0:T(8,128)(2,1)} %bitcast.24, ...), custom_call_target="tpu_custom_call" | custom-call | flops 1610612736 | bytes 4194304 | tf_op jit(solution)/shard_map/pallas_call | solution.py:130
  37.4 1.6 %collective-permute-start.3 = (bf16[1,128,2048]{2,1,0:T(8,128)(2,1)}, bf16[1,128,2048]{2,1,0:T(8,128)(2,1)S(1)}, u32[]{:S(2)}, u32[]{:S(2)}) collective-permute-start(bf16[1,128,2048]{2,1,0:T(8,128)(2,1)} %bitcast.26), channel_id=1, source_target_pairs={{0,16},{16,0},{1,17},{17,1},{2,18},{18,2},{3,19},{19,3},{4,20},{20... | collective-permute-start | bytes 1572872 | tf_op jit(solution)/shard_map/ppermute | solution.py:22
  39.0 1.3 %collective-permute-start.4 = (bf16[2,128,512]{2,1,0:T(8,128)(2,1)}, bf16[2,128,512]{2,1,0:T(8,128)(2,1)S(1)}, u32[]{:S(2)}, u32[]{:S(2)}) collective-permute-start(bf16[2,128,512]{2,1,0:T(8,128)(2,1)} %get-tuple-element.16), channel_id=1, source_target_pairs={{4,0},{8,4},{12,8},{5,1},{9,5},{13,9},{6,2},{10,6},{14,10},{7,3},{... | collective-permute-start | bytes 786440 | tf_op jit(solution)/shard_map/ppermute | solution.py:28
  40.3 0.6 collective-permute-start.6
  40.9 7.1 %collective-permute-done.4 = bf16[2,128,512]{2,1,0:T(8,128)(2,1)S(1)} collective-permute-done((bf16[2,128,512]{2,1,0:T(8,128)(2,1)}, bf16[2,128,512]{2,1,0:T(8,128)(2,1)S(1)}, u32[]{:S(2)}, u32[]{:S(2)}) %collective-permute-start.4) | collective-permute-done | bytes 262176 | tf_op jit(solution)/shard_map/ppermute | solution.py:28
  47.9 1.0 %add_convert_fusion.2 = bf16[2,128,512]{2,1,0:T(8,128)(2,1)S(1)} fusion(bf16[2,128,512]{2,1,0:T(8,128)(2,1)S(1)} %collective-permute-done.4, bf16[2,128,512]{2,1,0:T(8,128)(2,1)} %get-tuple-element.15), kind=kLoop, calls=%fused_computation.3 | loop fusion | flops 524288 | bytes 786432 | tf_op jit(solution)/shard_map/convert_element_type | solution.py:178
  48.9 0.0 copy-start.1
  49.0 1.4 %collective-permute-start.5 = (bf16[2,128,512]{2,1,0:T(8,128)(2,1)S(1)}, bf16[2,128,512]{2,1,0:T(8,128)(2,1)S(1)}, u32[]{:S(2)}, u32[]{:S(2)}) collective-permute-start(bf16[2,128,512]{2,1,0:T(8,128)(2,1)S(1)} %add_convert_fusion.2), channel_id=1, source_target_pairs={{4,0},{8,4},{12,8},{5,1},{9,5},{13,9},{6,2},{10,6},{14,10},{7,3},{... | collective-permute-start | bytes 786440 | tf_op jit(solution)/shard_map/ppermute | solution.py:28
  50.4 2.2 %collective-permute-done.3 = bf16[1,128,2048]{2,1,0:T(8,128)(2,1)S(1)} collective-permute-done((bf16[1,128,2048]{2,1,0:T(8,128)(2,1)}, bf16[1,128,2048]{2,1,0:T(8,128)(2,1)S(1)}, u32[]{:S(2)}, u32[]{:S(2)}) %collective-permute-start.3) | collective-permute-done | bytes 524320 | tf_op jit(solution)/shard_map/ppermute | solution.py:22
  52.5 0.8 %broadcast_select_fusion = bf16[1,128,2048]{2,1,0:T(8,128)(2,1)} fusion(bf16[1,128,2048]{2,1,0:T(8,128)(2,1)S(1)} %collective-permute-done.3, pred[]{:T(512)S(6)} %lt.19), kind=kLoop, calls=%fused_computation.4 | loop fusion | flops 262144 | bytes 1048577 | tf_op jit(solution)/shard_map/jit(_where)/select_n | solution.py:175
  53.4 4.0 %collective-permute-done.5 = bf16[2,128,512]{2,1,0:T(8,128)(2,1)S(1)} collective-permute-done((bf16[2,128,512]{2,1,0:T(8,128)(2,1)S(1)}, bf16[2,128,512]{2,1,0:T(8,128)(2,1)S(1)}, u32[]{:S(2)}, u32[]{:S(2)}) %collective-permute-start.5) | collective-permute-done | bytes 262176 | tf_op jit(solution)/shard_map/ppermute | solution.py:28
  57.4 0.0 copy-done.1
  57.4 0.0 copy-start
  57.4 0.1 add_convert_fusion.1
  57.4 1.3 %collective-permute-start.7 = (bf16[2,128,512]{2,1,0:T(8,128)(2,1)S(1)}, bf16[2,128,512]{2,1,0:T(8,128)(2,1)S(1)}, u32[]{:S(2)}, u32[]{:S(2)}) collective-permute-start(bf16[2,128,512]{2,1,0:T(8,128)(2,1)S(1)} %add_convert_fusion.1), channel_id=1, source_target_pairs={{4,0},{8,4},{12,8},{5,1},{9,5},{13,9},{6,2},{10,6},{14,10},{7,3},{... | collective-permute-start | bytes 786440 | tf_op jit(solution)/shard_map/ppermute | solution.py:28
  58.7 2.1 %collective-permute-done.6 = bf16[1,128,2048]{2,1,0:T(8,128)(2,1)S(1)} collective-permute-done((bf16[1,128,2048]{2,1,0:T(8,128)(2,1)}, bf16[1,128,2048]{2,1,0:T(8,128)(2,1)S(1)}, u32[]{:S(2)}, u32[]{:S(2)}) %collective-permute-start.6) | collective-permute-done | bytes 524320 | tf_op jit(solution)/shard_map/ppermute | solution.py:22
  60.8 4.9 %collective-permute-done.7 = bf16[2,128,512]{2,1,0:T(8,128)(2,1)S(1)} collective-permute-done((bf16[2,128,512]{2,1,0:T(8,128)(2,1)S(1)}, bf16[2,128,512]{2,1,0:T(8,128)(2,1)S(1)}, u32[]{:S(2)}, u32[]{:S(2)}) %collective-permute-start.7) | collective-permute-done | bytes 262176 | tf_op jit(solution)/shard_map/ppermute | solution.py:28
  65.7 0.0 copy-done
  65.7 0.1 add_convert_fusion
  65.8 0.6 collective-permute-start.8
  66.3 5.9 %collective-permute-done.8 = bf16[2,128,512]{2,1,0:T(8,128)(2,1)S(1)} collective-permute-done((bf16[2,128,512]{2,1,0:T(8,128)(2,1)S(1)}, bf16[2,128,512]{2,1,0:T(8,128)(2,1)S(1)}, u32[]{:S(2)}, u32[]{:S(2)}) %collective-permute-start.8) | collective-permute-done | bytes 262176 | tf_op jit(solution)/shard_map/ppermute | solution.py:22
  72.2 0.7 fusion.5
  72.9 0.8 %copy.21 = bf16[1,128,2048]{2,1,0:T(8,128)(2,1)} copy(bf16[1,128,2048]{2,1,0:T(8,128)(2,1)S(1)} %collective-permute-done.6) | data formatting | bytes 1048576
  (7 shorter events, 0.0 us)
Async XLA Ops:
  0.6 1.0 %copy-start.2 = (bf16[1,128,512]{2,1,0:T(8,128)(2,1)S(1)}, bf16[1,128,512]{2,1,0:T(8,128)(2,1)}, u32[]{:S(2)}) copy-start(bf16[1,128,512]{2,1,0:T(8,128)(2,1)} %param.8) | copy-start | bytes 393220
  1.6 24.4 %copy-start.3 = (bf16[2,128,512]{2,1,0:T(8,128)(2,1)}, bf16[2,128,512]{2,1,0:T(8,128)(2,1)S(1)}, u32[]{:S(2)}) copy-start(bf16[2,128,512]{2,1,0:T(8,128)(2,1)S(1)} %constant_dynamic-update-slice_fusion.refs_0_) | copy-start | bytes 786436
  1.6 24.4 %collective-permute-start.2 = (bf16[2,128,512]{2,1,0:T(8,128)(2,1)S(1)}, bf16[2,128,512]{2,1,0:T(8,128)(2,1)S(1)}, u32[]{:S(2)}, u32[]{:S(2)}) collective-permute-start(bf16[2,128,512]{2,1,0:T(8,128)(2,1)S(1)} %constant_dynamic-update-slice_fusion.refs_0_), channel_id=1, source_target_pairs={{0,12},{1,13},{2,14},{3,15},{16,28},{17,29},{18,30},{19,31}} | collective-permute-start | bytes 786440 | tf_op jit(solution)/shard_map/ppermute | solution.py:28
  8.6 11.2 %collective-permute-start = (bf16[2,128,512]{2,1,0:T(8,128)(2,1)S(1)}, bf16[2,128,512]{2,1,0:T(8,128)(2,1)S(1)}, u32[]{:S(2)}, u32[]{:S(2)}) collective-permute-start(bf16[2,128,512]{2,1,0:T(8,128)(2,1)S(1)} %constant_dynamic-update-slice_fusion.refs_0_), channel_id=1, source_target_pairs={{0,4},{4,8},{8,12},{1,5},{5,9},{9,13},{2,6},{6,10},{10,14},{3,7},{... | collective-permute-start | bytes 786440 | tf_op jit(solution)/shard_map/ppermute | solution.py:28
  10.3 0.7 copy-start.5
  11.1 13.1 %copy-start.4 = (s32[1,2,16,8]{2,3,1,0:T(8,128)S(1)}, s32[1,2,16,8]{2,3,1,0:T(8,128)}, u32[]{:S(2)}) copy-start(s32[1,2,16,8]{2,3,1,0:T(8,128)} %param.10) | copy-start | bytes 3076
  19.8 6.2 %copy-start.7 = (bf16[2,128,512]{2,1,0:T(8,128)(2,1)}, bf16[2,128,512]{2,1,0:T(8,128)(2,1)S(1)}, u32[]{:S(2)}) copy-start(bf16[2,128,512]{2,1,0:T(8,128)(2,1)S(1)} %collective-permute-done.refs_1_) | copy-start | bytes 786436
  19.8 9.1 %collective-permute-start.1 = (bf16[2,128,512]{2,1,0:T(8,128)(2,1)S(1)}, bf16[2,128,512]{2,1,0:T(8,128)(2,1)S(1)}, u32[]{:S(2)}, u32[]{:S(2)}) collective-permute-start(bf16[2,128,512]{2,1,0:T(8,128)(2,1)S(1)} %collective-permute-done.refs_1_), channel_id=1, source_target_pairs={{0,4},{4,8},{8,12},{1,5},{5,9},{9,13},{2,6},{6,10},{10,14},{3,7},{... | collective-permute-start | bytes 786440 | tf_op jit(solution)/shard_map/ppermute | solution.py:28
  26.0 2.9 %copy-start.6 = (bf16[2,128,512]{2,1,0:T(8,128)(2,1)}, bf16[2,128,512]{2,1,0:T(8,128)(2,1)S(1)}, u32[]{:S(2)}) copy-start(bf16[2,128,512]{2,1,0:T(8,128)(2,1)S(1)} %collective-permute-done.2.refs_3_) | copy-start | bytes 786436
  28.9 0.7 copy-start.8
  37.4 15.1 %collective-permute-start.3 = (bf16[1,128,2048]{2,1,0:T(8,128)(2,1)}, bf16[1,128,2048]{2,1,0:T(8,128)(2,1)S(1)}, u32[]{:S(2)}, u32[]{:S(2)}) collective-permute-start(bf16[1,128,2048]{2,1,0:T(8,128)(2,1)} %bitcast.26), channel_id=1, source_target_pairs={{0,16},{16,0},{1,17},{17,1},{2,18},{18,2},{3,19},{19,3},{4,20},{20... | collective-permute-start | bytes 1572872 | tf_op jit(solution)/shard_map/ppermute | solution.py:22
  39.0 8.9 %collective-permute-start.4 = (bf16[2,128,512]{2,1,0:T(8,128)(2,1)}, bf16[2,128,512]{2,1,0:T(8,128)(2,1)S(1)}, u32[]{:S(2)}, u32[]{:S(2)}) collective-permute-start(bf16[2,128,512]{2,1,0:T(8,128)(2,1)} %get-tuple-element.16), channel_id=1, source_target_pairs={{4,0},{8,4},{12,8},{5,1},{9,5},{13,9},{6,2},{10,6},{14,10},{7,3},{... | collective-permute-start | bytes 786440 | tf_op jit(solution)/shard_map/ppermute | solution.py:28
  40.3 20.6 %collective-permute-start.6 = (bf16[1,128,2048]{2,1,0:T(8,128)(2,1)}, bf16[1,128,2048]{2,1,0:T(8,128)(2,1)S(1)}, u32[]{:S(2)}, u32[]{:S(2)}) collective-permute-start(bf16[1,128,2048]{2,1,0:T(8,128)(2,1)} %bitcast.25), channel_id=1, source_target_pairs={{0,16},{16,0},{1,17},{17,1},{2,18},{18,2},{3,19},{19,3},{4,20},{20... | collective-permute-start | bytes 1572872 | tf_op jit(solution)/shard_map/ppermute | solution.py:22
  48.9 8.4 %copy-start.1 = (bf16[2,128,512]{2,1,0:T(8,128)(2,1)S(1)}, bf16[2,128,512]{2,1,0:T(8,128)(2,1)}, u32[]{:S(2)}) copy-start(bf16[2,128,512]{2,1,0:T(8,128)(2,1)} %get-tuple-element.19) | copy-start | bytes 786436
  49.0 8.4 %collective-permute-start.5 = (bf16[2,128,512]{2,1,0:T(8,128)(2,1)S(1)}, bf16[2,128,512]{2,1,0:T(8,128)(2,1)S(1)}, u32[]{:S(2)}, u32[]{:S(2)}) collective-permute-start(bf16[2,128,512]{2,1,0:T(8,128)(2,1)S(1)} %add_convert_fusion.2), channel_id=1, source_target_pairs={{4,0},{8,4},{12,8},{5,1},{9,5},{13,9},{6,2},{10,6},{14,10},{7,3},{... | collective-permute-start | bytes 786440 | tf_op jit(solution)/shard_map/ppermute | solution.py:28
  57.4 8.3 %copy-start = (bf16[2,128,512]{2,1,0:T(8,128)(2,1)S(1)}, bf16[2,128,512]{2,1,0:T(8,128)(2,1)}, u32[]{:S(2)}) copy-start(bf16[2,128,512]{2,1,0:T(8,128)(2,1)} %get-tuple-element.22) | copy-start | bytes 786436
  57.4 8.3 %collective-permute-start.7 = (bf16[2,128,512]{2,1,0:T(8,128)(2,1)S(1)}, bf16[2,128,512]{2,1,0:T(8,128)(2,1)S(1)}, u32[]{:S(2)}, u32[]{:S(2)}) collective-permute-start(bf16[2,128,512]{2,1,0:T(8,128)(2,1)S(1)} %add_convert_fusion.1), channel_id=1, source_target_pairs={{4,0},{8,4},{12,8},{5,1},{9,5},{13,9},{6,2},{10,6},{14,10},{7,3},{... | collective-permute-start | bytes 786440 | tf_op jit(solution)/shard_map/ppermute | solution.py:28
  65.8 6.4 %collective-permute-start.8 = (bf16[2,128,512]{2,1,0:T(8,128)(2,1)S(1)}, bf16[2,128,512]{2,1,0:T(8,128)(2,1)S(1)}, u32[]{:S(2)}, u32[]{:S(2)}) collective-permute-start(bf16[2,128,512]{2,1,0:T(8,128)(2,1)S(1)} %add_convert_fusion), channel_id=1, source_target_pairs={{0,16},{16,0},{1,17},{17,1},{2,18},{18,2},{3,19},{19,3},{4,20},{20... | collective-permute-start | bytes 786440 | tf_op jit(solution)/shard_map/ppermute | solution.py:22

commit v12 on v11

--- a/solution.py
+++ b/solution.py
@@ -178,6 +178,7 @@
         carried = shifted_open(part.astype(jnp.bfloat16), "ctx", -1)
     kv_sum = kv_terms[0].astype(jnp.float32)
     if carried is not None:
+        grad_query = jnp.where(ctx_index < 0, jnp.zeros_like(grad_query), grad_query)
         grad_query, carried = lax.optimization_barrier((grad_query, carried))
         kv_sum = kv_sum + carried.astype(jnp.float32)
     returned = passed_along(kv_sum.astype(jnp.bfloat16), "pipe", -1)

time: 74 us -> 73.4 us (level)
  waiting for transfers between devices: 37.2 us -> 36.3 us
  other arithmetic: 2.72 us -> 3.55 us
  local copies, waits for them, and re-layouts: 5.85 us -> 5.06 us
    select_n x0 -> x1, other arithmetic: none -> 0.83 us  [local(): jnp.where(ctx_index < 0, jnp.zeros_like(grad_query), grad_query)]
    unnamed x21 -> x20, local copies, waits for them, and re-layouts: 3.15 us -> 2.36 us
  transfers between devices with their start and end apart: 9 -> 9, of which waited for: 8 -> 8; matrix products, arithmetic and copies ran while one was open for 6% -> 7% of each run, Pallas kernels for 0% -> 0%
where the time goes in v12:
time: 73.4 us; the launch traced here: 73.1 us
  waiting for transfers between devices  36.3 us (49%)
  starting transfers between devices  19.5 us (27%)
  Pallas kernels  7.78 us (11%)
  local copies, waits for them, and re-layouts  5.06 us (7%)
  other arithmetic  3.55 us (5%)
  between operations  0.83 us (1%)
    ppermute x6, waiting for transfers between devices, shifted_open(): return lax.ppermute(value, axis, pairs)  26.3 us
    ppermute x6, starting transfers between devices, shifted_open(): return lax.ppermute(value, axis, pairs)  16.8 us
    ppermute x3, waiting for transfers between devices, passed_along(): return lax.ppermute(value, axis, pairs)  9.99 us
    pallas_call x1, Pallas kernels, attention(): pl.pallas_call(functools.partial(attention_kernel, piece_count, group_siz...  7.78 us
    ppermute x3, starting transfers between devices, passed_along(): return lax.ppermute(value, axis, pairs)  2.72 us
    unnamed x20, local copies, waits for them, and re-layouts  2.36 us
  transfers between devices with their start and end apart: 9, of which 8 were waited for; matrix products, arithmetic and copies ran while one was open for 7% of the time, Pallas kernels for 0%

profile of v12, /device:TPU:0, one launch (start us, length us, event | category | flops | bytes accessed | tf_op | source)
XLA Modules:
  0.0 73.1 jit_solution(7575086773306879197)
XLA Ops:
  0.6 0.0 copy-start.2
  0.6 0.9 %constant_dynamic-update-slice_fusion.1 = bf16[2,128,512]{2,1,0:T(8,128)(2,1)S(1)} fusion(bf16[1,128,512]{2,1,0:T(8,128)(2,1)} %param.7), kind=kLoop, calls=%fused_computation.14 | loop fusion | bytes 262144
  1.6 0.0 copy-done.2
  1.6 0.0 copy-start.3
  1.6 7.0 %collective-permute-start.2 = (bf16[2,128,512]{2,1,0:T(8,128)(2,1)S(1)}, bf16[2,128,512]{2,1,0:T(8,128)(2,1)S(1)}, u32[]{:S(2)}, u32[]{:S(2)}) collective-permute-start(bf16[2,128,512]{2,1,0:T(8,128)(2,1)S(1)} %constant_dynamic-update-slice_fusion.refs_0_), channel_id=1, source_target_pairs={{0,12},{1,13},{2,14},{3,15},{16,28},{17,29},{18,30},{19,31}} | collective-permute-start | bytes 786440 | tf_op jit(solution)/shard_map/ppermute | solution.py:28
  8.6 1.3 %collective-permute-start = (bf16[2,128,512]{2,1,0:T(8,128)(2,1)S(1)}, bf16[2,128,512]{2,1,0:T(8,128)(2,1)S(1)}, u32[]{:S(2)}, u32[]{:S(2)}) collective-permute-start(bf16[2,128,512]{2,1,0:T(8,128)(2,1)S(1)} %constant_dynamic-update-slice_fusion.refs_0_), channel_id=1, source_target_pairs={{0,4},{4,8},{8,12},{1,5},{5,9},{9,13},{2,6},{6,10},{10,14},{3,7},{... | collective-permute-start | bytes 786440 | tf_op jit(solution)/shard_map/ppermute | solution.py:28
  9.9 0.1 compare_and_fusion
  10.0 0.1 iota_add_fusion
  10.1 0.1 min.12
  10.2 0.1 copy.14
  10.3 0.0 copy-start.5
  10.3 0.7 copy-done.5
  10.9 0.2 compare_reduce_fusion.1
  11.1 0.0 copy-start.4
  11.1 0.2 compare_reduce_fusion
  11.4 0.1 copy.15
  11.5 0.1 or_or_fusion
  11.5 8.3 %collective-permute-done.refs_1_ = bf16[2,128,512]{2,1,0:T(8,128)(2,1)S(1)} collective-permute-done((bf16[2,128,512]{2,1,0:T(8,128)(2,1)S(1)}, bf16[2,128,512]{2,1,0:T(8,128)(2,1)S(1)}, u32[]{:S(2)}, u32[]{:S(2)}) %collective-permute-start) | collective-permute-done | bytes 262176 | tf_op jit(solution)/shard_map/ppermute | solution.py:28
  19.8 0.0 copy-start.7
  19.8 4.4 %collective-permute-start.1 = (bf16[2,128,512]{2,1,0:T(8,128)(2,1)S(1)}, bf16[2,128,512]{2,1,0:T(8,128)(2,1)S(1)}, u32[]{:S(2)}, u32[]{:S(2)}) collective-permute-start(bf16[2,128,512]{2,1,0:T(8,128)(2,1)S(1)} %collective-permute-done.refs_1_), channel_id=1, source_target_pairs={{0,4},{4,8},{8,12},{1,5},{5,9},{9,13},{2,6},{6,10},{10,14},{3,7},{... | collective-permute-start | bytes 786440 | tf_op jit(solution)/shard_map/ppermute | solution.py:28
  24.2 0.0 copy-done.4
  24.2 0.6 gather_fusion
  24.8 0.1 fusion.1
  24.9 0.1 copy.16
  25.0 0.2 broadcast_in_dim.18
  25.2 0.8 %convert_element_type.35.mask_ref = f32[4,16,2,128]{3,2,1,0:T(2,128)} reshape(f32[4,16,2,2,64]{4,3,2,1,0:T(2,128)S(1)} %broadcast_in_dim.18) | data formatting | bytes 131072 | tf_op jit(solution)/shard_map/convert_element_type | solution.py:48
  26.0 0.0 copy-done.3
  26.0 0.0 copy-done.7
  26.0 0.0 collective-permute-done.2.refs_3_
  26.0 0.0 copy-start.6
  26.1 2.9 %collective-permute-done.1.refs_2_ = bf16[2,128,512]{2,1,0:T(8,128)(2,1)S(1)} collective-permute-done((bf16[2,128,512]{2,1,0:T(8,128)(2,1)S(1)}, bf16[2,128,512]{2,1,0:T(8,128)(2,1)S(1)}, u32[]{:S(2)}, u32[]{:S(2)}) %collective-permute-start.1) | collective-permute-done | bytes 262176 | tf_op jit(solution)/shard_map/ppermute | solution.py:28
  28.9 0.0 copy-start.8
  28.9 0.0 copy-done.6
  28.9 0.7 copy-done.8
  29.6 7.8 %shard_map.93 = (bf16[128,2048]{1,0:T(8,128)(2,1)}, bf16[128,2048]{1,0:T(8,128)(2,1)}, bf16[2,128,512]{2,1,0:T(8,128)(2,1)}, bf16[2,128,512]{2,1,0:T(8,128)(2,1)...) custom-call(bf16[128,2048]{1,0:T(8,128)(2,1)} %bitcast.23, bf16[128,2048]{1,0:T(8,128)(2,1)} %bitcast.24, ...), custom_call_target="tpu_custom_call" | custom-call | flops 1610612736 | bytes 4194304 | tf_op jit(solution)/shard_map/pallas_call | solution.py:130
  37.4 1.6 %collective-permute-start.3 = (bf16[1,128,2048]{2,1,0:T(8,128)(2,1)}, bf16[1,128,2048]{2,1,0:T(8,128)(2,1)S(1)}, u32[]{:S(2)}, u32[]{:S(2)}) collective-permute-start(bf16[1,128,2048]{2,1,0:T(8,128)(2,1)} %bitcast.26), channel_id=1, source_target_pairs={{0,16},{16,0},{1,17},{17,1},{2,18},{18,2},{3,19},{19,3},{4,20},{20... | collective-permute-start | bytes 1572872 | tf_op jit(solution)/shard_map/ppermute | solution.py:22
  39.0 1.3 %collective-permute-start.4 = (bf16[2,128,512]{2,1,0:T(8,128)(2,1)}, bf16[2,128,512]{2,1,0:T(8,128)(2,1)S(1)}, u32[]{:S(2)}, u32[]{:S(2)}) collective-permute-start(bf16[2,128,512]{2,1,0:T(8,128)(2,1)} %get-tuple-element.16), channel_id=1, source_target_pairs={{4,0},{8,4},{12,8},{5,1},{9,5},{13,9},{6,2},{10,6},{14,10},{7,3},{... | collective-permute-start | bytes 786440 | tf_op jit(solution)/shard_map/ppermute | solution.py:28
  40.3 0.6 collective-permute-start.6
  40.9 7.1 %collective-permute-done.4 = bf16[2,128,512]{2,1,0:T(8,128)(2,1)S(1)} collective-permute-done((bf16[2,128,512]{2,1,0:T(8,128)(2,1)}, bf16[2,128,512]{2,1,0:T(8,128)(2,1)S(1)}, u32[]{:S(2)}, u32[]{:S(2)}) %collective-permute-start.4) | collective-permute-done | bytes 262176 | tf_op jit(solution)/shard_map/ppermute | solution.py:28
  47.9 1.0 %add_convert_fusion.2 = bf16[2,128,512]{2,1,0:T(8,128)(2,1)S(1)} fusion(bf16[2,128,512]{2,1,0:T(8,128)(2,1)S(1)} %collective-permute-done.4, bf16[2,128,512]{2,1,0:T(8,128)(2,1)} %get-tuple-element.15), kind=kLoop, calls=%fused_computation.3 | loop fusion | flops 524288 | bytes 786432 | tf_op jit(solution)/shard_map/convert_element_type | solution.py:178
  48.9 0.0 copy-start.1
  49.0 1.4 %collective-permute-start.5 = (bf16[2,128,512]{2,1,0:T(8,128)(2,1)S(1)}, bf16[2,128,512]{2,1,0:T(8,128)(2,1)S(1)}, u32[]{:S(2)}, u32[]{:S(2)}) collective-permute-start(bf16[2,128,512]{2,1,0:T(8,128)(2,1)S(1)} %add_convert_fusion.2), channel_id=1, source_target_pairs={{4,0},{8,4},{12,8},{5,1},{9,5},{13,9},{6,2},{10,6},{14,10},{7,3},{... | collective-permute-start | bytes 786440 | tf_op jit(solution)/shard_map/ppermute | solution.py:28
  50.4 2.2 %collective-permute-done.3 = bf16[1,128,2048]{2,1,0:T(8,128)(2,1)S(1)} collective-permute-done((bf16[1,128,2048]{2,1,0:T(8,128)(2,1)}, bf16[1,128,2048]{2,1,0:T(8,128)(2,1)S(1)}, u32[]{:S(2)}, u32[]{:S(2)}) %collective-permute-start.3) | collective-permute-done | bytes 524320 | tf_op jit(solution)/shard_map/ppermute | solution.py:22
  52.5 0.8 %broadcast_select_fusion.1 = bf16[1,128,2048]{2,1,0:T(8,128)(2,1)} fusion(bf16[1,128,2048]{2,1,0:T(8,128)(2,1)S(1)} %collective-permute-done.3, pred[]{:T(512)S(6)} %lt.20), kind=kLoop, calls=%fused_computation.5 | loop fusion | flops 262144 | bytes 1048577 | tf_op jit(solution)/shard_map/jit(_where)/select_n | solution.py:175
  53.4 4.0 %collective-permute-done.5 = bf16[2,128,512]{2,1,0:T(8,128)(2,1)S(1)} collective-permute-done((bf16[2,128,512]{2,1,0:T(8,128)(2,1)S(1)}, bf16[2,128,512]{2,1,0:T(8,128)(2,1)S(1)}, u32[]{:S(2)}, u32[]{:S(2)}) %collective-permute-start.5) | collective-permute-done | bytes 262176 | tf_op jit(solution)/shard_map/ppermute | solution.py:28
  57.4 0.0 copy-done.1
  57.4 0.1 add_convert_fusion.1
  57.4 0.0 copy-start
  57.4 1.4 %collective-permute-start.7 = (bf16[2,128,512]{2,1,0:T(8,128)(2,1)S(1)}, bf16[2,128,512]{2,1,0:T(8,128)(2,1)S(1)}, u32[]{:S(2)}, u32[]{:S(2)}) collective-permute-start(bf16[2,128,512]{2,1,0:T(8,128)(2,1)S(1)} %add_convert_fusion.1), channel_id=1, source_target_pairs={{4,0},{8,4},{12,8},{5,1},{9,5},{13,9},{6,2},{10,6},{14,10},{7,3},{... | collective-permute-start | bytes 786440 | tf_op jit(solution)/shard_map/ppermute | solution.py:28
  58.9 2.0 %collective-permute-done.6 = bf16[1,128,2048]{2,1,0:T(8,128)(2,1)S(1)} collective-permute-done((bf16[1,128,2048]{2,1,0:T(8,128)(2,1)}, bf16[1,128,2048]{2,1,0:T(8,128)(2,1)S(1)}, u32[]{:S(2)}, u32[]{:S(2)}) %collective-permute-start.6) | collective-permute-done | bytes 524320 | tf_op jit(solution)/shard_map/ppermute | solution.py:22
  60.8 0.8 %broadcast_select_fusion = bf16[1,128,2048]{2,1,0:T(8,128)(2,1)} fusion(bf16[1,128,2048]{2,1,0:T(8,128)(2,1)S(1)} %collective-permute-done.6, pred[]{:T(512)S(6)} %lt.20), kind=kLoop, calls=%fused_computation.4 | loop fusion | flops 262144 | bytes 1048577 | tf_op jit(solution)/shard_map/jit(_where)/select_n | solution.py:181
  61.7 4.2 %collective-permute-done.7 = bf16[2,128,512]{2,1,0:T(8,128)(2,1)S(1)} collective-permute-done((bf16[2,128,512]{2,1,0:T(8,128)(2,1)S(1)}, bf16[2,128,512]{2,1,0:T(8,128)(2,1)S(1)}, u32[]{:S(2)}, u32[]{:S(2)}) %collective-permute-start.7) | collective-permute-done | bytes 262176 | tf_op jit(solution)/shard_map/ppermute | solution.py:28
  65.8 0.0 copy-done
  65.8 0.1 add_convert_fusion
  65.9 0.6 collective-permute-start.8
  66.5 5.9 %collective-permute-done.8 = bf16[2,128,512]{2,1,0:T(8,128)(2,1)S(1)} collective-permute-done((bf16[2,128,512]{2,1,0:T(8,128)(2,1)S(1)}, bf16[2,128,512]{2,1,0:T(8,128)(2,1)S(1)}, u32[]{:S(2)}, u32[]{:S(2)}) %collective-permute-start.8) | collective-permute-done | bytes 262176 | tf_op jit(solution)/shard_map/ppermute | solution.py:22
  72.3 0.7 fusion.5
  (7 shorter events, 0.0 us)
Async XLA Ops:
  0.6 1.0 %copy-start.2 = (bf16[1,128,512]{2,1,0:T(8,128)(2,1)S(1)}, bf16[1,128,512]{2,1,0:T(8,128)(2,1)}, u32[]{:S(2)}) copy-start(bf16[1,128,512]{2,1,0:T(8,128)(2,1)} %param.8) | copy-start | bytes 393220
  1.6 24.4 %copy-start.3 = (bf16[2,128,512]{2,1,0:T(8,128)(2,1)}, bf16[2,128,512]{2,1,0:T(8,128)(2,1)S(1)}, u32[]{:S(2)}) copy-start(bf16[2,128,512]{2,1,0:T(8,128)(2,1)S(1)} %constant_dynamic-update-slice_fusion.refs_0_) | copy-start | bytes 786436
  1.6 24.4 %collective-permute-start.2 = (bf16[2,128,512]{2,1,0:T(8,128)(2,1)S(1)}, bf16[2,128,512]{2,1,0:T(8,128)(2,1)S(1)}, u32[]{:S(2)}, u32[]{:S(2)}) collective-permute-start(bf16[2,128,512]{2,1,0:T(8,128)(2,1)S(1)} %constant_dynamic-update-slice_fusion.refs_0_), channel_id=1, source_target_pairs={{0,12},{1,13},{2,14},{3,15},{16,28},{17,29},{18,30},{19,31}} | collective-permute-start | bytes 786440 | tf_op jit(solution)/shard_map/ppermute | solution.py:28
  8.6 11.2 %collective-permute-start = (bf16[2,128,512]{2,1,0:T(8,128)(2,1)S(1)}, bf16[2,128,512]{2,1,0:T(8,128)(2,1)S(1)}, u32[]{:S(2)}, u32[]{:S(2)}) collective-permute-start(bf16[2,128,512]{2,1,0:T(8,128)(2,1)S(1)} %constant_dynamic-update-slice_fusion.refs_0_), channel_id=1, source_target_pairs={{0,4},{4,8},{8,12},{1,5},{5,9},{9,13},{2,6},{6,10},{10,14},{3,7},{... | collective-permute-start | bytes 786440 | tf_op jit(solution)/shard_map/ppermute | solution.py:28
  10.3 0.7 copy-start.5
  11.1 13.1 %copy-start.4 = (s32[1,2,16,8]{2,3,1,0:T(8,128)S(1)}, s32[1,2,16,8]{2,3,1,0:T(8,128)}, u32[]{:S(2)}) copy-start(s32[1,2,16,8]{2,3,1,0:T(8,128)} %param.10) | copy-start | bytes 3076
  19.8 6.2 %copy-start.7 = (bf16[2,128,512]{2,1,0:T(8,128)(2,1)}, bf16[2,128,512]{2,1,0:T(8,128)(2,1)S(1)}, u32[]{:S(2)}) copy-start(bf16[2,128,512]{2,1,0:T(8,128)(2,1)S(1)} %collective-permute-done.refs_1_) | copy-start | bytes 786436
  19.8 9.1 %collective-permute-start.1 = (bf16[2,128,512]{2,1,0:T(8,128)(2,1)S(1)}, bf16[2,128,512]{2,1,0:T(8,128)(2,1)S(1)}, u32[]{:S(2)}, u32[]{:S(2)}) collective-permute-start(bf16[2,128,512]{2,1,0:T(8,128)(2,1)S(1)} %collective-permute-done.refs_1_), channel_id=1, source_target_pairs={{0,4},{4,8},{8,12},{1,5},{5,9},{9,13},{2,6},{6,10},{10,14},{3,7},{... | collective-permute-start | bytes 786440 | tf_op jit(solution)/shard_map/ppermute | solution.py:28
  26.0 2.9 %copy-start.6 = (bf16[2,128,512]{2,1,0:T(8,128)(2,1)}, bf16[2,128,512]{2,1,0:T(8,128)(2,1)S(1)}, u32[]{:S(2)}) copy-start(bf16[2,128,512]{2,1,0:T(8,128)(2,1)S(1)} %collective-permute-done.2.refs_3_) | copy-start | bytes 786436
  28.9 0.7 copy-start.8
  37.4 15.1 %collective-permute-start.3 = (bf16[1,128,2048]{2,1,0:T(8,128)(2,1)}, bf16[1,128,2048]{2,1,0:T(8,128)(2,1)S(1)}, u32[]{:S(2)}, u32[]{:S(2)}) collective-permute-start(bf16[1,128,2048]{2,1,0:T(8,128)(2,1)} %bitcast.26), channel_id=1, source_target_pairs={{0,16},{16,0},{1,17},{17,1},{2,18},{18,2},{3,19},{19,3},{4,20},{20... | collective-permute-start | bytes 1572872 | tf_op jit(solution)/shard_map/ppermute | solution.py:22
  39.0 8.9 %collective-permute-start.4 = (bf16[2,128,512]{2,1,0:T(8,128)(2,1)}, bf16[2,128,512]{2,1,0:T(8,128)(2,1)S(1)}, u32[]{:S(2)}, u32[]{:S(2)}) collective-permute-start(bf16[2,128,512]{2,1,0:T(8,128)(2,1)} %get-tuple-element.16), channel_id=1, source_target_pairs={{4,0},{8,4},{12,8},{5,1},{9,5},{13,9},{6,2},{10,6},{14,10},{7,3},{... | collective-permute-start | bytes 786440 | tf_op jit(solution)/shard_map/ppermute | solution.py:28
  40.3 20.6 %collective-permute-start.6 = (bf16[1,128,2048]{2,1,0:T(8,128)(2,1)}, bf16[1,128,2048]{2,1,0:T(8,128)(2,1)S(1)}, u32[]{:S(2)}, u32[]{:S(2)}) collective-permute-start(bf16[1,128,2048]{2,1,0:T(8,128)(2,1)} %bitcast.25), channel_id=1, source_target_pairs={{0,16},{16,0},{1,17},{17,1},{2,18},{18,2},{3,19},{19,3},{4,20},{20... | collective-permute-start | bytes 1572872 | tf_op jit(solution)/shard_map/ppermute | solution.py:22
  48.9 8.4 %copy-start.1 = (bf16[2,128,512]{2,1,0:T(8,128)(2,1)S(1)}, bf16[2,128,512]{2,1,0:T(8,128)(2,1)}, u32[]{:S(2)}) copy-start(bf16[2,128,512]{2,1,0:T(8,128)(2,1)} %get-tuple-element.19) | copy-start | bytes 786436
  49.0 8.4 %collective-permute-start.5 = (bf16[2,128,512]{2,1,0:T(8,128)(2,1)S(1)}, bf16[2,128,512]{2,1,0:T(8,128)(2,1)S(1)}, u32[]{:S(2)}, u32[]{:S(2)}) collective-permute-start(bf16[2,128,512]{2,1,0:T(8,128)(2,1)S(1)} %add_convert_fusion.2), channel_id=1, source_target_pairs={{4,0},{8,4},{12,8},{5,1},{9,5},{13,9},{6,2},{10,6},{14,10},{7,3},{... | collective-permute-start | bytes 786440 | tf_op jit(solution)/shard_map/ppermute | solution.py:28
  57.4 8.4 %copy-start = (bf16[2,128,512]{2,1,0:T(8,128)(2,1)S(1)}, bf16[2,128,512]{2,1,0:T(8,128)(2,1)}, u32[]{:S(2)}) copy-start(bf16[2,128,512]{2,1,0:T(8,128)(2,1)} %get-tuple-element.22) | copy-start | bytes 786436
  57.4 8.4 %collective-permute-start.7 = (bf16[2,128,512]{2,1,0:T(8,128)(2,1)S(1)}, bf16[2,128,512]{2,1,0:T(8,128)(2,1)S(1)}, u32[]{:S(2)}, u32[]{:S(2)}) collective-permute-start(bf16[2,128,512]{2,1,0:T(8,128)(2,1)S(1)} %add_convert_fusion.1), channel_id=1, source_target_pairs={{4,0},{8,4},{12,8},{5,1},{9,5},{13,9},{6,2},{10,6},{14,10},{7,3},{... | collective-permute-start | bytes 786440 | tf_op jit(solution)/shard_map/ppermute | solution.py:28
  65.9 6.4 %collective-permute-start.8 = (bf16[2,128,512]{2,1,0:T(8,128)(2,1)S(1)}, bf16[2,128,512]{2,1,0:T(8,128)(2,1)S(1)}, u32[]{:S(2)}, u32[]{:S(2)}) collective-permute-start(bf16[2,128,512]{2,1,0:T(8,128)(2,1)S(1)} %add_convert_fusion), channel_id=1, source_target_pairs={{0,16},{16,0},{1,17},{17,1},{2,18},{18,2},{3,19},{19,3},{4,20},{20... | collective-permute-start | bytes 786440 | tf_op jit(solution)/shard_map/ppermute | solution.py:22

commit v13 on v12

--- a/solution.py
+++ b/solution.py
@@ -155,14 +155,10 @@
     masks = block_masks(random_blocks[0], global_ids[0], ctx_index, ctx_count, tok_rows)
 
     own = jnp.stack([keys[0], values[0]])
-    if ctx_count == 4:
-        step_one = shifted_open(own, "ctx", 1)
-        step_three = shifted_open(own, "ctx", 3)
-        pieces = [own, step_one, shifted_open(step_one, "ctx", 1), step_three]
-    else:
-        pieces = [own]
-        for shift in range(1, ctx_count):
-            pieces.append(shifted_open(pieces[-1], "ctx", 1))
+    pieces = [own]
+    for shift in range(1, ctx_count):
+        pieces.append(shifted_open(pieces[-1], "ctx", 1))
+
     attended, query_grad, kv_terms = attention(query[0], grad_out[0], pieces, masks)
     next_input = passed_along(attended[None], "pipe", 1)
     grad_query = passed_along(query_grad[None], "pipe", -1)

time: 73.4 us -> 74.3 us (1.012)
  starting transfers between devices: 19.5 us -> 20.6 us
    ppermute x6, starting transfers between devices: 16.8 us -> 17.9 us  [shifted_open(): return lax.ppermute(value, axis, pairs)]
    ppermute x3, waiting for transfers between devices: 9.99 us -> 9.06 us  [passed_along(): return lax.ppermute(value, axis, pairs)]
    ppermute x6, waiting for transfers between devices: 26.3 us -> 27.1 us  [shifted_open(): return lax.ppermute(value, axis, pairs)]
  transfers between devices with their start and end apart: 9 -> 9, of which waited for: 8 -> 9; matrix products, arithmetic and copies ran while one was open for 7% -> 7% of each run, Pallas kernels for 0% -> 0%
where the time goes in v13:
time: 74.3 us; the launch traced here: 73.9 us
  waiting for transfers between devices  36.2 us (49%)
  starting transfers between devices  20.6 us (28%)
  Pallas kernels  7.78 us (10%)
  local copies, waits for them, and re-layouts  5.05 us (7%)
  other arithmetic  3.55 us (5%)
  between operations  0.82 us (1%)
    ppermute x6, waiting for transfers between devices, shifted_open(): return lax.ppermute(value, axis, pairs)  27.1 us
    ppermute x6, starting transfers between devices, shifted_open(): return lax.ppermute(value, axis, pairs)  17.9 us
    ppermute x3, waiting for transfers between devices, passed_along(): return lax.ppermute(value, axis, pairs)  9.06 us
    pallas_call x1, Pallas kernels, attention(): pl.pallas_call(functools.partial(attention_kernel, piece_count, group_siz...  7.78 us
    ppermute x3, starting transfers between devices, passed_along(): return lax.ppermute(value, axis, pairs)  2.7 us
    unnamed x20, local copies, waits for them, and re-layouts  2.36 us
  transfers between devices with their start and end apart: 9, of which 9 were waited for; matrix products, arithmetic and copies ran while one was open for 7% of the time, Pallas kernels for 0%

profile of v13, /device:TPU:0, one launch (start us, length us, event | category | flops | bytes accessed | tf_op | source)
XLA Modules:
  0.0 73.9 jit_solution(14890192755728932394)
XLA Ops:
  0.6 0.0 copy-start.2
  0.6 0.9 %constant_dynamic-update-slice_fusion.1 = bf16[2,128,512]{2,1,0:T(8,128)(2,1)S(1)} fusion(bf16[1,128,512]{2,1,0:T(8,128)(2,1)} %param.7), kind=kLoop, calls=%fused_computation.14 | loop fusion | bytes 262144
  1.6 0.0 copy-done.2
  1.6 0.0 copy-start.3
  1.6 4.9 %collective-permute-start = (bf16[2,128,512]{2,1,0:T(8,128)(2,1)S(1)}, bf16[2,128,512]{2,1,0:T(8,128)(2,1)S(1)}, u32[]{:S(2)}, u32[]{:S(2)}) collective-permute-start(bf16[2,128,512]{2,1,0:T(8,128)(2,1)S(1)} %constant_dynamic-update-slice_fusion.refs_0_), channel_id=1, source_target_pairs={{0,4},{4,8},{8,12},{1,5},{5,9},{9,13},{2,6},{6,10},{10,14},{3,7},{... | collective-permute-start | bytes 786440 | tf_op jit(solution)/shard_map/ppermute | solution.py:28
  6.6 0.1 compare_and_fusion
  6.7 0.1 iota_add_fusion
  6.8 0.1 copy.14
  6.8 0.0 copy-start.5
  6.9 0.7 copy-done.5
  7.5 0.2 compare_reduce_fusion
  7.7 0.2 compare_reduce_fusion.1
  7.9 0.1 min.12
  8.0 0.0 copy-start.4
  8.0 4.1 %collective-permute-done.refs_1_ = bf16[2,128,512]{2,1,0:T(8,128)(2,1)S(1)} collective-permute-done((bf16[2,128,512]{2,1,0:T(8,128)(2,1)S(1)}, bf16[2,128,512]{2,1,0:T(8,128)(2,1)S(1)}, u32[]{:S(2)}, u32[]{:S(2)}) %collective-permute-start) | collective-permute-done | bytes 262176 | tf_op jit(solution)/shard_map/ppermute | solution.py:28
  12.1 0.0 copy-start.6
  12.1 4.4 %collective-permute-start.1 = (bf16[2,128,512]{2,1,0:T(8,128)(2,1)S(1)}, bf16[2,128,512]{2,1,0:T(8,128)(2,1)S(1)}, u32[]{:S(2)}, u32[]{:S(2)}) collective-permute-start(bf16[2,128,512]{2,1,0:T(8,128)(2,1)S(1)} %collective-permute-done.refs_1_), channel_id=1, source_target_pairs={{0,4},{4,8},{8,12},{1,5},{5,9},{9,13},{2,6},{6,10},{10,14},{3,7},{... | collective-permute-start | bytes 786440 | tf_op jit(solution)/shard_map/ppermute | solution.py:28
  16.5 0.1 copy.15
  16.6 0.1 or_or_fusion
  16.7 4.5 %collective-permute-done.1.refs_2_ = bf16[2,128,512]{2,1,0:T(8,128)(2,1)S(1)} collective-permute-done((bf16[2,128,512]{2,1,0:T(8,128)(2,1)S(1)}, bf16[2,128,512]{2,1,0:T(8,128)(2,1)S(1)}, u32[]{:S(2)}, u32[]{:S(2)}) %collective-permute-start.1) | collective-permute-done | bytes 262176 | tf_op jit(solution)/shard_map/ppermute | solution.py:28
  21.2 0.0 copy-start.7
  21.2 4.4 %collective-permute-start.2 = (bf16[2,128,512]{2,1,0:T(8,128)(2,1)S(1)}, bf16[2,128,512]{2,1,0:T(8,128)(2,1)S(1)}, u32[]{:S(2)}, u32[]{:S(2)}) collective-permute-start(bf16[2,128,512]{2,1,0:T(8,128)(2,1)S(1)} %collective-permute-done.1.refs_2_), channel_id=1, source_target_pairs={{0,4},{4,8},{8,12},{1,5},{5,9},{9,13},{2,6},{6,10},{10,14},{3,7},{... | collective-permute-start | bytes 786440 | tf_op jit(solution)/shard_map/ppermute | solution.py:28
  25.6 0.0 copy-done.4
  25.6 0.6 gather_fusion
  26.2 0.1 fusion.1
  26.3 0.1 copy.16
  26.4 0.2 broadcast_in_dim.18
  26.6 0.8 %convert_element_type.35.mask_ref = f32[4,16,2,128]{3,2,1,0:T(2,128)} reshape(f32[4,16,2,2,64]{4,3,2,1,0:T(2,128)S(1)} %broadcast_in_dim.18) | data formatting | bytes 131072 | tf_op jit(solution)/shard_map/convert_element_type | solution.py:48
  27.4 0.0 copy-done.3
  27.4 0.0 copy-done.6
  27.4 2.0 %collective-permute-done.2.refs_3_ = bf16[2,128,512]{2,1,0:T(8,128)(2,1)S(1)} collective-permute-done((bf16[2,128,512]{2,1,0:T(8,128)(2,1)S(1)}, bf16[2,128,512]{2,1,0:T(8,128)(2,1)S(1)}, u32[]{:S(2)}, u32[]{:S(2)}) %collective-permute-start.2) | collective-permute-done | bytes 262176 | tf_op jit(solution)/shard_map/ppermute | solution.py:28
  29.4 0.0 copy-start.8
  29.4 0.0 copy-done.7
  29.4 0.7 copy-done.8
  30.1 7.8 %shard_map.93 = (bf16[128,2048]{1,0:T(8,128)(2,1)}, bf16[128,2048]{1,0:T(8,128)(2,1)}, bf16[2,128,512]{2,1,0:T(8,128)(2,1)}, bf16[2,128,512]{2,1,0:T(8,128)(2,1)...) custom-call(bf16[128,2048]{1,0:T(8,128)(2,1)} %bitcast.23, bf16[128,2048]{1,0:T(8,128)(2,1)} %bitcast.24, ...), custom_call_target="tpu_custom_call" | custom-call | flops 1610612736 | bytes 4194304 | tf_op jit(solution)/shard_map/pallas_call | solution.py:130
  37.9 1.6 %collective-permute-start.3 = (bf16[1,128,2048]{2,1,0:T(8,128)(2,1)}, bf16[1,128,2048]{2,1,0:T(8,128)(2,1)S(1)}, u32[]{:S(2)}, u32[]{:S(2)}) collective-permute-start(bf16[1,128,2048]{2,1,0:T(8,128)(2,1)} %bitcast.26), channel_id=1, source_target_pairs={{0,16},{16,0},{1,17},{17,1},{2,18},{18,2},{3,19},{19,3},{4,20},{20... | collective-permute-start | bytes 1572872 | tf_op jit(solution)/shard_map/ppermute | solution.py:22
  39.5 1.3 %collective-permute-start.4 = (bf16[2,128,512]{2,1,0:T(8,128)(2,1)}, bf16[2,128,512]{2,1,0:T(8,128)(2,1)S(1)}, u32[]{:S(2)}, u32[]{:S(2)}) collective-permute-start(bf16[2,128,512]{2,1,0:T(8,128)(2,1)} %get-tuple-element.16), channel_id=1, source_target_pairs={{4,0},{8,4},{12,8},{5,1},{9,5},{13,9},{6,2},{10,6},{14,10},{7,3},{... | collective-permute-start | bytes 786440 | tf_op jit(solution)/shard_map/ppermute | solution.py:28
  40.8 0.6 collective-permute-start.6
  41.4 7.1 %collective-permute-done.4 = bf16[2,128,512]{2,1,0:T(8,128)(2,1)S(1)} collective-permute-done((bf16[2,128,512]{2,1,0:T(8,128)(2,1)}, bf16[2,128,512]{2,1,0:T(8,128)(2,1)S(1)}, u32[]{:S(2)}, u32[]{:S(2)}) %collective-permute-start.4) | collective-permute-done | bytes 262176 | tf_op jit(solution)/shard_map/ppermute | solution.py:28
  48.4 1.0 %add_convert_fusion.2 = bf16[2,128,512]{2,1,0:T(8,128)(2,1)S(1)} fusion(bf16[2,128,512]{2,1,0:T(8,128)(2,1)S(1)} %collective-permute-done.4, bf16[2,128,512]{2,1,0:T(8,128)(2,1)} %get-tuple-element.15), kind=kLoop, calls=%fused_computation.3 | loop fusion | flops 524288 | bytes 786432 | tf_op jit(solution)/shard_map/convert_element_type | solution.py:174
  49.5 0.0 copy-start.1
  49.5 1.4 %collective-permute-start.5 = (bf16[2,128,512]{2,1,0:T(8,128)(2,1)S(1)}, bf16[2,128,512]{2,1,0:T(8,128)(2,1)S(1)}, u32[]{:S(2)}, u32[]{:S(2)}) collective-permute-start(bf16[2,128,512]{2,1,0:T(8,128)(2,1)S(1)} %add_convert_fusion.2), channel_id=1, source_target_pairs={{4,0},{8,4},{12,8},{5,1},{9,5},{13,9},{6,2},{10,6},{14,10},{7,3},{... | collective-permute-start | bytes 786440 | tf_op jit(solution)/shard_map/ppermute | solution.py:28
  50.9 2.2 %collective-permute-done.3 = bf16[1,128,2048]{2,1,0:T(8,128)(2,1)S(1)} collective-permute-done((bf16[1,128,2048]{2,1,0:T(8,128)(2,1)}, bf16[1,128,2048]{2,1,0:T(8,128)(2,1)S(1)}, u32[]{:S(2)}, u32[]{:S(2)}) %collective-permute-start.3) | collective-permute-done | bytes 524320 | tf_op jit(solution)/shard_map/ppermute | solution.py:22
  53.1 0.8 %broadcast_select_fusion.1 = bf16[1,128,2048]{2,1,0:T(8,128)(2,1)} fusion(bf16[1,128,2048]{2,1,0:T(8,128)(2,1)S(1)} %collective-permute-done.3, pred[]{:T(512)S(6)} %lt.20), kind=kLoop, calls=%fused_computation.5 | loop fusion | flops 262144 | bytes 1048577 | tf_op jit(solution)/shard_map/jit(_where)/select_n | solution.py:171
  53.9 4.0 %collective-permute-done.5 = bf16[2,128,512]{2,1,0:T(8,128)(2,1)S(1)} collective-permute-done((bf16[2,128,512]{2,1,0:T(8,128)(2,1)S(1)}, bf16[2,128,512]{2,1,0:T(8,128)(2,1)S(1)}, u32[]{:S(2)}, u32[]{:S(2)}) %collective-permute-start.5) | collective-permute-done | bytes 262176 | tf_op jit(solution)/shard_map/ppermute | solution.py:28
  57.9 0.0 copy-done.1
  57.9 0.1 add_convert_fusion.1
  58.0 0.0 copy-start
  58.0 1.4 %collective-permute-start.7 = (bf16[2,128,512]{2,1,0:T(8,128)(2,1)S(1)}, bf16[2,128,512]{2,1,0:T(8,128)(2,1)S(1)}, u32[]{:S(2)}, u32[]{:S(2)}) collective-permute-start(bf16[2,128,512]{2,1,0:T(8,128)(2,1)S(1)} %add_convert_fusion.1), channel_id=1, source_target_pairs={{4,0},{8,4},{12,8},{5,1},{9,5},{13,9},{6,2},{10,6},{14,10},{7,3},{... | collective-permute-start | bytes 786440 | tf_op jit(solution)/shard_map/ppermute | solution.py:28
  59.4 1.0 %collective-permute-done.6 = bf16[1,128,2048]{2,1,0:T(8,128)(2,1)S(1)} collective-permute-done((bf16[1,128,2048]{2,1,0:T(8,128)(2,1)}, bf16[1,128,2048]{2,1,0:T(8,128)(2,1)S(1)}, u32[]{:S(2)}, u32[]{:S(2)}) %collective-permute-start.6) | collective-permute-done | bytes 524320 | tf_op jit(solution)/shard_map/ppermute | solution.py:22
  60.5 0.8 %broadcast_select_fusion = bf16[1,128,2048]{2,1,0:T(8,128)(2,1)} fusion(bf16[1,128,2048]{2,1,0:T(8,128)(2,1)S(1)} %collective-permute-done.6, pred[]{:T(512)S(6)} %lt.20), kind=kLoop, calls=%fused_computation.4 | loop fusion | flops 262144 | bytes 1048577 | tf_op jit(solution)/shard_map/jit(_where)/select_n | solution.py:177
  61.3 5.4 %collective-permute-done.7 = bf16[2,128,512]{2,1,0:T(8,128)(2,1)S(1)} collective-permute-done((bf16[2,128,512]{2,1,0:T(8,128)(2,1)S(1)}, bf16[2,128,512]{2,1,0:T(8,128)(2,1)S(1)}, u32[]{:S(2)}, u32[]{:S(2)}) %collective-permute-start.7) | collective-permute-done | bytes 262176 | tf_op jit(solution)/shard_map/ppermute | solution.py:28
  66.7 0.0 copy-done
  66.7 0.1 add_convert_fusion
  66.8 0.6 collective-permute-start.8
  67.3 5.9 %collective-permute-done.8 = bf16[2,128,512]{2,1,0:T(8,128)(2,1)S(1)} collective-permute-done((bf16[2,128,512]{2,1,0:T(8,128)(2,1)S(1)}, bf16[2,128,512]{2,1,0:T(8,128)(2,1)S(1)}, u32[]{:S(2)}, u32[]{:S(2)}) %collective-permute-start.8) | collective-permute-done | bytes 262176 | tf_op jit(solution)/shard_map/ppermute | solution.py:22
  73.2 0.7 fusion.5
  (7 shorter events, 0.0 us)
Async XLA Ops:
  0.6 1.0 %copy-start.2 = (bf16[1,128,512]{2,1,0:T(8,128)(2,1)S(1)}, bf16[1,128,512]{2,1,0:T(8,128)(2,1)}, u32[]{:S(2)}) copy-start(bf16[1,128,512]{2,1,0:T(8,128)(2,1)} %param.8) | copy-start | bytes 393220
  1.6 25.8 %copy-start.3 = (bf16[2,128,512]{2,1,0:T(8,128)(2,1)}, bf16[2,128,512]{2,1,0:T(8,128)(2,1)S(1)}, u32[]{:S(2)}) copy-start(bf16[2,128,512]{2,1,0:T(8,128)(2,1)S(1)} %constant_dynamic-update-slice_fusion.refs_0_) | copy-start | bytes 786436
  1.6 10.5 %collective-permute-start = (bf16[2,128,512]{2,1,0:T(8,128)(2,1)S(1)}, bf16[2,128,512]{2,1,0:T(8,128)(2,1)S(1)}, u32[]{:S(2)}, u32[]{:S(2)}) collective-permute-start(bf16[2,128,512]{2,1,0:T(8,128)(2,1)S(1)} %constant_dynamic-update-slice_fusion.refs_0_), channel_id=1, source_target_pairs={{0,4},{4,8},{8,12},{1,5},{5,9},{9,13},{2,6},{6,10},{10,14},{3,7},{... | collective-permute-start | bytes 786440 | tf_op jit(solution)/shard_map/ppermute | solution.py:28
  6.8 0.7 copy-start.5
  8.0 17.6 %copy-start.4 = (s32[1,2,16,8]{2,3,1,0:T(8,128)S(1)}, s32[1,2,16,8]{2,3,1,0:T(8,128)}, u32[]{:S(2)}) copy-start(s32[1,2,16,8]{2,3,1,0:T(8,128)} %param.10) | copy-start | bytes 3076
  12.1 15.3 %copy-start.6 = (bf16[2,128,512]{2,1,0:T(8,128)(2,1)}, bf16[2,128,512]{2,1,0:T(8,128)(2,1)S(1)}, u32[]{:S(2)}) copy-start(bf16[2,128,512]{2,1,0:T(8,128)(2,1)S(1)} %collective-permute-done.refs_1_) | copy-start | bytes 786436
  12.1 9.1 %collective-permute-start.1 = (bf16[2,128,512]{2,1,0:T(8,128)(2,1)S(1)}, bf16[2,128,512]{2,1,0:T(8,128)(2,1)S(1)}, u32[]{:S(2)}, u32[]{:S(2)}) collective-permute-start(bf16[2,128,512]{2,1,0:T(8,128)(2,1)S(1)} %collective-permute-done.refs_1_), channel_id=1, source_target_pairs={{0,4},{4,8},{8,12},{1,5},{5,9},{9,13},{2,6},{6,10},{10,14},{3,7},{... | collective-permute-start | bytes 786440 | tf_op jit(solution)/shard_map/ppermute | solution.py:28
  21.2 8.3 %copy-start.7 = (bf16[2,128,512]{2,1,0:T(8,128)(2,1)}, bf16[2,128,512]{2,1,0:T(8,128)(2,1)S(1)}, u32[]{:S(2)}) copy-start(bf16[2,128,512]{2,1,0:T(8,128)(2,1)S(1)} %collective-permute-done.1.refs_2_) | copy-start | bytes 786436
  21.2 8.3 %collective-permute-start.2 = (bf16[2,128,512]{2,1,0:T(8,128)(2,1)S(1)}, bf16[2,128,512]{2,1,0:T(8,128)(2,1)S(1)}, u32[]{:S(2)}, u32[]{:S(2)}) collective-permute-start(bf16[2,128,512]{2,1,0:T(8,128)(2,1)S(1)} %collective-permute-done.1.refs_2_), channel_id=1, source_target_pairs={{0,4},{4,8},{8,12},{1,5},{5,9},{9,13},{2,6},{6,10},{10,14},{3,7},{... | collective-permute-start | bytes 786440 | tf_op jit(solution)/shard_map/ppermute | solution.py:28
  29.4 0.7 copy-start.8
  37.9 15.1 %collective-permute-start.3 = (bf16[1,128,2048]{2,1,0:T(8,128)(2,1)}, bf16[1,128,2048]{2,1,0:T(8,128)(2,1)S(1)}, u32[]{:S(2)}, u32[]{:S(2)}) collective-permute-start(bf16[1,128,2048]{2,1,0:T(8,128)(2,1)} %bitcast.26), channel_id=1, source_target_pairs={{0,16},{16,0},{1,17},{17,1},{2,18},{18,2},{3,19},{19,3},{4,20},{20... | collective-permute-start | bytes 1572872 | tf_op jit(solution)/shard_map/ppermute | solution.py:22
  39.5 8.9 %collective-permute-start.4 = (bf16[2,128,512]{2,1,0:T(8,128)(2,1)}, bf16[2,128,512]{2,1,0:T(8,128)(2,1)S(1)}, u32[]{:S(2)}, u32[]{:S(2)}) collective-permute-start(bf16[2,128,512]{2,1,0:T(8,128)(2,1)} %get-tuple-element.16), channel_id=1, source_target_pairs={{4,0},{8,4},{12,8},{5,1},{9,5},{13,9},{6,2},{10,6},{14,10},{7,3},{... | collective-permute-start | bytes 786440 | tf_op jit(solution)/shard_map/ppermute | solution.py:28
  40.8 19.7 %collective-permute-start.6 = (bf16[1,128,2048]{2,1,0:T(8,128)(2,1)}, bf16[1,128,2048]{2,1,0:T(8,128)(2,1)S(1)}, u32[]{:S(2)}, u32[]{:S(2)}) collective-permute-start(bf16[1,128,2048]{2,1,0:T(8,128)(2,1)} %bitcast.25), channel_id=1, source_target_pairs={{0,16},{16,0},{1,17},{17,1},{2,18},{18,2},{3,19},{19,3},{4,20},{20... | collective-permute-start | bytes 1572872 | tf_op jit(solution)/shard_map/ppermute | solution.py:22
  49.5 8.5 %copy-start.1 = (bf16[2,128,512]{2,1,0:T(8,128)(2,1)S(1)}, bf16[2,128,512]{2,1,0:T(8,128)(2,1)}, u32[]{:S(2)}) copy-start(bf16[2,128,512]{2,1,0:T(8,128)(2,1)} %get-tuple-element.19) | copy-start | bytes 786436
  49.5 8.4 %collective-permute-start.5 = (bf16[2,128,512]{2,1,0:T(8,128)(2,1)S(1)}, bf16[2,128,512]{2,1,0:T(8,128)(2,1)S(1)}, u32[]{:S(2)}, u32[]{:S(2)}) collective-permute-start(bf16[2,128,512]{2,1,0:T(8,128)(2,1)S(1)} %add_convert_fusion.2), channel_id=1, source_target_pairs={{4,0},{8,4},{12,8},{5,1},{9,5},{13,9},{6,2},{10,6},{14,10},{7,3},{... | collective-permute-start | bytes 786440 | tf_op jit(solution)/shard_map/ppermute | solution.py:28
  58.0 8.7 %copy-start = (bf16[2,128,512]{2,1,0:T(8,128)(2,1)S(1)}, bf16[2,128,512]{2,1,0:T(8,128)(2,1)}, u32[]{:S(2)}) copy-start(bf16[2,128,512]{2,1,0:T(8,128)(2,1)} %get-tuple-element.22) | copy-start | bytes 786436
  58.0 8.7 %collective-permute-start.7 = (bf16[2,128,512]{2,1,0:T(8,128)(2,1)S(1)}, bf16[2,128,512]{2,1,0:T(8,128)(2,1)S(1)}, u32[]{:S(2)}, u32[]{:S(2)}) collective-permute-start(bf16[2,128,512]{2,1,0:T(8,128)(2,1)S(1)} %add_convert_fusion.1), channel_id=1, source_target_pairs={{4,0},{8,4},{12,8},{5,1},{9,5},{13,9},{6,2},{10,6},{14,10},{7,3},{... | collective-permute-start | bytes 786440 | tf_op jit(solution)/shard_map/ppermute | solution.py:28
  66.8 6.4 %collective-permute-start.8 = (bf16[2,128,512]{2,1,0:T(8,128)(2,1)S(1)}, bf16[2,128,512]{2,1,0:T(8,128)(2,1)S(1)}, u32[]{:S(2)}, u32[]{:S(2)}) collective-permute-start(bf16[2,128,512]{2,1,0:T(8,128)(2,1)S(1)} %add_convert_fusion), channel_id=1, source_target_pairs={{0,16},{16,0},{1,17},{17,1},{2,18},{18,2},{3,19},{19,3},{4,20},{20... | collective-permute-start | bytes 786440 | tf_op jit(solution)/shard_map/ppermute | solution.py:22

commit v14 on v12

--- a/solution.py
+++ b/solution.py
@@ -167,21 +167,31 @@
     next_input = passed_along(attended[None], "pipe", 1)
     grad_query = passed_along(query_grad[None], "pipe", -1)
 
+    pipe_count = lax.axis_size("pipe")
+    own_part = passed_along(kv_terms[0], "pipe", -1)
     carried = None
     for step in range(1, ctx_count):
         part = kv_terms[ctx_count - step].astype(jnp.float32)
         if carried is not None:
             if step == ctx_count - 1:
                 next_input = jnp.where(ctx_index < 0, jnp.zeros_like(next_input), next_input)
-                next_input, carried = lax.optimization_barrier((next_input, carried))
+                next_input, own_part, carried = lax.optimization_barrier((next_input, own_part, carried))
             part = part + carried.astype(jnp.float32)
-        carried = shifted_open(part.astype(jnp.bfloat16), "ctx", -1)
-    kv_sum = kv_terms[0].astype(jnp.float32)
+        if step < ctx_count - 1:
+            carried = shifted_open(part.astype(jnp.bfloat16), "ctx", -1)
+        else:
+            pairs = [
+                (pipe * ctx_count + ctx, ((pipe - 1) % pipe_count) * ctx_count + ctx - 1)
+                for pipe in range(pipe_count)
+                for ctx in range(1, ctx_count)
+            ]
+            carried = lax.ppermute(part.astype(jnp.bfloat16), ("pipe", "ctx"), pairs)
+    kv_sum = own_part.astype(jnp.float32)
     if carried is not None:
         grad_query = jnp.where(ctx_index < 0, jnp.zeros_like(grad_query), grad_query)
         grad_query, carried = lax.optimization_barrier((grad_query, carried))
         kv_sum = kv_sum + carried.astype(jnp.float32)
-    returned = passed_along(kv_sum.astype(jnp.bfloat16), "pipe", -1)
+    returned = kv_sum.astype(jnp.bfloat16)
     grad_key = returned[0:1]
     grad_value = returned[1:2]
     return (next_input, grad_query, grad_key, grad_value)

time: 73.4 us -> 74 us (level)
  starting transfers between devices: 19.5 us -> 20.3 us
    ppermute x6 -> x5, waiting for transfers between devices: 26.3 us -> 16.7 us  [shifted_open(): return lax.ppermute(value, axis, pairs)]
    ppermute x3, waiting for transfers between devices: 9.99 us -> 19.5 us  [passed_along(): return lax.ppermute(value, axis, pairs)]
    ppermute x6 -> x5, starting transfers between devices: 16.8 us -> 15.4 us  [shifted_open(): return lax.ppermute(value, axis, pairs)]
    ppermute x0 -> x1, starting transfers between devices: none -> 1.29 us  [local(): carried = lax.ppermute(part.astype(jnp.bfloat16), ('pipe', 'ctx'), pairs)]
    ppermute x3, starting transfers between devices: 2.72 us -> 3.67 us  [passed_along(): return lax.ppermute(value, axis, pairs)]
    unnamed x20 -> x18, local copies, waits for them, and re-layouts: 2.36 us -> 2.36 us
  transfers between devices with their start and end apart: 9 -> 9, of which waited for: 8 -> 6; matrix products, arithmetic and copies ran while one was open for 7% -> 7% of each run, Pallas kernels for 0% -> 0%
where the time goes in v14:
time: 74 us; the launch traced here: 73.7 us
  waiting for transfers between devices  36.1 us (49%)
  starting transfers between devices  20.3 us (27%)
  Pallas kernels  7.78 us (11%)
  local copies, waits for them, and re-layouts  5.06 us (7%)
  other arithmetic  3.55 us (5%)
  between operations  0.82 us (1%)
    ppermute x3, waiting for transfers between devices, passed_along(): return lax.ppermute(value, axis, pairs)  19.5 us
    ppermute x5, waiting for transfers between devices, shifted_open(): return lax.ppermute(value, axis, pairs)  16.7 us
    ppermute x5, starting transfers between devices, shifted_open(): return lax.ppermute(value, axis, pairs)  15.4 us
    pallas_call x1, Pallas kernels, attention(): pl.pallas_call(functools.partial(attention_kernel, piece_count, group_siz...  7.78 us
    ppermute x3, starting transfers between devices, passed_along(): return lax.ppermute(value, axis, pairs)  3.67 us
    unnamed x18, local copies, waits for them, and re-layouts  2.36 us
  transfers between devices with their start and end apart: 9, of which 6 were waited for; matrix products, arithmetic and copies ran while one was open for 7% of the time, Pallas kernels for 0%

profile of v14, /device:TPU:0, one launch (start us, length us, event | category | flops | bytes accessed | tf_op | source)
XLA Modules:
  0.0 73.7 jit_solution(9054599489679558651)
XLA Ops:
  0.6 0.0 copy-start.1
  0.6 0.9 %constant_dynamic-update-slice_fusion.1 = bf16[2,128,512]{2,1,0:T(8,128)(2,1)S(1)} fusion(bf16[1,128,512]{2,1,0:T(8,128)(2,1)} %param.7), kind=kLoop, calls=%fused_computation.14 | loop fusion | bytes 262144
  1.6 0.0 copy-done.1
  1.6 0.0 copy-start.2
  1.6 7.0 %collective-permute-start.2 = (bf16[2,128,512]{2,1,0:T(8,128)(2,1)S(1)}, bf16[2,128,512]{2,1,0:T(8,128)(2,1)S(1)}, u32[]{:S(2)}, u32[]{:S(2)}) collective-permute-start(bf16[2,128,512]{2,1,0:T(8,128)(2,1)S(1)} %constant_dynamic-update-slice_fusion.refs_0_), channel_id=1, source_target_pairs={{0,12},{1,13},{2,14},{3,15},{16,28},{17,29},{18,30},{19,31}} | collective-permute-start | bytes 786440 | tf_op jit(solution)/shard_map/ppermute | solution.py:28
  8.6 1.3 %collective-permute-start = (bf16[2,128,512]{2,1,0:T(8,128)(2,1)S(1)}, bf16[2,128,512]{2,1,0:T(8,128)(2,1)S(1)}, u32[]{:S(2)}, u32[]{:S(2)}) collective-permute-start(bf16[2,128,512]{2,1,0:T(8,128)(2,1)S(1)} %constant_dynamic-update-slice_fusion.refs_0_), channel_id=1, source_target_pairs={{0,4},{4,8},{8,12},{1,5},{5,9},{9,13},{2,6},{6,10},{10,14},{3,7},{... | collective-permute-start | bytes 786440 | tf_op jit(solution)/shard_map/ppermute | solution.py:28
  9.9 0.1 compare_and_fusion
  10.0 0.1 iota_add_fusion
  10.1 0.1 min.12
  10.2 0.1 copy.14
  10.3 0.0 copy-start.4
  10.3 0.7 copy-done.4
  10.9 0.2 compare_reduce_fusion.1
  11.1 0.0 copy-start.3
  11.1 0.2 compare_reduce_fusion
  11.4 0.1 copy.15
  11.5 0.1 or_or_fusion
  11.5 8.3 %collective-permute-done.refs_1_ = bf16[2,128,512]{2,1,0:T(8,128)(2,1)S(1)} collective-permute-done((bf16[2,128,512]{2,1,0:T(8,128)(2,1)S(1)}, bf16[2,128,512]{2,1,0:T(8,128)(2,1)S(1)}, u32[]{:S(2)}, u32[]{:S(2)}) %collective-permute-start) | collective-permute-done | bytes 262176 | tf_op jit(solution)/shard_map/ppermute | solution.py:28
  19.8 0.0 copy-start.6
  19.8 4.4 %collective-permute-start.1 = (bf16[2,128,512]{2,1,0:T(8,128)(2,1)S(1)}, bf16[2,128,512]{2,1,0:T(8,128)(2,1)S(1)}, u32[]{:S(2)}, u32[]{:S(2)}) collective-permute-start(bf16[2,128,512]{2,1,0:T(8,128)(2,1)S(1)} %collective-permute-done.refs_1_), channel_id=1, source_target_pairs={{0,4},{4,8},{8,12},{1,5},{5,9},{9,13},{2,6},{6,10},{10,14},{3,7},{... | collective-permute-start | bytes 786440 | tf_op jit(solution)/shard_map/ppermute | solution.py:28
  24.2 0.0 copy-done.3
  24.2 0.6 gather_fusion
  24.8 0.1 fusion.1
  24.9 0.1 copy.16
  25.0 0.2 broadcast_in_dim.18
  25.2 0.8 %convert_element_type.35.mask_ref = f32[4,16,2,128]{3,2,1,0:T(2,128)} reshape(f32[4,16,2,2,64]{4,3,2,1,0:T(2,128)S(1)} %broadcast_in_dim.18) | data formatting | bytes 131072 | tf_op jit(solution)/shard_map/convert_element_type | solution.py:48
  26.0 0.0 copy-done.2
  26.0 0.0 copy-done.6
  26.0 0.0 collective-permute-done.2.refs_3_
  26.0 0.0 copy-start.5
  26.1 2.9 %collective-permute-done.1.refs_2_ = bf16[2,128,512]{2,1,0:T(8,128)(2,1)S(1)} collective-permute-done((bf16[2,128,512]{2,1,0:T(8,128)(2,1)S(1)}, bf16[2,128,512]{2,1,0:T(8,128)(2,1)S(1)}, u32[]{:S(2)}, u32[]{:S(2)}) %collective-permute-start.1) | collective-permute-done | bytes 262176 | tf_op jit(solution)/shard_map/ppermute | solution.py:28
  28.9 0.0 copy-start.7
  28.9 0.0 copy-done.5
  28.9 0.7 copy-done.7
  29.6 7.8 %shard_map.93 = (bf16[128,2048]{1,0:T(8,128)(2,1)}, bf16[128,2048]{1,0:T(8,128)(2,1)}, bf16[2,128,512]{2,1,0:T(8,128)(2,1)}, bf16[2,128,512]{2,1,0:T(8,128)(2,1)...) custom-call(bf16[128,2048]{1,0:T(8,128)(2,1)} %bitcast.23, bf16[128,2048]{1,0:T(8,128)(2,1)} %bitcast.24, ...), custom_call_target="tpu_custom_call" | custom-call | flops 1610612736 | bytes 4194304 | tf_op jit(solution)/shard_map/pallas_call | solution.py:130
  37.4 1.6 %collective-permute-start.3 = (bf16[1,128,2048]{2,1,0:T(8,128)(2,1)}, bf16[1,128,2048]{2,1,0:T(8,128)(2,1)S(1)}, u32[]{:S(2)}, u32[]{:S(2)}) collective-permute-start(bf16[1,128,2048]{2,1,0:T(8,128)(2,1)} %bitcast.26), channel_id=1, source_target_pairs={{0,16},{16,0},{1,17},{17,1},{2,18},{18,2},{3,19},{19,3},{4,20},{20... | collective-permute-start | bytes 1572872 | tf_op jit(solution)/shard_map/ppermute | solution.py:22
  39.0 1.3 %collective-permute-start.5 = (bf16[2,128,512]{2,1,0:T(8,128)(2,1)}, bf16[2,128,512]{2,1,0:T(8,128)(2,1)S(1)}, u32[]{:S(2)}, u32[]{:S(2)}) collective-permute-start(bf16[2,128,512]{2,1,0:T(8,128)(2,1)} %get-tuple-element.18), channel_id=1, source_target_pairs={{4,0},{8,4},{12,8},{5,1},{9,5},{13,9},{6,2},{10,6},{14,10},{7,3},{... | collective-permute-start | bytes 786440 | tf_op jit(solution)/shard_map/ppermute | solution.py:28
  40.3 0.6 collective-permute-start.4
  40.9 1.5 %collective-permute-start.7 = (bf16[1,128,2048]{2,1,0:T(8,128)(2,1)}, bf16[1,128,2048]{2,1,0:T(8,128)(2,1)S(1)}, u32[]{:S(2)}, u32[]{:S(2)}) collective-permute-start(bf16[1,128,2048]{2,1,0:T(8,128)(2,1)} %bitcast.25), channel_id=1, source_target_pairs={{0,16},{16,0},{1,17},{17,1},{2,18},{18,2},{3,19},{19,3},{4,20},{20... | collective-permute-start | bytes 1572872 | tf_op jit(solution)/shard_map/ppermute | solution.py:22
  42.4 5.6 %collective-permute-done.5 = bf16[2,128,512]{2,1,0:T(8,128)(2,1)S(1)} collective-permute-done((bf16[2,128,512]{2,1,0:T(8,128)(2,1)}, bf16[2,128,512]{2,1,0:T(8,128)(2,1)S(1)}, u32[]{:S(2)}, u32[]{:S(2)}) %collective-permute-start.5) | collective-permute-done | bytes 262176 | tf_op jit(solution)/shard_map/ppermute | solution.py:28
  47.9 1.0 %add_convert_fusion.2 = bf16[2,128,512]{2,1,0:T(8,128)(2,1)S(1)} fusion(bf16[2,128,512]{2,1,0:T(8,128)(2,1)S(1)} %collective-permute-done.5, bf16[2,128,512]{2,1,0:T(8,128)(2,1)} %get-tuple-element.17), kind=kLoop, calls=%fused_computation.3 | loop fusion | flops 524288 | bytes 786432 | tf_op jit(solution)/shard_map/convert_element_type | solution.py:181
  48.9 0.0 copy-start
  49.0 1.4 %collective-permute-start.6 = (bf16[2,128,512]{2,1,0:T(8,128)(2,1)S(1)}, bf16[2,128,512]{2,1,0:T(8,128)(2,1)S(1)}, u32[]{:S(2)}, u32[]{:S(2)}) collective-permute-start(bf16[2,128,512]{2,1,0:T(8,128)(2,1)S(1)} %add_convert_fusion.2), channel_id=1, source_target_pairs={{4,0},{8,4},{12,8},{5,1},{9,5},{13,9},{6,2},{10,6},{14,10},{7,3},{... | collective-permute-start | bytes 786440 | tf_op jit(solution)/shard_map/ppermute | solution.py:28
  50.4 2.2 %collective-permute-done.3 = bf16[1,128,2048]{2,1,0:T(8,128)(2,1)S(1)} collective-permute-done((bf16[1,128,2048]{2,1,0:T(8,128)(2,1)}, bf16[1,128,2048]{2,1,0:T(8,128)(2,1)S(1)}, u32[]{:S(2)}, u32[]{:S(2)}) %collective-permute-start.3) | collective-permute-done | bytes 524320 | tf_op jit(solution)/shard_map/ppermute | solution.py:22
  52.5 0.8 %broadcast_select_fusion.1 = bf16[1,128,2048]{2,1,0:T(8,128)(2,1)} fusion(bf16[1,128,2048]{2,1,0:T(8,128)(2,1)S(1)} %collective-permute-done.3, pred[]{:T(512)S(6)} %lt.20), kind=kLoop, calls=%fused_computation.5 | loop fusion | flops 262144 | bytes 1048577 | tf_op jit(solution)/shard_map/jit(_where)/select_n | solution.py:177
  53.4 4.8 %collective-permute-done.4 = bf16[2,128,512]{2,1,0:T(8,128)(2,1)S(1)} collective-permute-done((bf16[2,128,512]{2,1,0:T(8,128)(2,1)}, bf16[2,128,512]{2,1,0:T(8,128)(2,1)S(1)}, u32[]{:S(2)}, u32[]{:S(2)}) %collective-permute-start.4) | collective-permute-done | bytes 262176 | tf_op jit(solution)/shard_map/ppermute | solution.py:22
  58.2 0.0 collective-permute-done.6
  58.2 0.0 copy-done
  58.2 0.1 add_convert_fusion.1
  58.2 1.3 %collective-permute-start.8 = (bf16[2,128,512]{2,1,0:T(8,128)(2,1)S(1)}, bf16[2,128,512]{2,1,0:T(8,128)(2,1)S(1)}, u32[]{:S(2)}, u32[]{:S(2)}) collective-permute-start(bf16[2,128,512]{2,1,0:T(8,128)(2,1)S(1)} %add_convert_fusion.1), channel_id=1, source_target_pairs={{4,16},{8,20},{12,24},{20,0},{24,4},{28,8},{5,17},{9,21},{13,25},{... | collective-permute-start | bytes 786440 | tf_op jit(solution)/shard_map/ppermute | solution.py:188
  59.5 12.5 %collective-permute-done.7 = bf16[1,128,2048]{2,1,0:T(8,128)(2,1)S(1)} collective-permute-done((bf16[1,128,2048]{2,1,0:T(8,128)(2,1)}, bf16[1,128,2048]{2,1,0:T(8,128)(2,1)S(1)}, u32[]{:S(2)}, u32[]{:S(2)}) %collective-permute-start.7) | collective-permute-done | bytes 524320 | tf_op jit(solution)/shard_map/ppermute | solution.py:22
  72.1 0.8 %broadcast_select_fusion = bf16[1,128,2048]{2,1,0:T(8,128)(2,1)} fusion(bf16[1,128,2048]{2,1,0:T(8,128)(2,1)S(1)} %collective-permute-done.7, pred[]{:T(512)S(6)} %lt.20), kind=kLoop, calls=%fused_computation.4 | loop fusion | flops 262144 | bytes 1048577 | tf_op jit(solution)/shard_map/jit(_where)/select_n | solution.py:191
  72.9 0.0 collective-permute-done.8
  72.9 0.1 add_convert_fusion
  73.0 0.7 fusion.5
  (7 shorter events, 0.0 us)
Async XLA Ops:
  0.6 1.0 %copy-start.1 = (bf16[1,128,512]{2,1,0:T(8,128)(2,1)S(1)}, bf16[1,128,512]{2,1,0:T(8,128)(2,1)}, u32[]{:S(2)}) copy-start(bf16[1,128,512]{2,1,0:T(8,128)(2,1)} %param.8) | copy-start | bytes 393220
  1.6 24.4 %copy-start.2 = (bf16[2,128,512]{2,1,0:T(8,128)(2,1)}, bf16[2,128,512]{2,1,0:T(8,128)(2,1)S(1)}, u32[]{:S(2)}) copy-start(bf16[2,128,512]{2,1,0:T(8,128)(2,1)S(1)} %constant_dynamic-update-slice_fusion.refs_0_) | copy-start | bytes 786436
  1.6 24.4 %collective-permute-start.2 = (bf16[2,128,512]{2,1,0:T(8,128)(2,1)S(1)}, bf16[2,128,512]{2,1,0:T(8,128)(2,1)S(1)}, u32[]{:S(2)}, u32[]{:S(2)}) collective-permute-start(bf16[2,128,512]{2,1,0:T(8,128)(2,1)S(1)} %constant_dynamic-update-slice_fusion.refs_0_), channel_id=1, source_target_pairs={{0,12},{1,13},{2,14},{3,15},{16,28},{17,29},{18,30},{19,31}} | collective-permute-start | bytes 786440 | tf_op jit(solution)/shard_map/ppermute | solution.py:28
  8.6 11.2 %collective-permute-start = (bf16[2,128,512]{2,1,0:T(8,128)(2,1)S(1)}, bf16[2,128,512]{2,1,0:T(8,128)(2,1)S(1)}, u32[]{:S(2)}, u32[]{:S(2)}) collective-permute-start(bf16[2,128,512]{2,1,0:T(8,128)(2,1)S(1)} %constant_dynamic-update-slice_fusion.refs_0_), channel_id=1, source_target_pairs={{0,4},{4,8},{8,12},{1,5},{5,9},{9,13},{2,6},{6,10},{10,14},{3,7},{... | collective-permute-start | bytes 786440 | tf_op jit(solution)/shard_map/ppermute | solution.py:28
  10.3 0.7 copy-start.4
  11.1 13.1 %copy-start.3 = (s32[1,2,16,8]{2,3,1,0:T(8,128)S(1)}, s32[1,2,16,8]{2,3,1,0:T(8,128)}, u32[]{:S(2)}) copy-start(s32[1,2,16,8]{2,3,1,0:T(8,128)} %param.10) | copy-start | bytes 3076
  19.8 6.2 %copy-start.6 = (bf16[2,128,512]{2,1,0:T(8,128)(2,1)}, bf16[2,128,512]{2,1,0:T(8,128)(2,1)S(1)}, u32[]{:S(2)}) copy-start(bf16[2,128,512]{2,1,0:T(8,128)(2,1)S(1)} %collective-permute-done.refs_1_) | copy-start | bytes 786436
  19.8 9.1 %collective-permute-start.1 = (bf16[2,128,512]{2,1,0:T(8,128)(2,1)S(1)}, bf16[2,128,512]{2,1,0:T(8,128)(2,1)S(1)}, u32[]{:S(2)}, u32[]{:S(2)}) collective-permute-start(bf16[2,128,512]{2,1,0:T(8,128)(2,1)S(1)} %collective-permute-done.refs_1_), channel_id=1, source_target_pairs={{0,4},{4,8},{8,12},{1,5},{5,9},{9,13},{2,6},{6,10},{10,14},{3,7},{... | collective-permute-start | bytes 786440 | tf_op jit(solution)/shard_map/ppermute | solution.py:28
  26.0 2.9 %copy-start.5 = (bf16[2,128,512]{2,1,0:T(8,128)(2,1)}, bf16[2,128,512]{2,1,0:T(8,128)(2,1)S(1)}, u32[]{:S(2)}) copy-start(bf16[2,128,512]{2,1,0:T(8,128)(2,1)S(1)} %collective-permute-done.2.refs_3_) | copy-start | bytes 786436
  28.9 0.7 copy-start.7
  37.4 15.1 %collective-permute-start.3 = (bf16[1,128,2048]{2,1,0:T(8,128)(2,1)}, bf16[1,128,2048]{2,1,0:T(8,128)(2,1)S(1)}, u32[]{:S(2)}, u32[]{:S(2)}) collective-permute-start(bf16[1,128,2048]{2,1,0:T(8,128)(2,1)} %bitcast.26), channel_id=1, source_target_pairs={{0,16},{16,0},{1,17},{17,1},{2,18},{18,2},{3,19},{19,3},{4,20},{20... | collective-permute-start | bytes 1572872 | tf_op jit(solution)/shard_map/ppermute | solution.py:22
  39.0 8.9 %collective-permute-start.5 = (bf16[2,128,512]{2,1,0:T(8,128)(2,1)}, bf16[2,128,512]{2,1,0:T(8,128)(2,1)S(1)}, u32[]{:S(2)}, u32[]{:S(2)}) collective-permute-start(bf16[2,128,512]{2,1,0:T(8,128)(2,1)} %get-tuple-element.18), channel_id=1, source_target_pairs={{4,0},{8,4},{12,8},{5,1},{9,5},{13,9},{6,2},{10,6},{14,10},{7,3},{... | collective-permute-start | bytes 786440 | tf_op jit(solution)/shard_map/ppermute | solution.py:28
  40.3 17.9 %collective-permute-start.4 = (bf16[2,128,512]{2,1,0:T(8,128)(2,1)}, bf16[2,128,512]{2,1,0:T(8,128)(2,1)S(1)}, u32[]{:S(2)}, u32[]{:S(2)}) collective-permute-start(bf16[2,128,512]{2,1,0:T(8,128)(2,1)} %get-tuple-element.16), channel_id=1, source_target_pairs={{0,16},{16,0},{1,17},{17,1},{2,18},{18,2},{3,19},{19,3},{4,20},{20... | collective-permute-start | bytes 786440 | tf_op jit(solution)/shard_map/ppermute | solution.py:22
  40.9 31.2 %collective-permute-start.7 = (bf16[1,128,2048]{2,1,0:T(8,128)(2,1)}, bf16[1,128,2048]{2,1,0:T(8,128)(2,1)S(1)}, u32[]{:S(2)}, u32[]{:S(2)}) collective-permute-start(bf16[1,128,2048]{2,1,0:T(8,128)(2,1)} %bitcast.25), channel_id=1, source_target_pairs={{0,16},{16,0},{1,17},{17,1},{2,18},{18,2},{3,19},{19,3},{4,20},{20... | collective-permute-start | bytes 1572872 | tf_op jit(solution)/shard_map/ppermute | solution.py:22
  48.9 9.2 %copy-start = (bf16[2,128,512]{2,1,0:T(8,128)(2,1)S(1)}, bf16[2,128,512]{2,1,0:T(8,128)(2,1)}, u32[]{:S(2)}) copy-start(bf16[2,128,512]{2,1,0:T(8,128)(2,1)} %get-tuple-element.21) | copy-start | bytes 786436
  49.0 9.2 %collective-permute-start.6 = (bf16[2,128,512]{2,1,0:T(8,128)(2,1)S(1)}, bf16[2,128,512]{2,1,0:T(8,128)(2,1)S(1)}, u32[]{:S(2)}, u32[]{:S(2)}) collective-permute-start(bf16[2,128,512]{2,1,0:T(8,128)(2,1)S(1)} %add_convert_fusion.2), channel_id=1, source_target_pairs={{4,0},{8,4},{12,8},{5,1},{9,5},{13,9},{6,2},{10,6},{14,10},{7,3},{... | collective-permute-start | bytes 786440 | tf_op jit(solution)/shard_map/ppermute | solution.py:28
  58.2 14.7 %collective-permute-start.8 = (bf16[2,128,512]{2,1,0:T(8,128)(2,1)S(1)}, bf16[2,128,512]{2,1,0:T(8,128)(2,1)S(1)}, u32[]{:S(2)}, u32[]{:S(2)}) collective-permute-start(bf16[2,128,512]{2,1,0:T(8,128)(2,1)S(1)} %add_convert_fusion.1), channel_id=1, source_target_pairs={{4,16},{8,20},{12,24},{20,0},{24,4},{28,8},{5,17},{9,21},{13,25},{... | collective-permute-start | bytes 786440 | tf_op jit(solution)/shard_map/ppermute | solution.py:188

commit v15 on v12

--- a/solution.py
+++ b/solution.py
@@ -45,10 +45,10 @@
     fixed_part = nearby | query_global[None, :, None] | key_global[:, None, :]
     table = (random_part | fixed_part[:, None, :, :]) & (key_shard >= 0)[:, None, None, None]
     expanded = jnp.repeat(table, tok_rows // query_blocks, axis=3)
-    return expanded.astype(jnp.float32)
-
-
-def piece_allowed(mask_ref, shift, group_size, tok_rows):
+    return jnp.where(expanded, 0.0, NEG_FILL).astype(jnp.float32)
+
+
+def piece_fill(mask_ref, shift, group_size, tok_rows):
     query_blocks = mask_ref.shape[2]
     rows = group_size * tok_rows
     parts = [
@@ -56,12 +56,12 @@
         for head in range(group_size)
         for block in range(query_blocks)
     ]
-    allowed = jnp.concatenate(parts, axis=0) > 0.5
+    fill = jnp.concatenate(parts, axis=0)
     if shift == 0:
         row = lax.broadcasted_iota(jnp.int32, (rows, tok_rows), 0)
         col = lax.broadcasted_iota(jnp.int32, (rows, tok_rows), 1)
-        allowed = allowed & (col <= row % tok_rows)
-    return allowed
+        fill = jnp.where(col <= row % tok_rows, fill, NEG_FILL)
+    return fill
 
 
 def dot_nt(a, b):
@@ -76,9 +76,9 @@
     return jnp.concatenate([ref[:, head * HD : (head + 1) * HD] for head in range(group_size)], axis=0)
 
 
-def all_allowed(mask_ref, piece_count, group_size, tok_rows):
+def all_fill(mask_ref, piece_count, group_size, tok_rows):
     return jnp.concatenate(
-        [piece_allowed(mask_ref, shift, group_size, tok_rows) for shift in range(piece_count)], axis=1
+        [piece_fill(mask_ref, shift, group_size, tok_rows) for shift in range(piece_count)], axis=1
     )
 
 
@@ -93,7 +93,7 @@
     all_keys = jnp.concatenate([ref[0] for ref in kv_refs], axis=0)
     all_values = jnp.concatenate([ref[1] for ref in kv_refs], axis=0)
     raw = dot_nt(query_rows, all_keys) * score_scale
-    masked = jnp.where(all_allowed(mask_ref, piece_count, group_size, tok_rows), raw, NEG_FILL)
+    masked = raw + all_fill(mask_ref, piece_count, group_size, tok_rows)
     row_high = jnp.max(masked, axis=1, keepdims=True)
     weights = jnp.exp(masked - row_high)
     row_total = jnp.sum(weights, axis=1, keepdims=True)
@@ -101,10 +101,9 @@
     attended = (accumulated / row_total).astype(out_ref.dtype)
     for head in range(group_size):
         out_ref[:, head * HD : (head + 1) * HD] = attended[head * tok_rows : (head + 1) * tok_rows]
-    log_total = row_high + jnp.log(row_total)
     delta = jnp.sum(grad_rows.astype(jnp.float32) * attended.astype(jnp.float32), axis=1, keepdims=True)
 
-    row_probs = jnp.exp(masked - log_total)
+    row_probs = weights * (1.0 / row_total)
     value_terms = dot_tn(row_probs.astype(jnp.bfloat16), grad_rows)
     prob_grads = dot_nt(grad_rows, all_values)
     score_grads = (row_probs * (prob_grads - delta)).astype(jnp.bfloat16)

time: 73.4 us -> 73.1 us (level)
    convert_element_type x2 -> x0, local copies, waits for them, and re-layouts: 0.91 us -> none  [block_masks(): return expanded.astype(jnp.float32)]
    select_n x0 -> x2, local copies, waits for them, and re-layouts: none -> 0.91 us  [block_masks(): return jnp.where(expanded, 0.0, NEG_FILL).astype(jnp.float32)]
where the time goes in v15:
time: 73.1 us; the launch traced here: 72.8 us
  waiting for transfers between devices  36.3 us (50%)
  starting transfers between devices  19.5 us (27%)
  Pallas kernels  7.48 us (10%)
  local copies, waits for them, and re-layouts  5.06 us (7%)
  other arithmetic  3.55 us (5%)
  between operations  0.83 us (1%)
    ppermute x6, waiting for transfers between devices, shifted_open(): return lax.ppermute(value, axis, pairs)  26.3 us
    ppermute x6, starting transfers between devices, shifted_open(): return lax.ppermute(value, axis, pairs)  16.8 us
    ppermute x3, waiting for transfers between devices, passed_along(): return lax.ppermute(value, axis, pairs)  9.99 us
    pallas_call x1, Pallas kernels, attention(): pl.pallas_call(functools.partial(attention_kernel, piece_count, group_siz...  7.48 us
    ppermute x3, starting transfers between devices, passed_along(): return lax.ppermute(value, axis, pairs)  2.72 us
    unnamed x20, local copies, waits for them, and re-layouts  2.36 us
  transfers between devices with their start and end apart: 9, of which 8 were waited for; matrix products, arithmetic and copies ran while one was open for 7% of the time, Pallas kernels for 0%

profile of v15, /device:TPU:0, one launch (start us, length us, event | category | flops | bytes accessed | tf_op | source)
XLA Modules:
  0.0 72.8 jit_solution(8085028464639912977)
XLA Ops:
  0.6 0.0 copy-start.2
  0.6 0.9 %constant_dynamic-update-slice_fusion.1 = bf16[2,128,512]{2,1,0:T(8,128)(2,1)S(1)} fusion(bf16[1,128,512]{2,1,0:T(8,128)(2,1)} %param.7), kind=kLoop, calls=%fused_computation.14 | loop fusion | bytes 262144
  1.6 0.0 copy-done.2
  1.6 0.0 copy-start.3
  1.6 7.0 %collective-permute-start.2 = (bf16[2,128,512]{2,1,0:T(8,128)(2,1)S(1)}, bf16[2,128,512]{2,1,0:T(8,128)(2,1)S(1)}, u32[]{:S(2)}, u32[]{:S(2)}) collective-permute-start(bf16[2,128,512]{2,1,0:T(8,128)(2,1)S(1)} %constant_dynamic-update-slice_fusion.refs_0_), channel_id=1, source_target_pairs={{0,12},{1,13},{2,14},{3,15},{16,28},{17,29},{18,30},{19,31}} | collective-permute-start | bytes 786440 | tf_op jit(solution)/shard_map/ppermute | solution.py:28
  8.6 1.3 %collective-permute-start = (bf16[2,128,512]{2,1,0:T(8,128)(2,1)S(1)}, bf16[2,128,512]{2,1,0:T(8,128)(2,1)S(1)}, u32[]{:S(2)}, u32[]{:S(2)}) collective-permute-start(bf16[2,128,512]{2,1,0:T(8,128)(2,1)S(1)} %constant_dynamic-update-slice_fusion.refs_0_), channel_id=1, source_target_pairs={{0,4},{4,8},{8,12},{1,5},{5,9},{9,13},{2,6},{6,10},{10,14},{3,7},{... | collective-permute-start | bytes 786440 | tf_op jit(solution)/shard_map/ppermute | solution.py:28
  9.9 0.1 compare_and_fusion
  10.0 0.1 iota_add_fusion
  10.1 0.1 min.12
  10.2 0.1 copy.14
  10.3 0.0 copy-start.5
  10.3 0.7 copy-done.5
  10.9 0.2 compare_reduce_fusion.1
  11.1 0.0 copy-start.4
  11.1 0.2 compare_reduce_fusion
  11.4 0.1 copy.15
  11.5 0.1 or_or_fusion
  11.5 8.3 %collective-permute-done.refs_1_ = bf16[2,128,512]{2,1,0:T(8,128)(2,1)S(1)} collective-permute-done((bf16[2,128,512]{2,1,0:T(8,128)(2,1)S(1)}, bf16[2,128,512]{2,1,0:T(8,128)(2,1)S(1)}, u32[]{:S(2)}, u32[]{:S(2)}) %collective-permute-start) | collective-permute-done | bytes 262176 | tf_op jit(solution)/shard_map/ppermute | solution.py:28
  19.8 0.0 copy-start.7
  19.8 4.4 %collective-permute-start.1 = (bf16[2,128,512]{2,1,0:T(8,128)(2,1)S(1)}, bf16[2,128,512]{2,1,0:T(8,128)(2,1)S(1)}, u32[]{:S(2)}, u32[]{:S(2)}) collective-permute-start(bf16[2,128,512]{2,1,0:T(8,128)(2,1)S(1)} %collective-permute-done.refs_1_), channel_id=1, source_target_pairs={{0,4},{4,8},{8,12},{1,5},{5,9},{9,13},{2,6},{6,10},{10,14},{3,7},{... | collective-permute-start | bytes 786440 | tf_op jit(solution)/shard_map/ppermute | solution.py:28
  24.2 0.0 copy-done.4
  24.2 0.6 gather_fusion
  24.8 0.1 fusion.1
  24.9 0.1 copy.16
  25.0 0.2 broadcast_in_dim.41
  25.2 0.8 %select_n.45.mask_ref = f32[4,16,2,128]{3,2,1,0:T(2,128)} reshape(f32[4,16,2,2,64]{4,3,2,1,0:T(2,128)S(1)} %broadcast_in_dim.41) | data formatting | bytes 131072 | tf_op jit(solution)/shard_map/jit(_where)/select_n | solution.py:48
  26.0 0.0 copy-done.3
  26.0 0.0 copy-done.7
  26.0 0.0 collective-permute-done.2.refs_3_
  26.0 0.0 copy-start.6
  26.1 2.9 %collective-permute-done.1.refs_2_ = bf16[2,128,512]{2,1,0:T(8,128)(2,1)S(1)} collective-permute-done((bf16[2,128,512]{2,1,0:T(8,128)(2,1)S(1)}, bf16[2,128,512]{2,1,0:T(8,128)(2,1)S(1)}, u32[]{:S(2)}, u32[]{:S(2)}) %collective-permute-start.1) | collective-permute-done | bytes 262176 | tf_op jit(solution)/shard_map/ppermute | solution.py:28
  28.9 0.0 copy-start.8
  28.9 0.0 copy-done.6
  28.9 0.7 copy-done.8
  29.6 7.5 %shard_map.93 = (bf16[128,2048]{1,0:T(8,128)(2,1)}, bf16[128,2048]{1,0:T(8,128)(2,1)}, bf16[2,128,512]{2,1,0:T(8,128)(2,1)}, bf16[2,128,512]{2,1,0:T(8,128)(2,1)...) custom-call(bf16[128,2048]{1,0:T(8,128)(2,1)} %bitcast.23, bf16[128,2048]{1,0:T(8,128)(2,1)} %bitcast.24, ...), custom_call_target="tpu_custom_call" | custom-call | flops 1610612736 | bytes 4194304 | tf_op jit(solution)/shard_map/pallas_call | solution.py:129
  37.1 1.6 %collective-permute-start.3 = (bf16[1,128,2048]{2,1,0:T(8,128)(2,1)}, bf16[1,128,2048]{2,1,0:T(8,128)(2,1)S(1)}, u32[]{:S(2)}, u32[]{:S(2)}) collective-permute-start(bf16[1,128,2048]{2,1,0:T(8,128)(2,1)} %bitcast.26), channel_id=1, source_target_pairs={{0,16},{16,0},{1,17},{17,1},{2,18},{18,2},{3,19},{19,3},{4,20},{20... | collective-permute-start | bytes 1572872 | tf_op jit(solution)/shard_map/ppermute | solution.py:22
  38.7 1.3 %collective-permute-start.4 = (bf16[2,128,512]{2,1,0:T(8,128)(2,1)}, bf16[2,128,512]{2,1,0:T(8,128)(2,1)S(1)}, u32[]{:S(2)}, u32[]{:S(2)}) collective-permute-start(bf16[2,128,512]{2,1,0:T(8,128)(2,1)} %get-tuple-element.16), channel_id=1, source_target_pairs={{4,0},{8,4},{12,8},{5,1},{9,5},{13,9},{6,2},{10,6},{14,10},{7,3},{... | collective-permute-start | bytes 786440 | tf_op jit(solution)/shard_map/ppermute | solution.py:28
  40.0 0.6 collective-permute-start.6
  40.5 7.1 %collective-permute-done.4 = bf16[2,128,512]{2,1,0:T(8,128)(2,1)S(1)} collective-permute-done((bf16[2,128,512]{2,1,0:T(8,128)(2,1)}, bf16[2,128,512]{2,1,0:T(8,128)(2,1)S(1)}, u32[]{:S(2)}, u32[]{:S(2)}) %collective-permute-start.4) | collective-permute-done | bytes 262176 | tf_op jit(solution)/shard_map/ppermute | solution.py:28
  47.6 1.0 %add_convert_fusion.2 = bf16[2,128,512]{2,1,0:T(8,128)(2,1)S(1)} fusion(bf16[2,128,512]{2,1,0:T(8,128)(2,1)S(1)} %collective-permute-done.4, bf16[2,128,512]{2,1,0:T(8,128)(2,1)} %get-tuple-element.15), kind=kLoop, calls=%fused_computation.3 | loop fusion | flops 524288 | bytes 786432 | tf_op jit(solution)/shard_map/convert_element_type | solution.py:177
  48.6 0.0 copy-start.1
  48.6 1.4 %collective-permute-start.5 = (bf16[2,128,512]{2,1,0:T(8,128)(2,1)S(1)}, bf16[2,128,512]{2,1,0:T(8,128)(2,1)S(1)}, u32[]{:S(2)}, u32[]{:S(2)}) collective-permute-start(bf16[2,128,512]{2,1,0:T(8,128)(2,1)S(1)} %add_convert_fusion.2), channel_id=1, source_target_pairs={{4,0},{8,4},{12,8},{5,1},{9,5},{13,9},{6,2},{10,6},{14,10},{7,3},{... | collective-permute-start | bytes 786440 | tf_op jit(solution)/shard_map/ppermute | solution.py:28
  50.1 2.2 %collective-permute-done.3 = bf16[1,128,2048]{2,1,0:T(8,128)(2,1)S(1)} collective-permute-done((bf16[1,128,2048]{2,1,0:T(8,128)(2,1)}, bf16[1,128,2048]{2,1,0:T(8,128)(2,1)S(1)}, u32[]{:S(2)}, u32[]{:S(2)}) %collective-permute-start.3) | collective-permute-done | bytes 524320 | tf_op jit(solution)/shard_map/ppermute | solution.py:22
  52.2 0.8 %broadcast_select_fusion.1 = bf16[1,128,2048]{2,1,0:T(8,128)(2,1)} fusion(bf16[1,128,2048]{2,1,0:T(8,128)(2,1)S(1)} %collective-permute-done.3, pred[]{:T(512)S(6)} %lt.20), kind=kLoop, calls=%fused_computation.5 | loop fusion | flops 262144 | bytes 1048577 | tf_op jit(solution)/shard_map/jit(_where)/select_n | solution.py:174
  53.1 4.0 %collective-permute-done.5 = bf16[2,128,512]{2,1,0:T(8,128)(2,1)S(1)} collective-permute-done((bf16[2,128,512]{2,1,0:T(8,128)(2,1)S(1)}, bf16[2,128,512]{2,1,0:T(8,128)(2,1)S(1)}, u32[]{:S(2)}, u32[]{:S(2)}) %collective-permute-start.5) | collective-permute-done | bytes 262176 | tf_op jit(solution)/shard_map/ppermute | solution.py:28
  57.0 0.0 copy-done.1
  57.0 0.1 add_convert_fusion.1
  57.1 0.0 copy-start
  57.1 1.4 %collective-permute-start.7 = (bf16[2,128,512]{2,1,0:T(8,128)(2,1)S(1)}, bf16[2,128,512]{2,1,0:T(8,128)(2,1)S(1)}, u32[]{:S(2)}, u32[]{:S(2)}) collective-permute-start(bf16[2,128,512]{2,1,0:T(8,128)(2,1)S(1)} %add_convert_fusion.1), channel_id=1, source_target_pairs={{4,0},{8,4},{12,8},{5,1},{9,5},{13,9},{6,2},{10,6},{14,10},{7,3},{... | collective-permute-start | bytes 786440 | tf_op jit(solution)/shard_map/ppermute | solution.py:28
  58.6 2.0 %collective-permute-done.6 = bf16[1,128,2048]{2,1,0:T(8,128)(2,1)S(1)} collective-permute-done((bf16[1,128,2048]{2,1,0:T(8,128)(2,1)}, bf16[1,128,2048]{2,1,0:T(8,128)(2,1)S(1)}, u32[]{:S(2)}, u32[]{:S(2)}) %collective-permute-start.6) | collective-permute-done | bytes 524320 | tf_op jit(solution)/shard_map/ppermute | solution.py:22
  60.5 0.8 %broadcast_select_fusion = bf16[1,128,2048]{2,1,0:T(8,128)(2,1)} fusion(bf16[1,128,2048]{2,1,0:T(8,128)(2,1)S(1)} %collective-permute-done.6, pred[]{:T(512)S(6)} %lt.20), kind=kLoop, calls=%fused_computation.4 | loop fusion | flops 262144 | bytes 1048577 | tf_op jit(solution)/shard_map/jit(_where)/select_n | solution.py:180
  61.4 4.2 %collective-permute-done.7 = bf16[2,128,512]{2,1,0:T(8,128)(2,1)S(1)} collective-permute-done((bf16[2,128,512]{2,1,0:T(8,128)(2,1)S(1)}, bf16[2,128,512]{2,1,0:T(8,128)(2,1)S(1)}, u32[]{:S(2)}, u32[]{:S(2)}) %collective-permute-start.7) | collective-permute-done | bytes 262176 | tf_op jit(solution)/shard_map/ppermute | solution.py:28
  65.5 0.0 copy-done
  65.5 0.1 add_convert_fusion
  65.6 0.6 collective-permute-start.8
  66.2 5.9 %collective-permute-done.8 = bf16[2,128,512]{2,1,0:T(8,128)(2,1)S(1)} collective-permute-done((bf16[2,128,512]{2,1,0:T(8,128)(2,1)S(1)}, bf16[2,128,512]{2,1,0:T(8,128)(2,1)S(1)}, u32[]{:S(2)}, u32[]{:S(2)}) %collective-permute-start.8) | collective-permute-done | bytes 262176 | tf_op jit(solution)/shard_map/ppermute | solution.py:22
  72.0 0.7 fusion.5
  (7 shorter events, 0.0 us)
Async XLA Ops:
  0.6 1.0 %copy-start.2 = (bf16[1,128,512]{2,1,0:T(8,128)(2,1)S(1)}, bf16[1,128,512]{2,1,0:T(8,128)(2,1)}, u32[]{:S(2)}) copy-start(bf16[1,128,512]{2,1,0:T(8,128)(2,1)} %param.8) | copy-start | bytes 393220
  1.6 24.4 %copy-start.3 = (bf16[2,128,512]{2,1,0:T(8,128)(2,1)}, bf16[2,128,512]{2,1,0:T(8,128)(2,1)S(1)}, u32[]{:S(2)}) copy-start(bf16[2,128,512]{2,1,0:T(8,128)(2,1)S(1)} %constant_dynamic-update-slice_fusion.refs_0_) | copy-start | bytes 786436
  1.6 24.4 %collective-permute-start.2 = (bf16[2,128,512]{2,1,0:T(8,128)(2,1)S(1)}, bf16[2,128,512]{2,1,0:T(8,128)(2,1)S(1)}, u32[]{:S(2)}, u32[]{:S(2)}) collective-permute-start(bf16[2,128,512]{2,1,0:T(8,128)(2,1)S(1)} %constant_dynamic-update-slice_fusion.refs_0_), channel_id=1, source_target_pairs={{0,12},{1,13},{2,14},{3,15},{16,28},{17,29},{18,30},{19,31}} | collective-permute-start | bytes 786440 | tf_op jit(solution)/shard_map/ppermute | solution.py:28
  8.6 11.2 %collective-permute-start = (bf16[2,128,512]{2,1,0:T(8,128)(2,1)S(1)}, bf16[2,128,512]{2,1,0:T(8,128)(2,1)S(1)}, u32[]{:S(2)}, u32[]{:S(2)}) collective-permute-start(bf16[2,128,512]{2,1,0:T(8,128)(2,1)S(1)} %constant_dynamic-update-slice_fusion.refs_0_), channel_id=1, source_target_pairs={{0,4},{4,8},{8,12},{1,5},{5,9},{9,13},{2,6},{6,10},{10,14},{3,7},{... | collective-permute-start | bytes 786440 | tf_op jit(solution)/shard_map/ppermute | solution.py:28
  10.3 0.7 copy-start.5
  11.1 13.1 %copy-start.4 = (s32[1,2,16,8]{2,3,1,0:T(8,128)S(1)}, s32[1,2,16,8]{2,3,1,0:T(8,128)}, u32[]{:S(2)}) copy-start(s32[1,2,16,8]{2,3,1,0:T(8,128)} %param.10) | copy-start | bytes 3076
  19.8 6.2 %copy-start.7 = (bf16[2,128,512]{2,1,0:T(8,128)(2,1)}, bf16[2,128,512]{2,1,0:T(8,128)(2,1)S(1)}, u32[]{:S(2)}) copy-start(bf16[2,128,512]{2,1,0:T(8,128)(2,1)S(1)} %collective-permute-done.refs_1_) | copy-start | bytes 786436
  19.8 9.1 %collective-permute-start.1 = (bf16[2,128,512]{2,1,0:T(8,128)(2,1)S(1)}, bf16[2,128,512]{2,1,0:T(8,128)(2,1)S(1)}, u32[]{:S(2)}, u32[]{:S(2)}) collective-permute-start(bf16[2,128,512]{2,1,0:T(8,128)(2,1)S(1)} %collective-permute-done.refs_1_), channel_id=1, source_target_pairs={{0,4},{4,8},{8,12},{1,5},{5,9},{9,13},{2,6},{6,10},{10,14},{3,7},{... | collective-permute-start | bytes 786440 | tf_op jit(solution)/shard_map/ppermute | solution.py:28
  26.0 2.9 %copy-start.6 = (bf16[2,128,512]{2,1,0:T(8,128)(2,1)}, bf16[2,128,512]{2,1,0:T(8,128)(2,1)S(1)}, u32[]{:S(2)}) copy-start(bf16[2,128,512]{2,1,0:T(8,128)(2,1)S(1)} %collective-permute-done.2.refs_3_) | copy-start | bytes 786436
  28.9 0.7 copy-start.8
  37.1 15.1 %collective-permute-start.3 = (bf16[1,128,2048]{2,1,0:T(8,128)(2,1)}, bf16[1,128,2048]{2,1,0:T(8,128)(2,1)S(1)}, u32[]{:S(2)}, u32[]{:S(2)}) collective-permute-start(bf16[1,128,2048]{2,1,0:T(8,128)(2,1)} %bitcast.26), channel_id=1, source_target_pairs={{0,16},{16,0},{1,17},{17,1},{2,18},{18,2},{3,19},{19,3},{4,20},{20... | collective-permute-start | bytes 1572872 | tf_op jit(solution)/shard_map/ppermute | solution.py:22
  38.7 8.9 %collective-permute-start.4 = (bf16[2,128,512]{2,1,0:T(8,128)(2,1)}, bf16[2,128,512]{2,1,0:T(8,128)(2,1)S(1)}, u32[]{:S(2)}, u32[]{:S(2)}) collective-permute-start(bf16[2,128,512]{2,1,0:T(8,128)(2,1)} %get-tuple-element.16), channel_id=1, source_target_pairs={{4,0},{8,4},{12,8},{5,1},{9,5},{13,9},{6,2},{10,6},{14,10},{7,3},{... | collective-permute-start | bytes 786440 | tf_op jit(solution)/shard_map/ppermute | solution.py:28
  40.0 20.6 %collective-permute-start.6 = (bf16[1,128,2048]{2,1,0:T(8,128)(2,1)}, bf16[1,128,2048]{2,1,0:T(8,128)(2,1)S(1)}, u32[]{:S(2)}, u32[]{:S(2)}) collective-permute-start(bf16[1,128,2048]{2,1,0:T(8,128)(2,1)} %bitcast.25), channel_id=1, source_target_pairs={{0,16},{16,0},{1,17},{17,1},{2,18},{18,2},{3,19},{19,3},{4,20},{20... | collective-permute-start | bytes 1572872 | tf_op jit(solution)/shard_map/ppermute | solution.py:22
  48.6 8.4 %copy-start.1 = (bf16[2,128,512]{2,1,0:T(8,128)(2,1)S(1)}, bf16[2,128,512]{2,1,0:T(8,128)(2,1)}, u32[]{:S(2)}) copy-start(bf16[2,128,512]{2,1,0:T(8,128)(2,1)} %get-tuple-element.19) | copy-start | bytes 786436
  48.6 8.4 %collective-permute-start.5 = (bf16[2,128,512]{2,1,0:T(8,128)(2,1)S(1)}, bf16[2,128,512]{2,1,0:T(8,128)(2,1)S(1)}, u32[]{:S(2)}, u32[]{:S(2)}) collective-permute-start(bf16[2,128,512]{2,1,0:T(8,128)(2,1)S(1)} %add_convert_fusion.2), channel_id=1, source_target_pairs={{4,0},{8,4},{12,8},{5,1},{9,5},{13,9},{6,2},{10,6},{14,10},{7,3},{... | collective-permute-start | bytes 786440 | tf_op jit(solution)/shard_map/ppermute | solution.py:28
  57.1 8.4 %copy-start = (bf16[2,128,512]{2,1,0:T(8,128)(2,1)S(1)}, bf16[2,128,512]{2,1,0:T(8,128)(2,1)}, u32[]{:S(2)}) copy-start(bf16[2,128,512]{2,1,0:T(8,128)(2,1)} %get-tuple-element.22) | copy-start | bytes 786436
  57.1 8.4 %collective-permute-start.7 = (bf16[2,128,512]{2,1,0:T(8,128)(2,1)S(1)}, bf16[2,128,512]{2,1,0:T(8,128)(2,1)S(1)}, u32[]{:S(2)}, u32[]{:S(2)}) collective-permute-start(bf16[2,128,512]{2,1,0:T(8,128)(2,1)S(1)} %add_convert_fusion.1), channel_id=1, source_target_pairs={{4,0},{8,4},{12,8},{5,1},{9,5},{13,9},{6,2},{10,6},{14,10},{7,3},{... | collective-permute-start | bytes 786440 | tf_op jit(solution)/shard_map/ppermute | solution.py:28
  65.6 6.4 %collective-permute-start.8 = (bf16[2,128,512]{2,1,0:T(8,128)(2,1)S(1)}, bf16[2,128,512]{2,1,0:T(8,128)(2,1)S(1)}, u32[]{:S(2)}, u32[]{:S(2)}) collective-permute-start(bf16[2,128,512]{2,1,0:T(8,128)(2,1)S(1)} %add_convert_fusion), channel_id=1, source_target_pairs={{0,16},{16,0},{1,17},{17,1},{2,18},{18,2},{3,19},{19,3},{4,20},{20... | collective-permute-start | bytes 786440 | tf_op jit(solution)/shard_map/ppermute | solution.py:22

commit v16 on v15

--- a/solution.py
+++ b/solution.py
@@ -82,25 +82,28 @@
     )
 
 
-def attention_kernel(piece_count, group_size, query_ref, grad_ref, mask_ref, *refs):
-    kv_refs = refs[:piece_count]
-    out_ref, dq_ref = refs[piece_count : piece_count + 2]
-    dkv_refs = refs[piece_count + 2 :]
+def group_kernel(piece_count, group_size, sub, query_ref, grad_ref, mask_ref, kv_refs, out_ref, dq_ref, dkv_refs):
     tok_rows = query_ref.shape[0]
     score_scale = HD ** (-0.5)
-    query_rows = stacked(query_ref, group_size)
-    grad_rows = stacked(grad_ref, group_size)
-    all_keys = jnp.concatenate([ref[0] for ref in kv_refs], axis=0)
-    all_values = jnp.concatenate([ref[1] for ref in kv_refs], axis=0)
+    width = group_size * HD
+    cols = slice(sub * width, (sub + 1) * width)
+    lanes = slice(sub * HD, (sub + 1) * HD)
+    heads = slice(sub * group_size, (sub + 1) * group_size)
+    query_rows = stacked(query_ref.at[:, cols], group_size)
+    grad_rows = stacked(grad_ref.at[:, cols], group_size)
+    all_keys = jnp.concatenate([ref[0, :, lanes] for ref in kv_refs], axis=0)
+    all_values = jnp.concatenate([ref[1, :, lanes] for ref in kv_refs], axis=0)
     raw = dot_nt(query_rows, all_keys) * score_scale
-    masked = raw + all_fill(mask_ref, piece_count, group_size, tok_rows)
+    masked = raw + all_fill(mask_ref.at[:, heads], piece_count, group_size, tok_rows)
     row_high = jnp.max(masked, axis=1, keepdims=True)
     weights = jnp.exp(masked - row_high)
     row_total = jnp.sum(weights, axis=1, keepdims=True)
     accumulated = jnp.dot(weights.astype(jnp.bfloat16), all_values, preferred_element_type=jnp.float32)
     attended = (accumulated / row_total).astype(out_ref.dtype)
     for head in range(group_size):
-        out_ref[:, head * HD : (head + 1) * HD] = attended[head * tok_rows : (head + 1) * tok_rows]
+        out_ref[:, sub * width + head * HD : sub * width + (head + 1) * HD] = attended[
+            head * tok_rows : (head + 1) * tok_rows
+        ]
     delta = jnp.sum(grad_rows.astype(jnp.float32) * attended.astype(jnp.float32), axis=1, keepdims=True)
 
     row_probs = weights * (1.0 / row_total)
@@ -111,28 +114,41 @@
     key_terms = dot_tn(score_grads, query_rows) * score_scale
     for shift, ref in enumerate(dkv_refs):
         piece_rows = slice(shift * tok_rows, (shift + 1) * tok_rows)
-        ref[0] = key_terms[piece_rows].astype(ref.dtype)
-        ref[1] = value_terms[piece_rows].astype(ref.dtype)
+        ref[0, :, lanes] = key_terms[piece_rows].astype(ref.dtype)
+        ref[1, :, lanes] = value_terms[piece_rows].astype(ref.dtype)
     query_grad = (query_grad * score_scale).astype(dq_ref.dtype)
     for head in range(group_size):
-        dq_ref[:, head * HD : (head + 1) * HD] = query_grad[head * tok_rows : (head + 1) * tok_rows]
+        dq_ref[:, sub * width + head * HD : sub * width + (head + 1) * HD] = query_grad[
+            head * tok_rows : (head + 1) * tok_rows
+        ]
+
+
+def attention_kernel(piece_count, group_size, per_step, query_ref, grad_ref, mask_ref, *refs):
+    kv_refs = refs[:piece_count]
+    out_ref, dq_ref = refs[piece_count : piece_count + 2]
+    dkv_refs = refs[piece_count + 2 :]
+    for sub in range(per_step):
+        group_kernel(
+            piece_count, group_size, sub, query_ref, grad_ref, mask_ref, kv_refs, out_ref, dq_ref, dkv_refs
+        )
 
 
 def attention(query_rows, grad_rows, pieces, masks):
     tok_rows, query_width = query_rows.shape
     piece_count = len(pieces)
     group_size = H // KVH
-    group_width = group_size * HD
+    per_step = 2 if KVH % 2 == 0 else 1
+    group_width = group_size * HD * per_step
     flops = 12 * tok_rows * tok_rows * HD * H * piece_count
-    piece_block = pl.BlockSpec((2, tok_rows, HD), lambda g: (0, 0, g))
+    piece_block = pl.BlockSpec((2, tok_rows, HD * per_step), lambda g: (0, 0, g))
     group_block = pl.BlockSpec((tok_rows, group_width), lambda g: (0, g))
     outs = pl.pallas_call(
-        functools.partial(attention_kernel, piece_count, group_size),
-        grid=(KVH,),
+        functools.partial(attention_kernel, piece_count, group_size, per_step),
+        grid=(KVH // per_step,),
         in_specs=[
             group_block,
             group_block,
-            pl.BlockSpec((piece_count, group_size) + masks.shape[2:], lambda g: (0, g, 0, 0)),
+            pl.BlockSpec((piece_count, group_size * per_step) + masks.shape[2:], lambda g: (0, g, 0, 0)),
         ]
         + [piece_block] * piece_count,
         out_specs=[group_block, group_block] + [piece_block] * piece_count,

time: 73.1 us -> 72.9 us (level)
  transfers between devices with their start and end apart: 9 -> 9, of which waited for: 8 -> 8; matrix products, arithmetic and copies ran while one was open for 7% -> 8% of each run, Pallas kernels for 0% -> 0%
where the time goes in v16:
time: 72.9 us; the launch traced here: 72.6 us
  waiting for transfers between devices  36.3 us (50%)
  starting transfers between devices  19.5 us (27%)
  Pallas kernels  7.34 us (10%)
  local copies, waits for them, and re-layouts  5.06 us (7%)
  other arithmetic  3.55 us (5%)
  between operations  0.83 us (1%)
    ppermute x6, waiting for transfers between devices, shifted_open(): return lax.ppermute(value, axis, pairs)  26.3 us
    ppermute x6, starting transfers between devices, shifted_open(): return lax.ppermute(value, axis, pairs)  16.8 us
    ppermute x3, waiting for transfers between devices, passed_along(): return lax.ppermute(value, axis, pairs)  10 us
    pallas_call x1, Pallas kernels, attention(): pl.pallas_call(functools.partial(attention_kernel, piece_count, group_siz...  7.34 us
    ppermute x3, starting transfers between devices, passed_along(): return lax.ppermute(value, axis, pairs)  2.73 us
    unnamed x20, local copies, waits for them, and re-layouts  2.36 us
  transfers between devices with their start and end apart: 9, of which 8 were waited for; matrix products, arithmetic and copies ran while one was open for 8% of the time, Pallas kernels for 0%

profile of v16, /device:TPU:0, one launch (start us, length us, event | category | flops | bytes accessed | tf_op | source)
XLA Modules:
  0.0 72.6 jit_solution(3556289790658299187)
XLA Ops:
  0.6 0.0 copy-start.2
  0.6 0.9 %constant_dynamic-update-slice_fusion.1 = bf16[2,128,512]{2,1,0:T(8,128)(2,1)S(1)} fusion(bf16[1,128,512]{2,1,0:T(8,128)(2,1)} %param.7), kind=kLoop, calls=%fused_computation.14 | loop fusion | bytes 262144
  1.6 0.0 copy-done.2
  1.6 0.0 copy-start.3
  1.6 7.0 %collective-permute-start.2 = (bf16[2,128,512]{2,1,0:T(8,128)(2,1)S(1)}, bf16[2,128,512]{2,1,0:T(8,128)(2,1)S(1)}, u32[]{:S(2)}, u32[]{:S(2)}) collective-permute-start(bf16[2,128,512]{2,1,0:T(8,128)(2,1)S(1)} %constant_dynamic-update-slice_fusion.refs_0_), channel_id=1, source_target_pairs={{0,12},{1,13},{2,14},{3,15},{16,28},{17,29},{18,30},{19,31}} | collective-permute-start | bytes 786440 | tf_op jit(solution)/shard_map/ppermute | solution.py:28
  8.6 1.3 %collective-permute-start = (bf16[2,128,512]{2,1,0:T(8,128)(2,1)S(1)}, bf16[2,128,512]{2,1,0:T(8,128)(2,1)S(1)}, u32[]{:S(2)}, u32[]{:S(2)}) collective-permute-start(bf16[2,128,512]{2,1,0:T(8,128)(2,1)S(1)} %constant_dynamic-update-slice_fusion.refs_0_), channel_id=1, source_target_pairs={{0,4},{4,8},{8,12},{1,5},{5,9},{9,13},{2,6},{6,10},{10,14},{3,7},{... | collective-permute-start | bytes 786440 | tf_op jit(solution)/shard_map/ppermute | solution.py:28
  9.9 0.1 compare_and_fusion
  10.0 0.1 iota_add_fusion
  10.1 0.1 min.12
  10.2 0.1 copy.14
  10.3 0.0 copy-start.5
  10.3 0.7 copy-done.5
  10.9 0.2 compare_reduce_fusion.1
  11.1 0.0 copy-start.4
  11.1 0.2 compare_reduce_fusion
  11.4 0.1 copy.15
  11.5 0.1 or_or_fusion
  11.5 8.3 %collective-permute-done.refs_1_ = bf16[2,128,512]{2,1,0:T(8,128)(2,1)S(1)} collective-permute-done((bf16[2,128,512]{2,1,0:T(8,128)(2,1)S(1)}, bf16[2,128,512]{2,1,0:T(8,128)(2,1)S(1)}, u32[]{:S(2)}, u32[]{:S(2)}) %collective-permute-start) | collective-permute-done | bytes 262176 | tf_op jit(solution)/shard_map/ppermute | solution.py:28
  19.8 0.0 copy-start.7
  19.8 4.4 %collective-permute-start.1 = (bf16[2,128,512]{2,1,0:T(8,128)(2,1)S(1)}, bf16[2,128,512]{2,1,0:T(8,128)(2,1)S(1)}, u32[]{:S(2)}, u32[]{:S(2)}) collective-permute-start(bf16[2,128,512]{2,1,0:T(8,128)(2,1)S(1)} %collective-permute-done.refs_1_), channel_id=1, source_target_pairs={{0,4},{4,8},{8,12},{1,5},{5,9},{9,13},{2,6},{6,10},{10,14},{3,7},{... | collective-permute-start | bytes 786440 | tf_op jit(solution)/shard_map/ppermute | solution.py:28
  24.2 0.0 copy-done.4
  24.2 0.6 gather_fusion
  24.8 0.1 fusion.1
  24.9 0.1 copy.16
  25.0 0.2 broadcast_in_dim.41
  25.2 0.8 %select_n.45.mask_ref = f32[4,16,2,128]{3,2,1,0:T(2,128)} reshape(f32[4,16,2,2,64]{4,3,2,1,0:T(2,128)S(1)} %broadcast_in_dim.41) | data formatting | bytes 131072 | tf_op jit(solution)/shard_map/jit(_where)/select_n | solution.py:48
  26.0 0.0 copy-done.3
  26.0 0.0 copy-done.7
  26.0 0.0 collective-permute-done.2.refs_3_
  26.0 0.0 copy-start.6
  26.1 2.9 %collective-permute-done.1.refs_2_ = bf16[2,128,512]{2,1,0:T(8,128)(2,1)S(1)} collective-permute-done((bf16[2,128,512]{2,1,0:T(8,128)(2,1)S(1)}, bf16[2,128,512]{2,1,0:T(8,128)(2,1)S(1)}, u32[]{:S(2)}, u32[]{:S(2)}) %collective-permute-start.1) | collective-permute-done | bytes 262176 | tf_op jit(solution)/shard_map/ppermute | solution.py:28
  28.9 0.0 copy-start.8
  28.9 0.0 copy-done.6
  28.9 0.7 copy-done.8
  29.6 7.3 %shard_map.93 = (bf16[128,2048]{1,0:T(8,128)(2,1)}, bf16[128,2048]{1,0:T(8,128)(2,1)}, bf16[2,128,512]{2,1,0:T(8,128)(2,1)}, bf16[2,128,512]{2,1,0:T(8,128)(2,1)...) custom-call(bf16[128,2048]{1,0:T(8,128)(2,1)} %bitcast.23, bf16[128,2048]{1,0:T(8,128)(2,1)} %bitcast.24, ...), custom_call_target="tpu_custom_call" | custom-call | flops 1610612736 | bytes 4194304 | tf_op jit(solution)/shard_map/pallas_call | solution.py:145
  37.0 1.6 %collective-permute-start.3 = (bf16[1,128,2048]{2,1,0:T(8,128)(2,1)}, bf16[1,128,2048]{2,1,0:T(8,128)(2,1)S(1)}, u32[]{:S(2)}, u32[]{:S(2)}) collective-permute-start(bf16[1,128,2048]{2,1,0:T(8,128)(2,1)} %bitcast.26), channel_id=1, source_target_pairs={{0,16},{16,0},{1,17},{17,1},{2,18},{18,2},{3,19},{19,3},{4,20},{20... | collective-permute-start | bytes 1572872 | tf_op jit(solution)/shard_map/ppermute | solution.py:22
  38.5 1.3 %collective-permute-start.4 = (bf16[2,128,512]{2,1,0:T(8,128)(2,1)}, bf16[2,128,512]{2,1,0:T(8,128)(2,1)S(1)}, u32[]{:S(2)}, u32[]{:S(2)}) collective-permute-start(bf16[2,128,512]{2,1,0:T(8,128)(2,1)} %get-tuple-element.16), channel_id=1, source_target_pairs={{4,0},{8,4},{12,8},{5,1},{9,5},{13,9},{6,2},{10,6},{14,10},{7,3},{... | collective-permute-start | bytes 786440 | tf_op jit(solution)/shard_map/ppermute | solution.py:28
  39.8 0.6 collective-permute-start.6
  40.4 7.1 %collective-permute-done.4 = bf16[2,128,512]{2,1,0:T(8,128)(2,1)S(1)} collective-permute-done((bf16[2,128,512]{2,1,0:T(8,128)(2,1)}, bf16[2,128,512]{2,1,0:T(8,128)(2,1)S(1)}, u32[]{:S(2)}, u32[]{:S(2)}) %collective-permute-start.4) | collective-permute-done | bytes 262176 | tf_op jit(solution)/shard_map/ppermute | solution.py:28
  47.5 1.0 %add_convert_fusion.2 = bf16[2,128,512]{2,1,0:T(8,128)(2,1)S(1)} fusion(bf16[2,128,512]{2,1,0:T(8,128)(2,1)S(1)} %collective-permute-done.4, bf16[2,128,512]{2,1,0:T(8,128)(2,1)} %get-tuple-element.15), kind=kLoop, calls=%fused_computation.3 | loop fusion | flops 524288 | bytes 786432 | tf_op jit(solution)/shard_map/convert_element_type | solution.py:193
  48.5 0.0 copy-start.1
  48.5 1.4 %collective-permute-start.5 = (bf16[2,128,512]{2,1,0:T(8,128)(2,1)S(1)}, bf16[2,128,512]{2,1,0:T(8,128)(2,1)S(1)}, u32[]{:S(2)}, u32[]{:S(2)}) collective-permute-start(bf16[2,128,512]{2,1,0:T(8,128)(2,1)S(1)} %add_convert_fusion.2), channel_id=1, source_target_pairs={{4,0},{8,4},{12,8},{5,1},{9,5},{13,9},{6,2},{10,6},{14,10},{7,3},{... | collective-permute-start | bytes 786440 | tf_op jit(solution)/shard_map/ppermute | solution.py:28
  49.9 2.2 %collective-permute-done.3 = bf16[1,128,2048]{2,1,0:T(8,128)(2,1)S(1)} collective-permute-done((bf16[1,128,2048]{2,1,0:T(8,128)(2,1)}, bf16[1,128,2048]{2,1,0:T(8,128)(2,1)S(1)}, u32[]{:S(2)}, u32[]{:S(2)}) %collective-permute-start.3) | collective-permute-done | bytes 524320 | tf_op jit(solution)/shard_map/ppermute | solution.py:22
  52.1 0.8 %broadcast_select_fusion.1 = bf16[1,128,2048]{2,1,0:T(8,128)(2,1)} fusion(bf16[1,128,2048]{2,1,0:T(8,128)(2,1)S(1)} %collective-permute-done.3, pred[]{:T(512)S(6)} %lt.20), kind=kLoop, calls=%fused_computation.5 | loop fusion | flops 262144 | bytes 1048577 | tf_op jit(solution)/shard_map/jit(_where)/select_n | solution.py:190
  52.9 4.0 %collective-permute-done.5 = bf16[2,128,512]{2,1,0:T(8,128)(2,1)S(1)} collective-permute-done((bf16[2,128,512]{2,1,0:T(8,128)(2,1)S(1)}, bf16[2,128,512]{2,1,0:T(8,128)(2,1)S(1)}, u32[]{:S(2)}, u32[]{:S(2)}) %collective-permute-start.5) | collective-permute-done | bytes 262176 | tf_op jit(solution)/shard_map/ppermute | solution.py:28
  56.9 0.0 copy-done.1
  56.9 0.1 add_convert_fusion.1
  57.0 0.0 copy-start
  57.0 1.4 %collective-permute-start.7 = (bf16[2,128,512]{2,1,0:T(8,128)(2,1)S(1)}, bf16[2,128,512]{2,1,0:T(8,128)(2,1)S(1)}, u32[]{:S(2)}, u32[]{:S(2)}) collective-permute-start(bf16[2,128,512]{2,1,0:T(8,128)(2,1)S(1)} %add_convert_fusion.1), channel_id=1, source_target_pairs={{4,0},{8,4},{12,8},{5,1},{9,5},{13,9},{6,2},{10,6},{14,10},{7,3},{... | collective-permute-start | bytes 786440 | tf_op jit(solution)/shard_map/ppermute | solution.py:28
  58.4 2.0 %collective-permute-done.6 = bf16[1,128,2048]{2,1,0:T(8,128)(2,1)S(1)} collective-permute-done((bf16[1,128,2048]{2,1,0:T(8,128)(2,1)}, bf16[1,128,2048]{2,1,0:T(8,128)(2,1)S(1)}, u32[]{:S(2)}, u32[]{:S(2)}) %collective-permute-start.6) | collective-permute-done | bytes 524320 | tf_op jit(solution)/shard_map/ppermute | solution.py:22
  60.4 0.8 %broadcast_select_fusion = bf16[1,128,2048]{2,1,0:T(8,128)(2,1)} fusion(bf16[1,128,2048]{2,1,0:T(8,128)(2,1)S(1)} %collective-permute-done.6, pred[]{:T(512)S(6)} %lt.20), kind=kLoop, calls=%fused_computation.4 | loop fusion | flops 262144 | bytes 1048577 | tf_op jit(solution)/shard_map/jit(_where)/select_n | solution.py:196
  61.2 4.2 %collective-permute-done.7 = bf16[2,128,512]{2,1,0:T(8,128)(2,1)S(1)} collective-permute-done((bf16[2,128,512]{2,1,0:T(8,128)(2,1)S(1)}, bf16[2,128,512]{2,1,0:T(8,128)(2,1)S(1)}, u32[]{:S(2)}, u32[]{:S(2)}) %collective-permute-start.7) | collective-permute-done | bytes 262176 | tf_op jit(solution)/shard_map/ppermute | solution.py:28
  65.4 0.0 copy-done
  65.4 0.1 add_convert_fusion
  65.5 0.6 collective-permute-start.8
  66.0 5.9 %collective-permute-done.8 = bf16[2,128,512]{2,1,0:T(8,128)(2,1)S(1)} collective-permute-done((bf16[2,128,512]{2,1,0:T(8,128)(2,1)S(1)}, bf16[2,128,512]{2,1,0:T(8,128)(2,1)S(1)}, u32[]{:S(2)}, u32[]{:S(2)}) %collective-permute-start.8) | collective-permute-done | bytes 262176 | tf_op jit(solution)/shard_map/ppermute | solution.py:22
  71.9 0.7 fusion.5
  (7 shorter events, 0.0 us)
Async XLA Ops:
  0.6 1.0 %copy-start.2 = (bf16[1,128,512]{2,1,0:T(8,128)(2,1)S(1)}, bf16[1,128,512]{2,1,0:T(8,128)(2,1)}, u32[]{:S(2)}) copy-start(bf16[1,128,512]{2,1,0:T(8,128)(2,1)} %param.8) | copy-start | bytes 393220
  1.6 24.4 %copy-start.3 = (bf16[2,128,512]{2,1,0:T(8,128)(2,1)}, bf16[2,128,512]{2,1,0:T(8,128)(2,1)S(1)}, u32[]{:S(2)}) copy-start(bf16[2,128,512]{2,1,0:T(8,128)(2,1)S(1)} %constant_dynamic-update-slice_fusion.refs_0_) | copy-start | bytes 786436
  1.6 24.4 %collective-permute-start.2 = (bf16[2,128,512]{2,1,0:T(8,128)(2,1)S(1)}, bf16[2,128,512]{2,1,0:T(8,128)(2,1)S(1)}, u32[]{:S(2)}, u32[]{:S(2)}) collective-permute-start(bf16[2,128,512]{2,1,0:T(8,128)(2,1)S(1)} %constant_dynamic-update-slice_fusion.refs_0_), channel_id=1, source_target_pairs={{0,12},{1,13},{2,14},{3,15},{16,28},{17,29},{18,30},{19,31}} | collective-permute-start | bytes 786440 | tf_op jit(solution)/shard_map/ppermute | solution.py:28
  8.6 11.2 %collective-permute-start = (bf16[2,128,512]{2,1,0:T(8,128)(2,1)S(1)}, bf16[2,128,512]{2,1,0:T(8,128)(2,1)S(1)}, u32[]{:S(2)}, u32[]{:S(2)}) collective-permute-start(bf16[2,128,512]{2,1,0:T(8,128)(2,1)S(1)} %constant_dynamic-update-slice_fusion.refs_0_), channel_id=1, source_target_pairs={{0,4},{4,8},{8,12},{1,5},{5,9},{9,13},{2,6},{6,10},{10,14},{3,7},{... | collective-permute-start | bytes 786440 | tf_op jit(solution)/shard_map/ppermute | solution.py:28
  10.3 0.7 copy-start.5
  11.1 13.1 %copy-start.4 = (s32[1,2,16,8]{2,3,1,0:T(8,128)S(1)}, s32[1,2,16,8]{2,3,1,0:T(8,128)}, u32[]{:S(2)}) copy-start(s32[1,2,16,8]{2,3,1,0:T(8,128)} %param.10) | copy-start | bytes 3076
  19.8 6.2 %copy-start.7 = (bf16[2,128,512]{2,1,0:T(8,128)(2,1)}, bf16[2,128,512]{2,1,0:T(8,128)(2,1)S(1)}, u32[]{:S(2)}) copy-start(bf16[2,128,512]{2,1,0:T(8,128)(2,1)S(1)} %collective-permute-done.refs_1_) | copy-start | bytes 786436
  19.8 9.1 %collective-permute-start.1 = (bf16[2,128,512]{2,1,0:T(8,128)(2,1)S(1)}, bf16[2,128,512]{2,1,0:T(8,128)(2,1)S(1)}, u32[]{:S(2)}, u32[]{:S(2)}) collective-permute-start(bf16[2,128,512]{2,1,0:T(8,128)(2,1)S(1)} %collective-permute-done.refs_1_), channel_id=1, source_target_pairs={{0,4},{4,8},{8,12},{1,5},{5,9},{9,13},{2,6},{6,10},{10,14},{3,7},{... | collective-permute-start | bytes 786440 | tf_op jit(solution)/shard_map/ppermute | solution.py:28
  26.0 2.9 %copy-start.6 = (bf16[2,128,512]{2,1,0:T(8,128)(2,1)}, bf16[2,128,512]{2,1,0:T(8,128)(2,1)S(1)}, u32[]{:S(2)}) copy-start(bf16[2,128,512]{2,1,0:T(8,128)(2,1)S(1)} %collective-permute-done.2.refs_3_) | copy-start | bytes 786436
  28.9 0.7 copy-start.8
  37.0 15.1 %collective-permute-start.3 = (bf16[1,128,2048]{2,1,0:T(8,128)(2,1)}, bf16[1,128,2048]{2,1,0:T(8,128)(2,1)S(1)}, u32[]{:S(2)}, u32[]{:S(2)}) collective-permute-start(bf16[1,128,2048]{2,1,0:T(8,128)(2,1)} %bitcast.26), channel_id=1, source_target_pairs={{0,16},{16,0},{1,17},{17,1},{2,18},{18,2},{3,19},{19,3},{4,20},{20... | collective-permute-start | bytes 1572872 | tf_op jit(solution)/shard_map/ppermute | solution.py:22
  38.5 8.9 %collective-permute-start.4 = (bf16[2,128,512]{2,1,0:T(8,128)(2,1)}, bf16[2,128,512]{2,1,0:T(8,128)(2,1)S(1)}, u32[]{:S(2)}, u32[]{:S(2)}) collective-permute-start(bf16[2,128,512]{2,1,0:T(8,128)(2,1)} %get-tuple-element.16), channel_id=1, source_target_pairs={{4,0},{8,4},{12,8},{5,1},{9,5},{13,9},{6,2},{10,6},{14,10},{7,3},{... | collective-permute-start | bytes 786440 | tf_op jit(solution)/shard_map/ppermute | solution.py:28
  39.8 20.6 %collective-permute-start.6 = (bf16[1,128,2048]{2,1,0:T(8,128)(2,1)}, bf16[1,128,2048]{2,1,0:T(8,128)(2,1)S(1)}, u32[]{:S(2)}, u32[]{:S(2)}) collective-permute-start(bf16[1,128,2048]{2,1,0:T(8,128)(2,1)} %bitcast.25), channel_id=1, source_target_pairs={{0,16},{16,0},{1,17},{17,1},{2,18},{18,2},{3,19},{19,3},{4,20},{20... | collective-permute-start | bytes 1572872 | tf_op jit(solution)/shard_map/ppermute | solution.py:22
  48.5 8.4 %copy-start.1 = (bf16[2,128,512]{2,1,0:T(8,128)(2,1)S(1)}, bf16[2,128,512]{2,1,0:T(8,128)(2,1)}, u32[]{:S(2)}) copy-start(bf16[2,128,512]{2,1,0:T(8,128)(2,1)} %get-tuple-element.19) | copy-start | bytes 786436
  48.5 8.4 %collective-permute-start.5 = (bf16[2,128,512]{2,1,0:T(8,128)(2,1)S(1)}, bf16[2,128,512]{2,1,0:T(8,128)(2,1)S(1)}, u32[]{:S(2)}, u32[]{:S(2)}) collective-permute-start(bf16[2,128,512]{2,1,0:T(8,128)(2,1)S(1)} %add_convert_fusion.2), channel_id=1, source_target_pairs={{4,0},{8,4},{12,8},{5,1},{9,5},{13,9},{6,2},{10,6},{14,10},{7,3},{... | collective-permute-start | bytes 786440 | tf_op jit(solution)/shard_map/ppermute | solution.py:28
  57.0 8.4 %copy-start = (bf16[2,128,512]{2,1,0:T(8,128)(2,1)S(1)}, bf16[2,128,512]{2,1,0:T(8,128)(2,1)}, u32[]{:S(2)}) copy-start(bf16[2,128,512]{2,1,0:T(8,128)(2,1)} %get-tuple-element.22) | copy-start | bytes 786436
  57.0 8.4 %collective-permute-start.7 = (bf16[2,128,512]{2,1,0:T(8,128)(2,1)S(1)}, bf16[2,128,512]{2,1,0:T(8,128)(2,1)S(1)}, u32[]{:S(2)}, u32[]{:S(2)}) collective-permute-start(bf16[2,128,512]{2,1,0:T(8,128)(2,1)S(1)} %add_convert_fusion.1), channel_id=1, source_target_pairs={{4,0},{8,4},{12,8},{5,1},{9,5},{13,9},{6,2},{10,6},{14,10},{7,3},{... | collective-permute-start | bytes 786440 | tf_op jit(solution)/shard_map/ppermute | solution.py:28
  65.5 6.4 %collective-permute-start.8 = (bf16[2,128,512]{2,1,0:T(8,128)(2,1)S(1)}, bf16[2,128,512]{2,1,0:T(8,128)(2,1)S(1)}, u32[]{:S(2)}, u32[]{:S(2)}) collective-permute-start(bf16[2,128,512]{2,1,0:T(8,128)(2,1)S(1)} %add_convert_fusion), channel_id=1, source_target_pairs={{0,16},{16,0},{1,17},{17,1},{2,18},{18,2},{3,19},{19,3},{4,20},{20... | collective-permute-start | bytes 786440 | tf_op jit(solution)/shard_map/ppermute | solution.py:22

commit v17 on v15

--- a/solution.py
+++ b/solution.py
@@ -163,22 +163,25 @@
         for shift in range(1, ctx_count):
             pieces.append(shifted_open(pieces[-1], "ctx", 1))
     attended, query_grad, kv_terms = attention(query[0], grad_out[0], pieces, masks)
-    next_input = passed_along(attended[None], "pipe", 1)
     grad_query = passed_along(query_grad[None], "pipe", -1)
 
     carried = None
+    next_input = None
     for step in range(1, ctx_count):
         part = kv_terms[ctx_count - step].astype(jnp.float32)
         if carried is not None:
-            if step == ctx_count - 1:
-                next_input = jnp.where(ctx_index < 0, jnp.zeros_like(next_input), next_input)
-                next_input, carried = lax.optimization_barrier((next_input, carried))
             part = part + carried.astype(jnp.float32)
         carried = shifted_open(part.astype(jnp.bfloat16), "ctx", -1)
+        if step == 1:
+            attended, carried = lax.optimization_barrier((attended, carried))
+            next_input = passed_along(attended[None], "pipe", 1)
+    if next_input is None:
+        next_input = passed_along(attended[None], "pipe", 1)
     kv_sum = kv_terms[0].astype(jnp.float32)
     if carried is not None:
+        next_input = jnp.where(ctx_index < 0, jnp.zeros_like(next_input), next_input)
         grad_query = jnp.where(ctx_index < 0, jnp.zeros_like(grad_query), grad_query)
-        grad_query, carried = lax.optimization_barrier((grad_query, carried))
+        next_input, grad_query, carried = lax.optimization_barrier((next_input, grad_query, carried))
         kv_sum = kv_sum + carried.astype(jnp.float32)
     returned = passed_along(kv_sum.astype(jnp.bfloat16), "pipe", -1)
     grad_key = returned[0:1]

time: 73.1 us -> 71.6 us (0.979)
  waiting for transfers between devices: 36.3 us -> 32.9 us
  starting transfers between devices: 19.5 us -> 21.4 us
    ppermute x6, waiting for transfers between devices: 26.3 us -> 24 us  [shifted_open(): return lax.ppermute(value, axis, pairs)]
    ppermute x3, starting transfers between devices: 2.72 us -> 4.75 us  [passed_along(): return lax.ppermute(value, axis, pairs)]
    ppermute x3, waiting for transfers between devices: 9.99 us -> 8.89 us  [passed_along(): return lax.ppermute(value, axis, pairs)]
    unnamed x20 -> x22, local copies, waits for them, and re-layouts: 2.36 us -> 2.35 us
  transfers between devices with their start and end apart: 9 -> 9, of which waited for: 8 -> 7; matrix products, arithmetic and copies ran while one was open for 7% -> 8% of each run, Pallas kernels for 0% -> 0%
where the time goes in v17:
time: 71.6 us; the launch traced here: 71.3 us
  waiting for transfers between devices  32.9 us (46%)
  starting transfers between devices  21.4 us (30%)
  Pallas kernels  7.47 us (10%)
  local copies, waits for them, and re-layouts  5.05 us (7%)
  other arithmetic  3.59 us (5%)
  between operations  0.84 us (1%)
    ppermute x6, waiting for transfers between devices, shifted_open(): return lax.ppermute(value, axis, pairs)  24 us
    ppermute x6, starting transfers between devices, shifted_open(): return lax.ppermute(value, axis, pairs)  16.7 us
    ppermute x3, waiting for transfers between devices, passed_along(): return lax.ppermute(value, axis, pairs)  8.89 us
    pallas_call x1, Pallas kernels, attention(): pl.pallas_call(functools.partial(attention_kernel, piece_count, group_siz...  7.47 us
    ppermute x3, starting transfers between devices, passed_along(): return lax.ppermute(value, axis, pairs)  4.75 us
    unnamed x22, local copies, waits for them, and re-layouts  2.35 us
  transfers between devices with their start and end apart: 9, of which 7 were waited for; matrix products, arithmetic and copies ran while one was open for 8% of the time, Pallas kernels for 0%

profile of v17, /device:TPU:0, one launch (start us, length us, event | category | flops | bytes accessed | tf_op | source)
XLA Modules:
  0.0 71.3 jit_solution(16977514565192403268)
XLA Ops:
  0.6 0.0 copy-start.2
  0.6 0.9 %constant_dynamic-update-slice_fusion.1 = bf16[2,128,512]{2,1,0:T(8,128)(2,1)S(1)} fusion(bf16[1,128,512]{2,1,0:T(8,128)(2,1)} %param.7), kind=kLoop, calls=%fused_computation.14 | loop fusion | bytes 262144
  1.6 0.0 copy-done.2
  1.6 0.0 copy-start.3
  1.6 7.0 %collective-permute-start.2 = (bf16[2,128,512]{2,1,0:T(8,128)(2,1)S(1)}, bf16[2,128,512]{2,1,0:T(8,128)(2,1)S(1)}, u32[]{:S(2)}, u32[]{:S(2)}) collective-permute-start(bf16[2,128,512]{2,1,0:T(8,128)(2,1)S(1)} %constant_dynamic-update-slice_fusion.refs_0_), channel_id=1, source_target_pairs={{0,12},{1,13},{2,14},{3,15},{16,28},{17,29},{18,30},{19,31}} | collective-permute-start | bytes 786440 | tf_op jit(solution)/shard_map/ppermute | solution.py:28
  8.6 1.3 %collective-permute-start = (bf16[2,128,512]{2,1,0:T(8,128)(2,1)S(1)}, bf16[2,128,512]{2,1,0:T(8,128)(2,1)S(1)}, u32[]{:S(2)}, u32[]{:S(2)}) collective-permute-start(bf16[2,128,512]{2,1,0:T(8,128)(2,1)S(1)} %constant_dynamic-update-slice_fusion.refs_0_), channel_id=1, source_target_pairs={{0,4},{4,8},{8,12},{1,5},{5,9},{9,13},{2,6},{6,10},{10,14},{3,7},{... | collective-permute-start | bytes 786440 | tf_op jit(solution)/shard_map/ppermute | solution.py:28
  9.9 0.1 compare_and_fusion
  10.0 0.1 iota_add_fusion
  10.1 0.1 min.12
  10.2 0.1 copy.14
  10.3 0.0 copy-start.5
  10.3 0.7 copy-done.5
  10.9 0.2 compare_reduce_fusion.1
  11.1 0.0 copy-start.4
  11.1 0.2 compare_reduce_fusion
  11.3 0.1 copy.15
  11.5 0.1 or_or_fusion
  11.5 8.3 %collective-permute-done.refs_1_ = bf16[2,128,512]{2,1,0:T(8,128)(2,1)S(1)} collective-permute-done((bf16[2,128,512]{2,1,0:T(8,128)(2,1)S(1)}, bf16[2,128,512]{2,1,0:T(8,128)(2,1)S(1)}, u32[]{:S(2)}, u32[]{:S(2)}) %collective-permute-start) | collective-permute-done | bytes 262176 | tf_op jit(solution)/shard_map/ppermute | solution.py:28
  19.8 0.0 copy-start.8
  19.8 4.4 %collective-permute-start.1 = (bf16[2,128,512]{2,1,0:T(8,128)(2,1)S(1)}, bf16[2,128,512]{2,1,0:T(8,128)(2,1)S(1)}, u32[]{:S(2)}, u32[]{:S(2)}) collective-permute-start(bf16[2,128,512]{2,1,0:T(8,128)(2,1)S(1)} %collective-permute-done.refs_1_), channel_id=1, source_target_pairs={{0,4},{4,8},{8,12},{1,5},{5,9},{9,13},{2,6},{6,10},{10,14},{3,7},{... | collective-permute-start | bytes 786440 | tf_op jit(solution)/shard_map/ppermute | solution.py:28
  24.2 0.0 copy-done.4
  24.2 0.6 gather_fusion
  24.8 0.1 fusion.1
  24.9 0.1 copy.16
  25.0 0.2 broadcast_in_dim.41
  25.2 0.8 %select_n.45.mask_ref = f32[4,16,2,128]{3,2,1,0:T(2,128)} reshape(f32[4,16,2,2,64]{4,3,2,1,0:T(2,128)S(1)} %broadcast_in_dim.41) | data formatting | bytes 131072 | tf_op jit(solution)/shard_map/jit(_where)/select_n | solution.py:48
  26.0 0.0 copy-done.3
  26.0 0.0 copy-done.8
  26.0 0.0 collective-permute-done.2.refs_3_
  26.0 0.0 copy-start.7
  26.0 2.9 %collective-permute-done.1.refs_2_ = bf16[2,128,512]{2,1,0:T(8,128)(2,1)S(1)} collective-permute-done((bf16[2,128,512]{2,1,0:T(8,128)(2,1)S(1)}, bf16[2,128,512]{2,1,0:T(8,128)(2,1)S(1)}, u32[]{:S(2)}, u32[]{:S(2)}) %collective-permute-start.1) | collective-permute-done | bytes 262176 | tf_op jit(solution)/shard_map/ppermute | solution.py:28
  28.9 0.0 copy-start.9
  28.9 0.0 copy-done.7
  28.9 0.7 copy-done.9
  29.6 7.5 %shard_map.93 = (bf16[128,2048]{1,0:T(8,128)(2,1)}, bf16[128,2048]{1,0:T(8,128)(2,1)}, bf16[2,128,512]{2,1,0:T(8,128)(2,1)}, bf16[2,128,512]{2,1,0:T(8,128)(2,1)...) custom-call(bf16[128,2048]{1,0:T(8,128)(2,1)} %bitcast.23, bf16[128,2048]{1,0:T(8,128)(2,1)} %bitcast.24, ...), custom_call_target="tpu_custom_call" | custom-call | flops 1610612736 | bytes 4194304 | tf_op jit(solution)/shard_map/pallas_call | solution.py:129
  37.1 0.0 copy-start.6
  37.1 1.4 %collective-permute-start.3 = (bf16[2,128,512]{2,1,0:T(8,128)(2,1)}, bf16[2,128,512]{2,1,0:T(8,128)(2,1)S(1)}, u32[]{:S(2)}, u32[]{:S(2)}) collective-permute-start(bf16[2,128,512]{2,1,0:T(8,128)(2,1)} %get-tuple-element.16), channel_id=1, source_target_pairs={{4,0},{8,4},{12,8},{5,1},{9,5},{13,9},{6,2},{10,6},{14,10},{7,3},{... | collective-permute-start | bytes 786440 | tf_op jit(solution)/shard_map/ppermute | solution.py:28
  38.5 1.6 %collective-permute-start.5 = (bf16[1,128,2048]{2,1,0:T(8,128)(2,1)}, bf16[1,128,2048]{2,1,0:T(8,128)(2,1)S(1)}, u32[]{:S(2)}, u32[]{:S(2)}) collective-permute-start(bf16[1,128,2048]{2,1,0:T(8,128)(2,1)} %bitcast.26), channel_id=1, source_target_pairs={{0,16},{16,0},{1,17},{17,1},{2,18},{18,2},{3,19},{19,3},{4,20},{20... | collective-permute-start | bytes 1572872 | tf_op jit(solution)/shard_map/ppermute | solution.py:22
  40.1 6.3 %collective-permute-done.3 = bf16[2,128,512]{2,1,0:T(8,128)(2,1)S(1)} collective-permute-done((bf16[2,128,512]{2,1,0:T(8,128)(2,1)}, bf16[2,128,512]{2,1,0:T(8,128)(2,1)S(1)}, u32[]{:S(2)}, u32[]{:S(2)}) %collective-permute-start.3) | collective-permute-done | bytes 262176 | tf_op jit(solution)/shard_map/ppermute | solution.py:28
  46.4 0.0 copy-start.1
  46.4 1.1 %add_convert_fusion.2 = bf16[2,128,512]{2,1,0:T(8,128)(2,1)S(1)} fusion(bf16[2,128,512]{2,1,0:T(8,128)(2,1)S(1)} %collective-permute-done.3, bf16[2,128,512]{2,1,0:T(8,128)(2,1)} %get-tuple-element.20), kind=kLoop, calls=%fused_computation.3 | loop fusion | flops 524288 | bytes 786432 | tf_op jit(solution)/shard_map/convert_element_type | solution.py:174
  47.4 1.3 %collective-permute-start.6 = (bf16[2,128,512]{2,1,0:T(8,128)(2,1)S(1)}, bf16[2,128,512]{2,1,0:T(8,128)(2,1)S(1)}, u32[]{:S(2)}, u32[]{:S(2)}) collective-permute-start(bf16[2,128,512]{2,1,0:T(8,128)(2,1)S(1)} %add_convert_fusion.2), channel_id=1, source_target_pairs={{4,0},{8,4},{12,8},{5,1},{9,5},{13,9},{6,2},{10,6},{14,10},{7,3},{... | collective-permute-start | bytes 786440 | tf_op jit(solution)/shard_map/ppermute | solution.py:28
  48.7 0.0 copy-done.6
  48.8 1.6 %collective-permute-start.4 = (bf16[1,128,2048]{2,1,0:T(8,128)(2,1)S(1)}, bf16[1,128,2048]{2,1,0:T(8,128)(2,1)S(1)}, u32[]{:S(2)}, u32[]{:S(2)}) collective-permute-start(bf16[1,128,2048]{2,1,0:T(8,128)(2,1)S(1)} %bitcast.25), channel_id=1, source_target_pairs={{0,16},{16,0},{1,17},{17,1},{2,18},{18,2},{3,19},{19,3},{4,20},{20... | collective-permute-start | bytes 1572872 | tf_op jit(solution)/shard_map/ppermute | solution.py:22
  50.3 5.4 %collective-permute-done.6 = bf16[2,128,512]{2,1,0:T(8,128)(2,1)S(1)} collective-permute-done((bf16[2,128,512]{2,1,0:T(8,128)(2,1)S(1)}, bf16[2,128,512]{2,1,0:T(8,128)(2,1)S(1)}, u32[]{:S(2)}, u32[]{:S(2)}) %collective-permute-start.6) | collective-permute-done | bytes 262176 | tf_op jit(solution)/shard_map/ppermute | solution.py:28
  55.7 0.0 copy-done.1
  55.7 0.1 add_convert_fusion.1
  55.8 1.3 %collective-permute-start.7 = (bf16[2,128,512]{2,1,0:T(8,128)(2,1)S(1)}, bf16[2,128,512]{2,1,0:T(8,128)(2,1)S(1)}, u32[]{:S(2)}, u32[]{:S(2)}) collective-permute-start(bf16[2,128,512]{2,1,0:T(8,128)(2,1)S(1)} %add_convert_fusion.1), channel_id=1, source_target_pairs={{4,0},{8,4},{12,8},{5,1},{9,5},{13,9},{6,2},{10,6},{14,10},{7,3},{... | collective-permute-start | bytes 786440 | tf_op jit(solution)/shard_map/ppermute | solution.py:28
  57.1 0.0 collective-permute-done.5
  57.1 0.8 %broadcast_select_fusion = bf16[1,128,2048]{2,1,0:T(8,128)(2,1)} fusion(bf16[1,128,2048]{2,1,0:T(8,128)(2,1)S(1)} %collective-permute-done.5, pred[]{:T(512)S(6)} %lt.20), kind=kLoop, calls=%fused_computation.4 | loop fusion | flops 262144 | bytes 1048577 | tf_op jit(solution)/shard_map/jit(_where)/select_n | solution.py:183
  57.9 0.0 copy-start
  57.9 4.0 %collective-permute-done.4 = bf16[1,128,2048]{2,1,0:T(8,128)(2,1)S(1)} collective-permute-done((bf16[1,128,2048]{2,1,0:T(8,128)(2,1)S(1)}, bf16[1,128,2048]{2,1,0:T(8,128)(2,1)S(1)}, u32[]{:S(2)}, u32[]{:S(2)}) %collective-permute-start.4) | collective-permute-done | bytes 524320 | tf_op jit(solution)/shard_map/ppermute | solution.py:22
  62.0 0.8 %broadcast_select_fusion.1 = bf16[1,128,2048]{2,1,0:T(8,128)(2,1)} fusion(bf16[1,128,2048]{2,1,0:T(8,128)(2,1)S(1)} %collective-permute-done.4, pred[]{:T(512)S(6)} %lt.20), kind=kLoop, calls=%fused_computation.5 | loop fusion | flops 262144 | bytes 1048577 | tf_op jit(solution)/shard_map/jit(_where)/select_n | solution.py:182
  62.8 1.3 %collective-permute-done.7 = bf16[2,128,512]{2,1,0:T(8,128)(2,1)S(1)} collective-permute-done((bf16[2,128,512]{2,1,0:T(8,128)(2,1)S(1)}, bf16[2,128,512]{2,1,0:T(8,128)(2,1)S(1)}, u32[]{:S(2)}, u32[]{:S(2)}) %collective-permute-start.7) | collective-permute-done | bytes 262176 | tf_op jit(solution)/shard_map/ppermute | solution.py:28
  64.1 0.0 copy-done
  64.1 0.1 add_convert_fusion
  64.1 1.6 %collective-permute-start.8 = (bf16[2,128,512]{2,1,0:T(8,128)(2,1)S(1)}, bf16[2,128,512]{2,1,0:T(8,128)(2,1)S(1)}, u32[]{:S(2)}, u32[]{:S(2)}) collective-permute-start(bf16[2,128,512]{2,1,0:T(8,128)(2,1)S(1)} %add_convert_fusion), channel_id=1, source_target_pairs={{0,16},{16,0},{1,17},{17,1},{2,18},{18,2},{3,19},{19,3},{4,20},{20... | collective-permute-start | bytes 786440 | tf_op jit(solution)/shard_map/ppermute | solution.py:22
  65.7 4.9 %collective-permute-done.8 = bf16[2,128,512]{2,1,0:T(8,128)(2,1)S(1)} collective-permute-done((bf16[2,128,512]{2,1,0:T(8,128)(2,1)S(1)}, bf16[2,128,512]{2,1,0:T(8,128)(2,1)S(1)}, u32[]{:S(2)}, u32[]{:S(2)}) %collective-permute-start.8) | collective-permute-done | bytes 262176 | tf_op jit(solution)/shard_map/ppermute | solution.py:22
  70.6 0.7 %fusion.5 = (bf16[1,128,512]{2,1,0:T(8,128)(2,1)}, bf16[1,128,512]{2,1,0:T(8,128)(2,1)}) fusion(bf16[2,128,512]{2,1,0:T(8,128)(2,1)S(1)} %collective-permute-done.8), kind=kLoop, calls=%fused_computation.26 | loop fusion | bytes 524288 | tf_op jit(solution)/shard_map/slice | solution.py:188
  (7 shorter events, 0.0 us)
Async XLA Ops:
  0.6 1.0 %copy-start.2 = (bf16[1,128,512]{2,1,0:T(8,128)(2,1)S(1)}, bf16[1,128,512]{2,1,0:T(8,128)(2,1)}, u32[]{:S(2)}) copy-start(bf16[1,128,512]{2,1,0:T(8,128)(2,1)} %param.8) | copy-start | bytes 393220
  1.6 24.4 %copy-start.3 = (bf16[2,128,512]{2,1,0:T(8,128)(2,1)}, bf16[2,128,512]{2,1,0:T(8,128)(2,1)S(1)}, u32[]{:S(2)}) copy-start(bf16[2,128,512]{2,1,0:T(8,128)(2,1)S(1)} %constant_dynamic-update-slice_fusion.refs_0_) | copy-start | bytes 786436
  1.6 24.4 %collective-permute-start.2 = (bf16[2,128,512]{2,1,0:T(8,128)(2,1)S(1)}, bf16[2,128,512]{2,1,0:T(8,128)(2,1)S(1)}, u32[]{:S(2)}, u32[]{:S(2)}) collective-permute-start(bf16[2,128,512]{2,1,0:T(8,128)(2,1)S(1)} %constant_dynamic-update-slice_fusion.refs_0_), channel_id=1, source_target_pairs={{0,12},{1,13},{2,14},{3,15},{16,28},{17,29},{18,30},{19,31}} | collective-permute-start | bytes 786440 | tf_op jit(solution)/shard_map/ppermute | solution.py:28
  8.6 11.2 %collective-permute-start = (bf16[2,128,512]{2,1,0:T(8,128)(2,1)S(1)}, bf16[2,128,512]{2,1,0:T(8,128)(2,1)S(1)}, u32[]{:S(2)}, u32[]{:S(2)}) collective-permute-start(bf16[2,128,512]{2,1,0:T(8,128)(2,1)S(1)} %constant_dynamic-update-slice_fusion.refs_0_), channel_id=1, source_target_pairs={{0,4},{4,8},{8,12},{1,5},{5,9},{9,13},{2,6},{6,10},{10,14},{3,7},{... | collective-permute-start | bytes 786440 | tf_op jit(solution)/shard_map/ppermute | solution.py:28
  10.3 0.7 copy-start.5
  11.1 13.1 %copy-start.4 = (s32[1,2,16,8]{2,3,1,0:T(8,128)S(1)}, s32[1,2,16,8]{2,3,1,0:T(8,128)}, u32[]{:S(2)}) copy-start(s32[1,2,16,8]{2,3,1,0:T(8,128)} %param.10) | copy-start | bytes 3076
  19.8 6.2 %copy-start.8 = (bf16[2,128,512]{2,1,0:T(8,128)(2,1)}, bf16[2,128,512]{2,1,0:T(8,128)(2,1)S(1)}, u32[]{:S(2)}) copy-start(bf16[2,128,512]{2,1,0:T(8,128)(2,1)S(1)} %collective-permute-done.refs_1_) | copy-start | bytes 786436
  19.8 9.1 %collective-permute-start.1 = (bf16[2,128,512]{2,1,0:T(8,128)(2,1)S(1)}, bf16[2,128,512]{2,1,0:T(8,128)(2,1)S(1)}, u32[]{:S(2)}, u32[]{:S(2)}) collective-permute-start(bf16[2,128,512]{2,1,0:T(8,128)(2,1)S(1)} %collective-permute-done.refs_1_), channel_id=1, source_target_pairs={{0,4},{4,8},{8,12},{1,5},{5,9},{9,13},{2,6},{6,10},{10,14},{3,7},{... | collective-permute-start | bytes 786440 | tf_op jit(solution)/shard_map/ppermute | solution.py:28
  26.0 2.9 %copy-start.7 = (bf16[2,128,512]{2,1,0:T(8,128)(2,1)}, bf16[2,128,512]{2,1,0:T(8,128)(2,1)S(1)}, u32[]{:S(2)}) copy-start(bf16[2,128,512]{2,1,0:T(8,128)(2,1)S(1)} %collective-permute-done.2.refs_3_) | copy-start | bytes 786436
  28.9 0.7 copy-start.9
  37.1 11.7 %copy-start.6 = (bf16[128,2048]{1,0:T(8,128)(2,1)S(1)}, bf16[128,2048]{1,0:T(8,128)(2,1)}, u32[]{:S(2)}) copy-start(bf16[128,2048]{1,0:T(8,128)(2,1)} %get-tuple-element.17) | copy-start | bytes 1572868
  37.1 9.3 %collective-permute-start.3 = (bf16[2,128,512]{2,1,0:T(8,128)(2,1)}, bf16[2,128,512]{2,1,0:T(8,128)(2,1)S(1)}, u32[]{:S(2)}, u32[]{:S(2)}) collective-permute-start(bf16[2,128,512]{2,1,0:T(8,128)(2,1)} %get-tuple-element.16), channel_id=1, source_target_pairs={{4,0},{8,4},{12,8},{5,1},{9,5},{13,9},{6,2},{10,6},{14,10},{7,3},{... | collective-permute-start | bytes 786440 | tf_op jit(solution)/shard_map/ppermute | solution.py:28
  38.5 18.6 %collective-permute-start.5 = (bf16[1,128,2048]{2,1,0:T(8,128)(2,1)}, bf16[1,128,2048]{2,1,0:T(8,128)(2,1)S(1)}, u32[]{:S(2)}, u32[]{:S(2)}) collective-permute-start(bf16[1,128,2048]{2,1,0:T(8,128)(2,1)} %bitcast.26), channel_id=1, source_target_pairs={{0,16},{16,0},{1,17},{17,1},{2,18},{18,2},{3,19},{19,3},{4,20},{20... | collective-permute-start | bytes 1572872 | tf_op jit(solution)/shard_map/ppermute | solution.py:22
  46.4 9.3 %copy-start.1 = (bf16[2,128,512]{2,1,0:T(8,128)(2,1)S(1)}, bf16[2,128,512]{2,1,0:T(8,128)(2,1)}, u32[]{:S(2)}) copy-start(bf16[2,128,512]{2,1,0:T(8,128)(2,1)} %get-tuple-element.19) | copy-start | bytes 786436
  47.4 8.3 %collective-permute-start.6 = (bf16[2,128,512]{2,1,0:T(8,128)(2,1)S(1)}, bf16[2,128,512]{2,1,0:T(8,128)(2,1)S(1)}, u32[]{:S(2)}, u32[]{:S(2)}) collective-permute-start(bf16[2,128,512]{2,1,0:T(8,128)(2,1)S(1)} %add_convert_fusion.2), channel_id=1, source_target_pairs={{4,0},{8,4},{12,8},{5,1},{9,5},{13,9},{6,2},{10,6},{14,10},{7,3},{... | collective-permute-start | bytes 786440 | tf_op jit(solution)/shard_map/ppermute | solution.py:28
  48.8 13.2 %collective-permute-start.4 = (bf16[1,128,2048]{2,1,0:T(8,128)(2,1)S(1)}, bf16[1,128,2048]{2,1,0:T(8,128)(2,1)S(1)}, u32[]{:S(2)}, u32[]{:S(2)}) collective-permute-start(bf16[1,128,2048]{2,1,0:T(8,128)(2,1)S(1)} %bitcast.25), channel_id=1, source_target_pairs={{0,16},{16,0},{1,17},{17,1},{2,18},{18,2},{3,19},{19,3},{4,20},{20... | collective-permute-start | bytes 1572872 | tf_op jit(solution)/shard_map/ppermute | solution.py:22
  55.8 8.3 %collective-permute-start.7 = (bf16[2,128,512]{2,1,0:T(8,128)(2,1)S(1)}, bf16[2,128,512]{2,1,0:T(8,128)(2,1)S(1)}, u32[]{:S(2)}, u32[]{:S(2)}) collective-permute-start(bf16[2,128,512]{2,1,0:T(8,128)(2,1)S(1)} %add_convert_fusion.1), channel_id=1, source_target_pairs={{4,0},{8,4},{12,8},{5,1},{9,5},{13,9},{6,2},{10,6},{14,10},{7,3},{... | collective-permute-start | bytes 786440 | tf_op jit(solution)/shard_map/ppermute | solution.py:28
  57.9 6.1 %copy-start = (bf16[2,128,512]{2,1,0:T(8,128)(2,1)S(1)}, bf16[2,128,512]{2,1,0:T(8,128)(2,1)}, u32[]{:S(2)}) copy-start(bf16[2,128,512]{2,1,0:T(8,128)(2,1)} %get-tuple-element.24) | copy-start | bytes 786436
  64.1 6.4 %collective-permute-start.8 = (bf16[2,128,512]{2,1,0:T(8,128)(2,1)S(1)}, bf16[2,128,512]{2,1,0:T(8,128)(2,1)S(1)}, u32[]{:S(2)}, u32[]{:S(2)}) collective-permute-start(bf16[2,128,512]{2,1,0:T(8,128)(2,1)S(1)} %add_convert_fusion), channel_id=1, source_target_pairs={{0,16},{16,0},{1,17},{17,1},{2,18},{18,2},{3,19},{19,3},{4,20},{20... | collective-permute-start | bytes 786440 | tf_op jit(solution)/shard_map/ppermute | solution.py:22

commit v18 on v17

--- a/solution.py
+++ b/solution.py
@@ -156,7 +156,8 @@
     own = jnp.stack([keys[0], values[0]])
     if ctx_count == 4:
         step_one = shifted_open(own, "ctx", 1)
-        step_three = shifted_open(own, "ctx", 3)
+        own_later, step_one = lax.optimization_barrier((own, step_one))
+        step_three = shifted_open(own_later, "ctx", 3)
         pieces = [own, step_one, shifted_open(step_one, "ctx", 1), step_three]
     else:
         pieces = [own]

time: 71.6 us -> 71.5 us (level)
  transfers between devices with their start and end apart: 9 -> 9, of which waited for: 7 -> 8; matrix products, arithmetic and copies ran while one was open for 8% -> 8% of each run, Pallas kernels for 0% -> 0%
where the time goes in v18:
time: 71.5 us; the launch traced here: 71.2 us
  waiting for transfers between devices  32.9 us (46%)
  starting transfers between devices  21.4 us (30%)
  Pallas kernels  7.48 us (10%)
  local copies, waits for them, and re-layouts  5.04 us (7%)
  other arithmetic  3.59 us (5%)
  between operations  0.83 us (1%)
    ppermute x6, waiting for transfers between devices, shifted_open(): return lax.ppermute(value, axis, pairs)  24 us
    ppermute x6, starting transfers between devices, shifted_open(): return lax.ppermute(value, axis, pairs)  16.7 us
    ppermute x3, waiting for transfers between devices, passed_along(): return lax.ppermute(value, axis, pairs)  8.88 us
    pallas_call x1, Pallas kernels, attention(): pl.pallas_call(functools.partial(attention_kernel, piece_count, group_siz...  7.48 us
    ppermute x3, starting transfers between devices, passed_along(): return lax.ppermute(value, axis, pairs)  4.76 us
    unnamed x22, local copies, waits for them, and re-layouts  2.35 us
  transfers between devices with their start and end apart: 9, of which 8 were waited for; matrix products, arithmetic and copies ran while one was open for 8% of the time, Pallas kernels for 0%

profile of v18, /device:TPU:0, one launch (start us, length us, event | category | flops | bytes accessed | tf_op | source)
XLA Modules:
  0.0 71.2 jit_solution(15100519942923280017)
XLA Ops:
  0.6 0.0 copy-start.2
  0.6 0.9 %constant_dynamic-update-slice_fusion.1 = bf16[2,128,512]{2,1,0:T(8,128)(2,1)S(1)} fusion(bf16[1,128,512]{2,1,0:T(8,128)(2,1)} %param.7), kind=kLoop, calls=%fused_computation.14 | loop fusion | bytes 262144
  1.6 0.0 copy-done.2
  1.6 0.0 copy-start.3
  1.6 4.9 %collective-permute-start = (bf16[2,128,512]{2,1,0:T(8,128)(2,1)S(1)}, bf16[2,128,512]{2,1,0:T(8,128)(2,1)S(1)}, u32[]{:S(2)}, u32[]{:S(2)}) collective-permute-start(bf16[2,128,512]{2,1,0:T(8,128)(2,1)S(1)} %constant_dynamic-update-slice_fusion.refs_0_), channel_id=1, source_target_pairs={{0,4},{4,8},{8,12},{1,5},{5,9},{9,13},{2,6},{6,10},{10,14},{3,7},{... | collective-permute-start | bytes 786440 | tf_op jit(solution)/shard_map/ppermute | solution.py:28
  6.6 0.1 compare_and_fusion
  6.7 0.1 iota_add_fusion
  6.8 0.1 min.12
  6.8 0.1 copy.14
  6.9 0.0 copy-start.5
  6.9 0.7 copy-done.5
  7.6 0.2 compare_reduce_fusion.1
  7.8 0.0 copy-start.4
  7.8 0.2 compare_reduce_fusion
  8.0 0.1 copy.15
  8.1 0.1 or_or_fusion
  8.2 3.9 %collective-permute-done.refs_1_ = bf16[2,128,512]{2,1,0:T(8,128)(2,1)S(1)} collective-permute-done((bf16[2,128,512]{2,1,0:T(8,128)(2,1)S(1)}, bf16[2,128,512]{2,1,0:T(8,128)(2,1)S(1)}, u32[]{:S(2)}, u32[]{:S(2)}) %collective-permute-start) | collective-permute-done | bytes 262176 | tf_op jit(solution)/shard_map/ppermute | solution.py:28
  12.1 0.0 copy-start.7
  12.1 6.4 %collective-permute-start.2 = (bf16[2,128,512]{2,1,0:T(8,128)(2,1)S(1)}, bf16[2,128,512]{2,1,0:T(8,128)(2,1)S(1)}, u32[]{:S(2)}, u32[]{:S(2)}) collective-permute-start(bf16[2,128,512]{2,1,0:T(8,128)(2,1)S(1)} %constant_dynamic-update-slice_fusion.refs_0_), channel_id=1, source_target_pairs={{0,12},{1,13},{2,14},{3,15},{16,28},{17,29},{18,30},{19,31}} | collective-permute-start | bytes 786440 | tf_op jit(solution)/shard_map/ppermute | solution.py:28
  18.5 1.3 %collective-permute-start.1 = (bf16[2,128,512]{2,1,0:T(8,128)(2,1)S(1)}, bf16[2,128,512]{2,1,0:T(8,128)(2,1)S(1)}, u32[]{:S(2)}, u32[]{:S(2)}) collective-permute-start(bf16[2,128,512]{2,1,0:T(8,128)(2,1)S(1)} %collective-permute-done.refs_1_), channel_id=1, source_target_pairs={{0,4},{4,8},{8,12},{1,5},{5,9},{9,13},{2,6},{6,10},{10,14},{3,7},{... | collective-permute-start | bytes 786440 | tf_op jit(solution)/shard_map/ppermute | solution.py:28
  19.9 0.0 copy-done.4
  19.9 0.6 gather_fusion
  20.5 0.1 fusion.1
  20.6 0.1 copy.16
  20.7 0.2 broadcast_in_dim.41
  20.9 0.8 %select_n.45.mask_ref = f32[4,16,2,128]{3,2,1,0:T(2,128)} reshape(f32[4,16,2,2,64]{4,3,2,1,0:T(2,128)S(1)} %broadcast_in_dim.41) | data formatting | bytes 131072 | tf_op jit(solution)/shard_map/jit(_where)/select_n | solution.py:48
  21.7 0.0 copy-done.3
  21.7 0.0 copy-done.7
  21.7 3.6 %collective-permute-done.2.refs_3_ = bf16[2,128,512]{2,1,0:T(8,128)(2,1)S(1)} collective-permute-done((bf16[2,128,512]{2,1,0:T(8,128)(2,1)S(1)}, bf16[2,128,512]{2,1,0:T(8,128)(2,1)S(1)}, u32[]{:S(2)}, u32[]{:S(2)}) %collective-permute-start.2) | collective-permute-done | bytes 262176 | tf_op jit(solution)/shard_map/ppermute | solution.py:28
  25.3 0.0 copy-start.8
  25.3 3.6 %collective-permute-done.1.refs_2_ = bf16[2,128,512]{2,1,0:T(8,128)(2,1)S(1)} collective-permute-done((bf16[2,128,512]{2,1,0:T(8,128)(2,1)S(1)}, bf16[2,128,512]{2,1,0:T(8,128)(2,1)S(1)}, u32[]{:S(2)}, u32[]{:S(2)}) %collective-permute-start.1) | collective-permute-done | bytes 262176 | tf_op jit(solution)/shard_map/ppermute | solution.py:28
  28.9 0.0 copy-start.9
  28.9 0.0 copy-done.8
  28.9 0.7 copy-done.9
  29.6 7.5 %shard_map.93 = (bf16[128,2048]{1,0:T(8,128)(2,1)}, bf16[128,2048]{1,0:T(8,128)(2,1)}, bf16[2,128,512]{2,1,0:T(8,128)(2,1)}, bf16[2,128,512]{2,1,0:T(8,128)(2,1)...) custom-call(bf16[128,2048]{1,0:T(8,128)(2,1)} %bitcast.23, bf16[128,2048]{1,0:T(8,128)(2,1)} %bitcast.24, ...), custom_call_target="tpu_custom_call" | custom-call | flops 1610612736 | bytes 4194304 | tf_op jit(solution)/shard_map/pallas_call | solution.py:129
  37.0 0.0 copy-start.6
  37.1 1.4 %collective-permute-start.3 = (bf16[2,128,512]{2,1,0:T(8,128)(2,1)}, bf16[2,128,512]{2,1,0:T(8,128)(2,1)S(1)}, u32[]{:S(2)}, u32[]{:S(2)}) collective-permute-start(bf16[2,128,512]{2,1,0:T(8,128)(2,1)} %get-tuple-element.20), channel_id=1, source_target_pairs={{4,0},{8,4},{12,8},{5,1},{9,5},{13,9},{6,2},{10,6},{14,10},{7,3},{... | collective-permute-start | bytes 786440 | tf_op jit(solution)/shard_map/ppermute | solution.py:28
  38.5 1.6 %collective-permute-start.5 = (bf16[1,128,2048]{2,1,0:T(8,128)(2,1)}, bf16[1,128,2048]{2,1,0:T(8,128)(2,1)S(1)}, u32[]{:S(2)}, u32[]{:S(2)}) collective-permute-start(bf16[1,128,2048]{2,1,0:T(8,128)(2,1)} %bitcast.26), channel_id=1, source_target_pairs={{0,16},{16,0},{1,17},{17,1},{2,18},{18,2},{3,19},{19,3},{4,20},{20... | collective-permute-start | bytes 1572872 | tf_op jit(solution)/shard_map/ppermute | solution.py:22
  40.1 6.3 %collective-permute-done.3 = bf16[2,128,512]{2,1,0:T(8,128)(2,1)S(1)} collective-permute-done((bf16[2,128,512]{2,1,0:T(8,128)(2,1)}, bf16[2,128,512]{2,1,0:T(8,128)(2,1)S(1)}, u32[]{:S(2)}, u32[]{:S(2)}) %collective-permute-start.3) | collective-permute-done | bytes 262176 | tf_op jit(solution)/shard_map/ppermute | solution.py:28
  46.3 0.0 copy-start.1
  46.3 1.1 %add_convert_fusion.2 = bf16[2,128,512]{2,1,0:T(8,128)(2,1)S(1)} fusion(bf16[2,128,512]{2,1,0:T(8,128)(2,1)S(1)} %collective-permute-done.3, bf16[2,128,512]{2,1,0:T(8,128)(2,1)} %get-tuple-element.24), kind=kLoop, calls=%fused_computation.3 | loop fusion | flops 524288 | bytes 786432 | tf_op jit(solution)/shard_map/convert_element_type | solution.py:175
  47.4 1.3 %collective-permute-start.6 = (bf16[2,128,512]{2,1,0:T(8,128)(2,1)S(1)}, bf16[2,128,512]{2,1,0:T(8,128)(2,1)S(1)}, u32[]{:S(2)}, u32[]{:S(2)}) collective-permute-start(bf16[2,128,512]{2,1,0:T(8,128)(2,1)S(1)} %add_convert_fusion.2), channel_id=1, source_target_pairs={{4,0},{8,4},{12,8},{5,1},{9,5},{13,9},{6,2},{10,6},{14,10},{7,3},{... | collective-permute-start | bytes 786440 | tf_op jit(solution)/shard_map/ppermute | solution.py:28
  48.7 0.0 copy-done.6
  48.7 1.6 %collective-permute-start.4 = (bf16[1,128,2048]{2,1,0:T(8,128)(2,1)S(1)}, bf16[1,128,2048]{2,1,0:T(8,128)(2,1)S(1)}, u32[]{:S(2)}, u32[]{:S(2)}) collective-permute-start(bf16[1,128,2048]{2,1,0:T(8,128)(2,1)S(1)} %bitcast.25), channel_id=1, source_target_pairs={{0,16},{16,0},{1,17},{17,1},{2,18},{18,2},{3,19},{19,3},{4,20},{20... | collective-permute-start | bytes 1572872 | tf_op jit(solution)/shard_map/ppermute | solution.py:22
  50.3 5.4 %collective-permute-done.6 = bf16[2,128,512]{2,1,0:T(8,128)(2,1)S(1)} collective-permute-done((bf16[2,128,512]{2,1,0:T(8,128)(2,1)S(1)}, bf16[2,128,512]{2,1,0:T(8,128)(2,1)S(1)}, u32[]{:S(2)}, u32[]{:S(2)}) %collective-permute-start.6) | collective-permute-done | bytes 262176 | tf_op jit(solution)/shard_map/ppermute | solution.py:28
  55.7 0.0 copy-done.1
  55.7 0.1 add_convert_fusion.1
  55.7 1.3 %collective-permute-start.7 = (bf16[2,128,512]{2,1,0:T(8,128)(2,1)S(1)}, bf16[2,128,512]{2,1,0:T(8,128)(2,1)S(1)}, u32[]{:S(2)}, u32[]{:S(2)}) collective-permute-start(bf16[2,128,512]{2,1,0:T(8,128)(2,1)S(1)} %add_convert_fusion.1), channel_id=1, source_target_pairs={{4,0},{8,4},{12,8},{5,1},{9,5},{13,9},{6,2},{10,6},{14,10},{7,3},{... | collective-permute-start | bytes 786440 | tf_op jit(solution)/shard_map/ppermute | solution.py:28
  57.0 0.0 collective-permute-done.5
  57.1 0.8 %broadcast_select_fusion = bf16[1,128,2048]{2,1,0:T(8,128)(2,1)} fusion(bf16[1,128,2048]{2,1,0:T(8,128)(2,1)S(1)} %collective-permute-done.5, pred[]{:T(512)S(6)} %lt.20), kind=kLoop, calls=%fused_computation.4 | loop fusion | flops 262144 | bytes 1048577 | tf_op jit(solution)/shard_map/jit(_where)/select_n | solution.py:184
  57.9 0.0 copy-start
  57.9 4.0 %collective-permute-done.4 = bf16[1,128,2048]{2,1,0:T(8,128)(2,1)S(1)} collective-permute-done((bf16[1,128,2048]{2,1,0:T(8,128)(2,1)S(1)}, bf16[1,128,2048]{2,1,0:T(8,128)(2,1)S(1)}, u32[]{:S(2)}, u32[]{:S(2)}) %collective-permute-start.4) | collective-permute-done | bytes 524320 | tf_op jit(solution)/shard_map/ppermute | solution.py:22
  61.9 0.8 %broadcast_select_fusion.1 = bf16[1,128,2048]{2,1,0:T(8,128)(2,1)} fusion(bf16[1,128,2048]{2,1,0:T(8,128)(2,1)S(1)} %collective-permute-done.4, pred[]{:T(512)S(6)} %lt.20), kind=kLoop, calls=%fused_computation.5 | loop fusion | flops 262144 | bytes 1048577 | tf_op jit(solution)/shard_map/jit(_where)/select_n | solution.py:183
  62.7 1.3 %collective-permute-done.7 = bf16[2,128,512]{2,1,0:T(8,128)(2,1)S(1)} collective-permute-done((bf16[2,128,512]{2,1,0:T(8,128)(2,1)S(1)}, bf16[2,128,512]{2,1,0:T(8,128)(2,1)S(1)}, u32[]{:S(2)}, u32[]{:S(2)}) %collective-permute-start.7) | collective-permute-done | bytes 262176 | tf_op jit(solution)/shard_map/ppermute | solution.py:28
  64.0 0.0 copy-done
  64.0 0.1 add_convert_fusion
  64.1 1.6 %collective-permute-start.8 = (bf16[2,128,512]{2,1,0:T(8,128)(2,1)S(1)}, bf16[2,128,512]{2,1,0:T(8,128)(2,1)S(1)}, u32[]{:S(2)}, u32[]{:S(2)}) collective-permute-start(bf16[2,128,512]{2,1,0:T(8,128)(2,1)S(1)} %add_convert_fusion), channel_id=1, source_target_pairs={{0,16},{16,0},{1,17},{17,1},{2,18},{18,2},{3,19},{19,3},{4,20},{20... | collective-permute-start | bytes 786440 | tf_op jit(solution)/shard_map/ppermute | solution.py:22
  65.7 4.9 %collective-permute-done.8 = bf16[2,128,512]{2,1,0:T(8,128)(2,1)S(1)} collective-permute-done((bf16[2,128,512]{2,1,0:T(8,128)(2,1)S(1)}, bf16[2,128,512]{2,1,0:T(8,128)(2,1)S(1)}, u32[]{:S(2)}, u32[]{:S(2)}) %collective-permute-start.8) | collective-permute-done | bytes 262176 | tf_op jit(solution)/shard_map/ppermute | solution.py:22
  70.5 0.7 %fusion.5 = (bf16[1,128,512]{2,1,0:T(8,128)(2,1)}, bf16[1,128,512]{2,1,0:T(8,128)(2,1)}) fusion(bf16[2,128,512]{2,1,0:T(8,128)(2,1)S(1)} %collective-permute-done.8), kind=kLoop, calls=%fused_computation.26 | loop fusion | bytes 524288 | tf_op jit(solution)/shard_map/slice | solution.py:189
  (7 shorter events, 0.0 us)
Async XLA Ops:
  0.6 1.0 %copy-start.2 = (bf16[1,128,512]{2,1,0:T(8,128)(2,1)S(1)}, bf16[1,128,512]{2,1,0:T(8,128)(2,1)}, u32[]{:S(2)}) copy-start(bf16[1,128,512]{2,1,0:T(8,128)(2,1)} %param.8) | copy-start | bytes 393220
  1.6 20.1 %copy-start.3 = (bf16[2,128,512]{2,1,0:T(8,128)(2,1)}, bf16[2,128,512]{2,1,0:T(8,128)(2,1)S(1)}, u32[]{:S(2)}) copy-start(bf16[2,128,512]{2,1,0:T(8,128)(2,1)S(1)} %constant_dynamic-update-slice_fusion.refs_0_) | copy-start | bytes 786436
  1.6 10.5 %collective-permute-start = (bf16[2,128,512]{2,1,0:T(8,128)(2,1)S(1)}, bf16[2,128,512]{2,1,0:T(8,128)(2,1)S(1)}, u32[]{:S(2)}, u32[]{:S(2)}) collective-permute-start(bf16[2,128,512]{2,1,0:T(8,128)(2,1)S(1)} %constant_dynamic-update-slice_fusion.refs_0_), channel_id=1, source_target_pairs={{0,4},{4,8},{8,12},{1,5},{5,9},{9,13},{2,6},{6,10},{10,14},{3,7},{... | collective-permute-start | bytes 786440 | tf_op jit(solution)/shard_map/ppermute | solution.py:28
  6.9 0.7 copy-start.5
  7.8 12.1 %copy-start.4 = (s32[1,2,16,8]{2,3,1,0:T(8,128)S(1)}, s32[1,2,16,8]{2,3,1,0:T(8,128)}, u32[]{:S(2)}) copy-start(s32[1,2,16,8]{2,3,1,0:T(8,128)} %param.10) | copy-start | bytes 3076
  12.1 9.6 %copy-start.7 = (bf16[2,128,512]{2,1,0:T(8,128)(2,1)}, bf16[2,128,512]{2,1,0:T(8,128)(2,1)S(1)}, u32[]{:S(2)}) copy-start(bf16[2,128,512]{2,1,0:T(8,128)(2,1)S(1)} %collective-permute-done.refs_1_) | copy-start | bytes 786436
  12.1 13.2 %collective-permute-start.2 = (bf16[2,128,512]{2,1,0:T(8,128)(2,1)S(1)}, bf16[2,128,512]{2,1,0:T(8,128)(2,1)S(1)}, u32[]{:S(2)}, u32[]{:S(2)}) collective-permute-start(bf16[2,128,512]{2,1,0:T(8,128)(2,1)S(1)} %constant_dynamic-update-slice_fusion.refs_0_), channel_id=1, source_target_pairs={{0,12},{1,13},{2,14},{3,15},{16,28},{17,29},{18,30},{19,31}} | collective-permute-start | bytes 786440 | tf_op jit(solution)/shard_map/ppermute | solution.py:28
  18.5 10.3 %collective-permute-start.1 = (bf16[2,128,512]{2,1,0:T(8,128)(2,1)S(1)}, bf16[2,128,512]{2,1,0:T(8,128)(2,1)S(1)}, u32[]{:S(2)}, u32[]{:S(2)}) collective-permute-start(bf16[2,128,512]{2,1,0:T(8,128)(2,1)S(1)} %collective-permute-done.refs_1_), channel_id=1, source_target_pairs={{0,4},{4,8},{8,12},{1,5},{5,9},{9,13},{2,6},{6,10},{10,14},{3,7},{... | collective-permute-start | bytes 786440 | tf_op jit(solution)/shard_map/ppermute | solution.py:28
  25.3 3.6 %copy-start.8 = (bf16[2,128,512]{2,1,0:T(8,128)(2,1)}, bf16[2,128,512]{2,1,0:T(8,128)(2,1)S(1)}, u32[]{:S(2)}) copy-start(bf16[2,128,512]{2,1,0:T(8,128)(2,1)S(1)} %collective-permute-done.2.refs_3_) | copy-start | bytes 786436
  28.9 0.7 copy-start.9
  37.0 11.7 %copy-start.6 = (bf16[128,2048]{1,0:T(8,128)(2,1)S(1)}, bf16[128,2048]{1,0:T(8,128)(2,1)}, u32[]{:S(2)}) copy-start(bf16[128,2048]{1,0:T(8,128)(2,1)} %get-tuple-element.21) | copy-start | bytes 1572868
  37.1 9.3 %collective-permute-start.3 = (bf16[2,128,512]{2,1,0:T(8,128)(2,1)}, bf16[2,128,512]{2,1,0:T(8,128)(2,1)S(1)}, u32[]{:S(2)}, u32[]{:S(2)}) collective-permute-start(bf16[2,128,512]{2,1,0:T(8,128)(2,1)} %get-tuple-element.20), channel_id=1, source_target_pairs={{4,0},{8,4},{12,8},{5,1},{9,5},{13,9},{6,2},{10,6},{14,10},{7,3},{... | collective-permute-start | bytes 786440 | tf_op jit(solution)/shard_map/ppermute | solution.py:28
  38.5 18.6 %collective-permute-start.5 = (bf16[1,128,2048]{2,1,0:T(8,128)(2,1)}, bf16[1,128,2048]{2,1,0:T(8,128)(2,1)S(1)}, u32[]{:S(2)}, u32[]{:S(2)}) collective-permute-start(bf16[1,128,2048]{2,1,0:T(8,128)(2,1)} %bitcast.26), channel_id=1, source_target_pairs={{0,16},{16,0},{1,17},{17,1},{2,18},{18,2},{3,19},{19,3},{4,20},{20... | collective-permute-start | bytes 1572872 | tf_op jit(solution)/shard_map/ppermute | solution.py:22
  46.3 9.3 %copy-start.1 = (bf16[2,128,512]{2,1,0:T(8,128)(2,1)S(1)}, bf16[2,128,512]{2,1,0:T(8,128)(2,1)}, u32[]{:S(2)}) copy-start(bf16[2,128,512]{2,1,0:T(8,128)(2,1)} %get-tuple-element.23) | copy-start | bytes 786436
  47.4 8.3 %collective-permute-start.6 = (bf16[2,128,512]{2,1,0:T(8,128)(2,1)S(1)}, bf16[2,128,512]{2,1,0:T(8,128)(2,1)S(1)}, u32[]{:S(2)}, u32[]{:S(2)}) collective-permute-start(bf16[2,128,512]{2,1,0:T(8,128)(2,1)S(1)} %add_convert_fusion.2), channel_id=1, source_target_pairs={{4,0},{8,4},{12,8},{5,1},{9,5},{13,9},{6,2},{10,6},{14,10},{7,3},{... | collective-permute-start | bytes 786440 | tf_op jit(solution)/shard_map/ppermute | solution.py:28
  48.7 13.2 %collective-permute-start.4 = (bf16[1,128,2048]{2,1,0:T(8,128)(2,1)S(1)}, bf16[1,128,2048]{2,1,0:T(8,128)(2,1)S(1)}, u32[]{:S(2)}, u32[]{:S(2)}) collective-permute-start(bf16[1,128,2048]{2,1,0:T(8,128)(2,1)S(1)} %bitcast.25), channel_id=1, source_target_pairs={{0,16},{16,0},{1,17},{17,1},{2,18},{18,2},{3,19},{19,3},{4,20},{20... | collective-permute-start | bytes 1572872 | tf_op jit(solution)/shard_map/ppermute | solution.py:22
  55.7 8.3 %collective-permute-start.7 = (bf16[2,128,512]{2,1,0:T(8,128)(2,1)S(1)}, bf16[2,128,512]{2,1,0:T(8,128)(2,1)S(1)}, u32[]{:S(2)}, u32[]{:S(2)}) collective-permute-start(bf16[2,128,512]{2,1,0:T(8,128)(2,1)S(1)} %add_convert_fusion.1), channel_id=1, source_target_pairs={{4,0},{8,4},{12,8},{5,1},{9,5},{13,9},{6,2},{10,6},{14,10},{7,3},{... | collective-permute-start | bytes 786440 | tf_op jit(solution)/shard_map/ppermute | solution.py:28
  57.9 6.1 %copy-start = (bf16[2,128,512]{2,1,0:T(8,128)(2,1)S(1)}, bf16[2,128,512]{2,1,0:T(8,128)(2,1)}, u32[]{:S(2)}) copy-start(bf16[2,128,512]{2,1,0:T(8,128)(2,1)} %get-tuple-element.28) | copy-start | bytes 786436
  64.1 6.4 %collective-permute-start.8 = (bf16[2,128,512]{2,1,0:T(8,128)(2,1)S(1)}, bf16[2,128,512]{2,1,0:T(8,128)(2,1)S(1)}, u32[]{:S(2)}, u32[]{:S(2)}) collective-permute-start(bf16[2,128,512]{2,1,0:T(8,128)(2,1)S(1)} %add_convert_fusion), channel_id=1, source_target_pairs={{0,16},{16,0},{1,17},{17,1},{2,18},{18,2},{3,19},{19,3},{4,20},{20... | collective-permute-start | bytes 786440 | tf_op jit(solution)/shard_map/ppermute | solution.py:22
